TPU v7x, 32 devices: a whole 2x2x4 slice. The times are simulated.
32 devices in a mesh: ctx: 16 (over z, x, core), head: 2 (over y).
Axes of the slice: x: 2, y: 2, z: 4, core: 2. Of those that a mesh axis runs over, the one named last changes fastest.
Arguments:
- queries: bfloat16 [8192, 1024], P('ctx', 'head'), may hold values from -6 to 6
- key_rows: bfloat16 [8192, 1024], P('ctx', 'head'), may hold values from -6 to 6
- values: bfloat16 [8192, 1024], P('ctx', 'head'), may hold values from -6 to 6
- outputs: bfloat16 [8192, 1024], P('ctx', 'head'), may hold values from -6 to 6
- out_grad: bfloat16 [8192, 1024], P('ctx', 'head'), may hold values from -48 to 48
- log_norm: bfloat16 [8, 8192], P('head', 'ctx'), may hold values from 4.5 to 7.5
- rand_blocks: int32 [64, 3], P('ctx'), may hold values from -1 to 61, as said below
Outputs:
- query_grad: bfloat16 [8192, 1024], P('ctx', 'head')
- key_grad: bfloat16 [8192, 1024], P('ctx', 'head')
- value_grad: bfloat16 [8192, 1024], P('ctx', 'head')
Inputs may be any that keep to these rules, and one draw needn't show every extreme that they name: `rand_blocks`: an entry of row j is a sequence block index of a key block for the query block of row j, or -1 for none. A named block lies between 1 and that query block's sequence index minus 2; the blocks named in the 4 rows of one index of ctx lie on distinct indices of ctx, none of them index 0.
All inputs are finite; a program needn't handle non-finite values.
Results may differ from a plain program's by a relative error of at most 0.0065.
Values may be sent and summed in bfloat16 or wider, within the bound.
No kernel may reach another device: no remote copies, remote signals or barrier semaphores. Data moves between devices by JAX's collectives and lax.ppermute only.
A program may use at most 128 MiB of HBM per device.

v0:
```python
import functools

import jax
import jax.numpy as jnp
from jax import lax
from jax.experimental import pallas as pl
from jax.experimental.pallas import tpu as pltpu
from jax.sharding import PartitionSpec as P

PAIR = 2
WINDOW = 2
GLOBAL = 1
RANDOM = 3
KINDS = 3
STAT_ROWS = 16


def spread_2(array, axis, root):
    count = lax.axis_size(axis)
    mine = lax.axis_index(axis) == root
    array = jnp.where(mine, array, jnp.zeros_like(array))
    step = 1
    while step < count:
        pairs = [(i, i + step) for i in range(step) if i + step < count]
        array = array + lax.ppermute(array, axis, pairs)
        step *= 2
    return array


def gather_to_root(array, axis):
    count = lax.axis_size(axis)
    step = 1
    while step * 2 < count:
        step *= 2
    while step >= 1:
        pairs = [(i + step, i) for i in range(step) if i + step < count]
        array = array + lax.ppermute(array, axis, pairs)
        step //= 2
    return array


def shift(array, axis, offset):
    count = lax.axis_size(axis)
    pairs = [(i, i + offset) for i in range(count) if 0 <= i + offset < count]
    return lax.ppermute(array, axis, pairs)


def pair_math(q, do, k, v, nrm, dlt, mode):
    scale = q.shape[-1] ** (-0.5)
    nt = (((1,), (1,)), ((), ()))
    s_t = lax.dot_general(k, q, nt, preferred_element_type=jnp.float32) * scale
    rows = lax.broadcasted_iota(jnp.int32, s_t.shape, 0)
    cols = lax.broadcasted_iota(jnp.int32, s_t.shape, 1)
    full = (mode == 1).astype(jnp.float32)
    causal = (mode == 2).astype(jnp.float32)
    visible = full + causal * (rows <= cols).astype(jnp.float32)
    p_t = jnp.exp(s_t - nrm) * visible
    dv = jnp.dot(p_t.astype(jnp.bfloat16), do, preferred_element_type=jnp.float32)
    dp_t = lax.dot_general(v, do, nt, preferred_element_type=jnp.float32)
    ds_t = (p_t * (dp_t - dlt)).astype(jnp.bfloat16)
    dk = jnp.dot(ds_t, q, preferred_element_type=jnp.float32) * scale
    ds = jnp.transpose(ds_t.astype(jnp.float32)).astype(jnp.bfloat16)
    dq = jnp.dot(ds, k, preferred_element_type=jnp.float32) * scale
    return dq, dk, dv


def local_kernel(ktab, mtab, q_ref, do_ref, nrm_ref, dlt_ref, k_ref, v_ref, dq_ref, dk_ref, dv_ref):
    b = pl.program_id(0)
    kind = pl.program_id(1)
    mode = mtab[b * KINDS + kind]
    heads = nrm_ref.shape[0]
    width = q_ref.shape[1] // heads
    for h in range(heads):
        cols = slice(h * width, (h + 1) * width)
        dq, dk, dv = pair_math(
            q_ref[:, cols], do_ref[:, cols], k_ref[:, cols], v_ref[:, cols],
            nrm_ref[h], dlt_ref[h], mode,
        )

        @pl.when(kind == 0)
        def _():
            dq_ref[:, cols] = dq

        @pl.when(kind > 0)
        def _():
            dq_ref[:, cols] += dq

        dk_ref[:, cols] = dk
        dv_ref[:, cols] = dv


def rand_kernel(heads, ktab, mtab, q_ref, do_ref, st_ref, k_ref, v_ref, dq_ref, dk_ref, dv_ref):
    p = pl.program_id(0)
    mode = mtab[p]
    width = q_ref.shape[2] // heads
    for h in range(heads):
        cols = slice(h * width, (h + 1) * width)
        stats = st_ref[0, :, cols].astype(jnp.float32)
        dq, dk, dv = pair_math(
            q_ref[0, :, cols], do_ref[0, :, cols], k_ref[:, cols], v_ref[:, cols],
            stats[0:1, :], stats[1:2, :], mode,
        )
        dq_ref[0, :, cols] = dq.astype(jnp.bfloat16)
        dk_ref[0, :, cols] = dk
        dv_ref[0, :, cols] = dv


def local_pairs(ktab, mtab, queries, out_grad, norm3, delta3, key_cat, value_cat):
    slot_count = 2 * PAIR
    rows, features = queries.shape
    height = rows // slot_count
    heads = norm3.shape[0]
    blk = (height, features)
    stat = (heads, 1, height)
    grid_spec = pltpu.PrefetchScalarGridSpec(
        num_scalar_prefetch=2,
        grid=(slot_count, KINDS),
        in_specs=[
            pl.BlockSpec(blk, lambda b, c, kt, mt: (b, 0)),
            pl.BlockSpec(blk, lambda b, c, kt, mt: (b, 0)),
            pl.BlockSpec(stat, lambda b, c, kt, mt: (0, 0, b)),
            pl.BlockSpec(stat, lambda b, c, kt, mt: (0, 0, b)),
            pl.BlockSpec(blk, lambda b, c, kt, mt: (kt[b * KINDS + c], 0)),
            pl.BlockSpec(blk, lambda b, c, kt, mt: (kt[b * KINDS + c], 0)),
        ],
        out_specs=[
            pl.BlockSpec(blk, lambda b, c, kt, mt: (b, 0)),
            pl.BlockSpec(blk, lambda b, c, kt, mt: (b * KINDS + c, 0)),
            pl.BlockSpec(blk, lambda b, c, kt, mt: (b * KINDS + c, 0)),
        ],
    )
    return pl.pallas_call(
        local_kernel,
        grid_spec=grid_spec,
        out_shape=[
            jax.ShapeDtypeStruct((rows, features), jnp.float32),
            jax.ShapeDtypeStruct((rows * KINDS, features), jnp.float32),
            jax.ShapeDtypeStruct((rows * KINDS, features), jnp.float32),
        ],
    )(ktab, mtab, queries, out_grad, norm3, delta3, key_cat, value_cat)


def rand_pairs(ktab, mtab, arrived, key_rows, value_rows, heads):
    items, packed_rows, features = arrived.shape
    height = (packed_rows - STAT_ROWS) // 2
    grid_spec = pltpu.PrefetchScalarGridSpec(
        num_scalar_prefetch=2,
        grid=(items,),
        in_specs=[
            pl.BlockSpec((1, height, features), lambda p, kt, mt: (p, 0, 0)),
            pl.BlockSpec((1, height, features), lambda p, kt, mt: (p, 1, 0)),
            pl.BlockSpec(
                (1, STAT_ROWS, features), lambda p, kt, mt: (p, 2 * height // STAT_ROWS, 0)
            ),
            pl.BlockSpec((height, features), lambda p, kt, mt: (kt[p], 0)),
            pl.BlockSpec((height, features), lambda p, kt, mt: (kt[p], 0)),
        ],
        out_specs=[
            pl.BlockSpec((1, height, features), lambda p, kt, mt: (p, 0, 0)),
            pl.BlockSpec((1, height, features), lambda p, kt, mt: (p, 0, 0)),
            pl.BlockSpec((1, height, features), lambda p, kt, mt: (p, 0, 0)),
        ],
    )
    return pl.pallas_call(
        functools.partial(rand_kernel, heads),
        grid_spec=grid_spec,
        out_shape=[
            jax.ShapeDtypeStruct((items, height, features), jnp.bfloat16),
            jax.ShapeDtypeStruct((items, height, features), jnp.float32),
            jax.ShapeDtypeStruct((items, height, features), jnp.float32),
        ],
    )(ktab, mtab, arrived, arrived, arrived, key_rows, value_rows)


def shards(queries, key_rows, values, outputs, out_grad, log_norm, rand_blocks):
    ctx_size = lax.axis_size("ctx")
    my_index = lax.axis_index("ctx")
    row_count, features = queries.shape
    heads = log_norm.shape[0]
    slot_count = 2 * PAIR
    height = row_count // slot_count
    block_total = slot_count * ctx_size
    first_dev = my_index == 0
    last_dev = my_index == ctx_size - 1

    delta = jnp.sum(
        (out_grad.astype(jnp.float32) * outputs.astype(jnp.float32)).reshape(
            row_count, heads, features // heads
        ),
        axis=-1,
    )
    delta = jnp.transpose(delta).astype(jnp.bfloat16)
    norm3 = log_norm.astype(jnp.float32).reshape(heads, 1, row_count)
    delta3 = delta.astype(jnp.float32).reshape(heads, 1, row_count)

    def block(array, slot):
        return array[slot * height : (slot + 1) * height]

    from_left = shift(jnp.stack([block(key_rows, 1), block(values, 1)]), "ctx", 1)
    from_right = shift(jnp.stack([block(key_rows, 2), block(values, 2)]), "ctx", -1)
    global_kv = spread_2(jnp.stack([block(key_rows, 0), block(values, 0)]), "ctx", 0)
    key_cat = jnp.concatenate([key_rows, from_left[0], from_right[0], global_kv[0]])
    value_cat = jnp.concatenate([values, from_left[1], from_right[1], global_kv[1]])

    within = jnp.arange(slot_count, dtype=jnp.int32)
    seq_blk = jnp.where(
        within < PAIR, PAIR * my_index + within, block_total - 1 - PAIR * my_index - (within - PAIR)
    )
    last_prev = jnp.where(last_dev, 1, slot_count + 1).astype(jnp.int32)
    glob_slot = slot_count + 2
    ktab = jnp.stack(
        [
            jnp.int32(0), jnp.int32(slot_count), jnp.int32(glob_slot),
            jnp.int32(1), jnp.int32(0), jnp.int32(glob_slot),
            jnp.int32(2), jnp.int32(3), jnp.int32(glob_slot),
            jnp.int32(3), last_prev, jnp.int32(glob_slot),
        ]
    )
    glob_mode = (seq_blk >= WINDOW).astype(jnp.int32)
    first_prev = jnp.where(first_dev, 0, 1).astype(jnp.int32)
    mtab = jnp.stack(
        [
            jnp.int32(2), first_prev, glob_mode[0],
            jnp.int32(2), jnp.int32(1), glob_mode[1],
            jnp.int32(2), jnp.int32(1), glob_mode[2],
            jnp.int32(2), jnp.int32(1), glob_mode[3],
        ]
    )
    dq_local, dk_terms, dv_terms = local_pairs(
        ktab, mtab, queries, out_grad, norm3, delta3, key_cat, value_cat
    )
    dk_terms = dk_terms.reshape(slot_count, KINDS, height, features)
    dv_terms = dv_terms.reshape(slot_count, KINDS, height, features)

    ref_valid = rand_blocks >= 0
    in_front = rand_blocks < block_total // 2
    mirror = block_total - 1 - rand_blocks
    owner_dev = jnp.where(in_front, rand_blocks // PAIR, mirror // PAIR)
    owner_dev = jnp.where(ref_valid, owner_dev, ctx_size).reshape(-1)
    key_slot = jnp.where(in_front, rand_blocks % PAIR, PAIR + mirror % PAIR) + 1
    key_slot = jnp.where(ref_valid, key_slot, 0).reshape(-1)
    targets = jnp.arange(ctx_size, dtype=jnp.int32)
    matches = owner_dev[None, :] == targets[:, None]
    slot_send = jnp.sum(jnp.where(matches, key_slot[None, :], 0), axis=1)
    select = jnp.any(matches.reshape(ctx_size, slot_count, RANDOM), axis=2).astype(jnp.bfloat16)

    def per_slot_row(stat):
        return jnp.transpose(stat.reshape(heads, slot_count, height), (1, 0, 2)).reshape(
            slot_count, 1, features
        )

    packed = jnp.concatenate(
        [
            queries.reshape(slot_count, height, features),
            out_grad.reshape(slot_count, height, features),
            per_slot_row(log_norm),
            per_slot_row(delta),
        ],
        axis=1,
    )
    routed = jnp.dot(
        select, packed.reshape(slot_count, -1), preferred_element_type=jnp.float32
    ).astype(jnp.bfloat16)
    routed = routed.reshape(ctx_size, 2 * height + 2, features)
    slot_rows = jnp.broadcast_to(
        slot_send.astype(jnp.bfloat16)[:, None, None], (ctx_size, STAT_ROWS - 2, features)
    )
    routed = jnp.concatenate([routed, slot_rows], axis=1)
    arrived = lax.all_to_all(routed, "ctx", split_axis=0, concat_axis=0, tiled=True)
    slot_recv = arrived[:, 2 * height + 2, 0].astype(jnp.float32).astype(jnp.int32)
    ktab_r = jnp.maximum(slot_recv - 1, 0)
    mtab_r = (slot_recv > 0).astype(jnp.int32)
    dq_rand, dk_rand, dv_rand = rand_pairs(ktab_r, mtab_r, arrived, key_rows, values, heads)
    returned = lax.all_to_all(dq_rand, "ctx", split_axis=0, concat_axis=0, tiled=True)
    select_f = select.astype(jnp.float32)
    rand_query = jnp.sum(
        select_f[:, :, None, None] * returned.astype(jnp.float32)[:, None], axis=0
    )
    choose = (slot_recv[:, None] == jnp.arange(1, slot_count + 1)[None, :]).astype(jnp.float32)
    rand_key = jnp.sum(choose[:, :, None, None] * dk_rand[:, None], axis=0)
    rand_value = jnp.sum(choose[:, :, None, None] * dv_rand[:, None], axis=0)

    to_left = jnp.stack([dk_terms[0, 1], dv_terms[0, 1]]).astype(jnp.bfloat16)
    to_right = jnp.stack([dk_terms[slot_count - 1, 1], dv_terms[slot_count - 1, 1]]).astype(
        jnp.bfloat16
    )
    back_right = shift(to_left, "ctx", -1).astype(jnp.float32)
    back_left = shift(to_right, "ctx", 1).astype(jnp.float32)
    own_tail = jnp.where(last_dev, 1.0, 0.0).astype(jnp.float32)

    part = jnp.stack([jnp.sum(dk_terms[:, 2], axis=0), jnp.sum(dv_terms[:, 2], axis=0)])
    total = gather_to_root(part, "ctx")
    owner_flag = jnp.where(first_dev, 1.0, 0.0).astype(jnp.float32)

    def assemble(terms, which, rand_part):
        slots = [
            terms[0, 0] + terms[1, 1] + total[which] * owner_flag,
            terms[1, 0] + terms[slot_count - 1, 1] * own_tail + back_right[which],
            terms[2, 0] + back_left[which],
            terms[3, 0] + terms[2, 1],
        ]
        whole = jnp.stack(slots) + rand_part
        return whole.reshape(row_count, features).astype(jnp.bfloat16)

    query_total = (dq_local + rand_query.reshape(row_count, features)).astype(jnp.bfloat16)
    return (
        query_total,
        assemble(dk_terms, 0, rand_key),
        assemble(dv_terms, 1, rand_value),
    )


def solution(mesh):
    return jax.shard_map(
        shards,
        mesh=mesh,
        in_specs=(
            P("ctx", "head"),
            P("ctx", "head"),
            P("ctx", "head"),
            P("ctx", "head"),
            P("ctx", "head"),
            P("head", "ctx"),
            P("ctx", None),
        ),
        out_specs=(P("ctx", "head"), P("ctx", "head"), P("ctx", "head")),
        check_vma=False,
    )
```

profile of v0, /device:TPU:1, one launch (start us, length us, event | category | flops | bytes accessed | tf_op | source)
XLA Modules:
  0.0 295.2 jit_solution(12773947102655954220)
XLA Ops:
  2.6 1.3 convert_multiply_fusion
  5.8 3.0 %convolution_convert_fusion = bf16[16,132096]{1,0:T(8,128)(2,1)} fusion(pred[16,4]{0,1:T(4,128)(4,1)S(1)} %fusion.17, bf16[4,132096]{1,0:T(4,128)(2,1)S(1)} %bitcast.89), kind=kOutput, calls=%fused_computation | convolution fusion | flops 19021824 | bytes 5283904 | tf_op jit(solution)/shard_map/dot_general | solution.py:261
  8.9 4.9 %reshape.249 = bf16[16,258,512]{2,1,0:T(8,128)(2,1)} reshape(bf16[16,132096]{1,0:T(8,128)(2,1)} %convolution_convert_fusion) | data formatting | bytes 8454144 | tf_op jit(solution)/shard_map/reshape | solution.py:264
  13.9 4.9 %pad_maximum_fusion = bf16[16,272,512]{2,1,0:T(8,128)(2,1)} fusion(bf16[16,14,512]{2,1,0:T(8,128)(2,1)S(1)} %broadcast_in_dim.42, bf16[16,258,512]{2,1,0:T(8,128)(2,1)} %reshape.249), kind=kLoop, calls=%fused_computation.4 | loop fusion | flops 8912896 | bytes 8912896 | tf_op jit(solution)/shard_map/concatenate | solution.py:268
  18.7 7.5 %all-to-all-start = ((bf16[16,272,512]{2,1,0:T(8,128)(2,1)}), bf16[16,272,512]{2,1,0:T(8,128)(2,1)}, u32[]{:S(2)}, u32[]{:S(2)}) async-start(bf16[16,272,512]{2,1,0:T(8,128)(2,1)} %pad_maximum_fusion), calls=%async_computation | async-start | bytes 8912896 | tf_op jit(solution)/shard_map/all_to_all | solution.py:269
  27.6 2.1 collective-permute-done.2
  31.2 2.0 collective-permute-start.1
  33.2 3.5 %collective-permute-start = (bf16[2,128,512]{2,1,0:T(8,128)(2,1)S(1)}, bf16[2,128,512]{2,1,0:T(8,128)(2,1)S(1)}, u32[]{:S(2)}, u32[]{:S(2)}) collective-permute-start(bf16[2,128,512]{2,1,0:T(8,128)(2,1)S(1)} %pad_maximum_fusion.4), channel_id=1, source_target_pairs={{0,2},{2,4},{4,6},{6,8},{8,10},{10,12},{12,14},{14,16},{16,18},{18... | collective-permute-start | bytes 786440 | tf_op jit(solution)/shard_map/ppermute | solution.py:45
  36.8 19.4 %collective-permute-done.3 = bf16[2,128,512]{2,1,0:T(8,128)(2,1)S(1)} collective-permute-done((bf16[2,128,512]{2,1,0:T(8,128)(2,1)S(1)}, bf16[2,128,512]{2,1,0:T(8,128)(2,1)S(1)}, u32[]{:S(2)}, u32[]{:S(2)}) %collective-permute-start.3) | collective-permute-done | bytes 262176 | tf_op jit(solution)/shard_map/ppermute | solution.py:25
  60.0 3.1 %stack.73.mtab = s32[12]{0:T(128)} concatenate(s32[1]{0:T(128)} %constant.69.clone.1, s32[1]{0:T(128)} %bitcast.1, s32[1]{0:T(128)} %get-tuple-element.47, s32[1]{0:T(128)} %constant.69.clone.1, s32[1]{0:T(128)} %constant.68.clone.1, s32[1]{0:T(128)} %get-tuple-element.46, s32[1]{0:T(128)} %constant.69.clone.1, s32[1]{0:T(128)} %constant.68.clone.1, s32[1]{0:T(128)} %get-tuple-element.45, ...), dimensions={0} | concatenate | bytes 96 | tf_op jit(solution)/shard_map/stack | solution.py:221
  63.1 41.1 %collective-permute-done.4 = bf16[2,128,512]{2,1,0:T(8,128)(2,1)S(1)} collective-permute-done((bf16[2,128,512]{2,1,0:T(8,128)(2,1)S(1)}, bf16[2,128,512]{2,1,0:T(8,128)(2,1)S(1)}, u32[]{:S(2)}, u32[]{:S(2)}) %collective-permute-start.4) | collective-permute-done | bytes 262176 | tf_op jit(solution)/shard_map/ppermute | solution.py:25
  105.6 5.3 %collective-permute-done.5 = bf16[2,128,512]{2,1,0:T(8,128)(2,1)S(1)} collective-permute-done((bf16[2,128,512]{2,1,0:T(8,128)(2,1)S(1)}, bf16[2,128,512]{2,1,0:T(8,128)(2,1)S(1)}, u32[]{:S(2)}, u32[]{:S(2)}) %collective-permute-start.5) | collective-permute-done | bytes 262176 | tf_op jit(solution)/shard_map/ppermute | solution.py:25
  113.1 30.2 %shard_map.94 = (f32[512,512]{1,0:T(8,128)}, f32[1536,512]{1,0:T(8,128)}, f32[1536,512]{1,0:T(8,128)}) custom-call(s32[12]{0:T(128)} %stack.71.ktab, s32[12]{0:T(128)} %stack.73.mtab, bf16[512,512]{1,0:T(8,128)(2,1)} %q_ref.1, bf16[512,512]{1,0:T(8,128)(2,1)} %do_ref.1, f32[4,1,512]{2,1,0:T(1,128)} %reshape.254.nrm_ref, f32[4,1,512]{2,1,0:T(1,128)} %reshape.256.dlt_ref, ...), custom_call_target="tpu_custom_call" | custom-call | tf_op jit(solution)/shard_map/pallas_call | solution.py:132
  150.3 24.4 %shard_map.95 = (bf16[16,128,512]{2,1,0:T(8,128)(2,1)}, f32[16,128,512]{2,1,0:T(8,128)}, f32[16,128,512]{2,1,0:T(8,128)}) custom-call(s32[16]{0:T(128)} %add_maximum_fusion.ktab, s32[16]{0:T(128)} %compare_convert_fusion.1.mtab, bf16[16,272,512]{2,1,0:T(8,128)(2,1)} %all-to-all-done.q_ref.do_ref.st_ref, ...), custom_call_target="tpu_custom_call" | custom-call | tf_op jit(solution)/shard_map/pallas_call | solution.py:164
  174.6 32.2 %all-to-all-start.1 = ((bf16[16,128,512]{2,1,0:T(8,128)(2,1)}), bf16[16,128,512]{2,1,0:T(8,128)(2,1)S(1)}, u32[]{:S(2)}, u32[]{:S(2)}) async-start(bf16[16,128,512]{2,1,0:T(8,128)(2,1)} %get-tuple-element.10), calls=%async_computation.1 | async-start | bytes 4194304 | tf_op jit(solution)/shard_map/all_to_all | solution.py:274
  209.1 45.1 %collective-permute-done.7 = f32[2,128,512]{2,1,0:T(8,128)} collective-permute-done((f32[2,128,512]{2,1,0:T(8,128)}, f32[2,128,512]{2,1,0:T(8,128)}, u32[]{:S(2)}, u32[]{:S(2)}) %collective-permute-start.7) | collective-permute-done | bytes 524320 | tf_op jit(solution)/shard_map/ppermute | solution.py:37
  258.9 5.1 %collective-permute-start.11 = (bf16[2,128,512]{2,1,0:T(8,128)(2,1)S(1)}, bf16[2,128,512]{2,1,0:T(8,128)(2,1)S(1)}, u32[]{:S(2)}, u32[]{:S(2)}) collective-permute-start(bf16[2,128,512]{2,1,0:T(8,128)(2,1)S(1)} %pad_maximum_fusion.7), channel_id=1, source_target_pairs={{0,2},{2,4},{4,6},{6,8},{8,10},{10,12},{12,14},{14,16},{16,18},{18... | collective-permute-start | bytes 786440 | tf_op jit(solution)/shard_map/ppermute | solution.py:45
  264.0 5.9 %collective-permute-done.8 = f32[2,128,512]{2,1,0:T(8,128)S(1)} collective-permute-done((f32[2,128,512]{2,1,0:T(8,128)S(1)}, f32[2,128,512]{2,1,0:T(8,128)S(1)}, u32[]{:S(2)}, u32[]{:S(2)}) %collective-permute-start.8) | collective-permute-done | bytes 524320 | tf_op jit(solution)/shard_map/ppermute | solution.py:37
  270.0 3.7 %collective-permute-start.9 = (f32[2,128,512]{2,1,0:T(8,128)S(1)}, f32[2,128,512]{2,1,0:T(8,128)S(1)}, u32[]{:S(2)}, u32[]{:S(2)}) collective-permute-start(f32[2,128,512]{2,1,0:T(8,128)S(1)} %add.181), channel_id=1, source_target_pairs={{2,0},{3,1}} | collective-permute-start | bytes 1572872 | tf_op jit(solution)/shard_map/ppermute | solution.py:37
  273.8 2.1 collective-permute-start.10
  276.0 5.4 %collective-permute-done.10 = bf16[2,128,512]{2,1,0:T(8,128)(2,1)S(1)} collective-permute-done((bf16[2,128,512]{2,1,0:T(8,128)(2,1)S(1)}, bf16[2,128,512]{2,1,0:T(8,128)(2,1)S(1)}, u32[]{:S(2)}, u32[]{:S(2)}) %collective-permute-start.10) | collective-permute-done | bytes 262176 | tf_op jit(solution)/shard_map/ppermute | solution.py:45
  284.1 5.1 %multiply_reduce_fusion = (f32[4,128,512]{2,1,0:T(8,128)S(1)}, f32[4,128,512]{2,1,0:T(8,128)S(1)}) fusion(f32[16,128,512]{2,1,0:T(8,128)} %get-tuple-element.14, f32[16,4]{1,0:T(8,128)S(1)} %compare_convert_fusion, f32[16,128,512]{2,1,0:T(8,128)S(1)} %copy-done.1), kind=kLoop, calls=%fused_computation.1 | loop fusion | flops 16252928 | bytes 10486016 | tf_op jit(solution)/shard_map/reduce_sum | solution.py:281
  289.2 2.1 fusion
  292.8 1.4 multiply_reduce_fusion.2
  (92 shorter events, 33.3 us)
Async XLA Ops:
  0.6 4.5 %copy-start = (bf16[512,512]{1,0:T(8,128)(2,1)S(1)}, bf16[512,512]{1,0:T(8,128)(2,1)}, u32[]{:S(2)}) copy-start(bf16[512,512]{1,0:T(8,128)(2,1)} %do_ref.1) | copy-start | bytes 1572868
  0.6 4.5 %copy-start.6 = (bf16[512,512]{1,0:T(8,128)(2,1)S(1)}, bf16[512,512]{1,0:T(8,128)(2,1)}, u32[]{:S(2)}) copy-start(bf16[512,512]{1,0:T(8,128)(2,1)} %q_ref.1) | copy-start | bytes 1572868
  18.7 7.5 %copy-start.2 = (bf16[512,512]{1,0:T(8,128)(2,1)S(1)}, bf16[512,512]{1,0:T(8,128)(2,1)}, u32[]{:S(2)}) copy-start(bf16[512,512]{1,0:T(8,128)(2,1)} %v_ref.1) | copy-start | bytes 1572868
  18.7 7.5 %copy-start.3 = (bf16[512,512]{1,0:T(8,128)(2,1)S(1)}, bf16[512,512]{1,0:T(8,128)(2,1)}, u32[]{:S(2)}) copy-start(bf16[512,512]{1,0:T(8,128)(2,1)} %k_ref.1) | copy-start | bytes 1572868
  18.7 129.3 %all-to-all-start = ((bf16[16,272,512]{2,1,0:T(8,128)(2,1)}), bf16[16,272,512]{2,1,0:T(8,128)(2,1)}, u32[]{:S(2)}, u32[]{:S(2)}) async-start(bf16[16,272,512]{2,1,0:T(8,128)(2,1)} %pad_maximum_fusion), calls=%async_computation | async-start | bytes 8912896 | tf_op jit(solution)/shard_map/all_to_all | solution.py:269
  26.2 32.0 %copy-start.8 = (bf16[4,512]{1,0:T(4,128)(2,1)S(1)}, bf16[4,512]{1,0:T(4,128)(2,1)}, u32[]{:S(2)}) copy-start(bf16[4,512]{1,0:T(4,128)(2,1)} %param.12) | copy-start | bytes 12292
  26.3 3.4 %collective-permute-start.2 = (bf16[2,128,512]{2,1,0:T(8,128)(2,1)S(1)}, bf16[2,128,512]{2,1,0:T(8,128)(2,1)S(1)}, u32[]{:S(2)}, u32[]{:S(2)}) collective-permute-start(bf16[2,128,512]{2,1,0:T(8,128)(2,1)S(1)} %maximum_select_fusion), channel_id=1, source_target_pairs={{0,2},{1,3}} | collective-permute-start | bytes 786440 | tf_op jit(solution)/shard_map/ppermute | solution.py:25
  29.8 26.3 %collective-permute-start.3 = (bf16[2,128,512]{2,1,0:T(8,128)(2,1)S(1)}, bf16[2,128,512]{2,1,0:T(8,128)(2,1)S(1)}, u32[]{:S(2)}, u32[]{:S(2)}) collective-permute-start(bf16[2,128,512]{2,1,0:T(8,128)(2,1)S(1)} %fusion.31), channel_id=1, source_target_pairs={{0,4},{2,6},{1,5},{3,7}} | collective-permute-start | bytes 786440 | tf_op jit(solution)/shard_map/ppermute | solution.py:25
  31.2 74.4 %collective-permute-start.1 = (bf16[2,128,512]{2,1,0:T(8,128)(2,1)S(1)}, bf16[2,128,512]{2,1,0:T(8,128)(2,1)S(1)}, u32[]{:S(2)}, u32[]{:S(2)}) collective-permute-start(bf16[2,128,512]{2,1,0:T(8,128)(2,1)S(1)} %pad_maximum_fusion.5), channel_id=1, source_target_pairs={{2,0},{4,2},{6,4},{8,6},{10,8},{12,10},{14,12},{16,14},{18,16},{20... | collective-permute-start | bytes 786440 | tf_op jit(solution)/shard_map/ppermute | solution.py:45
  33.2 72.3 %collective-permute-start = (bf16[2,128,512]{2,1,0:T(8,128)(2,1)S(1)}, bf16[2,128,512]{2,1,0:T(8,128)(2,1)S(1)}, u32[]{:S(2)}, u32[]{:S(2)}) collective-permute-start(bf16[2,128,512]{2,1,0:T(8,128)(2,1)S(1)} %pad_maximum_fusion.4), channel_id=1, source_target_pairs={{0,2},{2,4},{4,6},{6,8},{8,10},{10,12},{12,14},{14,16},{16,18},{18... | collective-permute-start | bytes 786440 | tf_op jit(solution)/shard_map/ppermute | solution.py:45
  56.2 48.0 %collective-permute-start.4 = (bf16[2,128,512]{2,1,0:T(8,128)(2,1)S(1)}, bf16[2,128,512]{2,1,0:T(8,128)(2,1)S(1)}, u32[]{:S(2)}, u32[]{:S(2)}) collective-permute-start(bf16[2,128,512]{2,1,0:T(8,128)(2,1)S(1)} %fusion.32), channel_id=1, source_target_pairs={{0,8},{2,10},{4,12},{6,14},{1,9},{3,11},{5,13},{7,15}} | collective-permute-start | bytes 786440 | tf_op jit(solution)/shard_map/ppermute | solution.py:25
  104.2 6.7 %collective-permute-start.5 = (bf16[2,128,512]{2,1,0:T(8,128)(2,1)S(1)}, bf16[2,128,512]{2,1,0:T(8,128)(2,1)S(1)}, u32[]{:S(2)}, u32[]{:S(2)}) collective-permute-start(bf16[2,128,512]{2,1,0:T(8,128)(2,1)S(1)} %add.170), channel_id=1, source_target_pairs={{0,16},{2,18},{4,20},{6,22},{8,24},{10,26},{12,28},{14,30},{1,17},... | collective-permute-start | bytes 786440 | tf_op jit(solution)/shard_map/ppermute | solution.py:25
  146.8 60.1 %collective-permute-start.6 = (f32[2,128,512]{2,1,0:T(8,128)}, f32[2,128,512]{2,1,0:T(8,128)S(1)}, u32[]{:S(2)}, u32[]{:S(2)}) collective-permute-start(f32[2,128,512]{2,1,0:T(8,128)} %pad_maximum_fusion.3), channel_id=1, source_target_pairs={{16,0},{18,2},{20,4},{22,6},{24,8},{26,10},{28,12},{30,14},{17,1},... | collective-permute-start | bytes 1572872 | tf_op jit(solution)/shard_map/ppermute | solution.py:37
  174.6 117.6 %all-to-all-start.1 = ((bf16[16,128,512]{2,1,0:T(8,128)(2,1)}), bf16[16,128,512]{2,1,0:T(8,128)(2,1)S(1)}, u32[]{:S(2)}, u32[]{:S(2)}) async-start(bf16[16,128,512]{2,1,0:T(8,128)(2,1)} %get-tuple-element.10), calls=%async_computation.1 | async-start | bytes 4194304 | tf_op jit(solution)/shard_map/all_to_all | solution.py:274
  207.7 46.5 %collective-permute-start.7 = (f32[2,128,512]{2,1,0:T(8,128)}, f32[2,128,512]{2,1,0:T(8,128)}, u32[]{:S(2)}, u32[]{:S(2)}) collective-permute-start(f32[2,128,512]{2,1,0:T(8,128)} %fusion.26), channel_id=1, source_target_pairs={{8,0},{10,2},{12,4},{14,6},{9,1},{11,3},{13,5},{15,7}} | collective-permute-start | bytes 1572872 | tf_op jit(solution)/shard_map/ppermute | solution.py:37
  209.1 66.7 %copy-start.4 = (f32[1536,512]{1,0:T(8,128)S(1)}, f32[1536,512]{1,0:T(8,128)}, u32[]{:S(2)}) copy-start(f32[1536,512]{1,0:T(8,128)} %get-tuple-element.11) | copy-start | bytes 9437188
  209.1 66.8 %copy-start.5 = (f32[1536,512]{1,0:T(8,128)S(1)}, f32[1536,512]{1,0:T(8,128)}, u32[]{:S(2)}) copy-start(f32[1536,512]{1,0:T(8,128)} %get-tuple-element.12) | copy-start | bytes 9437188
  255.5 14.5 %collective-permute-start.8 = (f32[2,128,512]{2,1,0:T(8,128)S(1)}, f32[2,128,512]{2,1,0:T(8,128)S(1)}, u32[]{:S(2)}, u32[]{:S(2)}) collective-permute-start(f32[2,128,512]{2,1,0:T(8,128)S(1)} %fusion.30), channel_id=1, source_target_pairs={{4,0},{6,2},{5,1},{7,3}} | collective-permute-start | bytes 1572872 | tf_op jit(solution)/shard_map/ppermute | solution.py:37
  258.9 17.1 %collective-permute-start.11 = (bf16[2,128,512]{2,1,0:T(8,128)(2,1)S(1)}, bf16[2,128,512]{2,1,0:T(8,128)(2,1)S(1)}, u32[]{:S(2)}, u32[]{:S(2)}) collective-permute-start(bf16[2,128,512]{2,1,0:T(8,128)(2,1)S(1)} %pad_maximum_fusion.7), channel_id=1, source_target_pairs={{0,2},{2,4},{4,6},{6,8},{8,10},{10,12},{12,14},{14,16},{16,18},{18... | collective-permute-start | bytes 786440 | tf_op jit(solution)/shard_map/ppermute | solution.py:45
  270.0 11.5 %collective-permute-start.9 = (f32[2,128,512]{2,1,0:T(8,128)S(1)}, f32[2,128,512]{2,1,0:T(8,128)S(1)}, u32[]{:S(2)}, u32[]{:S(2)}) collective-permute-start(f32[2,128,512]{2,1,0:T(8,128)S(1)} %add.181), channel_id=1, source_target_pairs={{2,0},{3,1}} | collective-permute-start | bytes 1572872 | tf_op jit(solution)/shard_map/ppermute | solution.py:37
  273.8 7.7 %collective-permute-start.10 = (bf16[2,128,512]{2,1,0:T(8,128)(2,1)S(1)}, bf16[2,128,512]{2,1,0:T(8,128)(2,1)S(1)}, u32[]{:S(2)}, u32[]{:S(2)}) collective-permute-start(bf16[2,128,512]{2,1,0:T(8,128)(2,1)S(1)} %pad_maximum_fusion.6), channel_id=1, source_target_pairs={{2,0},{4,2},{6,4},{8,6},{10,8},{12,10},{14,12},{16,14},{18,16},{20... | collective-permute-start | bytes 786440 | tf_op jit(solution)/shard_map/ppermute | solution.py:45
  281.6 2.5 copy-start.1
  292.8 1.4 copy-start.7
where the time goes:
time: 296 us; the launch traced here: 295 us
  waiting for transfers between devices  124 us (42%)
  starting transfers between devices  65.2 us (22%)
  Pallas kernels  54.6 us (18%)
  other arithmetic  30.9 us (10%)
  local copies, waits for them, and re-layouts  15.9 us (5%)
  matrix products  3.04 us (1%)
    ppermute x4, waiting for transfers between devices, spread_2(): array = array + lax.ppermute(array, axis, pairs)  68 us
    ppermute x4, waiting for transfers between devices, gather_to_root(): array = array + lax.ppermute(array, axis, pairs)  51.1 us
    all_to_all x1, starting transfers between devices, shards(): lax.all_to_all(dq_rand, 'ctx', split_axis=0, concat_axis=0, tiled=True)  32.2 us
    pallas_call x1, Pallas kernels, local_pairs(): pl.pallas_call(local_kernel, grid_spec=grid_spec, out_shape=[jax.ShapeDty...  30.2 us
    pallas_call x1, Pallas kernels, rand_pairs(): pl.pallas_call(functools.partial(rand_kernel, heads), grid_spec=grid_spec...  24.4 us
    ppermute x4, starting transfers between devices, shift(): return lax.ppermute(array, axis, pairs)  12.7 us
    ppermute x4, starting transfers between devices, gather_to_root(): array = array + lax.ppermute(array, axis, pairs)  7.56 us
    all_to_all x1, starting transfers between devices, shards(): lax.all_to_all(routed, 'ctx', split_axis=0, concat_axis=0, tiled=True)  7.45 us
  transfers between devices with their start and end apart: 14, of which 7 were waited for; matrix products, arithmetic and copies ran while one was open for 9% of the time, Pallas kernels for 18%

commit v1 on v0

--- a/solution.py
+++ b/solution.py
@@ -11,7 +11,6 @@
 WINDOW = 2
 GLOBAL = 1
 RANDOM = 3
-KINDS = 3
 STAT_ROWS = 16
 
 
@@ -64,10 +63,10 @@
     return dq, dk, dv
 
 
-def local_kernel(ktab, mtab, q_ref, do_ref, nrm_ref, dlt_ref, k_ref, v_ref, dq_ref, dk_ref, dv_ref):
+def local_kernel(kinds, ktab, mtab, q_ref, do_ref, nrm_ref, dlt_ref, k_ref, v_ref, dq_ref, dk_ref, dv_ref):
     b = pl.program_id(0)
     kind = pl.program_id(1)
-    mode = mtab[b * KINDS + kind]
+    mode = mtab[b * kinds + kind]
     heads = nrm_ref.shape[0]
     width = q_ref.shape[1] // heads
     for h in range(heads):
@@ -92,7 +91,14 @@
 def rand_kernel(heads, ktab, mtab, q_ref, do_ref, st_ref, k_ref, v_ref, dq_ref, dk_ref, dv_ref):
     p = pl.program_id(0)
     mode = mtab[p]
+    slot = ktab[p]
     width = q_ref.shape[2] // heads
+
+    @pl.when(p == 0)
+    def _():
+        dk_ref[...] = jnp.zeros_like(dk_ref)
+        dv_ref[...] = jnp.zeros_like(dv_ref)
+
     for h in range(heads):
         cols = slice(h * width, (h + 1) * width)
         stats = st_ref[0, :, cols].astype(jnp.float32)
@@ -101,11 +107,14 @@
             stats[0:1, :], stats[1:2, :], mode,
         )
         dq_ref[0, :, cols] = dq.astype(jnp.bfloat16)
-        dk_ref[0, :, cols] = dk
-        dv_ref[0, :, cols] = dv
-
-
-def local_pairs(ktab, mtab, queries, out_grad, norm3, delta3, key_cat, value_cat):
+
+        @pl.when(mode > 0)
+        def _():
+            dk_ref[slot, :, cols] += dk
+            dv_ref[slot, :, cols] += dv
+
+
+def local_pairs(kinds, ktab, mtab, queries, out_grad, norm3, delta3, key_cat, value_cat):
     slot_count = 2 * PAIR
     rows, features = queries.shape
     height = rows // slot_count
@@ -114,28 +123,28 @@
     stat = (heads, 1, height)
     grid_spec = pltpu.PrefetchScalarGridSpec(
         num_scalar_prefetch=2,
-        grid=(slot_count, KINDS),
+        grid=(slot_count, kinds),
         in_specs=[
             pl.BlockSpec(blk, lambda b, c, kt, mt: (b, 0)),
             pl.BlockSpec(blk, lambda b, c, kt, mt: (b, 0)),
             pl.BlockSpec(stat, lambda b, c, kt, mt: (0, 0, b)),
             pl.BlockSpec(stat, lambda b, c, kt, mt: (0, 0, b)),
-            pl.BlockSpec(blk, lambda b, c, kt, mt: (kt[b * KINDS + c], 0)),
-            pl.BlockSpec(blk, lambda b, c, kt, mt: (kt[b * KINDS + c], 0)),
+            pl.BlockSpec(blk, lambda b, c, kt, mt: (kt[b * kinds + c], 0)),
+            pl.BlockSpec(blk, lambda b, c, kt, mt: (kt[b * kinds + c], 0)),
         ],
         out_specs=[
             pl.BlockSpec(blk, lambda b, c, kt, mt: (b, 0)),
-            pl.BlockSpec(blk, lambda b, c, kt, mt: (b * KINDS + c, 0)),
-            pl.BlockSpec(blk, lambda b, c, kt, mt: (b * KINDS + c, 0)),
+            pl.BlockSpec(blk, lambda b, c, kt, mt: (b * kinds + c, 0)),
+            pl.BlockSpec(blk, lambda b, c, kt, mt: (b * kinds + c, 0)),
         ],
     )
     return pl.pallas_call(
-        local_kernel,
+        functools.partial(local_kernel, kinds),
         grid_spec=grid_spec,
         out_shape=[
             jax.ShapeDtypeStruct((rows, features), jnp.float32),
-            jax.ShapeDtypeStruct((rows * KINDS, features), jnp.float32),
-            jax.ShapeDtypeStruct((rows * KINDS, features), jnp.float32),
+            jax.ShapeDtypeStruct((rows * kinds, features), jnp.float32),
+            jax.ShapeDtypeStruct((rows * kinds, features), jnp.float32),
         ],
     )(ktab, mtab, queries, out_grad, norm3, delta3, key_cat, value_cat)
 
@@ -143,6 +152,7 @@
 def rand_pairs(ktab, mtab, arrived, key_rows, value_rows, heads):
     items, packed_rows, features = arrived.shape
     height = (packed_rows - STAT_ROWS) // 2
+    slots = key_rows.shape[0] // height
     grid_spec = pltpu.PrefetchScalarGridSpec(
         num_scalar_prefetch=2,
         grid=(items,),
@@ -157,8 +167,8 @@
         ],
         out_specs=[
             pl.BlockSpec((1, height, features), lambda p, kt, mt: (p, 0, 0)),
-            pl.BlockSpec((1, height, features), lambda p, kt, mt: (p, 0, 0)),
-            pl.BlockSpec((1, height, features), lambda p, kt, mt: (p, 0, 0)),
+            pl.BlockSpec((slots, height, features), lambda p, kt, mt: (0, 0, 0)),
+            pl.BlockSpec((slots, height, features), lambda p, kt, mt: (0, 0, 0)),
         ],
     )
     return pl.pallas_call(
@@ -166,8 +176,8 @@
         grid_spec=grid_spec,
         out_shape=[
             jax.ShapeDtypeStruct((items, height, features), jnp.bfloat16),
-            jax.ShapeDtypeStruct((items, height, features), jnp.float32),
-            jax.ShapeDtypeStruct((items, height, features), jnp.float32),
+            jax.ShapeDtypeStruct((slots, height, features), jnp.float32),
+            jax.ShapeDtypeStruct((slots, height, features), jnp.float32),
         ],
     )(ktab, mtab, arrived, arrived, arrived, key_rows, value_rows)
 
@@ -199,38 +209,57 @@
     from_left = shift(jnp.stack([block(key_rows, 1), block(values, 1)]), "ctx", 1)
     from_right = shift(jnp.stack([block(key_rows, 2), block(values, 2)]), "ctx", -1)
     global_kv = spread_2(jnp.stack([block(key_rows, 0), block(values, 0)]), "ctx", 0)
-    key_cat = jnp.concatenate([key_rows, from_left[0], from_right[0], global_kv[0]])
-    value_cat = jnp.concatenate([values, from_left[1], from_right[1], global_kv[1]])
+    key_win = jnp.concatenate([key_rows, from_left[0], from_right[0]])
+    value_win = jnp.concatenate([values, from_left[1], from_right[1]])
 
     within = jnp.arange(slot_count, dtype=jnp.int32)
     seq_blk = jnp.where(
         within < PAIR, PAIR * my_index + within, block_total - 1 - PAIR * my_index - (within - PAIR)
     )
     last_prev = jnp.where(last_dev, 1, slot_count + 1).astype(jnp.int32)
-    glob_slot = slot_count + 2
+    first_prev = jnp.where(first_dev, 0, 1).astype(jnp.int32)
     ktab = jnp.stack(
         [
-            jnp.int32(0), jnp.int32(slot_count), jnp.int32(glob_slot),
-            jnp.int32(1), jnp.int32(0), jnp.int32(glob_slot),
-            jnp.int32(2), jnp.int32(3), jnp.int32(glob_slot),
-            jnp.int32(3), last_prev, jnp.int32(glob_slot),
+            jnp.int32(0), jnp.int32(slot_count),
+            jnp.int32(1), jnp.int32(0),
+            jnp.int32(2), jnp.int32(3),
+            jnp.int32(3), last_prev,
         ]
     )
-    glob_mode = (seq_blk >= WINDOW).astype(jnp.int32)
-    first_prev = jnp.where(first_dev, 0, 1).astype(jnp.int32)
     mtab = jnp.stack(
         [
-            jnp.int32(2), first_prev, glob_mode[0],
-            jnp.int32(2), jnp.int32(1), glob_mode[1],
-            jnp.int32(2), jnp.int32(1), glob_mode[2],
-            jnp.int32(2), jnp.int32(1), glob_mode[3],
+            jnp.int32(2), first_prev,
+            jnp.int32(2), jnp.int32(1),
+            jnp.int32(2), jnp.int32(1),
+            jnp.int32(2), jnp.int32(1),
         ]
     )
-    dq_local, dk_terms, dv_terms = local_pairs(
-        ktab, mtab, queries, out_grad, norm3, delta3, key_cat, value_cat
-    )
-    dk_terms = dk_terms.reshape(slot_count, KINDS, height, features)
-    dv_terms = dv_terms.reshape(slot_count, KINDS, height, features)
+    dq_win, dk_terms, dv_terms = local_pairs(
+        2, ktab, mtab, queries, out_grad, norm3, delta3, key_win, value_win
+    )
+    dk_terms = dk_terms.reshape(slot_count, 2, height, features)
+    dv_terms = dv_terms.reshape(slot_count, 2, height, features)
+    glob_mode = (seq_blk >= WINDOW).astype(jnp.int32)
+    dq_glob, dk_glob, dv_glob = local_pairs(
+        1, jnp.zeros((slot_count,), jnp.int32), glob_mode, queries, out_grad, norm3, delta3,
+        global_kv[0], global_kv[1],
+    )
+    dq_local = dq_win + dq_glob
+
+    to_left = jnp.stack([dk_terms[0, 1], dv_terms[0, 1]]).astype(jnp.bfloat16)
+    to_right = jnp.stack([dk_terms[slot_count - 1, 1], dv_terms[slot_count - 1, 1]]).astype(
+        jnp.bfloat16
+    )
+    back_right = shift(to_left, "ctx", -1)
+    back_left = shift(to_right, "ctx", 1)
+
+    part = jnp.stack(
+        [
+            jnp.sum(dk_glob.reshape(slot_count, height, features), axis=0),
+            jnp.sum(dv_glob.reshape(slot_count, height, features), axis=0),
+        ]
+    )
+    total = gather_to_root(part, "ctx")
 
     ref_valid = rand_blocks >= 0
     in_front = rand_blocks < block_total // 2
@@ -271,25 +300,21 @@
     ktab_r = jnp.maximum(slot_recv - 1, 0)
     mtab_r = (slot_recv > 0).astype(jnp.int32)
     dq_rand, dk_rand, dv_rand = rand_pairs(ktab_r, mtab_r, arrived, key_rows, values, heads)
+    dq_rand, total, back_left, back_right = lax.optimization_barrier(
+        (dq_rand, total, back_left, back_right)
+    )
+    back_left = back_left.astype(jnp.float32)
+    back_right = back_right.astype(jnp.float32)
     returned = lax.all_to_all(dq_rand, "ctx", split_axis=0, concat_axis=0, tiled=True)
     select_f = select.astype(jnp.float32)
     rand_query = jnp.sum(
         select_f[:, :, None, None] * returned.astype(jnp.float32)[:, None], axis=0
     )
-    choose = (slot_recv[:, None] == jnp.arange(1, slot_count + 1)[None, :]).astype(jnp.float32)
-    rand_key = jnp.sum(choose[:, :, None, None] * dk_rand[:, None], axis=0)
-    rand_value = jnp.sum(choose[:, :, None, None] * dv_rand[:, None], axis=0)
-
-    to_left = jnp.stack([dk_terms[0, 1], dv_terms[0, 1]]).astype(jnp.bfloat16)
-    to_right = jnp.stack([dk_terms[slot_count - 1, 1], dv_terms[slot_count - 1, 1]]).astype(
-        jnp.bfloat16
-    )
-    back_right = shift(to_left, "ctx", -1).astype(jnp.float32)
-    back_left = shift(to_right, "ctx", 1).astype(jnp.float32)
+    rand_key = dk_rand
+    rand_value = dv_rand
+
     own_tail = jnp.where(last_dev, 1.0, 0.0).astype(jnp.float32)
 
-    part = jnp.stack([jnp.sum(dk_terms[:, 2], axis=0), jnp.sum(dv_terms[:, 2], axis=0)])
-    total = gather_to_root(part, "ctx")
     owner_flag = jnp.where(first_dev, 1.0, 0.0).astype(jnp.float32)
 
     def assemble(terms, which, rand_part):

time: 296 us -> 307 us (1.037)
  the two profiles are of different devices: /device:TPU:1 before, /device:TPU:11 now
where the time goes in v1:
time: 307 us; the launch traced here: 306 us
  waiting for transfers between devices  157 us (51%)
  Pallas kernels  68 us (22%)
  starting transfers between devices  35.9 us (12%)
  other arithmetic  26.8 us (9%)
  local copies, waits for them, and re-layouts  14.7 us (5%)
    ppermute x4, waiting for transfers between devices, spread_2(): array = array + lax.ppermute(array, axis, pairs)  100 us
    all_to_all x1, waiting for transfers between devices, shards(): lax.all_to_all(dq_rand, 'ctx', split_axis=0, concat_axis=0, tiled=True)  41.6 us
    pallas_call x1, Pallas kernels, rand_pairs(): pl.pallas_call(functools.partial(rand_kernel, heads), grid_spec=grid_spec...  39 us
    pallas_call x2, Pallas kernels, local_pairs(): pl.pallas_call(functools.partial(local_kernel, kinds), grid_spec=grid_spe...  29 us
    ppermute x4, waiting for transfers between devices, gather_to_root(): array = array + lax.ppermute(array, axis, pairs)  14.3 us
    ppermute x4, starting transfers between devices, shift(): return lax.ppermute(array, axis, pairs)  13.5 us
    all_to_all x1, starting transfers between devices, shards(): lax.all_to_all(dq_rand, 'ctx', split_axis=0, concat_axis=0, tiled=True)  7.72 us
    all_to_all x1, starting transfers between devices, shards(): lax.all_to_all(routed, 'ctx', split_axis=0, concat_axis=0, tiled=True)  6.69 us
  transfers between devices with their start and end apart: 14, of which 5 were waited for; matrix products, arithmetic and copies ran while one was open for 8% of the time, Pallas kernels for 22%

profile of v1, /device:TPU:11, one launch (start us, length us, event | category | flops | bytes accessed | tf_op | source)
XLA Modules:
  0.0 306.4 jit_solution(9101704846460232703)
XLA Ops:
  2.5 1.3 convert_multiply_fusion
  5.8 3.1 convolution_convert_fusion
  8.8 4.9 %reshape.217 = bf16[16,258,512]{2,1,0:T(8,128)(2,1)} reshape(bf16[16,132096]{1,0:T(8,128)(2,1)} %convolution_convert_fusion) | data formatting | bytes 8454144 | tf_op jit(solution)/shard_map/reshape | solution.py:293
  13.8 4.9 %pad_maximum_fusion = bf16[16,272,512]{2,1,0:T(8,128)(2,1)} fusion(bf16[16,14,512]{2,1,0:T(8,128)(2,1)S(1)} %broadcast_in_dim.36, bf16[16,258,512]{2,1,0:T(8,128)(2,1)} %reshape.217), kind=kLoop, calls=%fused_computation.2 | loop fusion | flops 8912896 | bytes 8912896 | tf_op jit(solution)/shard_map/concatenate | solution.py:297
  18.6 6.7 %all-to-all-start = ((bf16[16,272,512]{2,1,0:T(8,128)(2,1)}), bf16[16,272,512]{2,1,0:T(8,128)(2,1)}, u32[]{:S(2)}, u32[]{:S(2)}) async-start(bf16[16,272,512]{2,1,0:T(8,128)(2,1)} %pad_maximum_fusion), calls=%async_computation | async-start | bytes 8912896 | tf_op jit(solution)/shard_map/all_to_all | solution.py:298
  29.5 75.4 %collective-permute-done.4 = bf16[2,128,512]{2,1,0:T(8,128)(2,1)S(1)} collective-permute-done((bf16[2,128,512]{2,1,0:T(8,128)(2,1)S(1)}, bf16[2,128,512]{2,1,0:T(8,128)(2,1)S(1)}, u32[]{:S(2)}, u32[]{:S(2)}) %collective-permute-start.4) | collective-permute-done | bytes 262176 | tf_op jit(solution)/shard_map/ppermute | solution.py:24
  107.5 24.9 %collective-permute-done.5 = bf16[2,128,512]{2,1,0:T(8,128)(2,1)S(1)} collective-permute-done((bf16[2,128,512]{2,1,0:T(8,128)(2,1)S(1)}, bf16[2,128,512]{2,1,0:T(8,128)(2,1)S(1)}, u32[]{:S(2)}, u32[]{:S(2)}) %collective-permute-start.5) | collective-permute-done | bytes 262176 | tf_op jit(solution)/shard_map/ppermute | solution.py:24
  133.7 8.0 %shard_map.95 = (f32[512,512]{1,0:T(8,128)}, f32[512,512]{1,0:T(8,128)}, f32[512,512]{1,0:T(8,128)}) custom-call(s32[4]{0:T(128)} %broadcast_23_ktab.2.ktab, s32[4]{0:T(128)} %compare_convert_fusion.1.mtab, bf16[512,512]{1,0:T(8,128)(2,1)} %q_ref.3, bf16[512,512]{1,0:T(8,128)(2,1)} %do_ref.3, f32[4,1,512]{2,1,0:T(1,128)} %reshape.224.nrm_ref, ...), custom_call_target="tpu_custom_call" | custom-call | tf_op jit(solution)/shard_map/pallas_call | solution.py:141
  141.8 1.3 reduce_sum.47
  143.1 1.3 reduce_sum.48
  145.8 14.3 %collective-permute-done.6 = f32[2,128,512]{2,1,0:T(8,128)S(1)} collective-permute-done((f32[2,128,512]{2,1,0:T(8,128)S(1)}, f32[2,128,512]{2,1,0:T(8,128)S(1)}, u32[]{:S(2)}, u32[]{:S(2)}) %collective-permute-start.6) | collective-permute-done | bytes 524320 | tf_op jit(solution)/shard_map/ppermute | solution.py:36
  161.5 1.6 pad_maximum_fusion.5
  163.1 3.5 %collective-permute-start.1 = (bf16[2,128,512]{2,1,0:T(8,128)(2,1)}, bf16[2,128,512]{2,1,0:T(8,128)(2,1)}, u32[]{:S(2)}, u32[]{:S(2)}) collective-permute-start(bf16[2,128,512]{2,1,0:T(8,128)(2,1)} %pad_maximum_fusion.5), channel_id=1, source_target_pairs={{2,0},{4,2},{6,4},{8,6},{10,8},{12,10},{14,12},{16,14},{18,16},{20... | collective-permute-start | bytes 786440 | tf_op jit(solution)/shard_map/ppermute | solution.py:44
  167.4 2.9 collective-permute-start
  175.9 21.0 %shard_map.94 = (f32[512,512]{1,0:T(8,128)}, f32[1024,512]{1,0:T(8,128)}, f32[1024,512]{1,0:T(8,128)}) custom-call(s32[8]{0:T(128)} %stack.71.ktab, s32[8]{0:T(128)} %stack.73.mtab, bf16[512,512]{1,0:T(8,128)(2,1)} %q_ref.3, bf16[512,512]{1,0:T(8,128)(2,1)} %do_ref.3, f32[4,1,512]{2,1,0:T(1,128)} %reshape.224.nrm_ref, f32[4,1,512]{2,1,0:T(1,128)} %reshape.226.dlt_ref, ...), custom_call_target="tpu_custom_call" | custom-call | tf_op jit(solution)/shard_map/pallas_call | solution.py:141
  199.8 5.2 %collective-permute-start.10 = (bf16[2,128,512]{2,1,0:T(8,128)(2,1)S(1)}, bf16[2,128,512]{2,1,0:T(8,128)(2,1)S(1)}, u32[]{:S(2)}, u32[]{:S(2)}) collective-permute-start(bf16[2,128,512]{2,1,0:T(8,128)(2,1)S(1)} %pad_maximum_fusion.6), channel_id=1, source_target_pairs={{0,2},{2,4},{4,6},{6,8},{8,10},{10,12},{12,14},{14,16},{16,18},{18... | collective-permute-start | bytes 786440 | tf_op jit(solution)/shard_map/ppermute | solution.py:44
  205.0 1.9 collective-permute-start.11
  207.0 1.9 fusion.15
  209.0 39.0 %shard_map.96 = (bf16[16,128,512]{2,1,0:T(8,128)(2,1)}, f32[4,128,512]{2,1,0:T(8,128)}, f32[4,128,512]{2,1,0:T(8,128)}) custom-call(s32[16]{0:T(128)} %get-tuple-element.30.ktab, s32[16]{0:T(128)} %get-tuple-element.29.mtab, bf16[16,272,512]{2,1,0:T(8,128)(2,1)} %all-to-all-done.q_ref.do_ref.st_ref, bf16[16,272,512]{2,1,0:T(8,128)(2,1)} %all-to-all-done.q_ref.do_ref.st_ref, ...), custom_call_target="tpu_custom_call" | custom-call | tf_op jit(solution)/shard_map/pallas_call | solution.py:174
  247.9 7.7 %all-to-all-start.1 = ((bf16[16,128,512]{2,1,0:T(8,128)(2,1)}), bf16[16,128,512]{2,1,0:T(8,128)(2,1)S(1)}, u32[]{:S(2)}, u32[]{:S(2)}) async-start(bf16[16,128,512]{2,1,0:T(8,128)(2,1)} %get-tuple-element.23), calls=%async_computation.1 | async-start | bytes 4194304 | tf_op jit(solution)/shard_map/all_to_all | solution.py:308
  258.2 1.9 fusion.10
  260.1 1.3 fusion
  261.5 41.6 %all-to-all-done.1 = bf16[16,128,512]{2,1,0:T(8,128)(2,1)S(1)} async-done(((bf16[16,128,512]{2,1,0:T(8,128)(2,1)}), bf16[16,128,512]{2,1,0:T(8,128)(2,1)S(1)}, u32[]{:S(2)}, u32[]{:S(2)}) %all-to-all-start.1) | async-done | bytes 2097184 | tf_op jit(solution)/shard_map/all_to_all | solution.py:308
  303.7 1.4 multiply_reduce_fusion
  (91 shorter events, 28.1 us)
Async XLA Ops:
  3.9 1.2 copy-start
  3.9 1.2 copy-start.1
  18.6 6.7 %copy-start.2 = (bf16[512,512]{1,0:T(8,128)(2,1)S(1)}, bf16[512,512]{1,0:T(8,128)(2,1)}, u32[]{:S(2)}) copy-start(bf16[512,512]{1,0:T(8,128)(2,1)} %k_ref.1) | copy-start | bytes 1572868
  18.6 6.8 %copy-start.3 = (bf16[512,512]{1,0:T(8,128)(2,1)S(1)}, bf16[512,512]{1,0:T(8,128)(2,1)}, u32[]{:S(2)}) copy-start(bf16[512,512]{1,0:T(8,128)(2,1)} %v_ref.1) | copy-start | bytes 1572868
  18.6 188.4 %all-to-all-start = ((bf16[16,272,512]{2,1,0:T(8,128)(2,1)}), bf16[16,272,512]{2,1,0:T(8,128)(2,1)}, u32[]{:S(2)}, u32[]{:S(2)}) async-start(bf16[16,272,512]{2,1,0:T(8,128)(2,1)} %pad_maximum_fusion), calls=%async_computation | async-start | bytes 8912896 | tf_op jit(solution)/shard_map/all_to_all | solution.py:298
  25.3 3.6 %copy-start.9 = (bf16[4,512]{1,0:T(4,128)(2,1)S(1)}, bf16[4,512]{1,0:T(4,128)(2,1)}, u32[]{:S(2)}) copy-start(bf16[4,512]{1,0:T(4,128)(2,1)} %param.12) | copy-start | bytes 12292
  26.1 0.7 collective-permute-start.2
  26.9 0.7 collective-permute-start.3
  27.6 77.3 %collective-permute-start.4 = (bf16[2,128,512]{2,1,0:T(8,128)(2,1)S(1)}, bf16[2,128,512]{2,1,0:T(8,128)(2,1)S(1)}, u32[]{:S(2)}, u32[]{:S(2)}) collective-permute-start(bf16[2,128,512]{2,1,0:T(8,128)(2,1)S(1)} %fusion.31), channel_id=1, source_target_pairs={{0,8},{2,10},{4,12},{6,14},{1,9},{3,11},{5,13},{7,15}} | collective-permute-start | bytes 786440 | tf_op jit(solution)/shard_map/ppermute | solution.py:24
  105.0 27.3 %collective-permute-start.5 = (bf16[2,128,512]{2,1,0:T(8,128)(2,1)S(1)}, bf16[2,128,512]{2,1,0:T(8,128)(2,1)S(1)}, u32[]{:S(2)}, u32[]{:S(2)}) collective-permute-start(bf16[2,128,512]{2,1,0:T(8,128)(2,1)S(1)} %add.163), channel_id=1, source_target_pairs={{0,16},{2,18},{4,20},{6,22},{8,24},{10,26},{12,28},{14,30},{1,17},... | collective-permute-start | bytes 786440 | tf_op jit(solution)/shard_map/ppermute | solution.py:24
  144.5 15.6 %collective-permute-start.6 = (f32[2,128,512]{2,1,0:T(8,128)S(1)}, f32[2,128,512]{2,1,0:T(8,128)S(1)}, u32[]{:S(2)}, u32[]{:S(2)}) collective-permute-start(f32[2,128,512]{2,1,0:T(8,128)S(1)} %pad_maximum_fusion.3), channel_id=1, source_target_pairs={{16,0},{18,2},{20,4},{22,6},{24,8},{26,10},{28,12},{30,14},{17,1},... | collective-permute-start | bytes 1572872 | tf_op jit(solution)/shard_map/ppermute | solution.py:36
  160.2 12.9 %collective-permute-start.7 = (f32[2,128,512]{2,1,0:T(8,128)S(1)}, f32[2,128,512]{2,1,0:T(8,128)S(1)}, u32[]{:S(2)}, u32[]{:S(2)}) collective-permute-start(f32[2,128,512]{2,1,0:T(8,128)S(1)} %fusion.26), channel_id=1, source_target_pairs={{8,0},{10,2},{12,4},{14,6},{9,1},{11,3},{13,5},{15,7}} | collective-permute-start | bytes 1572872 | tf_op jit(solution)/shard_map/ppermute | solution.py:36
  163.1 8.9 %collective-permute-start.1 = (bf16[2,128,512]{2,1,0:T(8,128)(2,1)}, bf16[2,128,512]{2,1,0:T(8,128)(2,1)}, u32[]{:S(2)}, u32[]{:S(2)}) collective-permute-start(bf16[2,128,512]{2,1,0:T(8,128)(2,1)} %pad_maximum_fusion.5), channel_id=1, source_target_pairs={{2,0},{4,2},{6,4},{8,6},{10,8},{12,10},{14,12},{16,14},{18,16},{20... | collective-permute-start | bytes 786440 | tf_op jit(solution)/shard_map/ppermute | solution.py:44
  167.4 6.5 %collective-permute-start = (bf16[2,128,512]{2,1,0:T(8,128)(2,1)}, bf16[2,128,512]{2,1,0:T(8,128)(2,1)S(1)}, u32[]{:S(2)}, u32[]{:S(2)}) collective-permute-start(bf16[2,128,512]{2,1,0:T(8,128)(2,1)} %pad_maximum_fusion.4), channel_id=1, source_target_pairs={{0,2},{2,4},{4,6},{6,8},{8,10},{10,12},{12,14},{14,16},{16,18},{18... | collective-permute-start | bytes 786440 | tf_op jit(solution)/shard_map/ppermute | solution.py:44
  173.2 24.7 %collective-permute-start.8 = (f32[2,128,512]{2,1,0:T(8,128)S(1)}, f32[2,128,512]{2,1,0:T(8,128)S(1)}, u32[]{:S(2)}, u32[]{:S(2)}) collective-permute-start(f32[2,128,512]{2,1,0:T(8,128)S(1)} %fusion.29), channel_id=1, source_target_pairs={{4,0},{6,2},{5,1},{7,3}} | collective-permute-start | bytes 1572872 | tf_op jit(solution)/shard_map/ppermute | solution.py:36
  198.0 9.0 %collective-permute-start.9 = (f32[2,128,512]{2,1,0:T(8,128)S(1)}, f32[2,128,512]{2,1,0:T(8,128)S(1)}, u32[]{:S(2)}, u32[]{:S(2)}) collective-permute-start(f32[2,128,512]{2,1,0:T(8,128)S(1)} %add.172), channel_id=1, source_target_pairs={{2,0},{3,1}} | collective-permute-start | bytes 1572872 | tf_op jit(solution)/shard_map/ppermute | solution.py:36
  199.8 48.2 %collective-permute-start.10 = (bf16[2,128,512]{2,1,0:T(8,128)(2,1)S(1)}, bf16[2,128,512]{2,1,0:T(8,128)(2,1)S(1)}, u32[]{:S(2)}, u32[]{:S(2)}) collective-permute-start(bf16[2,128,512]{2,1,0:T(8,128)(2,1)S(1)} %pad_maximum_fusion.6), channel_id=1, source_target_pairs={{0,2},{2,4},{4,6},{6,8},{8,10},{10,12},{12,14},{14,16},{16,18},{18... | collective-permute-start | bytes 786440 | tf_op jit(solution)/shard_map/ppermute | solution.py:44
  205.0 42.9 %collective-permute-start.11 = (bf16[2,128,512]{2,1,0:T(8,128)(2,1)S(1)}, bf16[2,128,512]{2,1,0:T(8,128)(2,1)S(1)}, u32[]{:S(2)}, u32[]{:S(2)}) collective-permute-start(bf16[2,128,512]{2,1,0:T(8,128)(2,1)S(1)} %pad_maximum_fusion.7), channel_id=1, source_target_pairs={{2,0},{4,2},{6,4},{8,6},{10,8},{12,10},{14,12},{16,14},{18,16},{20... | collective-permute-start | bytes 786440 | tf_op jit(solution)/shard_map/ppermute | solution.py:44
  247.9 55.1 %all-to-all-start.1 = ((bf16[16,128,512]{2,1,0:T(8,128)(2,1)}), bf16[16,128,512]{2,1,0:T(8,128)(2,1)S(1)}, u32[]{:S(2)}, u32[]{:S(2)}) async-start(bf16[16,128,512]{2,1,0:T(8,128)(2,1)} %get-tuple-element.23), calls=%async_computation.1 | async-start | bytes 4194304 | tf_op jit(solution)/shard_map/all_to_all | solution.py:308
  255.8 2.4 copy-start.4
  258.2 1.9 copy-start.7
  258.2 1.9 copy-start.8
  303.7 1.4 copy-start.5
  303.7 1.5 copy-start.6

commit v2 on v1

--- a/solution.py
+++ b/solution.py
@@ -91,27 +91,26 @@
 def rand_kernel(heads, ktab, mtab, q_ref, do_ref, st_ref, k_ref, v_ref, dq_ref, dk_ref, dv_ref):
     p = pl.program_id(0)
     mode = mtab[p]
-    slot = ktab[p]
     width = q_ref.shape[2] // heads
 
-    @pl.when(p == 0)
+    @pl.when(mode == 0)
     def _():
+        dq_ref[...] = jnp.zeros_like(dq_ref)
         dk_ref[...] = jnp.zeros_like(dk_ref)
         dv_ref[...] = jnp.zeros_like(dv_ref)
 
-    for h in range(heads):
-        cols = slice(h * width, (h + 1) * width)
-        stats = st_ref[0, :, cols].astype(jnp.float32)
-        dq, dk, dv = pair_math(
-            q_ref[0, :, cols], do_ref[0, :, cols], k_ref[:, cols], v_ref[:, cols],
-            stats[0:1, :], stats[1:2, :], mode,
-        )
-        dq_ref[0, :, cols] = dq.astype(jnp.bfloat16)
-
-        @pl.when(mode > 0)
-        def _():
-            dk_ref[slot, :, cols] += dk
-            dv_ref[slot, :, cols] += dv
+    @pl.when(mode > 0)
+    def _():
+        for h in range(heads):
+            cols = slice(h * width, (h + 1) * width)
+            stats = st_ref[0, :, cols].astype(jnp.float32)
+            dq, dk, dv = pair_math(
+                q_ref[0, :, cols], do_ref[0, :, cols], k_ref[:, cols], v_ref[:, cols],
+                stats[0:1, :], stats[1:2, :], mode,
+            )
+            dq_ref[0, :, cols] = dq.astype(jnp.bfloat16)
+            dk_ref[0, :, cols] = dk
+            dv_ref[0, :, cols] = dv
 
 
 def local_pairs(kinds, ktab, mtab, queries, out_grad, norm3, delta3, key_cat, value_cat):
@@ -152,7 +151,6 @@
 def rand_pairs(ktab, mtab, arrived, key_rows, value_rows, heads):
     items, packed_rows, features = arrived.shape
     height = (packed_rows - STAT_ROWS) // 2
-    slots = key_rows.shape[0] // height
     grid_spec = pltpu.PrefetchScalarGridSpec(
         num_scalar_prefetch=2,
         grid=(items,),
@@ -167,8 +165,8 @@
         ],
         out_specs=[
             pl.BlockSpec((1, height, features), lambda p, kt, mt: (p, 0, 0)),
-            pl.BlockSpec((slots, height, features), lambda p, kt, mt: (0, 0, 0)),
-            pl.BlockSpec((slots, height, features), lambda p, kt, mt: (0, 0, 0)),
+            pl.BlockSpec((1, height, features), lambda p, kt, mt: (p, 0, 0)),
+            pl.BlockSpec((1, height, features), lambda p, kt, mt: (p, 0, 0)),
         ],
     )
     return pl.pallas_call(
@@ -176,8 +174,8 @@
         grid_spec=grid_spec,
         out_shape=[
             jax.ShapeDtypeStruct((items, height, features), jnp.bfloat16),
-            jax.ShapeDtypeStruct((slots, height, features), jnp.float32),
-            jax.ShapeDtypeStruct((slots, height, features), jnp.float32),
+            jax.ShapeDtypeStruct((items, height, features), jnp.float32),
+            jax.ShapeDtypeStruct((items, height, features), jnp.float32),
         ],
     )(ktab, mtab, arrived, arrived, arrived, key_rows, value_rows)
 
@@ -240,6 +238,9 @@
     dk_terms = dk_terms.reshape(slot_count, 2, height, features)
     dv_terms = dv_terms.reshape(slot_count, 2, height, features)
     glob_mode = (seq_blk >= WINDOW).astype(jnp.int32)
+    global_kv, dq_win, dk_terms, dv_terms = lax.optimization_barrier(
+        (global_kv, dq_win, dk_terms, dv_terms)
+    )
     dq_glob, dk_glob, dv_glob = local_pairs(
         1, jnp.zeros((slot_count,), jnp.int32), glob_mode, queries, out_grad, norm3, delta3,
         global_kv[0], global_kv[1],
@@ -300,9 +301,7 @@
     ktab_r = jnp.maximum(slot_recv - 1, 0)
     mtab_r = (slot_recv > 0).astype(jnp.int32)
     dq_rand, dk_rand, dv_rand = rand_pairs(ktab_r, mtab_r, arrived, key_rows, values, heads)
-    dq_rand, total, back_left, back_right = lax.optimization_barrier(
-        (dq_rand, total, back_left, back_right)
-    )
+    dq_rand, back_left, back_right = lax.optimization_barrier((dq_rand, back_left, back_right))
     back_left = back_left.astype(jnp.float32)
     back_right = back_right.astype(jnp.float32)
     returned = lax.all_to_all(dq_rand, "ctx", split_axis=0, concat_axis=0, tiled=True)
@@ -310,8 +309,9 @@
     rand_query = jnp.sum(
         select_f[:, :, None, None] * returned.astype(jnp.float32)[:, None], axis=0
     )
-    rand_key = dk_rand
-    rand_value = dv_rand
+    choose = (slot_recv[:, None] == jnp.arange(1, slot_count + 1)[None, :]).astype(jnp.float32)
+    rand_key = jnp.sum(choose[:, :, None, None] * dk_rand[:, None], axis=0)
+    rand_value = jnp.sum(choose[:, :, None, None] * dv_rand[:, None], axis=0)
 
     own_tail = jnp.where(last_dev, 1.0, 0.0).astype(jnp.float32)
 

time: 307 us -> 299 us (0.974)
  the two profiles are of different devices: /device:TPU:11 before, /device:TPU:1 now
where the time goes in v2:
time: 299 us; the launch traced here: 297 us
  waiting for transfers between devices  122 us (41%)
  starting transfers between devices  70.4 us (24%)
  Pallas kernels  52.6 us (18%)
  other arithmetic  33.9 us (11%)
  local copies, waits for them, and re-layouts  14.4 us (5%)
  matrix products  3.02 us (1%)
    ppermute x4, waiting for transfers between devices, spread_2(): array = array + lax.ppermute(array, axis, pairs)  62.8 us
    ppermute x4, waiting for transfers between devices, gather_to_root(): array = array + lax.ppermute(array, axis, pairs)  59.1 us
    ppermute x4, starting transfers between devices, shift(): return lax.ppermute(array, axis, pairs)  43.3 us
    pallas_call x2, Pallas kernels, local_pairs(): pl.pallas_call(functools.partial(local_kernel, kinds), grid_spec=grid_spe...  29 us
    pallas_call x1, Pallas kernels, rand_pairs(): pl.pallas_call(functools.partial(rand_kernel, heads), grid_spec=grid_spec...  23.6 us
    ppermute x4, starting transfers between devices, gather_to_root(): array = array + lax.ppermute(array, axis, pairs)  8.35 us
    ppermute x4, starting transfers between devices, spread_2(): array = array + lax.ppermute(array, axis, pairs)  7.49 us
    all_to_all x1, starting transfers between devices, shards(): lax.all_to_all(routed, 'ctx', split_axis=0, concat_axis=0, tiled=True)  7.45 us
  transfers between devices with their start and end apart: 14, of which 4 were waited for; matrix products, arithmetic and copies ran while one was open for 10% of the time, Pallas kernels for 18%

profile of v2, /device:TPU:1, one launch (start us, length us, event | category | flops | bytes accessed | tf_op | source)
XLA Modules:
  0.0 297.4 jit_solution(2968096772270323436)
XLA Ops:
  1.8 1.4 convert_multiply_fusion
  5.1 3.0 %convolution_convert_fusion = bf16[16,132096]{1,0:T(8,128)(2,1)} fusion(pred[16,4]{0,1:T(4,128)(4,1)S(1)} %fusion.11, bf16[4,132096]{1,0:T(4,128)(2,1)S(1)} %bitcast.80), kind=kOutput, calls=%fused_computation | convolution fusion | flops 19021824 | bytes 5283904 | tf_op jit(solution)/shard_map/dot_general | solution.py:291
  8.1 4.9 %reshape.257 = bf16[16,258,512]{2,1,0:T(8,128)(2,1)} reshape(bf16[16,132096]{1,0:T(8,128)(2,1)} %convolution_convert_fusion) | data formatting | bytes 8454144 | tf_op jit(solution)/shard_map/reshape | solution.py:294
  13.1 4.9 %pad_maximum_fusion = bf16[16,272,512]{2,1,0:T(8,128)(2,1)} fusion(bf16[16,14,512]{2,1,0:T(8,128)(2,1)S(1)} %broadcast_in_dim.42, bf16[16,258,512]{2,1,0:T(8,128)(2,1)} %reshape.257), kind=kLoop, calls=%fused_computation.4 | loop fusion | flops 8912896 | bytes 8912896 | tf_op jit(solution)/shard_map/concatenate | solution.py:298
  18.0 7.5 %all-to-all-start = ((bf16[16,272,512]{2,1,0:T(8,128)(2,1)}), bf16[16,272,512]{2,1,0:T(8,128)(2,1)}, u32[]{:S(2)}, u32[]{:S(2)}) async-start(bf16[16,272,512]{2,1,0:T(8,128)(2,1)} %pad_maximum_fusion), calls=%async_computation | async-start | bytes 8912896 | tf_op jit(solution)/shard_map/all_to_all | solution.py:299
  26.9 3.0 %collective-permute-start.5 = (bf16[2,128,512]{2,1,0:T(8,128)(2,1)S(1)}, bf16[2,128,512]{2,1,0:T(8,128)(2,1)S(1)}, u32[]{:S(2)}, u32[]{:S(2)}) collective-permute-start(bf16[2,128,512]{2,1,0:T(8,128)(2,1)S(1)} %pad_maximum_fusion.5), channel_id=1, source_target_pairs={{2,0},{4,2},{6,4},{8,6},{10,8},{12,10},{14,12},{16,14},{18,16},{20... | collective-permute-start | bytes 786440 | tf_op jit(solution)/shard_map/ppermute | solution.py:44
  30.0 2.5 collective-permute-start.4
  32.5 3.6 %collective-permute-start.1 = (bf16[2,128,512]{2,1,0:T(8,128)(2,1)S(1)}, bf16[2,128,512]{2,1,0:T(8,128)(2,1)S(1)}, u32[]{:S(2)}, u32[]{:S(2)}) collective-permute-start(bf16[2,128,512]{2,1,0:T(8,128)(2,1)S(1)} %fusion.24), channel_id=1, source_target_pairs={{0,4},{2,6},{1,5},{3,7}} | collective-permute-start | bytes 786440 | tf_op jit(solution)/shard_map/ppermute | solution.py:24
  39.1 19.8 %collective-permute-done.1 = bf16[2,128,512]{2,1,0:T(8,128)(2,1)S(1)} collective-permute-done((bf16[2,128,512]{2,1,0:T(8,128)(2,1)S(1)}, bf16[2,128,512]{2,1,0:T(8,128)(2,1)S(1)}, u32[]{:S(2)}, u32[]{:S(2)}) %collective-permute-start.1) | collective-permute-done | bytes 262176 | tf_op jit(solution)/shard_map/ppermute | solution.py:24
  60.3 43.0 %collective-permute-done.2 = bf16[2,128,512]{2,1,0:T(8,128)(2,1)S(1)} collective-permute-done((bf16[2,128,512]{2,1,0:T(8,128)(2,1)S(1)}, bf16[2,128,512]{2,1,0:T(8,128)(2,1)S(1)}, u32[]{:S(2)}, u32[]{:S(2)}) %collective-permute-start.2) | collective-permute-done | bytes 262176 | tf_op jit(solution)/shard_map/ppermute | solution.py:24
  106.7 20.9 %shard_map.94 = (f32[512,512]{1,0:T(8,128)}, f32[1024,512]{1,0:T(8,128)}, f32[1024,512]{1,0:T(8,128)}) custom-call(s32[8]{0:T(128)} %stack.74.ktab, s32[8]{0:T(128)} %stack.76.mtab, bf16[512,512]{1,0:T(8,128)(2,1)} %q_ref.3, bf16[512,512]{1,0:T(8,128)(2,1)} %do_ref.3, f32[4,1,512]{2,1,0:T(1,128)} %reshape.262.nrm_ref, f32[4,1,512]{2,1,0:T(1,128)} %reshape.264.dlt_ref, ...), custom_call_target="tpu_custom_call" | custom-call | tf_op jit(solution)/shard_map/pallas_call | solution.py:140
  129.9 5.2 %collective-permute-start.6 = (bf16[2,128,512]{2,1,0:T(8,128)(2,1)S(1)}, bf16[2,128,512]{2,1,0:T(8,128)(2,1)S(1)}, u32[]{:S(2)}, u32[]{:S(2)}) collective-permute-start(bf16[2,128,512]{2,1,0:T(8,128)(2,1)S(1)} %pad_maximum_fusion.6), channel_id=1, source_target_pairs={{0,2},{2,4},{4,6},{6,8},{8,10},{10,12},{12,14},{14,16},{16,18},{18... | collective-permute-start | bytes 786440 | tf_op jit(solution)/shard_map/ppermute | solution.py:44
  135.1 32.6 %collective-permute-start.7 = (bf16[2,128,512]{2,1,0:T(8,128)(2,1)S(1)}, bf16[2,128,512]{2,1,0:T(8,128)(2,1)S(1)}, u32[]{:S(2)}, u32[]{:S(2)}) collective-permute-start(bf16[2,128,512]{2,1,0:T(8,128)(2,1)S(1)} %pad_maximum_fusion.7), channel_id=1, source_target_pairs={{2,0},{4,2},{6,4},{8,6},{10,8},{12,10},{14,12},{16,14},{18,16},{20... | collective-permute-start | bytes 786440 | tf_op jit(solution)/shard_map/ppermute | solution.py:44
  169.0 8.0 %shard_map.95 = (f32[512,512]{1,0:T(8,128)}, f32[512,512]{1,0:T(8,128)}, f32[512,512]{1,0:T(8,128)}) custom-call(s32[4]{0:T(128)} %broadcast_25_ktab.2.ktab, s32[4]{0:T(128)} %compare_convert_fusion.2.mtab, bf16[512,512]{1,0:T(8,128)(2,1)} %q_ref.3, bf16[512,512]{1,0:T(8,128)(2,1)} %do_ref.3, f32[4,1,512]{2,1,0:T(1,128)} %reshape.262.nrm_ref, ...), custom_call_target="tpu_custom_call" | custom-call | tf_op jit(solution)/shard_map/pallas_call | solution.py:140
  177.0 1.3 reduce_sum.67
  178.3 1.3 reduce_sum.66
  184.0 23.6 %shard_map.96 = (bf16[16,128,512]{2,1,0:T(8,128)(2,1)}, f32[16,128,512]{2,1,0:T(8,128)}, f32[16,128,512]{2,1,0:T(8,128)}) custom-call(s32[16]{0:T(128)} %add_maximum_fusion.ktab, s32[16]{0:T(128)} %compare_convert_fusion.1.mtab, bf16[16,272,512]{2,1,0:T(8,128)(2,1)} %all-to-all-done.q_ref.do_ref.st_ref, ...), custom_call_target="tpu_custom_call" | custom-call | tf_op jit(solution)/shard_map/pallas_call | solution.py:172
  208.3 3.8 %all-to-all-start.1 = ((bf16[16,128,512]{2,1,0:T(8,128)(2,1)}), bf16[16,128,512]{2,1,0:T(8,128)(2,1)S(1)}, u32[]{:S(2)}, u32[]{:S(2)}) async-start(bf16[16,128,512]{2,1,0:T(8,128)(2,1)} %get-tuple-element.28), calls=%async_computation.1 | async-start | bytes 4194304 | tf_op jit(solution)/shard_map/all_to_all | solution.py:307
  213.5 45.9 %collective-permute-done.9 = f32[2,128,512]{2,1,0:T(8,128)S(1)} collective-permute-done((f32[2,128,512]{2,1,0:T(8,128)S(1)}, f32[2,128,512]{2,1,0:T(8,128)S(1)}, u32[]{:S(2)}, u32[]{:S(2)}) %collective-permute-start.9) | collective-permute-done | bytes 524320 | tf_op jit(solution)/shard_map/ppermute | solution.py:36
  260.9 13.1 %collective-permute-done.10 = f32[2,128,512]{2,1,0:T(8,128)S(1)} collective-permute-done((f32[2,128,512]{2,1,0:T(8,128)S(1)}, f32[2,128,512]{2,1,0:T(8,128)S(1)}, u32[]{:S(2)}, u32[]{:S(2)}) %collective-permute-start.10) | collective-permute-done | bytes 524320 | tf_op jit(solution)/shard_map/ppermute | solution.py:36
  274.1 4.5 %collective-permute-start.11 = (f32[2,128,512]{2,1,0:T(8,128)S(1)}, f32[2,128,512]{2,1,0:T(8,128)}, u32[]{:S(2)}, u32[]{:S(2)}) collective-permute-start(f32[2,128,512]{2,1,0:T(8,128)S(1)} %add.185), channel_id=1, source_target_pairs={{2,0},{3,1}} | collective-permute-start | bytes 1572872 | tf_op jit(solution)/shard_map/ppermute | solution.py:36
  285.9 5.1 %multiply_reduce_fusion = (f32[4,128,512]{2,1,0:T(8,128)S(1)}, f32[4,128,512]{2,1,0:T(8,128)S(1)}) fusion(f32[16,128,512]{2,1,0:T(8,128)} %get-tuple-element.34, f32[16,4]{1,0:T(8,128)S(1)} %compare_convert_fusion, f32[16,128,512]{2,1,0:T(8,128)S(1)} %copy-done.2), kind=kLoop, calls=%fused_computation.1 | loop fusion | flops 16252928 | bytes 10486016 | tf_op jit(solution)/shard_map/reduce_sum | solution.py:314
  291.0 2.1 fusion
  294.6 1.4 multiply_reduce_fusion.2
  (98 shorter events, 33.7 us)
Async XLA Ops:
  3.2 1.2 copy-start.10
  3.2 1.3 copy-start
  3.2 1.3 copy-start.1
  18.0 7.5 %copy-start.3 = (bf16[512,512]{1,0:T(8,128)(2,1)S(1)}, bf16[512,512]{1,0:T(8,128)(2,1)}, u32[]{:S(2)}) copy-start(bf16[512,512]{1,0:T(8,128)(2,1)} %k_ref.1) | copy-start | bytes 1572868
  18.0 7.5 %copy-start.4 = (bf16[512,512]{1,0:T(8,128)(2,1)S(1)}, bf16[512,512]{1,0:T(8,128)(2,1)}, u32[]{:S(2)}) copy-start(bf16[512,512]{1,0:T(8,128)(2,1)} %v_ref.1) | copy-start | bytes 1572868
  18.0 163.8 %all-to-all-start = ((bf16[16,272,512]{2,1,0:T(8,128)(2,1)}), bf16[16,272,512]{2,1,0:T(8,128)(2,1)}, u32[]{:S(2)}, u32[]{:S(2)}) async-start(bf16[16,272,512]{2,1,0:T(8,128)(2,1)} %pad_maximum_fusion), calls=%async_computation | async-start | bytes 8912896 | tf_op jit(solution)/shard_map/all_to_all | solution.py:299
  25.5 7.0 %collective-permute-start = (bf16[2,128,512]{2,1,0:T(8,128)(2,1)S(1)}, bf16[2,128,512]{2,1,0:T(8,128)(2,1)S(1)}, u32[]{:S(2)}, u32[]{:S(2)}) collective-permute-start(bf16[2,128,512]{2,1,0:T(8,128)(2,1)S(1)} %maximum_select_fusion), channel_id=1, source_target_pairs={{0,2},{1,3}} | collective-permute-start | bytes 786440 | tf_op jit(solution)/shard_map/ppermute | solution.py:24
  26.9 33.4 %collective-permute-start.5 = (bf16[2,128,512]{2,1,0:T(8,128)(2,1)S(1)}, bf16[2,128,512]{2,1,0:T(8,128)(2,1)S(1)}, u32[]{:S(2)}, u32[]{:S(2)}) collective-permute-start(bf16[2,128,512]{2,1,0:T(8,128)(2,1)S(1)} %pad_maximum_fusion.5), channel_id=1, source_target_pairs={{2,0},{4,2},{6,4},{8,6},{10,8},{12,10},{14,12},{16,14},{18,16},{20... | collective-permute-start | bytes 786440 | tf_op jit(solution)/shard_map/ppermute | solution.py:44
  30.0 30.4 %collective-permute-start.4 = (bf16[2,128,512]{2,1,0:T(8,128)(2,1)S(1)}, bf16[2,128,512]{2,1,0:T(8,128)(2,1)S(1)}, u32[]{:S(2)}, u32[]{:S(2)}) collective-permute-start(bf16[2,128,512]{2,1,0:T(8,128)(2,1)S(1)} %pad_maximum_fusion.4), channel_id=1, source_target_pairs={{0,2},{2,4},{4,6},{6,8},{8,10},{10,12},{12,14},{14,16},{16,18},{18... | collective-permute-start | bytes 786440 | tf_op jit(solution)/shard_map/ppermute | solution.py:44
  32.5 26.4 %collective-permute-start.1 = (bf16[2,128,512]{2,1,0:T(8,128)(2,1)S(1)}, bf16[2,128,512]{2,1,0:T(8,128)(2,1)S(1)}, u32[]{:S(2)}, u32[]{:S(2)}) collective-permute-start(bf16[2,128,512]{2,1,0:T(8,128)(2,1)S(1)} %fusion.24), channel_id=1, source_target_pairs={{0,4},{2,6},{1,5},{3,7}} | collective-permute-start | bytes 786440 | tf_op jit(solution)/shard_map/ppermute | solution.py:24
  59.0 44.4 %collective-permute-start.2 = (bf16[2,128,512]{2,1,0:T(8,128)(2,1)S(1)}, bf16[2,128,512]{2,1,0:T(8,128)(2,1)S(1)}, u32[]{:S(2)}, u32[]{:S(2)}) collective-permute-start(bf16[2,128,512]{2,1,0:T(8,128)(2,1)S(1)} %fusion.25), channel_id=1, source_target_pairs={{0,8},{2,10},{4,12},{6,14},{1,9},{3,11},{5,13},{7,15}} | collective-permute-start | bytes 786440 | tf_op jit(solution)/shard_map/ppermute | solution.py:24
  103.5 24.2 %collective-permute-start.3 = (bf16[2,128,512]{2,1,0:T(8,128)(2,1)S(1)}, bf16[2,128,512]{2,1,0:T(8,128)(2,1)S(1)}, u32[]{:S(2)}, u32[]{:S(2)}) collective-permute-start(bf16[2,128,512]{2,1,0:T(8,128)(2,1)S(1)} %add.171), channel_id=1, source_target_pairs={{0,16},{2,18},{4,20},{6,22},{8,24},{10,26},{12,28},{14,30},{1,17},... | collective-permute-start | bytes 786440 | tf_op jit(solution)/shard_map/ppermute | solution.py:24
  129.9 77.7 %collective-permute-start.6 = (bf16[2,128,512]{2,1,0:T(8,128)(2,1)S(1)}, bf16[2,128,512]{2,1,0:T(8,128)(2,1)S(1)}, u32[]{:S(2)}, u32[]{:S(2)}) collective-permute-start(bf16[2,128,512]{2,1,0:T(8,128)(2,1)S(1)} %pad_maximum_fusion.6), channel_id=1, source_target_pairs={{0,2},{2,4},{4,6},{6,8},{8,10},{10,12},{12,14},{14,16},{16,18},{18... | collective-permute-start | bytes 786440 | tf_op jit(solution)/shard_map/ppermute | solution.py:44
  135.1 72.5 %collective-permute-start.7 = (bf16[2,128,512]{2,1,0:T(8,128)(2,1)S(1)}, bf16[2,128,512]{2,1,0:T(8,128)(2,1)S(1)}, u32[]{:S(2)}, u32[]{:S(2)}) collective-permute-start(bf16[2,128,512]{2,1,0:T(8,128)(2,1)S(1)} %pad_maximum_fusion.7), channel_id=1, source_target_pairs={{2,0},{4,2},{6,4},{8,6},{10,8},{12,10},{14,12},{16,14},{18,16},{20... | collective-permute-start | bytes 786440 | tf_op jit(solution)/shard_map/ppermute | solution.py:44
  180.5 31.6 %collective-permute-start.8 = (f32[2,128,512]{2,1,0:T(8,128)}, f32[2,128,512]{2,1,0:T(8,128)S(1)}, u32[]{:S(2)}, u32[]{:S(2)}) collective-permute-start(f32[2,128,512]{2,1,0:T(8,128)} %pad_maximum_fusion.3), channel_id=1, source_target_pairs={{16,0},{18,2},{20,4},{22,6},{24,8},{26,10},{28,12},{30,14},{17,1},... | collective-permute-start | bytes 1572872 | tf_op jit(solution)/shard_map/ppermute | solution.py:36
  208.3 85.7 %all-to-all-start.1 = ((bf16[16,128,512]{2,1,0:T(8,128)(2,1)}), bf16[16,128,512]{2,1,0:T(8,128)(2,1)S(1)}, u32[]{:S(2)}, u32[]{:S(2)}) async-start(bf16[16,128,512]{2,1,0:T(8,128)(2,1)} %get-tuple-element.28), calls=%async_computation.1 | async-start | bytes 4194304 | tf_op jit(solution)/shard_map/all_to_all | solution.py:307
  212.2 47.2 %collective-permute-start.9 = (f32[2,128,512]{2,1,0:T(8,128)S(1)}, f32[2,128,512]{2,1,0:T(8,128)S(1)}, u32[]{:S(2)}, u32[]{:S(2)}) collective-permute-start(f32[2,128,512]{2,1,0:T(8,128)S(1)} %fusion.20), channel_id=1, source_target_pairs={{8,0},{10,2},{12,4},{14,6},{9,1},{11,3},{13,5},{15,7}} | collective-permute-start | bytes 1572872 | tf_op jit(solution)/shard_map/ppermute | solution.py:36
  259.6 14.5 %collective-permute-start.10 = (f32[2,128,512]{2,1,0:T(8,128)S(1)}, f32[2,128,512]{2,1,0:T(8,128)S(1)}, u32[]{:S(2)}, u32[]{:S(2)}) collective-permute-start(f32[2,128,512]{2,1,0:T(8,128)S(1)} %fusion.23), channel_id=1, source_target_pairs={{4,0},{6,2},{5,1},{7,3}} | collective-permute-start | bytes 1572872 | tf_op jit(solution)/shard_map/ppermute | solution.py:36
  274.1 7.0 %collective-permute-start.11 = (f32[2,128,512]{2,1,0:T(8,128)S(1)}, f32[2,128,512]{2,1,0:T(8,128)}, u32[]{:S(2)}, u32[]{:S(2)}) collective-permute-start(f32[2,128,512]{2,1,0:T(8,128)S(1)} %add.185), channel_id=1, source_target_pairs={{2,0},{3,1}} | collective-permute-start | bytes 1572872 | tf_op jit(solution)/shard_map/ppermute | solution.py:36
  278.7 4.7 %copy-start.6 = (f32[1024,512]{1,0:T(8,128)S(1)}, f32[1024,512]{1,0:T(8,128)}, u32[]{:S(2)}) copy-start(f32[1024,512]{1,0:T(8,128)} %get-tuple-element.21) | copy-start | bytes 6291460
  279.9 3.5 %copy-start.5 = (f32[1024,512]{1,0:T(8,128)S(1)}, f32[1024,512]{1,0:T(8,128)}, u32[]{:S(2)}) copy-start(f32[1024,512]{1,0:T(8,128)} %get-tuple-element.20) | copy-start | bytes 6291460
  283.4 2.5 copy-start.2
  294.6 1.4 copy-start.7
  294.6 1.5 copy-start.8
  (1 other events, 0.7 us)

commit v3 on v2

--- a/solution.py
+++ b/solution.py
@@ -63,10 +63,10 @@
     return dq, dk, dv
 
 
-def local_kernel(kinds, ktab, mtab, q_ref, do_ref, nrm_ref, dlt_ref, k_ref, v_ref, dq_ref, dk_ref, dv_ref):
-    b = pl.program_id(0)
-    kind = pl.program_id(1)
-    mode = mtab[b * kinds + kind]
+def list_kernel(qin, qout, first, ktab, mtab, q_ref, do_ref, nrm_ref, dlt_ref, k_ref, v_ref, dq_ref, dk_ref, dv_ref):
+    p = pl.program_id(0)
+    mode = mtab[p]
+    lead = first[p]
     heads = nrm_ref.shape[0]
     width = q_ref.shape[1] // heads
     for h in range(heads):
@@ -76,11 +76,11 @@
             nrm_ref[h], dlt_ref[h], mode,
         )
 
-        @pl.when(kind == 0)
+        @pl.when(lead == 1)
         def _():
             dq_ref[:, cols] = dq
 
-        @pl.when(kind > 0)
+        @pl.when(lead == 0)
         def _():
             dq_ref[:, cols] += dq
 
@@ -113,39 +113,39 @@
             dv_ref[0, :, cols] = dv
 
 
-def local_pairs(kinds, ktab, mtab, queries, out_grad, norm3, delta3, key_cat, value_cat):
-    slot_count = 2 * PAIR
+def list_pairs(qin, qout, first, ktab, mtab, outs, queries, out_grad, norm3, delta3, key_src, value_src):
     rows, features = queries.shape
-    height = rows // slot_count
     heads = norm3.shape[0]
+    height = rows // (2 * PAIR)
+    count = ktab.shape[0]
     blk = (height, features)
     stat = (heads, 1, height)
     grid_spec = pltpu.PrefetchScalarGridSpec(
-        num_scalar_prefetch=2,
-        grid=(slot_count, kinds),
+        num_scalar_prefetch=5,
+        grid=(count,),
         in_specs=[
-            pl.BlockSpec(blk, lambda b, c, kt, mt: (b, 0)),
-            pl.BlockSpec(blk, lambda b, c, kt, mt: (b, 0)),
-            pl.BlockSpec(stat, lambda b, c, kt, mt: (0, 0, b)),
-            pl.BlockSpec(stat, lambda b, c, kt, mt: (0, 0, b)),
-            pl.BlockSpec(blk, lambda b, c, kt, mt: (kt[b * kinds + c], 0)),
-            pl.BlockSpec(blk, lambda b, c, kt, mt: (kt[b * kinds + c], 0)),
+            pl.BlockSpec(blk, lambda p, qi, qo, f, kt, mt: (qi[p], 0)),
+            pl.BlockSpec(blk, lambda p, qi, qo, f, kt, mt: (qi[p], 0)),
+            pl.BlockSpec(stat, lambda p, qi, qo, f, kt, mt: (0, 0, qi[p])),
+            pl.BlockSpec(stat, lambda p, qi, qo, f, kt, mt: (0, 0, qi[p])),
+            pl.BlockSpec(blk, lambda p, qi, qo, f, kt, mt: (kt[p], 0)),
+            pl.BlockSpec(blk, lambda p, qi, qo, f, kt, mt: (kt[p], 0)),
         ],
         out_specs=[
-            pl.BlockSpec(blk, lambda b, c, kt, mt: (b, 0)),
-            pl.BlockSpec(blk, lambda b, c, kt, mt: (b * kinds + c, 0)),
-            pl.BlockSpec(blk, lambda b, c, kt, mt: (b * kinds + c, 0)),
+            pl.BlockSpec(blk, lambda p, qi, qo, f, kt, mt: (qo[p], 0)),
+            pl.BlockSpec(blk, lambda p, qi, qo, f, kt, mt: (p, 0)),
+            pl.BlockSpec(blk, lambda p, qi, qo, f, kt, mt: (p, 0)),
         ],
     )
     return pl.pallas_call(
-        functools.partial(local_kernel, kinds),
+        list_kernel,
         grid_spec=grid_spec,
         out_shape=[
-            jax.ShapeDtypeStruct((rows, features), jnp.float32),
-            jax.ShapeDtypeStruct((rows * kinds, features), jnp.float32),
-            jax.ShapeDtypeStruct((rows * kinds, features), jnp.float32),
-        ],
-    )(ktab, mtab, queries, out_grad, norm3, delta3, key_cat, value_cat)
+            jax.ShapeDtypeStruct((outs * height, features), jnp.float32),
+            jax.ShapeDtypeStruct((count * height, features), jnp.float32),
+            jax.ShapeDtypeStruct((count * height, features), jnp.float32),
+        ],
+    )(qin, qout, first, ktab, mtab, queries, out_grad, norm3, delta3, key_src, value_src)
 
 
 def rand_pairs(ktab, mtab, arrived, key_rows, value_rows, heads):
@@ -216,41 +216,39 @@
     )
     last_prev = jnp.where(last_dev, 1, slot_count + 1).astype(jnp.int32)
     first_prev = jnp.where(first_dev, 0, 1).astype(jnp.int32)
-    ktab = jnp.stack(
-        [
-            jnp.int32(0), jnp.int32(slot_count),
-            jnp.int32(1), jnp.int32(0),
-            jnp.int32(2), jnp.int32(3),
-            jnp.int32(3), last_prev,
-        ]
-    )
-    mtab = jnp.stack(
-        [
-            jnp.int32(2), first_prev,
-            jnp.int32(2), jnp.int32(1),
-            jnp.int32(2), jnp.int32(1),
-            jnp.int32(2), jnp.int32(1),
-        ]
-    )
-    dq_win, dk_terms, dv_terms = local_pairs(
-        2, ktab, mtab, queries, out_grad, norm3, delta3, key_win, value_win
-    )
-    dk_terms = dk_terms.reshape(slot_count, 2, height, features)
-    dv_terms = dv_terms.reshape(slot_count, 2, height, features)
+    def table(*items):
+        return jnp.stack([jnp.asarray(x, jnp.int32) for x in items])
+
+    dq_own, dk_own, dv_own = list_pairs(
+        table(0, 1, 1, 2, 2, 3), table(0, 1, 1, 2, 2, 3), table(1, 1, 0, 1, 0, 1),
+        table(0, 1, 0, 2, 3, 3), table(2, 2, 1, 2, 1, 2), slot_count,
+        queries, out_grad, norm3, delta3, key_rows, values,
+    )
+    dk_own = dk_own.reshape(6, height, features)
+    dv_own = dv_own.reshape(6, height, features)
+    dq_rim, dk_rim, dv_rim = list_pairs(
+        table(0, slot_count - 1), table(0, 1), table(1, 1),
+        table(slot_count, last_prev), table(first_prev, 1), 2,
+        queries, out_grad, norm3, delta3, key_win, value_win,
+    )
+    dq_rim = dq_rim.reshape(2, height, features)
+    dk_rim = dk_rim.reshape(2, height, features)
+    dv_rim = dv_rim.reshape(2, height, features)
     glob_mode = (seq_blk >= WINDOW).astype(jnp.int32)
-    global_kv, dq_win, dk_terms, dv_terms = lax.optimization_barrier(
-        (global_kv, dq_win, dk_terms, dv_terms)
-    )
-    dq_glob, dk_glob, dv_glob = local_pairs(
-        1, jnp.zeros((slot_count,), jnp.int32), glob_mode, queries, out_grad, norm3, delta3,
-        global_kv[0], global_kv[1],
-    )
-    dq_local = dq_win + dq_glob
-
-    to_left = jnp.stack([dk_terms[0, 1], dv_terms[0, 1]]).astype(jnp.bfloat16)
-    to_right = jnp.stack([dk_terms[slot_count - 1, 1], dv_terms[slot_count - 1, 1]]).astype(
-        jnp.bfloat16
-    )
+    dq_glob, dk_glob, dv_glob = list_pairs(
+        table(0, 1, 2, 3), table(0, 1, 2, 3), table(1, 1, 1, 1), table(0, 0, 0, 0), glob_mode,
+        slot_count, queries, out_grad, norm3, delta3, global_kv[0], global_kv[1],
+    )
+    zero_blk = jnp.zeros((height, features), jnp.float32)
+    dq_local = (
+        dq_own + dq_glob
+        + jnp.concatenate([dq_rim[0:1], zero_blk[None], zero_blk[None], dq_rim[1:2]]).reshape(
+            row_count, features
+        )
+    )
+
+    to_left = jnp.stack([dk_rim[0], dv_rim[0]]).astype(jnp.bfloat16)
+    to_right = jnp.stack([dk_rim[1], dv_rim[1]]).astype(jnp.bfloat16)
     back_right = shift(to_left, "ctx", -1)
     back_left = shift(to_right, "ctx", 1)
 
@@ -301,7 +299,9 @@
     ktab_r = jnp.maximum(slot_recv - 1, 0)
     mtab_r = (slot_recv > 0).astype(jnp.int32)
     dq_rand, dk_rand, dv_rand = rand_pairs(ktab_r, mtab_r, arrived, key_rows, values, heads)
-    dq_rand, back_left, back_right = lax.optimization_barrier((dq_rand, back_left, back_right))
+    dq_rand, total, back_left, back_right = lax.optimization_barrier(
+        (dq_rand, total, back_left, back_right)
+    )
     back_left = back_left.astype(jnp.float32)
     back_right = back_right.astype(jnp.float32)
     returned = lax.all_to_all(dq_rand, "ctx", split_axis=0, concat_axis=0, tiled=True)
@@ -317,12 +317,12 @@
 
     owner_flag = jnp.where(first_dev, 1.0, 0.0).astype(jnp.float32)
 
-    def assemble(terms, which, rand_part):
+    def assemble(own, rim, which, rand_part):
         slots = [
-            terms[0, 0] + terms[1, 1] + total[which] * owner_flag,
-            terms[1, 0] + terms[slot_count - 1, 1] * own_tail + back_right[which],
-            terms[2, 0] + back_left[which],
-            terms[3, 0] + terms[2, 1],
+            own[0] + own[2] + total[which] * owner_flag,
+            own[1] + rim[1] * own_tail + back_right[which],
+            own[3] + back_left[which],
+            own[5] + own[4],
         ]
         whole = jnp.stack(slots) + rand_part
         return whole.reshape(row_count, features).astype(jnp.bfloat16)
@@ -330,8 +330,8 @@
     query_total = (dq_local + rand_query.reshape(row_count, features)).astype(jnp.bfloat16)
     return (
         query_total,
-        assemble(dk_terms, 0, rand_key),
-        assemble(dv_terms, 1, rand_value),
+        assemble(dk_own, dk_rim, 0, rand_key),
+        assemble(dv_own, dv_rim, 1, rand_value),
     )
 
 

time: 299 us -> 285 us (0.953)
  the two profiles are of different devices: /device:TPU:1 before, /device:TPU:11 now
where the time goes in v3:
time: 285 us; the launch traced here: 282 us
  waiting for transfers between devices  131 us (46%)
  Pallas kernels  57.6 us (20%)
  starting transfers between devices  37.9 us (13%)
  other arithmetic  35 us (12%)
  local copies, waits for them, and re-layouts  16.2 us (6%)
  matrix products  3.05 us (1%)
    ppermute x4, waiting for transfers between devices, spread_2(): array = array + lax.ppermute(array, axis, pairs)  101 us
    pallas_call x3, Pallas kernels, list_pairs(): pl.pallas_call(list_kernel, grid_spec=grid_spec, out_shape=[jax.ShapeDtyp...  35.7 us
    pallas_call x1, Pallas kernels, rand_pairs(): pl.pallas_call(functools.partial(rand_kernel, heads), grid_spec=grid_spec...  21.9 us
    all_to_all x1, waiting for transfers between devices, shards(): lax.all_to_all(dq_rand, 'ctx', split_axis=0, concat_axis=0, tiled=True)  15.3 us
    ppermute x4, waiting for transfers between devices, gather_to_root(): array = array + lax.ppermute(array, axis, pairs)  15 us
    ppermute x4, starting transfers between devices, shift(): return lax.ppermute(array, axis, pairs)  13.4 us
    all_to_all x1, starting transfers between devices, shards(): lax.all_to_all(dq_rand, 'ctx', split_axis=0, concat_axis=0, tiled=True)  8.99 us
    all_to_all x1, starting transfers between devices, shards(): lax.all_to_all(routed, 'ctx', split_axis=0, concat_axis=0, tiled=True)  6.69 us
  transfers between devices with their start and end apart: 14, of which 5 were waited for; matrix products, arithmetic and copies ran while one was open for 11% of the time, Pallas kernels for 20%

profile of v3, /device:TPU:11, one launch (start us, length us, event | category | flops | bytes accessed | tf_op | source)
XLA Modules:
  0.0 282.3 jit_solution(16620923215462447516)
XLA Ops:
  1.8 1.4 convert_multiply_fusion
  5.1 3.1 %convolution_convert_fusion = bf16[16,132096]{1,0:T(8,128)(2,1)} fusion(pred[16,4]{0,1:T(4,128)(4,1)S(1)} %fusion.9, bf16[4,132096]{1,0:T(4,128)(2,1)S(1)} %bitcast.86), kind=kOutput, calls=%fused_computation | convolution fusion | flops 19021824 | bytes 5283904 | tf_op jit(solution)/shard_map/dot_general | solution.py:289
  8.2 4.9 %reshape.202 = bf16[16,258,512]{2,1,0:T(8,128)(2,1)} reshape(bf16[16,132096]{1,0:T(8,128)(2,1)} %convolution_convert_fusion) | data formatting | bytes 8454144 | tf_op jit(solution)/shard_map/reshape | solution.py:292
  13.1 4.8 %pad_maximum_fusion = bf16[16,272,512]{2,1,0:T(8,128)(2,1)} fusion(bf16[16,14,512]{2,1,0:T(8,128)(2,1)S(1)} %broadcast_in_dim.42, bf16[16,258,512]{2,1,0:T(8,128)(2,1)} %reshape.202), kind=kLoop, calls=%fused_computation.4 | loop fusion | flops 8912896 | bytes 8912896 | tf_op jit(solution)/shard_map/concatenate | solution.py:296
  18.0 6.7 %all-to-all-start = ((bf16[16,272,512]{2,1,0:T(8,128)(2,1)}), bf16[16,272,512]{2,1,0:T(8,128)(2,1)}, u32[]{:S(2)}, u32[]{:S(2)}) async-start(bf16[16,272,512]{2,1,0:T(8,128)(2,1)} %pad_maximum_fusion), calls=%async_computation | async-start | bytes 8912896 | tf_op jit(solution)/shard_map/all_to_all | solution.py:297
  28.2 76.1 %collective-permute-done.2 = bf16[2,128,512]{2,1,0:T(8,128)(2,1)S(1)} collective-permute-done((bf16[2,128,512]{2,1,0:T(8,128)(2,1)S(1)}, bf16[2,128,512]{2,1,0:T(8,128)(2,1)S(1)}, u32[]{:S(2)}, u32[]{:S(2)}) %collective-permute-start.2) | collective-permute-done | bytes 262176 | tf_op jit(solution)/shard_map/ppermute | solution.py:24
  106.8 24.9 %collective-permute-done.3 = bf16[2,128,512]{2,1,0:T(8,128)(2,1)S(1)} collective-permute-done((bf16[2,128,512]{2,1,0:T(8,128)(2,1)S(1)}, bf16[2,128,512]{2,1,0:T(8,128)(2,1)S(1)}, u32[]{:S(2)}, u32[]{:S(2)}) %collective-permute-start.3) | collective-permute-done | bytes 262176 | tf_op jit(solution)/shard_map/ppermute | solution.py:24
  134.0 11.9 %shard_map.95 = (f32[512,512]{1,0:T(8,128)}, f32[512,512]{1,0:T(8,128)}, f32[512,512]{1,0:T(8,128)}) custom-call(s32[4]{0:T(128)} %iota.31.qin.qout, s32[4]{0:T(128)} %iota.31.qin.qout, s32[4]{0:T(128)} %broadcast_25_first.2.first, s32[4]{0:T(128)} %broadcast_24_ktab.2.ktab, s32[4]{0:T(128)} %compare_convert_fusion.2.mtab, bf16[512,512]{1,0:T(8,128)(2,1)} %q_ref.5, ...), custom_call_target="tpu_custom_call" | custom-call | tf_op jit(solution)/shard_map/pallas_call | solution.py:140
  149.9 14.3 %collective-permute-done.6 = f32[2,128,512]{2,1,0:T(8,128)S(1)} collective-permute-done((f32[2,128,512]{2,1,0:T(8,128)S(1)}, f32[2,128,512]{2,1,0:T(8,128)S(1)}, u32[]{:S(2)}, u32[]{:S(2)}) %collective-permute-start.6) | collective-permute-done | bytes 524320 | tf_op jit(solution)/shard_map/ppermute | solution.py:36
  164.3 2.1 collective-permute-start.7
  166.4 3.5 %collective-permute-start.5 = (bf16[2,128,512]{2,1,0:T(8,128)(2,1)S(1)}, bf16[2,128,512]{2,1,0:T(8,128)(2,1)S(1)}, u32[]{:S(2)}, u32[]{:S(2)}) collective-permute-start(bf16[2,128,512]{2,1,0:T(8,128)(2,1)S(1)} %pad_maximum_fusion.6), channel_id=1, source_target_pairs={{2,0},{4,2},{6,4},{8,6},{10,8},{12,10},{14,12},{16,14},{18,16},{20... | collective-permute-start | bytes 786440 | tf_op jit(solution)/shard_map/ppermute | solution.py:44
  170.7 2.9 %collective-permute-start.4 = (bf16[2,128,512]{2,1,0:T(8,128)(2,1)}, bf16[2,128,512]{2,1,0:T(8,128)(2,1)S(1)}, u32[]{:S(2)}, u32[]{:S(2)}) collective-permute-start(bf16[2,128,512]{2,1,0:T(8,128)(2,1)} %pad_maximum_fusion.5), channel_id=1, source_target_pairs={{0,2},{2,4},{4,6},{6,8},{8,10},{10,12},{12,14},{14,16},{16,18},{18... | collective-permute-start | bytes 786440 | tf_op jit(solution)/shard_map/ppermute | solution.py:44
  180.3 7.2 %shard_map.96 = (f32[256,512]{1,0:T(8,128)}, f32[256,512]{1,0:T(8,128)}, f32[256,512]{1,0:T(8,128)}) custom-call(s32[2]{0:T(128)} %iota_multiply_fusion.qin, s32[2]{0:T(128)} %iota.36.qout, s32[2]{0:T(128)} %broadcast_26_first.2.first, s32[2]{0:T(128)} %get-tuple-element.69.ktab, s32[2]{0:T(128)} %get-tuple-element.70.mtab, bf16[512,512]{1,0:T(8,128)(2,1)} %q_ref.5, ...), custom_call_target="tpu_custom_call" | custom-call | tf_op jit(solution)/shard_map/pallas_call | solution.py:140
  189.7 5.0 %collective-permute-start.10 = (bf16[2,128,512]{2,1,0:T(8,128)(2,1)S(1)}, bf16[2,128,512]{2,1,0:T(8,128)(2,1)S(1)}, u32[]{:S(2)}, u32[]{:S(2)}) collective-permute-start(bf16[2,128,512]{2,1,0:T(8,128)(2,1)S(1)} %pad_maximum_fusion.7), channel_id=1, source_target_pairs={{0,2},{2,4},{4,6},{6,8},{8,10},{10,12},{12,14},{14,16},{16,18},{18... | collective-permute-start | bytes 786440 | tf_op jit(solution)/shard_map/ppermute | solution.py:44
  194.7 1.9 collective-permute-start.11
  199.8 21.9 %shard_map.97 = (bf16[16,128,512]{2,1,0:T(8,128)(2,1)}, f32[16,128,512]{2,1,0:T(8,128)}, f32[16,128,512]{2,1,0:T(8,128)}) custom-call(s32[16]{0:T(128)} %add_maximum_fusion.ktab, s32[16]{0:T(128)} %compare_convert_fusion.1.mtab, bf16[16,272,512]{2,1,0:T(8,128)(2,1)} %all-to-all-done.q_ref.do_ref.st_ref, ...), custom_call_target="tpu_custom_call" | custom-call | tf_op jit(solution)/shard_map/pallas_call | solution.py:172
  222.4 9.0 %all-to-all-start.1 = ((bf16[16,128,512]{2,1,0:T(8,128)(2,1)}), bf16[16,128,512]{2,1,0:T(8,128)(2,1)S(1)}, u32[]{:S(2)}, u32[]{:S(2)}) async-start(bf16[16,128,512]{2,1,0:T(8,128)(2,1)} %get-tuple-element.27), calls=%async_computation.1 | async-start | bytes 4194304 | tf_op jit(solution)/shard_map/all_to_all | solution.py:307
  231.6 16.6 %shard_map.94 = (f32[512,512]{1,0:T(8,128)}, f32[768,512]{1,0:T(8,128)}, f32[768,512]{1,0:T(8,128)}) custom-call(s32[6]{0:T(128)} %constant.33.clone.1.qin.qout, s32[6]{0:T(128)} %constant.33.clone.1.qin.qout, s32[6]{0:T(128)} %constant.34.clone.1.first, s32[6]{0:T(128)} %constant.35.clone.1.ktab, s32[6]{0:T(128)} %constant.38.clone.1.mtab, ...), custom_call_target="tpu_custom_call" | custom-call | tf_op jit(solution)/shard_map/pallas_call | solution.py:140
  248.3 2.1 add_bitcast_fusion
  253.8 1.4 copy-done.4
  255.2 5.1 %multiply_reduce_fusion = (f32[4,128,512]{2,1,0:T(8,128)S(1)}, f32[4,128,512]{2,1,0:T(8,128)S(1)}) fusion(f32[16,128,512]{2,1,0:T(8,128)} %get-tuple-element.34, f32[16,4]{1,0:T(8,128)S(1)} %compare_convert_fusion, f32[16,128,512]{2,1,0:T(8,128)S(1)} %copy-done.4), kind=kLoop, calls=%fused_computation.1 | loop fusion | flops 16252928 | bytes 10486016 | tf_op jit(solution)/shard_map/reduce_sum | solution.py:314
  260.3 2.2 fusion
  263.5 15.3 %all-to-all-done.1 = bf16[16,128,512]{2,1,0:T(8,128)(2,1)S(1)} async-done(((bf16[16,128,512]{2,1,0:T(8,128)(2,1)}), bf16[16,128,512]{2,1,0:T(8,128)(2,1)S(1)}, u32[]{:S(2)}, u32[]{:S(2)}) %all-to-all-start.1) | async-done | bytes 2097184 | tf_op jit(solution)/shard_map/all_to_all | solution.py:307
  279.4 1.4 multiply_reduce_fusion.2
  (123 shorter events, 35.3 us)
Async XLA Ops:
  18.0 6.7 %copy-start.2 = (bf16[512,512]{1,0:T(8,128)(2,1)S(1)}, bf16[512,512]{1,0:T(8,128)(2,1)}, u32[]{:S(2)}) copy-start(bf16[512,512]{1,0:T(8,128)(2,1)} %k_ref.3) | copy-start | bytes 1572868
  18.0 6.7 %copy-start.3 = (bf16[512,512]{1,0:T(8,128)(2,1)S(1)}, bf16[512,512]{1,0:T(8,128)(2,1)}, u32[]{:S(2)}) copy-start(bf16[512,512]{1,0:T(8,128)(2,1)} %v_ref.3) | copy-start | bytes 1572868
  18.0 179.6 %all-to-all-start = ((bf16[16,272,512]{2,1,0:T(8,128)(2,1)}), bf16[16,272,512]{2,1,0:T(8,128)(2,1)}, u32[]{:S(2)}, u32[]{:S(2)}) async-start(bf16[16,272,512]{2,1,0:T(8,128)(2,1)} %pad_maximum_fusion), calls=%async_computation | async-start | bytes 8912896 | tf_op jit(solution)/shard_map/all_to_all | solution.py:297
  24.8 0.7 collective-permute-start
  25.5 0.7 collective-permute-start.1
  26.3 78.0 %collective-permute-start.2 = (bf16[2,128,512]{2,1,0:T(8,128)(2,1)S(1)}, bf16[2,128,512]{2,1,0:T(8,128)(2,1)S(1)}, u32[]{:S(2)}, u32[]{:S(2)}) collective-permute-start(bf16[2,128,512]{2,1,0:T(8,128)(2,1)S(1)} %fusion.23), channel_id=1, source_target_pairs={{0,8},{2,10},{4,12},{6,14},{1,9},{3,11},{5,13},{7,15}} | collective-permute-start | bytes 786440 | tf_op jit(solution)/shard_map/ppermute | solution.py:24
  104.3 27.3 %collective-permute-start.3 = (bf16[2,128,512]{2,1,0:T(8,128)(2,1)S(1)}, bf16[2,128,512]{2,1,0:T(8,128)(2,1)S(1)}, u32[]{:S(2)}, u32[]{:S(2)}) collective-permute-start(bf16[2,128,512]{2,1,0:T(8,128)(2,1)S(1)} %add.146), channel_id=1, source_target_pairs={{0,16},{2,18},{4,20},{6,22},{8,24},{10,26},{12,28},{14,30},{1,17},... | collective-permute-start | bytes 786440 | tf_op jit(solution)/shard_map/ppermute | solution.py:24
  148.6 15.6 %collective-permute-start.6 = (f32[2,128,512]{2,1,0:T(8,128)S(1)}, f32[2,128,512]{2,1,0:T(8,128)S(1)}, u32[]{:S(2)}, u32[]{:S(2)}) collective-permute-start(f32[2,128,512]{2,1,0:T(8,128)S(1)} %pad_maximum_fusion.4), channel_id=1, source_target_pairs={{16,0},{18,2},{20,4},{22,6},{24,8},{26,10},{28,12},{30,14},{17,1},... | collective-permute-start | bytes 1572872 | tf_op jit(solution)/shard_map/ppermute | solution.py:36
  164.3 11.1 %collective-permute-start.7 = (f32[2,128,512]{2,1,0:T(8,128)S(1)}, f32[2,128,512]{2,1,0:T(8,128)}, u32[]{:S(2)}, u32[]{:S(2)}) collective-permute-start(f32[2,128,512]{2,1,0:T(8,128)S(1)} %fusion.18), channel_id=1, source_target_pairs={{8,0},{10,2},{12,4},{14,6},{9,1},{11,3},{13,5},{15,7}} | collective-permute-start | bytes 1572872 | tf_op jit(solution)/shard_map/ppermute | solution.py:36
  166.4 10.9 %collective-permute-start.5 = (bf16[2,128,512]{2,1,0:T(8,128)(2,1)S(1)}, bf16[2,128,512]{2,1,0:T(8,128)(2,1)S(1)}, u32[]{:S(2)}, u32[]{:S(2)}) collective-permute-start(bf16[2,128,512]{2,1,0:T(8,128)(2,1)S(1)} %pad_maximum_fusion.6), channel_id=1, source_target_pairs={{2,0},{4,2},{6,4},{8,6},{10,8},{12,10},{14,12},{16,14},{18,16},{20... | collective-permute-start | bytes 786440 | tf_op jit(solution)/shard_map/ppermute | solution.py:44
  170.7 6.7 %collective-permute-start.4 = (bf16[2,128,512]{2,1,0:T(8,128)(2,1)}, bf16[2,128,512]{2,1,0:T(8,128)(2,1)S(1)}, u32[]{:S(2)}, u32[]{:S(2)}) collective-permute-start(bf16[2,128,512]{2,1,0:T(8,128)(2,1)} %pad_maximum_fusion.5), channel_id=1, source_target_pairs={{0,2},{2,4},{4,6},{6,8},{8,10},{10,12},{12,14},{14,16},{16,18},{18... | collective-permute-start | bytes 786440 | tf_op jit(solution)/shard_map/ppermute | solution.py:44
  176.6 11.0 %collective-permute-start.8 = (f32[2,128,512]{2,1,0:T(8,128)S(1)}, f32[2,128,512]{2,1,0:T(8,128)S(1)}, u32[]{:S(2)}, u32[]{:S(2)}) collective-permute-start(f32[2,128,512]{2,1,0:T(8,128)S(1)} %fusion.21), channel_id=1, source_target_pairs={{4,0},{6,2},{5,1},{7,3}} | collective-permute-start | bytes 1572872 | tf_op jit(solution)/shard_map/ppermute | solution.py:36
  187.7 9.0 %collective-permute-start.9 = (f32[2,128,512]{2,1,0:T(8,128)S(1)}, f32[2,128,512]{2,1,0:T(8,128)S(1)}, u32[]{:S(2)}, u32[]{:S(2)}) collective-permute-start(f32[2,128,512]{2,1,0:T(8,128)S(1)} %add.156), channel_id=1, source_target_pairs={{2,0},{3,1}} | collective-permute-start | bytes 1572872 | tf_op jit(solution)/shard_map/ppermute | solution.py:36
  189.7 32.0 %collective-permute-start.10 = (bf16[2,128,512]{2,1,0:T(8,128)(2,1)S(1)}, bf16[2,128,512]{2,1,0:T(8,128)(2,1)S(1)}, u32[]{:S(2)}, u32[]{:S(2)}) collective-permute-start(bf16[2,128,512]{2,1,0:T(8,128)(2,1)S(1)} %pad_maximum_fusion.7), channel_id=1, source_target_pairs={{0,2},{2,4},{4,6},{6,8},{8,10},{10,12},{12,14},{14,16},{16,18},{18... | collective-permute-start | bytes 786440 | tf_op jit(solution)/shard_map/ppermute | solution.py:44
  194.7 27.0 %collective-permute-start.11 = (bf16[2,128,512]{2,1,0:T(8,128)(2,1)S(1)}, bf16[2,128,512]{2,1,0:T(8,128)(2,1)S(1)}, u32[]{:S(2)}, u32[]{:S(2)}) collective-permute-start(bf16[2,128,512]{2,1,0:T(8,128)(2,1)S(1)} %pad_maximum_fusion.8), channel_id=1, source_target_pairs={{2,0},{4,2},{6,4},{8,6},{10,8},{12,10},{14,12},{16,14},{18,16},{20... | collective-permute-start | bytes 786440 | tf_op jit(solution)/shard_map/ppermute | solution.py:44
  222.4 56.4 %all-to-all-start.1 = ((bf16[16,128,512]{2,1,0:T(8,128)(2,1)}), bf16[16,128,512]{2,1,0:T(8,128)(2,1)S(1)}, u32[]{:S(2)}, u32[]{:S(2)}) async-start(bf16[16,128,512]{2,1,0:T(8,128)(2,1)} %get-tuple-element.27), calls=%async_computation.1 | async-start | bytes 4194304 | tf_op jit(solution)/shard_map/all_to_all | solution.py:307
  231.4 19.0 %copy-start.16 = (f32[256,512]{1,0:T(8,128)S(1)}, f32[256,512]{1,0:T(8,128)}, u32[]{:S(2)}) copy-start(f32[256,512]{1,0:T(8,128)} %get-tuple-element.21) | copy-start | bytes 1572868
  248.2 2.5 copy-start.18
  248.2 2.6 copy-start.15
  250.4 2.1 copy-start.14
  252.5 2.7 copy-start.4
  260.3 2.3 copy-start.8
  260.3 2.3 copy-start.9
  260.3 2.2 copy-start.10
  (10 other events, 14.1 us)

commit v4 on v3

--- a/solution.py
+++ b/solution.py
@@ -294,6 +294,9 @@
         slot_send.astype(jnp.bfloat16)[:, None, None], (ctx_size, STAT_ROWS - 2, features)
     )
     routed = jnp.concatenate([routed, slot_rows], axis=1)
+    routed, global_kv, from_left, from_right = lax.optimization_barrier(
+        (routed, global_kv, from_left, from_right)
+    )
     arrived = lax.all_to_all(routed, "ctx", split_axis=0, concat_axis=0, tiled=True)
     slot_recv = arrived[:, 2 * height + 2, 0].astype(jnp.float32).astype(jnp.int32)
     ktab_r = jnp.maximum(slot_recv - 1, 0)

time: 285 us -> 293 us (1.028)
  starting transfers between devices: 37.9 us -> 74.1 us
  waiting for transfers between devices: 131 us -> 103 us
  local copies, waits for them, and re-layouts: 16.2 us -> 19.8 us
    ppermute x4, waiting for transfers between devices: 101 us -> 12 us  [spread_2(): array = array + lax.ppermute(array, axis, pairs)]
    ppermute x4, waiting for transfers between devices: 15 us -> 75.2 us  [gather_to_root(): array = array + lax.ppermute(array, axis, pairs)]
    ppermute x4, starting transfers between devices: 4.91 us -> 40.1 us  [gather_to_root(): array = array + lax.ppermute(array, axis, pairs)]
  transfers between devices with their start and end apart: 14 -> 14, of which waited for: 5 -> 5; matrix products, arithmetic and copies ran while one was open for 11% -> 17% of each run, Pallas kernels for 20% -> 19%
where the time goes in v4:
time: 293 us; the launch traced here: 291 us
  waiting for transfers between devices  103 us (35%)
  starting transfers between devices  74.1 us (25%)
  Pallas kernels  56 us (19%)
  other arithmetic  34.4 us (12%)
  local copies, waits for them, and re-layouts  19.8 us (7%)
  matrix products  3.05 us (1%)
    ppermute x4, waiting for transfers between devices, gather_to_root(): array = array + lax.ppermute(array, axis, pairs)  75.2 us
    ppermute x4, starting transfers between devices, gather_to_root(): array = array + lax.ppermute(array, axis, pairs)  40.1 us
    pallas_call x3, Pallas kernels, list_pairs(): pl.pallas_call(list_kernel, grid_spec=grid_spec, out_shape=[jax.ShapeDtyp...  35.7 us
    pallas_call x1, Pallas kernels, rand_pairs(): pl.pallas_call(functools.partial(rand_kernel, heads), grid_spec=grid_spec...  20.3 us
    all_to_all x1, waiting for transfers between devices, shards(): lax.all_to_all(dq_rand, 'ctx', split_axis=0, concat_axis=0, tiled=True)  15.3 us
    ppermute x4, waiting for transfers between devices, spread_2(): array = array + lax.ppermute(array, axis, pairs)  12 us
    ppermute x4, starting transfers between devices, shift(): return lax.ppermute(array, axis, pairs)  11.2 us
    all_to_all x1, starting transfers between devices, shards(): lax.all_to_all(dq_rand, 'ctx', split_axis=0, concat_axis=0, tiled=True)  10.9 us
  transfers between devices with their start and end apart: 14, of which 5 were waited for; matrix products, arithmetic and copies ran while one was open for 17% of the time, Pallas kernels for 19%

profile of v4, /device:TPU:11, one launch (start us, length us, event | category | flops | bytes accessed | tf_op | source)
XLA Modules:
  0.0 291.2 jit_solution(6846481249007273863)
XLA Ops:
  3.5 3.7 %collective-permute-start.4 = (bf16[2,128,512]{2,1,0:T(8,128)(2,1)}, bf16[2,128,512]{2,1,0:T(8,128)(2,1)}, u32[]{:S(2)}, u32[]{:S(2)}) collective-permute-start(bf16[2,128,512]{2,1,0:T(8,128)(2,1)} %pad_maximum_fusion.5), channel_id=1, source_target_pairs={{0,2},{2,4},{4,6},{6,8},{8,10},{10,12},{12,14},{14,16},{16,18},{18... | collective-permute-start | bytes 786440 | tf_op jit(solution)/shard_map/ppermute | solution.py:44
  7.9 1.9 collective-permute-start.5
  16.9 3.0 %convolution_convert_fusion = bf16[16,132096]{1,0:T(8,128)(2,1)} fusion(pred[16,4]{0,1:T(4,128)(4,1)S(1)} %fusion.9, bf16[4,132096]{1,0:T(4,128)(2,1)S(1)} %bitcast.86), kind=kOutput, calls=%fused_computation | convolution fusion | flops 19021824 | bytes 5283904 | tf_op jit(solution)/shard_map/dot_general | solution.py:289
  20.0 11.4 %collective-permute-done.2 = bf16[2,128,512]{2,1,0:T(8,128)(2,1)S(1)} collective-permute-done((bf16[2,128,512]{2,1,0:T(8,128)(2,1)S(1)}, bf16[2,128,512]{2,1,0:T(8,128)(2,1)S(1)}, u32[]{:S(2)}, u32[]{:S(2)}) %collective-permute-start.2) | collective-permute-done | bytes 262176 | tf_op jit(solution)/shard_map/ppermute | solution.py:24
  32.8 4.9 %reshape.202 = bf16[16,258,512]{2,1,0:T(8,128)(2,1)} reshape(bf16[16,132096]{1,0:T(8,128)(2,1)} %convolution_convert_fusion) | data formatting | bytes 8454144 | tf_op jit(solution)/shard_map/reshape | solution.py:292
  37.8 4.8 %pad_maximum_fusion = bf16[16,272,512]{2,1,0:T(8,128)(2,1)} fusion(bf16[16,14,512]{2,1,0:T(8,128)(2,1)S(1)} %broadcast_in_dim.42, bf16[16,258,512]{2,1,0:T(8,128)(2,1)} %reshape.202), kind=kLoop, calls=%fused_computation.4 | loop fusion | flops 8912896 | bytes 8912896 | tf_op jit(solution)/shard_map/concatenate | solution.py:296
  43.4 7.2 %all-to-all-start = ((bf16[16,272,512]{2,1,0:T(8,128)(2,1)}), bf16[16,272,512]{2,1,0:T(8,128)(2,1)}, u32[]{:S(2)}, u32[]{:S(2)}) async-start(bf16[16,272,512]{2,1,0:T(8,128)(2,1)} %pad_maximum_fusion), calls=%async_computation | async-start | bytes 8912896 | tf_op jit(solution)/shard_map/all_to_all | solution.py:300
  54.7 11.9 %shard_map.95 = (f32[512,512]{1,0:T(8,128)}, f32[512,512]{1,0:T(8,128)}, f32[512,512]{1,0:T(8,128)}) custom-call(s32[4]{0:T(128)} %iota.31.qin.qout, s32[4]{0:T(128)} %iota.31.qin.qout, s32[4]{0:T(128)} %broadcast_25_first.2.first, s32[4]{0:T(128)} %broadcast_24_ktab.2.ktab, s32[4]{0:T(128)} %compare_convert_fusion.2.mtab, bf16[512,512]{1,0:T(8,128)(2,1)} %q_ref.5, ...), custom_call_target="tpu_custom_call" | custom-call | tf_op jit(solution)/shard_map/pallas_call | solution.py:140
  69.3 1.4 collective-permute-start.6
  70.7 66.1 %collective-permute-done.6 = f32[2,128,512]{2,1,0:T(8,128)S(1)} collective-permute-done((f32[2,128,512]{2,1,0:T(8,128)S(1)}, f32[2,128,512]{2,1,0:T(8,128)S(1)}, u32[]{:S(2)}, u32[]{:S(2)}) %collective-permute-start.6) | collective-permute-done | bytes 524320 | tf_op jit(solution)/shard_map/ppermute | solution.py:36
  136.9 37.2 %collective-permute-start.7 = (f32[2,128,512]{2,1,0:T(8,128)S(1)}, f32[2,128,512]{2,1,0:T(8,128)S(1)}, u32[]{:S(2)}, u32[]{:S(2)}) collective-permute-start(f32[2,128,512]{2,1,0:T(8,128)S(1)} %fusion.18), channel_id=1, source_target_pairs={{8,0},{10,2},{12,4},{14,6},{9,1},{11,3},{13,5},{15,7}} | collective-permute-start | bytes 1572872 | tf_op jit(solution)/shard_map/ppermute | solution.py:36
  175.2 9.2 %collective-permute-done.7 = f32[2,128,512]{2,1,0:T(8,128)S(1)} collective-permute-done((f32[2,128,512]{2,1,0:T(8,128)S(1)}, f32[2,128,512]{2,1,0:T(8,128)S(1)}, u32[]{:S(2)}, u32[]{:S(2)}) %collective-permute-start.7) | collective-permute-done | bytes 524320 | tf_op jit(solution)/shard_map/ppermute | solution.py:36
  190.3 7.2 %shard_map.96 = (f32[256,512]{1,0:T(8,128)}, f32[256,512]{1,0:T(8,128)}, f32[256,512]{1,0:T(8,128)}) custom-call(s32[2]{0:T(128)} %iota_multiply_fusion.qin, s32[2]{0:T(128)} %iota.36.qout, s32[2]{0:T(128)} %broadcast_26_first.2.first, s32[2]{0:T(128)} %get-tuple-element.71.ktab, s32[2]{0:T(128)} %get-tuple-element.72.mtab, bf16[512,512]{1,0:T(8,128)(2,1)} %q_ref.5, ...), custom_call_target="tpu_custom_call" | custom-call | tf_op jit(solution)/shard_map/pallas_call | solution.py:140
  199.6 1.9 collective-permute-start.10
  201.6 3.7 %collective-permute-start.11 = (bf16[2,128,512]{2,1,0:T(8,128)(2,1)S(1)}, bf16[2,128,512]{2,1,0:T(8,128)(2,1)S(1)}, u32[]{:S(2)}, u32[]{:S(2)}) collective-permute-start(bf16[2,128,512]{2,1,0:T(8,128)(2,1)S(1)} %pad_maximum_fusion.8), channel_id=1, source_target_pairs={{2,0},{4,2},{6,4},{8,6},{10,8},{12,10},{14,12},{16,14},{18,16},{20... | collective-permute-start | bytes 786440 | tf_op jit(solution)/shard_map/ppermute | solution.py:44
  208.4 20.3 %shard_map.97 = (bf16[16,128,512]{2,1,0:T(8,128)(2,1)}, f32[16,128,512]{2,1,0:T(8,128)}, f32[16,128,512]{2,1,0:T(8,128)}) custom-call(s32[16]{0:T(128)} %add_maximum_fusion.ktab, s32[16]{0:T(128)} %compare_convert_fusion.1.mtab, bf16[16,272,512]{2,1,0:T(8,128)(2,1)} %all-to-all-done.q_ref.do_ref.st_ref, ...), custom_call_target="tpu_custom_call" | custom-call | tf_op jit(solution)/shard_map/pallas_call | solution.py:172
  229.4 10.9 %all-to-all-start.1 = ((bf16[16,128,512]{2,1,0:T(8,128)(2,1)}), bf16[16,128,512]{2,1,0:T(8,128)(2,1)S(1)}, u32[]{:S(2)}, u32[]{:S(2)}) async-start(bf16[16,128,512]{2,1,0:T(8,128)(2,1)} %get-tuple-element.29), calls=%async_computation.1 | async-start | bytes 4194304 | tf_op jit(solution)/shard_map/all_to_all | solution.py:310
  240.6 16.6 %shard_map.94 = (f32[512,512]{1,0:T(8,128)}, f32[768,512]{1,0:T(8,128)}, f32[768,512]{1,0:T(8,128)}) custom-call(s32[6]{0:T(128)} %constant.33.clone.1.qin.qout, s32[6]{0:T(128)} %constant.33.clone.1.qin.qout, s32[6]{0:T(128)} %constant.34.clone.1.first, s32[6]{0:T(128)} %constant.35.clone.1.ktab, s32[6]{0:T(128)} %constant.38.clone.1.mtab, ...), custom_call_target="tpu_custom_call" | custom-call | tf_op jit(solution)/shard_map/pallas_call | solution.py:140
  257.2 2.1 add_bitcast_fusion
  262.8 1.4 copy-done.4
  264.1 5.1 %multiply_reduce_fusion = (f32[4,128,512]{2,1,0:T(8,128)S(1)}, f32[4,128,512]{2,1,0:T(8,128)S(1)}) fusion(f32[16,128,512]{2,1,0:T(8,128)} %get-tuple-element.36, f32[16,4]{1,0:T(8,128)S(1)} %compare_convert_fusion, f32[16,128,512]{2,1,0:T(8,128)S(1)} %copy-done.4), kind=kLoop, calls=%fused_computation.1 | loop fusion | flops 16252928 | bytes 10486016 | tf_op jit(solution)/shard_map/reduce_sum | solution.py:317
  269.3 2.2 fusion
  272.5 15.3 %all-to-all-done.1 = bf16[16,128,512]{2,1,0:T(8,128)(2,1)S(1)} async-done(((bf16[16,128,512]{2,1,0:T(8,128)(2,1)}), bf16[16,128,512]{2,1,0:T(8,128)(2,1)S(1)}, u32[]{:S(2)}, u32[]{:S(2)}) %all-to-all-start.1) | async-done | bytes 2097184 | tf_op jit(solution)/shard_map/all_to_all | solution.py:310
  288.4 1.4 multiply_reduce_fusion.2
  (131 shorter events, 39.1 us)
Async XLA Ops:
  0.6 9.2 %copy-start.19 = (bf16[512,512]{1,0:T(8,128)(2,1)S(1)}, bf16[512,512]{1,0:T(8,128)(2,1)}, u32[]{:S(2)}) copy-start(bf16[512,512]{1,0:T(8,128)(2,1)} %param.10) | copy-start | bytes 1572868
  0.6 9.2 %copy-start = (bf16[512,512]{1,0:T(8,128)(2,1)S(1)}, bf16[512,512]{1,0:T(8,128)(2,1)}, u32[]{:S(2)}) copy-start(bf16[512,512]{1,0:T(8,128)(2,1)} %do_ref.5) | copy-start | bytes 1572868
  2.0 10.2 %copy-start.23 = (s32[4,3]{1,0:T(4,128)S(1)}, s32[4,3]{1,0:T(4,128)}, u32[]{:S(2)}) copy-start(s32[4,3]{1,0:T(4,128)} %param.13) | copy-start | bytes 148
  2.1 8.0 %collective-permute-start = (bf16[2,128,512]{2,1,0:T(8,128)(2,1)S(1)}, bf16[2,128,512]{2,1,0:T(8,128)(2,1)S(1)}, u32[]{:S(2)}, u32[]{:S(2)}) collective-permute-start(bf16[2,128,512]{2,1,0:T(8,128)(2,1)S(1)} %maximum_select_fusion), channel_id=1, source_target_pairs={{0,2},{1,3}} | collective-permute-start | bytes 786440 | tf_op jit(solution)/shard_map/ppermute | solution.py:24
  3.5 39.9 %collective-permute-start.4 = (bf16[2,128,512]{2,1,0:T(8,128)(2,1)}, bf16[2,128,512]{2,1,0:T(8,128)(2,1)}, u32[]{:S(2)}, u32[]{:S(2)}) collective-permute-start(bf16[2,128,512]{2,1,0:T(8,128)(2,1)} %pad_maximum_fusion.5), channel_id=1, source_target_pairs={{0,2},{2,4},{4,6},{6,8},{8,10},{10,12},{12,14},{14,16},{16,18},{18... | collective-permute-start | bytes 786440 | tf_op jit(solution)/shard_map/ppermute | solution.py:44
  7.9 35.5 %collective-permute-start.5 = (bf16[2,128,512]{2,1,0:T(8,128)(2,1)}, bf16[2,128,512]{2,1,0:T(8,128)(2,1)}, u32[]{:S(2)}, u32[]{:S(2)}) collective-permute-start(bf16[2,128,512]{2,1,0:T(8,128)(2,1)} %pad_maximum_fusion.6), channel_id=1, source_target_pairs={{2,0},{4,2},{6,4},{8,6},{10,8},{12,10},{14,12},{16,14},{18,16},{20... | collective-permute-start | bytes 786440 | tf_op jit(solution)/shard_map/ppermute | solution.py:44
  10.0 3.6 %copy-start.22 = (bf16[4,512]{1,0:T(4,128)(2,1)S(1)}, bf16[4,512]{1,0:T(4,128)(2,1)}, u32[]{:S(2)}) copy-start(bf16[4,512]{1,0:T(4,128)(2,1)} %param.12) | copy-start | bytes 12292
  10.0 3.7 %copy-start.1 = (bf16[512,512]{1,0:T(8,128)(2,1)S(1)}, bf16[512,512]{1,0:T(8,128)(2,1)}, u32[]{:S(2)}) copy-start(bf16[512,512]{1,0:T(8,128)(2,1)} %q_ref.5) | copy-start | bytes 1572868
  10.8 3.6 %collective-permute-start.1 = (bf16[2,128,512]{2,1,0:T(8,128)(2,1)}, bf16[2,128,512]{2,1,0:T(8,128)(2,1)}, u32[]{:S(2)}, u32[]{:S(2)}) collective-permute-start(bf16[2,128,512]{2,1,0:T(8,128)(2,1)} %fusion.22), channel_id=1, source_target_pairs={{0,4},{2,6},{1,5},{3,7}} | collective-permute-start | bytes 786440 | tf_op jit(solution)/shard_map/ppermute | solution.py:24
  15.6 15.7 %collective-permute-start.2 = (bf16[2,128,512]{2,1,0:T(8,128)(2,1)S(1)}, bf16[2,128,512]{2,1,0:T(8,128)(2,1)S(1)}, u32[]{:S(2)}, u32[]{:S(2)}) collective-permute-start(bf16[2,128,512]{2,1,0:T(8,128)(2,1)S(1)} %fusion.23), channel_id=1, source_target_pairs={{0,8},{2,10},{4,12},{6,14},{1,9},{3,11},{5,13},{7,15}} | collective-permute-start | bytes 786440 | tf_op jit(solution)/shard_map/ppermute | solution.py:24
  31.4 11.9 %collective-permute-start.3 = (bf16[2,128,512]{2,1,0:T(8,128)(2,1)S(1)}, bf16[2,128,512]{2,1,0:T(8,128)(2,1)S(1)}, u32[]{:S(2)}, u32[]{:S(2)}) collective-permute-start(bf16[2,128,512]{2,1,0:T(8,128)(2,1)S(1)} %add.146), channel_id=1, source_target_pairs={{0,16},{2,18},{4,20},{6,22},{8,24},{10,26},{12,28},{14,30},{1,17},... | collective-permute-start | bytes 786440 | tf_op jit(solution)/shard_map/ppermute | solution.py:24
  43.4 162.8 %all-to-all-start = ((bf16[16,272,512]{2,1,0:T(8,128)(2,1)}), bf16[16,272,512]{2,1,0:T(8,128)(2,1)}, u32[]{:S(2)}, u32[]{:S(2)}) async-start(bf16[16,272,512]{2,1,0:T(8,128)(2,1)} %pad_maximum_fusion), calls=%async_computation | async-start | bytes 8912896 | tf_op jit(solution)/shard_map/all_to_all | solution.py:300
  69.3 117.9 %copy-start.2 = (bf16[512,512]{1,0:T(8,128)(2,1)S(1)}, bf16[512,512]{1,0:T(8,128)(2,1)}, u32[]{:S(2)}) copy-start(bf16[512,512]{1,0:T(8,128)(2,1)} %k_ref.3) | copy-start | bytes 1572868
  69.3 67.5 %collective-permute-start.6 = (f32[2,128,512]{2,1,0:T(8,128)S(1)}, f32[2,128,512]{2,1,0:T(8,128)S(1)}, u32[]{:S(2)}, u32[]{:S(2)}) collective-permute-start(f32[2,128,512]{2,1,0:T(8,128)S(1)} %pad_maximum_fusion.4), channel_id=1, source_target_pairs={{16,0},{18,2},{20,4},{22,6},{24,8},{26,10},{28,12},{30,14},{17,1},... | collective-permute-start | bytes 1572872 | tf_op jit(solution)/shard_map/ppermute | solution.py:36
  136.9 47.5 %collective-permute-start.7 = (f32[2,128,512]{2,1,0:T(8,128)S(1)}, f32[2,128,512]{2,1,0:T(8,128)S(1)}, u32[]{:S(2)}, u32[]{:S(2)}) collective-permute-start(f32[2,128,512]{2,1,0:T(8,128)S(1)} %fusion.18), channel_id=1, source_target_pairs={{8,0},{10,2},{12,4},{14,6},{9,1},{11,3},{13,5},{15,7}} | collective-permute-start | bytes 1572872 | tf_op jit(solution)/shard_map/ppermute | solution.py:36
  175.2 13.0 %copy-start.3 = (bf16[512,512]{1,0:T(8,128)(2,1)S(1)}, bf16[512,512]{1,0:T(8,128)(2,1)}, u32[]{:S(2)}) copy-start(bf16[512,512]{1,0:T(8,128)(2,1)} %v_ref.3) | copy-start | bytes 1572868
  184.5 13.0 %collective-permute-start.8 = (f32[2,128,512]{2,1,0:T(8,128)S(1)}, f32[2,128,512]{2,1,0:T(8,128)S(1)}, u32[]{:S(2)}, u32[]{:S(2)}) collective-permute-start(f32[2,128,512]{2,1,0:T(8,128)S(1)} %fusion.21), channel_id=1, source_target_pairs={{4,0},{6,2},{5,1},{7,3}} | collective-permute-start | bytes 1572872 | tf_op jit(solution)/shard_map/ppermute | solution.py:36
  197.6 7.6 %collective-permute-start.9 = (f32[2,128,512]{2,1,0:T(8,128)S(1)}, f32[2,128,512]{2,1,0:T(8,128)S(1)}, u32[]{:S(2)}, u32[]{:S(2)}) collective-permute-start(f32[2,128,512]{2,1,0:T(8,128)S(1)} %add.156), channel_id=1, source_target_pairs={{2,0},{3,1}} | collective-permute-start | bytes 1572872 | tf_op jit(solution)/shard_map/ppermute | solution.py:36
  199.6 29.1 %collective-permute-start.10 = (bf16[2,128,512]{2,1,0:T(8,128)(2,1)S(1)}, bf16[2,128,512]{2,1,0:T(8,128)(2,1)S(1)}, u32[]{:S(2)}, u32[]{:S(2)}) collective-permute-start(bf16[2,128,512]{2,1,0:T(8,128)(2,1)S(1)} %pad_maximum_fusion.7), channel_id=1, source_target_pairs={{0,2},{2,4},{4,6},{6,8},{8,10},{10,12},{12,14},{14,16},{16,18},{18... | collective-permute-start | bytes 786440 | tf_op jit(solution)/shard_map/ppermute | solution.py:44
  201.6 27.1 %collective-permute-start.11 = (bf16[2,128,512]{2,1,0:T(8,128)(2,1)S(1)}, bf16[2,128,512]{2,1,0:T(8,128)(2,1)S(1)}, u32[]{:S(2)}, u32[]{:S(2)}) collective-permute-start(bf16[2,128,512]{2,1,0:T(8,128)(2,1)S(1)} %pad_maximum_fusion.8), channel_id=1, source_target_pairs={{2,0},{4,2},{6,4},{8,6},{10,8},{12,10},{14,12},{16,14},{18,16},{20... | collective-permute-start | bytes 786440 | tf_op jit(solution)/shard_map/ppermute | solution.py:44
  229.4 58.4 %all-to-all-start.1 = ((bf16[16,128,512]{2,1,0:T(8,128)(2,1)}), bf16[16,128,512]{2,1,0:T(8,128)(2,1)S(1)}, u32[]{:S(2)}, u32[]{:S(2)}) async-start(bf16[16,128,512]{2,1,0:T(8,128)(2,1)} %get-tuple-element.29), calls=%async_computation.1 | async-start | bytes 4194304 | tf_op jit(solution)/shard_map/all_to_all | solution.py:310
  240.4 19.0 %copy-start.18 = (f32[256,512]{1,0:T(8,128)S(1)}, f32[256,512]{1,0:T(8,128)}, u32[]{:S(2)}) copy-start(f32[256,512]{1,0:T(8,128)} %get-tuple-element.22) | copy-start | bytes 1572868
  257.2 2.6 copy-start.17
  261.5 2.7 copy-start.4
  (14 other events, 25.0 us)

commit v5 on v4

--- a/solution.py
+++ b/solution.py
@@ -235,6 +235,9 @@
     dk_rim = dk_rim.reshape(2, height, features)
     dv_rim = dv_rim.reshape(2, height, features)
     glob_mode = (seq_blk >= WINDOW).astype(jnp.int32)
+    global_kv, dq_own, dk_own, dv_own, dq_rim, dk_rim, dv_rim = lax.optimization_barrier(
+        (global_kv, dq_own, dk_own, dv_own, dq_rim, dk_rim, dv_rim)
+    )
     dq_glob, dk_glob, dv_glob = list_pairs(
         table(0, 1, 2, 3), table(0, 1, 2, 3), table(1, 1, 1, 1), table(0, 0, 0, 0), glob_mode,
         slot_count, queries, out_grad, norm3, delta3, global_kv[0], global_kv[1],

time: 293 us -> 317 us (1.082)
  waiting for transfers between devices: 103 us -> 117 us
  starting transfers between devices: 74.1 us -> 84.4 us
  local copies, waits for them, and re-layouts: 19.8 us -> 15.7 us
    all_to_all x1, waiting for transfers between devices: 15.3 us -> 33.3 us  [shards(): lax.all_to_all(dq_rand, 'ctx', split_axis=0, concat_axis=0, tiled=True)]
    all_to_all x1, starting transfers between devices: 10.9 us -> 20.6 us  [shards(): lax.all_to_all(dq_rand, 'ctx', split_axis=0, concat_axis=0, tiled=True)]
    ppermute x4, waiting for transfers between devices: 12 us -> 6.01 us  [spread_2(): array = array + lax.ppermute(array, axis, pairs)]
  transfers between devices with their start and end apart: 14 -> 14, of which waited for: 5 -> 5; matrix products, arithmetic and copies ran while one was open for 17% -> 15% of each run, Pallas kernels for 19% -> 18%
where the time goes in v5:
time: 317 us; the launch traced here: 316 us
  waiting for transfers between devices  117 us (37%)
  starting transfers between devices  84.4 us (27%)
  Pallas kernels  58.3 us (18%)
  other arithmetic  36.2 us (11%)
  local copies, waits for them, and re-layouts  15.7 us (5%)
    ppermute x4, waiting for transfers between devices, gather_to_root(): array = array + lax.ppermute(array, axis, pairs)  77.6 us
    ppermute x4, starting transfers between devices, gather_to_root(): array = array + lax.ppermute(array, axis, pairs)  40 us
    pallas_call x3, Pallas kernels, list_pairs(): pl.pallas_call(list_kernel, grid_spec=grid_spec, out_shape=[jax.ShapeDtyp...  35.9 us
    all_to_all x1, waiting for transfers between devices, shards(): lax.all_to_all(dq_rand, 'ctx', split_axis=0, concat_axis=0, tiled=True)  33.3 us
    pallas_call x1, Pallas kernels, rand_pairs(): pl.pallas_call(functools.partial(rand_kernel, heads), grid_spec=grid_spec...  22.4 us
    all_to_all x1, starting transfers between devices, shards(): lax.all_to_all(dq_rand, 'ctx', split_axis=0, concat_axis=0, tiled=True)  20.6 us
    ppermute x4, starting transfers between devices, shift(): return lax.ppermute(array, axis, pairs)  12 us
    all_to_all x1, starting transfers between devices, shards(): lax.all_to_all(routed, 'ctx', split_axis=0, concat_axis=0, tiled=True)  7.06 us
  transfers between devices with their start and end apart: 14, of which 5 were waited for; matrix products, arithmetic and copies ran while one was open for 15% of the time, Pallas kernels for 18%

profile of v5, /device:TPU:11, one launch (start us, length us, event | category | flops | bytes accessed | tf_op | source)
XLA Modules:
  0.0 315.7 jit_solution(3914352498364346980)
XLA Ops:
  2.7 1.4 collective-permute-start
  4.8 2.6 collective-permute-start.5
  8.1 3.9 %collective-permute-start.4 = (bf16[2,128,512]{2,1,0:T(8,128)(2,1)}, bf16[2,128,512]{2,1,0:T(8,128)(2,1)}, u32[]{:S(2)}, u32[]{:S(2)}) collective-permute-start(bf16[2,128,512]{2,1,0:T(8,128)(2,1)} %pad_maximum_fusion.5), channel_id=1, source_target_pairs={{0,2},{2,4},{4,6},{6,8},{8,10},{10,12},{12,14},{14,16},{16,18},{18... | collective-permute-start | bytes 786440 | tf_op jit(solution)/shard_map/ppermute | solution.py:44
  14.5 3.0 convolution_convert_fusion
  17.6 5.0 %reshape.159 = bf16[16,258,512]{2,1,0:T(8,128)(2,1)} reshape(bf16[16,132096]{1,0:T(8,128)(2,1)} %convolution_convert_fusion) | data formatting | bytes 8454144 | tf_op jit(solution)/shard_map/reshape | solution.py:295
  22.6 4.8 %pad_maximum_fusion = bf16[16,272,512]{2,1,0:T(8,128)(2,1)} fusion(bf16[16,14,512]{2,1,0:T(8,128)(2,1)S(1)} %broadcast_in_dim.42, bf16[16,258,512]{2,1,0:T(8,128)(2,1)} %reshape.159), kind=kLoop, calls=%fused_computation.4 | loop fusion | flops 8912896 | bytes 8912896 | tf_op jit(solution)/shard_map/concatenate | solution.py:299
  31.5 16.8 %shard_map.94 = (f32[512,512]{1,0:T(8,128)}, f32[768,512]{1,0:T(8,128)}, f32[768,512]{1,0:T(8,128)}) custom-call(s32[6]{0:T(128)} %constant.39.clone.1.qin.qout, s32[6]{0:T(128)} %constant.39.clone.1.qin.qout, s32[6]{0:T(128)} %constant.40.clone.1.first, s32[6]{0:T(128)} %constant.78.clone.1.ktab, s32[6]{0:T(128)} %constant.79.clone.1.mtab, ...), custom_call_target="tpu_custom_call" | custom-call | tf_op jit(solution)/shard_map/pallas_call | solution.py:140
  52.6 5.6 %collective-permute-done.2 = bf16[2,128,512]{2,1,0:T(8,128)(2,1)S(1)} collective-permute-done((bf16[2,128,512]{2,1,0:T(8,128)(2,1)S(1)}, bf16[2,128,512]{2,1,0:T(8,128)(2,1)S(1)}, u32[]{:S(2)}, u32[]{:S(2)}) %collective-permute-start.2) | collective-permute-done | bytes 262176 | tf_op jit(solution)/shard_map/ppermute | solution.py:24
  62.6 7.2 %shard_map.95 = (f32[256,512]{1,0:T(8,128)}, f32[256,512]{1,0:T(8,128)}, f32[256,512]{1,0:T(8,128)}) custom-call(s32[2]{0:T(128)} %iota_multiply_fusion.qin, s32[2]{0:T(128)} %iota.32.qout, s32[2]{0:T(128)} %broadcast_26_first.2.first, s32[2]{0:T(128)} %get-tuple-element.84.ktab, s32[2]{0:T(128)} %get-tuple-element.85.mtab, bf16[512,512]{1,0:T(8,128)(2,1)} %q_ref.5, ...), custom_call_target="tpu_custom_call" | custom-call | tf_op jit(solution)/shard_map/pallas_call | solution.py:140
  70.3 7.1 %all-to-all-start = ((bf16[16,272,512]{2,1,0:T(8,128)(2,1)}), bf16[16,272,512]{2,1,0:T(8,128)(2,1)}, u32[]{:S(2)}, u32[]{:S(2)}) async-start(bf16[16,272,512]{2,1,0:T(8,128)(2,1)} %pad_maximum_fusion), calls=%async_computation | async-start | bytes 8912896 | tf_op jit(solution)/shard_map/all_to_all | solution.py:303
  80.3 11.9 %shard_map.96 = (f32[512,512]{1,0:T(8,128)}, f32[512,512]{1,0:T(8,128)}, f32[512,512]{1,0:T(8,128)}) custom-call(s32[4]{0:T(128)} %iota.33.qin.qout, s32[4]{0:T(128)} %iota.33.qin.qout, s32[4]{0:T(128)} %broadcast_25_first.2.first, s32[4]{0:T(128)} %broadcast_24_ktab.2.ktab, s32[4]{0:T(128)} %compare_convert_fusion.2.mtab, bf16[512,512]{1,0:T(8,128)(2,1)} %q_ref.5, ...), custom_call_target="tpu_custom_call" | custom-call | tf_op jit(solution)/shard_map/pallas_call | solution.py:140
  96.2 67.3 %collective-permute-done.6 = f32[2,128,512]{2,1,0:T(8,128)S(1)} collective-permute-done((f32[2,128,512]{2,1,0:T(8,128)S(1)}, f32[2,128,512]{2,1,0:T(8,128)S(1)}, u32[]{:S(2)}, u32[]{:S(2)}) %collective-permute-start.6) | collective-permute-done | bytes 524320 | tf_op jit(solution)/shard_map/ppermute | solution.py:36
  163.6 37.3 %collective-permute-start.7 = (f32[2,128,512]{2,1,0:T(8,128)S(1)}, f32[2,128,512]{2,1,0:T(8,128)S(1)}, u32[]{:S(2)}, u32[]{:S(2)}) collective-permute-start(f32[2,128,512]{2,1,0:T(8,128)S(1)} %fusion.14), channel_id=1, source_target_pairs={{8,0},{10,2},{12,4},{14,6},{9,1},{11,3},{13,5},{15,7}} | collective-permute-start | bytes 1572872 | tf_op jit(solution)/shard_map/ppermute | solution.py:36
  200.9 10.3 %collective-permute-done.7 = f32[2,128,512]{2,1,0:T(8,128)S(1)} collective-permute-done((f32[2,128,512]{2,1,0:T(8,128)S(1)}, f32[2,128,512]{2,1,0:T(8,128)S(1)}, u32[]{:S(2)}, u32[]{:S(2)}) %collective-permute-start.7) | collective-permute-done | bytes 524320 | tf_op jit(solution)/shard_map/ppermute | solution.py:36
  213.1 1.9 collective-permute-start.10
  215.0 3.7 %collective-permute-start.11 = (bf16[2,128,512]{2,1,0:T(8,128)(2,1)S(1)}, bf16[2,128,512]{2,1,0:T(8,128)(2,1)S(1)}, u32[]{:S(2)}, u32[]{:S(2)}) collective-permute-start(bf16[2,128,512]{2,1,0:T(8,128)(2,1)S(1)} %pad_maximum_fusion.8), channel_id=1, source_target_pairs={{2,0},{4,2},{6,4},{8,6},{10,8},{12,10},{14,12},{16,14},{18,16},{20... | collective-permute-start | bytes 786440 | tf_op jit(solution)/shard_map/ppermute | solution.py:44
  221.8 22.4 %shard_map.97 = (bf16[16,128,512]{2,1,0:T(8,128)(2,1)}, f32[16,128,512]{2,1,0:T(8,128)}, f32[16,128,512]{2,1,0:T(8,128)}) custom-call(s32[16]{0:T(128)} %add_maximum_fusion.ktab, s32[16]{0:T(128)} %compare_convert_fusion.1.mtab, bf16[16,272,512]{2,1,0:T(8,128)(2,1)} %all-to-all-done.q_ref.do_ref.st_ref, ...), custom_call_target="tpu_custom_call" | custom-call | tf_op jit(solution)/shard_map/pallas_call | solution.py:172
  244.3 20.6 %all-to-all-start.1 = ((bf16[16,128,512]{2,1,0:T(8,128)(2,1)}), bf16[16,128,512]{2,1,0:T(8,128)(2,1)S(1)}, u32[]{:S(2)}, u32[]{:S(2)}) async-start(bf16[16,128,512]{2,1,0:T(8,128)(2,1)} %get-tuple-element.43), calls=%async_computation.1 | async-start | bytes 4194304 | tf_op jit(solution)/shard_map/all_to_all | solution.py:313
  266.5 2.6 multiply_add_fusion.1
  269.1 5.1 %multiply_reduce_fusion = (f32[4,128,512]{2,1,0:T(8,128)S(1)}, f32[4,128,512]{2,1,0:T(8,128)S(1)}) fusion(f32[16,128,512]{2,1,0:T(8,128)} %get-tuple-element.50, f32[16,4]{1,0:T(8,128)S(1)} %compare_convert_fusion, f32[16,128,512]{2,1,0:T(8,128)S(1)} %copy-done.4), kind=kLoop, calls=%fused_computation.1 | loop fusion | flops 16252928 | bytes 10486016 | tf_op jit(solution)/shard_map/reduce_sum | solution.py:320
  274.2 2.2 fusion
  276.5 1.6 multiply_add_fusion
  279.1 33.3 %all-to-all-done.1 = bf16[16,128,512]{2,1,0:T(8,128)(2,1)S(1)} async-done(((bf16[16,128,512]{2,1,0:T(8,128)(2,1)}), bf16[16,128,512]{2,1,0:T(8,128)(2,1)S(1)}, u32[]{:S(2)}, u32[]{:S(2)}) %all-to-all-start.1) | async-done | bytes 2097184 | tf_op jit(solution)/shard_map/all_to_all | solution.py:313
  312.9 1.4 multiply_reduce_fusion.2
  (127 shorter events, 35.6 us)
Async XLA Ops:
  0.6 11.4 %copy-start.21 = (s32[4,3]{1,0:T(4,128)S(1)}, s32[4,3]{1,0:T(4,128)}, u32[]{:S(2)}) copy-start(s32[4,3]{1,0:T(4,128)} %param.13) | copy-start | bytes 148
  0.6 11.8 %copy-start.14 = (bf16[512,512]{1,0:T(8,128)(2,1)S(1)}, bf16[512,512]{1,0:T(8,128)(2,1)}, u32[]{:S(2)}) copy-start(bf16[512,512]{1,0:T(8,128)(2,1)} %param.10) | copy-start | bytes 1572868
  0.7 11.7 %copy-start = (bf16[512,512]{1,0:T(8,128)(2,1)S(1)}, bf16[512,512]{1,0:T(8,128)(2,1)}, u32[]{:S(2)}) copy-start(bf16[512,512]{1,0:T(8,128)(2,1)} %do_ref.5) | copy-start | bytes 1572868
  2.7 24.7 %collective-permute-start = (bf16[2,128,512]{2,1,0:T(8,128)(2,1)}, bf16[2,128,512]{2,1,0:T(8,128)(2,1)}, u32[]{:S(2)}, u32[]{:S(2)}) collective-permute-start(bf16[2,128,512]{2,1,0:T(8,128)(2,1)} %maximum_select_fusion), channel_id=1, source_target_pairs={{0,2},{1,3}} | collective-permute-start | bytes 786440 | tf_op jit(solution)/shard_map/ppermute | solution.py:24
  4.8 45.8 %collective-permute-start.5 = (bf16[2,128,512]{2,1,0:T(8,128)(2,1)}, bf16[2,128,512]{2,1,0:T(8,128)(2,1)}, u32[]{:S(2)}, u32[]{:S(2)}) collective-permute-start(bf16[2,128,512]{2,1,0:T(8,128)(2,1)} %pad_maximum_fusion.6), channel_id=1, source_target_pairs={{2,0},{4,2},{6,4},{8,6},{10,8},{12,10},{14,12},{16,14},{18,16},{20... | collective-permute-start | bytes 786440 | tf_op jit(solution)/shard_map/ppermute | solution.py:44
  8.1 43.5 %collective-permute-start.4 = (bf16[2,128,512]{2,1,0:T(8,128)(2,1)}, bf16[2,128,512]{2,1,0:T(8,128)(2,1)}, u32[]{:S(2)}, u32[]{:S(2)}) collective-permute-start(bf16[2,128,512]{2,1,0:T(8,128)(2,1)} %pad_maximum_fusion.5), channel_id=1, source_target_pairs={{0,2},{2,4},{4,6},{6,8},{8,10},{10,12},{12,14},{14,16},{16,18},{18... | collective-permute-start | bytes 786440 | tf_op jit(solution)/shard_map/ppermute | solution.py:44
  28.4 19.9 %collective-permute-start.1 = (bf16[2,128,512]{2,1,0:T(8,128)(2,1)S(1)}, bf16[2,128,512]{2,1,0:T(8,128)(2,1)S(1)}, u32[]{:S(2)}, u32[]{:S(2)}) collective-permute-start(bf16[2,128,512]{2,1,0:T(8,128)(2,1)S(1)} %fusion.21), channel_id=1, source_target_pairs={{0,4},{2,6},{1,5},{3,7}} | collective-permute-start | bytes 786440 | tf_op jit(solution)/shard_map/ppermute | solution.py:24
  31.5 28.2 %copy-start.2 = (bf16[512,512]{1,0:T(8,128)(2,1)S(1)}, bf16[512,512]{1,0:T(8,128)(2,1)}, u32[]{:S(2)}) copy-start(bf16[512,512]{1,0:T(8,128)(2,1)} %k_ref.3) | copy-start | bytes 1572868
  48.2 12.3 %copy-start.3 = (bf16[512,512]{1,0:T(8,128)(2,1)S(1)}, bf16[512,512]{1,0:T(8,128)(2,1)}, u32[]{:S(2)}) copy-start(bf16[512,512]{1,0:T(8,128)(2,1)} %v_ref.3) | copy-start | bytes 1572868
  49.3 8.9 %collective-permute-start.2 = (bf16[2,128,512]{2,1,0:T(8,128)(2,1)S(1)}, bf16[2,128,512]{2,1,0:T(8,128)(2,1)S(1)}, u32[]{:S(2)}, u32[]{:S(2)}) collective-permute-start(bf16[2,128,512]{2,1,0:T(8,128)(2,1)S(1)} %fusion.22), channel_id=1, source_target_pairs={{0,8},{2,10},{4,12},{6,14},{1,9},{3,11},{5,13},{7,15}} | collective-permute-start | bytes 786440 | tf_op jit(solution)/shard_map/ppermute | solution.py:24
  58.3 11.9 %collective-permute-start.3 = (bf16[2,128,512]{2,1,0:T(8,128)(2,1)S(1)}, bf16[2,128,512]{2,1,0:T(8,128)(2,1)S(1)}, u32[]{:S(2)}, u32[]{:S(2)}) collective-permute-start(bf16[2,128,512]{2,1,0:T(8,128)(2,1)S(1)} %add.126), channel_id=1, source_target_pairs={{0,16},{2,18},{4,20},{6,22},{8,24},{10,26},{12,28},{14,30},{1,17},... | collective-permute-start | bytes 786440 | tf_op jit(solution)/shard_map/ppermute | solution.py:24
  70.3 149.3 %all-to-all-start = ((bf16[16,272,512]{2,1,0:T(8,128)(2,1)}), bf16[16,272,512]{2,1,0:T(8,128)(2,1)}, u32[]{:S(2)}, u32[]{:S(2)}) async-start(bf16[16,272,512]{2,1,0:T(8,128)(2,1)} %pad_maximum_fusion), calls=%async_computation | async-start | bytes 8912896 | tf_op jit(solution)/shard_map/all_to_all | solution.py:303
  94.9 68.6 %collective-permute-start.6 = (f32[2,128,512]{2,1,0:T(8,128)S(1)}, f32[2,128,512]{2,1,0:T(8,128)S(1)}, u32[]{:S(2)}, u32[]{:S(2)}) collective-permute-start(f32[2,128,512]{2,1,0:T(8,128)S(1)} %pad_maximum_fusion.4), channel_id=1, source_target_pairs={{16,0},{18,2},{20,4},{22,6},{24,8},{26,10},{28,12},{30,14},{17,1},... | collective-permute-start | bytes 1572872 | tf_op jit(solution)/shard_map/ppermute | solution.py:36
  163.6 49.3 %copy-start.15 = (f32[256,512]{1,0:T(8,128)S(1)}, f32[256,512]{1,0:T(8,128)}, u32[]{:S(2)}) copy-start(f32[256,512]{1,0:T(8,128)} %get-tuple-element.32) | copy-start | bytes 1572868
  163.6 49.4 %copy-start.17 = (f32[256,512]{1,0:T(8,128)S(1)}, f32[256,512]{1,0:T(8,128)}, u32[]{:S(2)}) copy-start(f32[256,512]{1,0:T(8,128)} %get-tuple-element.31) | copy-start | bytes 1572868
  163.6 47.6 %collective-permute-start.7 = (f32[2,128,512]{2,1,0:T(8,128)S(1)}, f32[2,128,512]{2,1,0:T(8,128)S(1)}, u32[]{:S(2)}, u32[]{:S(2)}) collective-permute-start(f32[2,128,512]{2,1,0:T(8,128)S(1)} %fusion.14), channel_id=1, source_target_pairs={{8,0},{10,2},{12,4},{14,6},{9,1},{11,3},{13,5},{15,7}} | collective-permute-start | bytes 1572872 | tf_op jit(solution)/shard_map/ppermute | solution.py:36
  211.4 0.7 collective-permute-start.8
  212.2 6.5 %collective-permute-start.9 = (f32[2,128,512]{2,1,0:T(8,128)S(1)}, f32[2,128,512]{2,1,0:T(8,128)S(1)}, u32[]{:S(2)}, u32[]{:S(2)}) collective-permute-start(f32[2,128,512]{2,1,0:T(8,128)S(1)} %add.138), channel_id=1, source_target_pairs={{2,0},{3,1}} | collective-permute-start | bytes 1572872 | tf_op jit(solution)/shard_map/ppermute | solution.py:36
  213.1 31.2 %collective-permute-start.10 = (bf16[2,128,512]{2,1,0:T(8,128)(2,1)S(1)}, bf16[2,128,512]{2,1,0:T(8,128)(2,1)S(1)}, u32[]{:S(2)}, u32[]{:S(2)}) collective-permute-start(bf16[2,128,512]{2,1,0:T(8,128)(2,1)S(1)} %pad_maximum_fusion.7), channel_id=1, source_target_pairs={{0,2},{2,4},{4,6},{6,8},{8,10},{10,12},{12,14},{14,16},{16,18},{18... | collective-permute-start | bytes 786440 | tf_op jit(solution)/shard_map/ppermute | solution.py:44
  215.0 29.2 %collective-permute-start.11 = (bf16[2,128,512]{2,1,0:T(8,128)(2,1)S(1)}, bf16[2,128,512]{2,1,0:T(8,128)(2,1)S(1)}, u32[]{:S(2)}, u32[]{:S(2)}) collective-permute-start(bf16[2,128,512]{2,1,0:T(8,128)(2,1)S(1)} %pad_maximum_fusion.8), channel_id=1, source_target_pairs={{2,0},{4,2},{6,4},{8,6},{10,8},{12,10},{14,12},{16,14},{18,16},{20... | collective-permute-start | bytes 786440 | tf_op jit(solution)/shard_map/ppermute | solution.py:44
  244.2 20.9 %copy-start.13 = (f32[256,512]{1,0:T(8,128)S(1)}, f32[256,512]{1,0:T(8,128)}, u32[]{:S(2)}) copy-start(f32[256,512]{1,0:T(8,128)} %get-tuple-element.30) | copy-start | bytes 1572868
  244.3 20.9 %copy-start.18 = (bf16[2,128,512]{2,1,0:T(8,128)(2,1)}, bf16[2,128,512]{2,1,0:T(8,128)(2,1)S(1)}, u32[]{:S(2)}) copy-start(bf16[2,128,512]{2,1,0:T(8,128)(2,1)S(1)} %collective-permute-done.11) | copy-start | bytes 786436
  244.3 68.1 %all-to-all-start.1 = ((bf16[16,128,512]{2,1,0:T(8,128)(2,1)}), bf16[16,128,512]{2,1,0:T(8,128)(2,1)S(1)}, u32[]{:S(2)}, u32[]{:S(2)}) async-start(bf16[16,128,512]{2,1,0:T(8,128)(2,1)} %get-tuple-element.43), calls=%async_computation.1 | async-start | bytes 4194304 | tf_op jit(solution)/shard_map/all_to_all | solution.py:313
  266.2 2.9 copy-start.4
  (12 other events, 22.7 us)

commit v6 on v3

--- a/solution.py
+++ b/solution.py
@@ -283,17 +283,18 @@
             out_grad.reshape(slot_count, height, features),
             per_slot_row(log_norm),
             per_slot_row(delta),
+            jnp.zeros((slot_count, STAT_ROWS - 2, features), jnp.bfloat16),
         ],
         axis=1,
     )
-    routed = jnp.dot(
-        select, packed.reshape(slot_count, -1), preferred_element_type=jnp.float32
-    ).astype(jnp.bfloat16)
-    routed = routed.reshape(ctx_size, 2 * height + 2, features)
-    slot_rows = jnp.broadcast_to(
-        slot_send.astype(jnp.bfloat16)[:, None, None], (ctx_size, STAT_ROWS - 2, features)
-    )
-    routed = jnp.concatenate([routed, slot_rows], axis=1)
+    pick = select > 0
+    routed = jnp.sum(jnp.where(pick[:, :, None, None], packed[None], 0), axis=1).astype(
+        jnp.bfloat16
+    )
+    row_id = lax.broadcasted_iota(jnp.int32, (1, packed.shape[1], 1), 1)
+    routed = jnp.where(
+        row_id == 2 * height + 2, slot_send.astype(jnp.bfloat16)[:, None, None], routed
+    )
     arrived = lax.all_to_all(routed, "ctx", split_axis=0, concat_axis=0, tiled=True)
     slot_recv = arrived[:, 2 * height + 2, 0].astype(jnp.float32).astype(jnp.int32)
     ktab_r = jnp.maximum(slot_recv - 1, 0)

time: 285 us -> 284 us (level)
  other arithmetic: 35 us -> 43.6 us
  local copies, waits for them, and re-layouts: 16.2 us -> 9.14 us
  starting transfers between devices: 37.9 us -> 42.3 us
  matrix products: 3.05 us -> 0 us
    reduce_sum x0 -> x1, other arithmetic: none -> 5.31 us  [shards(): jnp.sum(jnp.where(pick[:, :, None, None], packed[None], 0), axis=1)]
    reshape x1 -> x0, local copies, waits for them, and re-layouts: 4.89 us -> none  [shards(): routed = routed.reshape(ctx_size, 2 * height + 2, features)]
    select_n x1 -> x2, other arithmetic: 0.7 us -> 5.53 us  [the longest x1 4.75 us: shards(): jnp.where(row_id == 2 * height + 2, slot_send.astype(jnp.bfloat16)[:, Non...]
    concatenate x1 -> x0, other arithmetic: 4.83 us -> none  [shards(): routed = jnp.concatenate([routed, slot_rows], axis=1)]
    all_to_all x1, starting transfers between devices: 8.99 us -> 13.5 us  [shards(): lax.all_to_all(dq_rand, 'ctx', split_axis=0, concat_axis=0, tiled=True)]
    unnamed x42 -> x25, local copies, waits for them, and re-layouts: 4.6 us -> 0.28 us
    dot_general x1 -> x0, matrix products: 3.05 us -> none  [shards(): jnp.dot(select, packed.reshape(slot_count, -1), preferred_element_type=jn...]
  transfers between devices with their start and end apart: 14 -> 14, of which waited for: 5 -> 5; matrix products, arithmetic and copies ran while one was open for 11% -> 12% of each run, Pallas kernels for 20% -> 20%
where the time goes in v6:
time: 284 us; the launch traced here: 283 us
  waiting for transfers between devices  131 us (46%)
  Pallas kernels  56 us (20%)
  other arithmetic  43.6 us (15%)
  starting transfers between devices  42.3 us (15%)
  local copies, waits for them, and re-layouts  9.14 us (3%)
    ppermute x4, waiting for transfers between devices, spread_2(): array = array + lax.ppermute(array, axis, pairs)  101 us
    pallas_call x3, Pallas kernels, list_pairs(): pl.pallas_call(list_kernel, grid_spec=grid_spec, out_shape=[jax.ShapeDtyp...  35.8 us
    pallas_call x1, Pallas kernels, rand_pairs(): pl.pallas_call(functools.partial(rand_kernel, heads), grid_spec=grid_spec...  20.3 us
    all_to_all x1, waiting for transfers between devices, shards(): lax.all_to_all(dq_rand, 'ctx', split_axis=0, concat_axis=0, tiled=True)  15 us
    ppermute x4, waiting for transfers between devices, gather_to_root(): array = array + lax.ppermute(array, axis, pairs)  15 us
    all_to_all x1, starting transfers between devices, shards(): lax.all_to_all(dq_rand, 'ctx', split_axis=0, concat_axis=0, tiled=True)  13.5 us
    ppermute x4, starting transfers between devices, shift(): return lax.ppermute(array, axis, pairs)  13.4 us
    all_to_all x1, starting transfers between devices, shards(): lax.all_to_all(routed, 'ctx', split_axis=0, concat_axis=0, tiled=True)  6.69 us
  transfers between devices with their start and end apart: 14, of which 5 were waited for; matrix products, arithmetic and copies ran while one was open for 12% of the time, Pallas kernels for 20%

profile of v6, /device:TPU:11, one launch (start us, length us, event | category | flops | bytes accessed | tf_op | source)
XLA Modules:
  0.0 283.3 jit_solution(4953587159230965605)
XLA Ops:
  2.5 1.3 convert_multiply_fusion
  5.9 5.3 %select_reduce_fusion = bf16[16,272,512]{2,1,0:T(8,128)(2,1)} fusion(pred[16,4]{1,0:T(8,128)(4,1)S(1)} %copy.22, bf16[4,272,512]{2,1,0:T(8,128)(2,1)S(1)} %concatenate.19), kind=kLoop, calls=%fused_computation | loop fusion | flops 15597568 | bytes 5570624 | tf_op jit(solution)/shard_map/reduce_sum | solution.py:291
  11.2 4.8 %broadcast_select_fusion = bf16[16,272,512]{2,1,0:T(8,128)(2,1)} fusion(bf16[16,272,512]{2,1,0:T(8,128)(2,1)} %select_reduce_fusion, pred[272]{0:T(512)(128)(4,1)S(1)} %iota_compare_fusion.2, bf16[16]{0:T(256)(128)(2,1)S(1)} %convert_element_type.106), kind=kLoop, calls=%fused_computation.4 | loop fusion | flops 2228224 | bytes 8913200 | tf_op jit(solution)/shard_map/jit(_where)/select_n | solution.py:295
  15.9 6.7 %all-to-all-start = ((bf16[16,272,512]{2,1,0:T(8,128)(2,1)}), bf16[16,272,512]{2,1,0:T(8,128)(2,1)}, u32[]{:S(2)}, u32[]{:S(2)}) async-start(bf16[16,272,512]{2,1,0:T(8,128)(2,1)} %broadcast_select_fusion), calls=%async_computation | async-start | bytes 8912896 | tf_op jit(solution)/shard_map/all_to_all | solution.py:298
  26.2 76.1 %collective-permute-done.2 = bf16[2,128,512]{2,1,0:T(8,128)(2,1)S(1)} collective-permute-done((bf16[2,128,512]{2,1,0:T(8,128)(2,1)S(1)}, bf16[2,128,512]{2,1,0:T(8,128)(2,1)S(1)}, u32[]{:S(2)}, u32[]{:S(2)}) %collective-permute-start.2) | collective-permute-done | bytes 262176 | tf_op jit(solution)/shard_map/ppermute | solution.py:24
  104.8 24.8 %collective-permute-done.3 = bf16[2,128,512]{2,1,0:T(8,128)(2,1)S(1)} collective-permute-done((bf16[2,128,512]{2,1,0:T(8,128)(2,1)S(1)}, bf16[2,128,512]{2,1,0:T(8,128)(2,1)S(1)}, u32[]{:S(2)}, u32[]{:S(2)}) %collective-permute-start.3) | collective-permute-done | bytes 262176 | tf_op jit(solution)/shard_map/ppermute | solution.py:24
  132.0 11.9 %shard_map.95 = (f32[512,512]{1,0:T(8,128)}, f32[512,512]{1,0:T(8,128)}, f32[512,512]{1,0:T(8,128)}) custom-call(s32[4]{0:T(128)} %iota.37.qin.qout, s32[4]{0:T(128)} %iota.37.qin.qout, s32[4]{0:T(128)} %broadcast_25_first.2.first, s32[4]{0:T(128)} %broadcast_24_ktab.2.ktab, s32[4]{0:T(128)} %compare_convert_fusion.2.mtab, bf16[512,512]{1,0:T(8,128)(2,1)} %q_ref.5, ...), custom_call_target="tpu_custom_call" | custom-call | tf_op jit(solution)/shard_map/pallas_call | solution.py:140
  147.9 14.3 %collective-permute-done.6 = f32[2,128,512]{2,1,0:T(8,128)S(1)} collective-permute-done((f32[2,128,512]{2,1,0:T(8,128)S(1)}, f32[2,128,512]{2,1,0:T(8,128)S(1)}, u32[]{:S(2)}, u32[]{:S(2)}) %collective-permute-start.6) | collective-permute-done | bytes 524320 | tf_op jit(solution)/shard_map/ppermute | solution.py:36
  162.3 2.1 collective-permute-start.7
  164.4 3.5 %collective-permute-start.5 = (bf16[2,128,512]{2,1,0:T(8,128)(2,1)S(1)}, bf16[2,128,512]{2,1,0:T(8,128)(2,1)S(1)}, u32[]{:S(2)}, u32[]{:S(2)}) collective-permute-start(bf16[2,128,512]{2,1,0:T(8,128)(2,1)S(1)} %pad_maximum_fusion.5), channel_id=1, source_target_pairs={{2,0},{4,2},{6,4},{8,6},{10,8},{12,10},{14,12},{16,14},{18,16},{20... | collective-permute-start | bytes 786440 | tf_op jit(solution)/shard_map/ppermute | solution.py:44
  168.7 2.9 %collective-permute-start.4 = (bf16[2,128,512]{2,1,0:T(8,128)(2,1)}, bf16[2,128,512]{2,1,0:T(8,128)(2,1)S(1)}, u32[]{:S(2)}, u32[]{:S(2)}) collective-permute-start(bf16[2,128,512]{2,1,0:T(8,128)(2,1)} %pad_maximum_fusion.4), channel_id=1, source_target_pairs={{0,2},{2,4},{4,6},{6,8},{8,10},{10,12},{12,14},{14,16},{16,18},{18... | collective-permute-start | bytes 786440 | tf_op jit(solution)/shard_map/ppermute | solution.py:44
  178.3 7.2 %shard_map.96 = (f32[256,512]{1,0:T(8,128)}, f32[256,512]{1,0:T(8,128)}, f32[256,512]{1,0:T(8,128)}) custom-call(s32[2]{0:T(128)} %iota_multiply_fusion.qin, s32[2]{0:T(128)} %iota.42.qout, s32[2]{0:T(128)} %broadcast_26_first.2.first, s32[2]{0:T(128)} %get-tuple-element.71.ktab, s32[2]{0:T(128)} %get-tuple-element.72.mtab, bf16[512,512]{1,0:T(8,128)(2,1)} %q_ref.5, ...), custom_call_target="tpu_custom_call" | custom-call | tf_op jit(solution)/shard_map/pallas_call | solution.py:140
  188.5 5.0 %collective-permute-start.10 = (bf16[2,128,512]{2,1,0:T(8,128)(2,1)S(1)}, bf16[2,128,512]{2,1,0:T(8,128)(2,1)S(1)}, u32[]{:S(2)}, u32[]{:S(2)}) collective-permute-start(bf16[2,128,512]{2,1,0:T(8,128)(2,1)S(1)} %pad_maximum_fusion.6), channel_id=1, source_target_pairs={{0,2},{2,4},{4,6},{6,8},{8,10},{10,12},{12,14},{14,16},{16,18},{18... | collective-permute-start | bytes 786440 | tf_op jit(solution)/shard_map/ppermute | solution.py:44
  193.6 1.9 collective-permute-start.11
  198.6 20.3 %shard_map.97 = (bf16[16,128,512]{2,1,0:T(8,128)(2,1)}, f32[16,128,512]{2,1,0:T(8,128)}, f32[16,128,512]{2,1,0:T(8,128)}) custom-call(s32[16]{0:T(128)} %add_maximum_fusion.ktab, s32[16]{0:T(128)} %compare_convert_fusion.1.mtab, bf16[16,272,512]{2,1,0:T(8,128)(2,1)} %all-to-all-done.q_ref.do_ref.st_ref, ...), custom_call_target="tpu_custom_call" | custom-call | tf_op jit(solution)/shard_map/pallas_call | solution.py:172
  218.9 13.5 %all-to-all-start.1 = ((bf16[16,128,512]{2,1,0:T(8,128)(2,1)}), bf16[16,128,512]{2,1,0:T(8,128)(2,1)S(1)}, u32[]{:S(2)}, u32[]{:S(2)}) async-start(bf16[16,128,512]{2,1,0:T(8,128)(2,1)} %get-tuple-element.27), calls=%async_computation.1 | async-start | bytes 4194304 | tf_op jit(solution)/shard_map/all_to_all | solution.py:308
  232.6 16.6 %shard_map.94 = (f32[512,512]{1,0:T(8,128)}, f32[768,512]{1,0:T(8,128)}, f32[768,512]{1,0:T(8,128)}) custom-call(s32[6]{0:T(128)} %constant.35.clone.1.qin.qout, s32[6]{0:T(128)} %constant.35.clone.1.qin.qout, s32[6]{0:T(128)} %constant.36.clone.1.first, s32[6]{0:T(128)} %constant.37.clone.1.ktab, s32[6]{0:T(128)} %constant.38.clone.1.mtab, ...), custom_call_target="tpu_custom_call" | custom-call | tf_op jit(solution)/shard_map/pallas_call | solution.py:140
  249.2 2.2 add_bitcast_fusion
  253.0 2.5 bitcast_add_fusion.3
  255.5 5.1 %multiply_reduce_fusion = (f32[4,128,512]{2,1,0:T(8,128)S(1)}, f32[4,128,512]{2,1,0:T(8,128)S(1)}) fusion(f32[16,128,512]{2,1,0:T(8,128)} %get-tuple-element.34, f32[16,4]{1,0:T(8,128)S(1)} %compare_convert_fusion, f32[16,128,512]{2,1,0:T(8,128)S(1)} %copy-done.4), kind=kLoop, calls=%fused_computation.1 | loop fusion | flops 16252928 | bytes 10486016 | tf_op jit(solution)/shard_map/reduce_sum | solution.py:315
  260.6 2.2 fusion
  262.7 2.1 fusion.1
  264.8 15.0 %all-to-all-done.1 = bf16[16,128,512]{2,1,0:T(8,128)(2,1)S(1)} async-done(((bf16[16,128,512]{2,1,0:T(8,128)(2,1)}), bf16[16,128,512]{2,1,0:T(8,128)(2,1)S(1)}, u32[]{:S(2)}, u32[]{:S(2)}) %all-to-all-start.1) | async-done | bytes 2097184 | tf_op jit(solution)/shard_map/all_to_all | solution.py:308
  280.4 1.4 multiply_reduce_fusion.2
  (107 shorter events, 33.3 us)
Async XLA Ops:
  0.6 4.7 %copy-start = (bf16[512,512]{1,0:T(8,128)(2,1)S(1)}, bf16[512,512]{1,0:T(8,128)(2,1)}, u32[]{:S(2)}) copy-start(bf16[512,512]{1,0:T(8,128)(2,1)} %do_ref.5) | copy-start | bytes 1572868
  0.6 4.7 %copy-start.1 = (bf16[512,512]{1,0:T(8,128)(2,1)S(1)}, bf16[512,512]{1,0:T(8,128)(2,1)}, u32[]{:S(2)}) copy-start(bf16[512,512]{1,0:T(8,128)(2,1)} %q_ref.5) | copy-start | bytes 1572868
  15.9 6.7 %copy-start.2 = (bf16[512,512]{1,0:T(8,128)(2,1)S(1)}, bf16[512,512]{1,0:T(8,128)(2,1)}, u32[]{:S(2)}) copy-start(bf16[512,512]{1,0:T(8,128)(2,1)} %k_ref.3) | copy-start | bytes 1572868
  15.9 6.7 %copy-start.3 = (bf16[512,512]{1,0:T(8,128)(2,1)S(1)}, bf16[512,512]{1,0:T(8,128)(2,1)}, u32[]{:S(2)}) copy-start(bf16[512,512]{1,0:T(8,128)(2,1)} %v_ref.3) | copy-start | bytes 1572868
  15.9 9.6 %copy-start.11 = (bf16[4,512]{1,0:T(4,128)(2,1)S(1)}, bf16[4,512]{1,0:T(4,128)(2,1)}, u32[]{:S(2)}) copy-start(bf16[4,512]{1,0:T(4,128)(2,1)} %param.12) | copy-start | bytes 12292
  15.9 180.4 %all-to-all-start = ((bf16[16,272,512]{2,1,0:T(8,128)(2,1)}), bf16[16,272,512]{2,1,0:T(8,128)(2,1)}, u32[]{:S(2)}, u32[]{:S(2)}) async-start(bf16[16,272,512]{2,1,0:T(8,128)(2,1)} %broadcast_select_fusion), calls=%async_computation | async-start | bytes 8912896 | tf_op jit(solution)/shard_map/all_to_all | solution.py:298
  22.8 0.7 collective-permute-start
  23.5 0.7 collective-permute-start.1
  24.3 78.0 %collective-permute-start.2 = (bf16[2,128,512]{2,1,0:T(8,128)(2,1)S(1)}, bf16[2,128,512]{2,1,0:T(8,128)(2,1)S(1)}, u32[]{:S(2)}, u32[]{:S(2)}) collective-permute-start(bf16[2,128,512]{2,1,0:T(8,128)(2,1)S(1)} %fusion.21), channel_id=1, source_target_pairs={{0,8},{2,10},{4,12},{6,14},{1,9},{3,11},{5,13},{7,15}} | collective-permute-start | bytes 786440 | tf_op jit(solution)/shard_map/ppermute | solution.py:24
  102.3 27.3 %collective-permute-start.3 = (bf16[2,128,512]{2,1,0:T(8,128)(2,1)S(1)}, bf16[2,128,512]{2,1,0:T(8,128)(2,1)S(1)}, u32[]{:S(2)}, u32[]{:S(2)}) collective-permute-start(bf16[2,128,512]{2,1,0:T(8,128)(2,1)S(1)} %add.146), channel_id=1, source_target_pairs={{0,16},{2,18},{4,20},{6,22},{8,24},{10,26},{12,28},{14,30},{1,17},... | collective-permute-start | bytes 786440 | tf_op jit(solution)/shard_map/ppermute | solution.py:24
  146.6 15.6 %collective-permute-start.6 = (f32[2,128,512]{2,1,0:T(8,128)S(1)}, f32[2,128,512]{2,1,0:T(8,128)S(1)}, u32[]{:S(2)}, u32[]{:S(2)}) collective-permute-start(f32[2,128,512]{2,1,0:T(8,128)S(1)} %pad_maximum_fusion.3), channel_id=1, source_target_pairs={{16,0},{18,2},{20,4},{22,6},{24,8},{26,10},{28,12},{30,14},{17,1},... | collective-permute-start | bytes 1572872 | tf_op jit(solution)/shard_map/ppermute | solution.py:36
  162.3 11.1 %collective-permute-start.7 = (f32[2,128,512]{2,1,0:T(8,128)S(1)}, f32[2,128,512]{2,1,0:T(8,128)}, u32[]{:S(2)}, u32[]{:S(2)}) collective-permute-start(f32[2,128,512]{2,1,0:T(8,128)S(1)} %fusion.18), channel_id=1, source_target_pairs={{8,0},{10,2},{12,4},{14,6},{9,1},{11,3},{13,5},{15,7}} | collective-permute-start | bytes 1572872 | tf_op jit(solution)/shard_map/ppermute | solution.py:36
  164.4 10.9 %collective-permute-start.5 = (bf16[2,128,512]{2,1,0:T(8,128)(2,1)S(1)}, bf16[2,128,512]{2,1,0:T(8,128)(2,1)S(1)}, u32[]{:S(2)}, u32[]{:S(2)}) collective-permute-start(bf16[2,128,512]{2,1,0:T(8,128)(2,1)S(1)} %pad_maximum_fusion.5), channel_id=1, source_target_pairs={{2,0},{4,2},{6,4},{8,6},{10,8},{12,10},{14,12},{16,14},{18,16},{20... | collective-permute-start | bytes 786440 | tf_op jit(solution)/shard_map/ppermute | solution.py:44
  168.7 6.7 %collective-permute-start.4 = (bf16[2,128,512]{2,1,0:T(8,128)(2,1)}, bf16[2,128,512]{2,1,0:T(8,128)(2,1)S(1)}, u32[]{:S(2)}, u32[]{:S(2)}) collective-permute-start(bf16[2,128,512]{2,1,0:T(8,128)(2,1)} %pad_maximum_fusion.4), channel_id=1, source_target_pairs={{0,2},{2,4},{4,6},{6,8},{8,10},{10,12},{12,14},{14,16},{16,18},{18... | collective-permute-start | bytes 786440 | tf_op jit(solution)/shard_map/ppermute | solution.py:44
  174.6 10.9 %collective-permute-start.8 = (f32[2,128,512]{2,1,0:T(8,128)S(1)}, f32[2,128,512]{2,1,0:T(8,128)S(1)}, u32[]{:S(2)}, u32[]{:S(2)}) collective-permute-start(f32[2,128,512]{2,1,0:T(8,128)S(1)} %fusion.19), channel_id=1, source_target_pairs={{4,0},{6,2},{5,1},{7,3}} | collective-permute-start | bytes 1572872 | tf_op jit(solution)/shard_map/ppermute | solution.py:36
  185.6 9.9 %collective-permute-start.9 = (f32[2,128,512]{2,1,0:T(8,128)S(1)}, f32[2,128,512]{2,1,0:T(8,128)S(1)}, u32[]{:S(2)}, u32[]{:S(2)}) collective-permute-start(f32[2,128,512]{2,1,0:T(8,128)S(1)} %add.156), channel_id=1, source_target_pairs={{2,0},{3,1}} | collective-permute-start | bytes 1572872 | tf_op jit(solution)/shard_map/ppermute | solution.py:36
  188.5 30.4 %collective-permute-start.10 = (bf16[2,128,512]{2,1,0:T(8,128)(2,1)S(1)}, bf16[2,128,512]{2,1,0:T(8,128)(2,1)S(1)}, u32[]{:S(2)}, u32[]{:S(2)}) collective-permute-start(bf16[2,128,512]{2,1,0:T(8,128)(2,1)S(1)} %pad_maximum_fusion.6), channel_id=1, source_target_pairs={{0,2},{2,4},{4,6},{6,8},{8,10},{10,12},{12,14},{14,16},{16,18},{18... | collective-permute-start | bytes 786440 | tf_op jit(solution)/shard_map/ppermute | solution.py:44
  193.6 25.4 %collective-permute-start.11 = (bf16[2,128,512]{2,1,0:T(8,128)(2,1)S(1)}, bf16[2,128,512]{2,1,0:T(8,128)(2,1)S(1)}, u32[]{:S(2)}, u32[]{:S(2)}) collective-permute-start(bf16[2,128,512]{2,1,0:T(8,128)(2,1)S(1)} %pad_maximum_fusion.7), channel_id=1, source_target_pairs={{2,0},{4,2},{6,4},{8,6},{10,8},{12,10},{14,12},{16,14},{18,16},{20... | collective-permute-start | bytes 786440 | tf_op jit(solution)/shard_map/ppermute | solution.py:44
  218.9 32.5 %copy-start.9 = (f32[256,512]{1,0:T(8,128)S(1)}, f32[256,512]{1,0:T(8,128)}, u32[]{:S(2)}) copy-start(f32[256,512]{1,0:T(8,128)} %get-tuple-element.21) | copy-start | bytes 1572868
  218.9 32.6 %copy-start.10 = (bf16[2,128,512]{2,1,0:T(8,128)(2,1)}, bf16[2,128,512]{2,1,0:T(8,128)(2,1)S(1)}, u32[]{:S(2)}) copy-start(bf16[2,128,512]{2,1,0:T(8,128)(2,1)S(1)} %collective-permute-done.11) | copy-start | bytes 786436
  218.9 60.9 %all-to-all-start.1 = ((bf16[16,128,512]{2,1,0:T(8,128)(2,1)}), bf16[16,128,512]{2,1,0:T(8,128)(2,1)S(1)}, u32[]{:S(2)}, u32[]{:S(2)}) async-start(bf16[16,128,512]{2,1,0:T(8,128)(2,1)} %get-tuple-element.27), calls=%async_computation.1 | async-start | bytes 4194304 | tf_op jit(solution)/shard_map/all_to_all | solution.py:308
  249.2 3.8 %copy-start.5 = (f32[768,512]{1,0:T(8,128)S(1)}, f32[768,512]{1,0:T(8,128)}, u32[]{:S(2)}) copy-start(f32[768,512]{1,0:T(8,128)} %get-tuple-element.28) | copy-start | bytes 4718596
  249.2 3.8 %copy-start.6 = (f32[768,512]{1,0:T(8,128)S(1)}, f32[768,512]{1,0:T(8,128)}, u32[]{:S(2)}) copy-start(f32[768,512]{1,0:T(8,128)} %get-tuple-element.33) | copy-start | bytes 4718596
  251.5 4.0 %copy-start.4 = (f32[16,128,512]{2,1,0:T(8,128)S(1)}, f32[16,128,512]{2,1,0:T(8,128)}, u32[]{:S(2)}) copy-start(f32[16,128,512]{2,1,0:T(8,128)} %get-tuple-element.32) | copy-start | bytes 12582916
  (2 other events, 2.9 us)

commit v7 on v6

--- a/solution.py
+++ b/solution.py
@@ -14,27 +14,40 @@
 STAT_ROWS = 16
 
 
+RADIX = 4
+
+
 def spread_2(array, axis, root):
     count = lax.axis_size(axis)
     mine = lax.axis_index(axis) == root
     array = jnp.where(mine, array, jnp.zeros_like(array))
     step = 1
-    while step < count:
-        pairs = [(i, i + step) for i in range(step) if i + step < count]
-        array = array + lax.ppermute(array, axis, pairs)
-        step *= 2
+    while step * RADIX < count:
+        step *= RADIX
+    while step >= 1:
+        arrived = [
+            lax.ppermute(array, axis, [(i, i + j * step) for i in range(0, count, RADIX * step) if i + j * step < count])
+            for j in range(1, RADIX)
+            if j * step < count
+        ]
+        for part in arrived:
+            array = array + part
+        step //= RADIX
     return array
 
 
 def gather_to_root(array, axis):
     count = lax.axis_size(axis)
     step = 1
-    while step * 2 < count:
-        step *= 2
-    while step >= 1:
-        pairs = [(i + step, i) for i in range(step) if i + step < count]
-        array = array + lax.ppermute(array, axis, pairs)
-        step //= 2
+    while step < count:
+        arrived = [
+            lax.ppermute(array, axis, [(i + j * step, i) for i in range(0, count, RADIX * step) if i + j * step < count])
+            for j in range(1, RADIX)
+            if j * step < count
+        ]
+        for part in arrived:
+            array = array + part
+        step *= RADIX
     return array
 
 

time: 284 us -> 253 us (0.89)
  waiting for transfers between devices: 131 us -> 87 us
  starting transfers between devices: 42.3 us -> 52 us
    ppermute x8 -> x12, waiting for transfers between devices: 116 us -> 72 us  [the longest x6 72 us: spread_2(): lax.ppermute(array, axis, [(i, i + j * step) for i in range(0, count, RAD...]
    ppermute x8 -> x12, starting transfers between devices: 8.75 us -> 12.7 us  [the longest x6 8.04 us: gather_to_root(): lax.ppermute(array, axis, [(i + j * step, i) for i in range(0, count, RAD...]
    ppermute x4, starting transfers between devices: 13.4 us -> 17.2 us  [shift(): return lax.ppermute(array, axis, pairs)]
  transfers between devices with their start and end apart: 14 -> 18, of which waited for: 5 -> 2; matrix products, arithmetic and copies ran while one was open for 12% -> 14% of each run, Pallas kernels for 20% -> 23%
where the time goes in v7:
time: 253 us; the launch traced here: 252 us
  waiting for transfers between devices  87 us (34%)
  Pallas kernels  57.4 us (23%)
  starting transfers between devices  52 us (21%)
  other arithmetic  44.1 us (17%)
  local copies, waits for them, and re-layouts  10.2 us (4%)
    ppermute x6, waiting for transfers between devices, spread_2(): lax.ppermute(array, axis, [(i, i + j * step) for i in range(0, count, RAD...  72 us
    pallas_call x3, Pallas kernels, list_pairs(): pl.pallas_call(list_kernel, grid_spec=grid_spec, out_shape=[jax.ShapeDtyp...  35.8 us
    pallas_call x1, Pallas kernels, rand_pairs(): pl.pallas_call(functools.partial(rand_kernel, heads), grid_spec=grid_spec...  21.7 us
    ppermute x4, starting transfers between devices, shift(): return lax.ppermute(array, axis, pairs)  17.2 us
    all_to_all x1, starting transfers between devices, shards(): lax.all_to_all(dq_rand, 'ctx', split_axis=0, concat_axis=0, tiled=True)  15.4 us
    all_to_all x1, waiting for transfers between devices, shards(): lax.all_to_all(dq_rand, 'ctx', split_axis=0, concat_axis=0, tiled=True)  15 us
    ppermute x6, starting transfers between devices, gather_to_root(): lax.ppermute(array, axis, [(i + j * step, i) for i in range(0, count, RAD...  8.04 us
    all_to_all x1, starting transfers between devices, shards(): lax.all_to_all(routed, 'ctx', split_axis=0, concat_axis=0, tiled=True)  6.69 us
  transfers between devices with their start and end apart: 18, of which 2 were waited for; matrix products, arithmetic and copies ran while one was open for 14% of the time, Pallas kernels for 23%

profile of v7, /device:TPU:11, one launch (start us, length us, event | category | flops | bytes accessed | tf_op | source)
XLA Modules:
  0.0 252.0 jit_solution(4711260613804021518)
XLA Ops:
  2.5 1.3 convert_multiply_fusion
  5.9 5.3 %select_reduce_fusion = bf16[16,272,512]{2,1,0:T(8,128)(2,1)} fusion(pred[16,4]{1,0:T(8,128)(4,1)S(1)} %copy.22, bf16[4,272,512]{2,1,0:T(8,128)(2,1)S(1)} %concatenate.19), kind=kLoop, calls=%fused_computation | loop fusion | flops 15597568 | bytes 5570624 | tf_op jit(solution)/shard_map/reduce_sum | solution.py:304
  11.2 4.7 %broadcast_select_fusion = bf16[16,272,512]{2,1,0:T(8,128)(2,1)} fusion(bf16[16,272,512]{2,1,0:T(8,128)(2,1)} %select_reduce_fusion, pred[272]{0:T(512)(128)(4,1)S(1)} %iota_compare_fusion.2, bf16[16]{0:T(256)(128)(2,1)S(1)} %convert_element_type.106), kind=kLoop, calls=%fused_computation.4 | loop fusion | flops 2228224 | bytes 8913200 | tf_op jit(solution)/shard_map/jit(_where)/select_n | solution.py:308
  15.9 6.7 %all-to-all-start = ((bf16[16,272,512]{2,1,0:T(8,128)(2,1)}), bf16[16,272,512]{2,1,0:T(8,128)(2,1)}, u32[]{:S(2)}, u32[]{:S(2)}) async-start(bf16[16,272,512]{2,1,0:T(8,128)(2,1)} %broadcast_select_fusion), calls=%async_computation | async-start | bytes 8912896 | tf_op jit(solution)/shard_map/all_to_all | solution.py:311
  25.5 2.3 collective-permute-start.7
  28.5 4.2 %collective-permute-start.6 = (bf16[2,128,512]{2,1,0:T(8,128)(2,1)}, bf16[2,128,512]{2,1,0:T(8,128)(2,1)}, u32[]{:S(2)}, u32[]{:S(2)}) collective-permute-start(bf16[2,128,512]{2,1,0:T(8,128)(2,1)} %pad_maximum_fusion.4), channel_id=1, source_target_pairs={{0,2},{2,4},{4,6},{6,8},{8,10},{10,12},{12,14},{14,16},{16,18},{18... | collective-permute-start | bytes 786440 | tf_op jit(solution)/shard_map/ppermute | solution.py:57
  38.4 72.0 %collective-permute-done.5 = bf16[2,128,512]{2,1,0:T(8,128)(2,1)S(1)} collective-permute-done((bf16[2,128,512]{2,1,0:T(8,128)(2,1)S(1)}, bf16[2,128,512]{2,1,0:T(8,128)(2,1)S(1)}, u32[]{:S(2)}, u32[]{:S(2)}) %collective-permute-start.5) | collective-permute-done | bytes 262176 | tf_op jit(solution)/shard_map/ppermute | solution.py:29
  112.8 11.9 %shard_map.95 = (f32[512,512]{1,0:T(8,128)}, f32[512,512]{1,0:T(8,128)}, f32[512,512]{1,0:T(8,128)}) custom-call(s32[4]{0:T(128)} %iota.37.qin.qout, s32[4]{0:T(128)} %iota.37.qin.qout, s32[4]{0:T(128)} %broadcast_25_first.2.first, s32[4]{0:T(128)} %broadcast_24_ktab.2.ktab, s32[4]{0:T(128)} %compare_convert_fusion.2.mtab, bf16[512,512]{1,0:T(8,128)(2,1)} %q_ref.5, ...), custom_call_target="tpu_custom_call" | custom-call | tf_op jit(solution)/shard_map/pallas_call | solution.py:153
  124.7 1.3 reduce_sum.79
  126.0 1.3 reduce_sum.78
  128.2 4.6 %collective-permute-start.10 = (f32[2,128,512]{2,1,0:T(8,128)}, f32[2,128,512]{2,1,0:T(8,128)S(1)}, u32[]{:S(2)}, u32[]{:S(2)}) collective-permute-start(f32[2,128,512]{2,1,0:T(8,128)} %pad_maximum_fusion.3), channel_id=1, source_target_pairs={{6,0},{14,8},{22,16},{30,24},{7,1},{15,9},{23,17},{31,25}} | collective-permute-start | bytes 1572872 | tf_op jit(solution)/shard_map/ppermute | solution.py:44
  138.2 7.2 %shard_map.96 = (f32[256,512]{1,0:T(8,128)}, f32[256,512]{1,0:T(8,128)}, f32[256,512]{1,0:T(8,128)}) custom-call(s32[2]{0:T(128)} %iota_multiply_fusion.qin, s32[2]{0:T(128)} %iota.42.qout, s32[2]{0:T(128)} %broadcast_26_first.2.first, s32[2]{0:T(128)} %get-tuple-element.71.ktab, s32[2]{0:T(128)} %get-tuple-element.72.mtab, bf16[512,512]{1,0:T(8,128)(2,1)} %q_ref.5, ...), custom_call_target="tpu_custom_call" | custom-call | tf_op jit(solution)/shard_map/pallas_call | solution.py:153
  149.9 8.9 %collective-permute-start.14 = (bf16[2,128,512]{2,1,0:T(8,128)(2,1)S(1)}, bf16[2,128,512]{2,1,0:T(8,128)(2,1)S(1)}, u32[]{:S(2)}, u32[]{:S(2)}) collective-permute-start(bf16[2,128,512]{2,1,0:T(8,128)(2,1)S(1)} %pad_maximum_fusion.6), channel_id=1, source_target_pairs={{0,2},{2,4},{4,6},{6,8},{8,10},{10,12},{12,14},{14,16},{16,18},{18... | collective-permute-start | bytes 786440 | tf_op jit(solution)/shard_map/ppermute | solution.py:57
  158.9 1.9 collective-permute-start.15
  164.1 21.7 %shard_map.97 = (bf16[16,128,512]{2,1,0:T(8,128)(2,1)}, f32[16,128,512]{2,1,0:T(8,128)}, f32[16,128,512]{2,1,0:T(8,128)}) custom-call(s32[16]{0:T(128)} %add_maximum_fusion.ktab, s32[16]{0:T(128)} %compare_convert_fusion.1.mtab, bf16[16,272,512]{2,1,0:T(8,128)(2,1)} %all-to-all-done.q_ref.do_ref.st_ref, ...), custom_call_target="tpu_custom_call" | custom-call | tf_op jit(solution)/shard_map/pallas_call | solution.py:185
  185.8 15.4 %all-to-all-start.1 = ((bf16[16,128,512]{2,1,0:T(8,128)(2,1)}), bf16[16,128,512]{2,1,0:T(8,128)(2,1)S(1)}, u32[]{:S(2)}, u32[]{:S(2)}) async-start(bf16[16,128,512]{2,1,0:T(8,128)(2,1)} %get-tuple-element.27), calls=%async_computation.1 | async-start | bytes 4194304 | tf_op jit(solution)/shard_map/all_to_all | solution.py:321
  201.3 16.6 %shard_map.94 = (f32[512,512]{1,0:T(8,128)}, f32[768,512]{1,0:T(8,128)}, f32[768,512]{1,0:T(8,128)}) custom-call(s32[6]{0:T(128)} %constant.35.clone.1.qin.qout, s32[6]{0:T(128)} %constant.35.clone.1.qin.qout, s32[6]{0:T(128)} %constant.36.clone.1.first, s32[6]{0:T(128)} %constant.37.clone.1.ktab, s32[6]{0:T(128)} %constant.38.clone.1.mtab, ...), custom_call_target="tpu_custom_call" | custom-call | tf_op jit(solution)/shard_map/pallas_call | solution.py:153
  218.0 2.2 add_bitcast_fusion
  221.7 2.5 bitcast_add_fusion.3
  224.2 5.1 %multiply_reduce_fusion = (f32[4,128,512]{2,1,0:T(8,128)S(1)}, f32[4,128,512]{2,1,0:T(8,128)S(1)}) fusion(f32[16,128,512]{2,1,0:T(8,128)} %get-tuple-element.34, f32[16,4]{1,0:T(8,128)S(1)} %compare_convert_fusion, f32[16,128,512]{2,1,0:T(8,128)S(1)} %copy-done.4), kind=kLoop, calls=%fused_computation.1 | loop fusion | flops 16252928 | bytes 10486016 | tf_op jit(solution)/shard_map/reduce_sum | solution.py:328
  229.3 2.2 fusion
  231.5 2.1 fusion.1
  233.6 15.0 %all-to-all-done.1 = bf16[16,128,512]{2,1,0:T(8,128)(2,1)S(1)} async-done(((bf16[16,128,512]{2,1,0:T(8,128)(2,1)}), bf16[16,128,512]{2,1,0:T(8,128)(2,1)S(1)}, u32[]{:S(2)}, u32[]{:S(2)}) %all-to-all-start.1) | async-done | bytes 2097184 | tf_op jit(solution)/shard_map/all_to_all | solution.py:321
  249.2 1.4 multiply_reduce_fusion.2
  (111 shorter events, 33.1 us)
Async XLA Ops:
  0.6 4.7 %copy-start = (bf16[512,512]{1,0:T(8,128)(2,1)S(1)}, bf16[512,512]{1,0:T(8,128)(2,1)}, u32[]{:S(2)}) copy-start(bf16[512,512]{1,0:T(8,128)(2,1)} %do_ref.5) | copy-start | bytes 1572868
  15.9 6.7 %copy-start.2 = (bf16[512,512]{1,0:T(8,128)(2,1)S(1)}, bf16[512,512]{1,0:T(8,128)(2,1)}, u32[]{:S(2)}) copy-start(bf16[512,512]{1,0:T(8,128)(2,1)} %k_ref.3) | copy-start | bytes 1572868
  15.9 6.7 %copy-start.3 = (bf16[512,512]{1,0:T(8,128)(2,1)S(1)}, bf16[512,512]{1,0:T(8,128)(2,1)}, u32[]{:S(2)}) copy-start(bf16[512,512]{1,0:T(8,128)(2,1)} %v_ref.3) | copy-start | bytes 1572868
  15.9 146.0 %all-to-all-start = ((bf16[16,272,512]{2,1,0:T(8,128)(2,1)}), bf16[16,272,512]{2,1,0:T(8,128)(2,1)}, u32[]{:S(2)}, u32[]{:S(2)}) async-start(bf16[16,272,512]{2,1,0:T(8,128)(2,1)} %broadcast_select_fusion), calls=%async_computation | async-start | bytes 8912896 | tf_op jit(solution)/shard_map/all_to_all | solution.py:311
  22.6 13.4 %copy-start.11 = (bf16[4,512]{1,0:T(4,128)(2,1)S(1)}, bf16[4,512]{1,0:T(4,128)(2,1)}, u32[]{:S(2)}) copy-start(bf16[4,512]{1,0:T(4,128)(2,1)} %param.12) | copy-start | bytes 12292
  22.7 10.0 %collective-permute-start.2 = (bf16[2,128,512]{2,1,0:T(8,128)(2,1)S(1)}, bf16[2,128,512]{2,1,0:T(8,128)(2,1)S(1)}, u32[]{:S(2)}, u32[]{:S(2)}) collective-permute-start(bf16[2,128,512]{2,1,0:T(8,128)(2,1)S(1)} %maximum_select_fusion), channel_id=1, source_target_pairs={{0,24},{1,25}} | collective-permute-start | bytes 786440 | tf_op jit(solution)/shard_map/ppermute | solution.py:29
  23.4 9.3 %collective-permute-start.1 = (bf16[2,128,512]{2,1,0:T(8,128)(2,1)S(1)}, bf16[2,128,512]{2,1,0:T(8,128)(2,1)S(1)}, u32[]{:S(2)}, u32[]{:S(2)}) collective-permute-start(bf16[2,128,512]{2,1,0:T(8,128)(2,1)S(1)} %maximum_select_fusion), channel_id=1, source_target_pairs={{0,16},{1,17}} | collective-permute-start | bytes 786440 | tf_op jit(solution)/shard_map/ppermute | solution.py:29
  24.1 8.6 %collective-permute-start = (bf16[2,128,512]{2,1,0:T(8,128)(2,1)S(1)}, bf16[2,128,512]{2,1,0:T(8,128)(2,1)S(1)}, u32[]{:S(2)}, u32[]{:S(2)}) collective-permute-start(bf16[2,128,512]{2,1,0:T(8,128)(2,1)S(1)} %maximum_select_fusion), channel_id=1, source_target_pairs={{0,8},{1,9}} | collective-permute-start | bytes 786440 | tf_op jit(solution)/shard_map/ppermute | solution.py:29
  25.5 108.7 %collective-permute-start.7 = (bf16[2,128,512]{2,1,0:T(8,128)(2,1)}, bf16[2,128,512]{2,1,0:T(8,128)(2,1)S(1)}, u32[]{:S(2)}, u32[]{:S(2)}) collective-permute-start(bf16[2,128,512]{2,1,0:T(8,128)(2,1)} %pad_maximum_fusion.5), channel_id=1, source_target_pairs={{2,0},{4,2},{6,4},{8,6},{10,8},{12,10},{14,12},{16,14},{18,16},{20... | collective-permute-start | bytes 786440 | tf_op jit(solution)/shard_map/ppermute | solution.py:57
  28.5 105.7 %collective-permute-start.6 = (bf16[2,128,512]{2,1,0:T(8,128)(2,1)}, bf16[2,128,512]{2,1,0:T(8,128)(2,1)}, u32[]{:S(2)}, u32[]{:S(2)}) collective-permute-start(bf16[2,128,512]{2,1,0:T(8,128)(2,1)} %pad_maximum_fusion.4), channel_id=1, source_target_pairs={{0,2},{2,4},{4,6},{6,8},{8,10},{10,12},{12,14},{14,16},{16,18},{18... | collective-permute-start | bytes 786440 | tf_op jit(solution)/shard_map/ppermute | solution.py:57
  32.8 77.5 %collective-permute-start.5 = (bf16[2,128,512]{2,1,0:T(8,128)(2,1)S(1)}, bf16[2,128,512]{2,1,0:T(8,128)(2,1)S(1)}, u32[]{:S(2)}, u32[]{:S(2)}) collective-permute-start(bf16[2,128,512]{2,1,0:T(8,128)(2,1)S(1)} %add_add_fusion.3), channel_id=1, source_target_pairs={{0,6},{8,14},{16,22},{24,30},{1,7},{9,15},{17,23},{25,31}} | collective-permute-start | bytes 786440 | tf_op jit(solution)/shard_map/ppermute | solution.py:29
  34.1 76.2 %collective-permute-start.4 = (bf16[2,128,512]{2,1,0:T(8,128)(2,1)S(1)}, bf16[2,128,512]{2,1,0:T(8,128)(2,1)S(1)}, u32[]{:S(2)}, u32[]{:S(2)}) collective-permute-start(bf16[2,128,512]{2,1,0:T(8,128)(2,1)S(1)} %add_add_fusion.3), channel_id=1, source_target_pairs={{0,4},{8,12},{16,20},{24,28},{1,5},{9,13},{17,21},{25,29}} | collective-permute-start | bytes 786440 | tf_op jit(solution)/shard_map/ppermute | solution.py:29
  34.8 75.6 %collective-permute-start.3 = (bf16[2,128,512]{2,1,0:T(8,128)(2,1)S(1)}, bf16[2,128,512]{2,1,0:T(8,128)(2,1)S(1)}, u32[]{:S(2)}, u32[]{:S(2)}) collective-permute-start(bf16[2,128,512]{2,1,0:T(8,128)(2,1)S(1)} %add_add_fusion.3), channel_id=1, source_target_pairs={{0,2},{8,10},{16,18},{24,26},{1,3},{9,11},{17,19},{25,27}} | collective-permute-start | bytes 786440 | tf_op jit(solution)/shard_map/ppermute | solution.py:29
  128.2 17.2 %collective-permute-start.10 = (f32[2,128,512]{2,1,0:T(8,128)}, f32[2,128,512]{2,1,0:T(8,128)S(1)}, u32[]{:S(2)}, u32[]{:S(2)}) collective-permute-start(f32[2,128,512]{2,1,0:T(8,128)} %pad_maximum_fusion.3), channel_id=1, source_target_pairs={{6,0},{14,8},{22,16},{30,24},{7,1},{15,9},{23,17},{31,25}} | collective-permute-start | bytes 1572872 | tf_op jit(solution)/shard_map/ppermute | solution.py:44
  132.8 12.7 %collective-permute-start.9 = (f32[2,128,512]{2,1,0:T(8,128)}, f32[2,128,512]{2,1,0:T(8,128)S(1)}, u32[]{:S(2)}, u32[]{:S(2)}) collective-permute-start(f32[2,128,512]{2,1,0:T(8,128)} %pad_maximum_fusion.3), channel_id=1, source_target_pairs={{4,0},{12,8},{20,16},{28,24},{5,1},{13,9},{21,17},{29,25}} | collective-permute-start | bytes 1572872 | tf_op jit(solution)/shard_map/ppermute | solution.py:44
  133.5 12.0 %collective-permute-start.8 = (f32[2,128,512]{2,1,0:T(8,128)}, f32[2,128,512]{2,1,0:T(8,128)S(1)}, u32[]{:S(2)}, u32[]{:S(2)}) collective-permute-start(f32[2,128,512]{2,1,0:T(8,128)} %pad_maximum_fusion.3), channel_id=1, source_target_pairs={{2,0},{10,8},{18,16},{26,24},{3,1},{11,9},{19,17},{27,25}} | collective-permute-start | bytes 1572872 | tf_op jit(solution)/shard_map/ppermute | solution.py:44
  145.7 15.1 %collective-permute-start.13 = (f32[2,128,512]{2,1,0:T(8,128)S(1)}, f32[2,128,512]{2,1,0:T(8,128)S(1)}, u32[]{:S(2)}, u32[]{:S(2)}) collective-permute-start(f32[2,128,512]{2,1,0:T(8,128)S(1)} %add_add_fusion.1), channel_id=1, source_target_pairs={{24,0},{25,1}} | collective-permute-start | bytes 1572872 | tf_op jit(solution)/shard_map/ppermute | solution.py:44
  146.4 14.4 %collective-permute-start.12 = (f32[2,128,512]{2,1,0:T(8,128)S(1)}, f32[2,128,512]{2,1,0:T(8,128)S(1)}, u32[]{:S(2)}, u32[]{:S(2)}) collective-permute-start(f32[2,128,512]{2,1,0:T(8,128)S(1)} %add_add_fusion.1), channel_id=1, source_target_pairs={{16,0},{17,1}} | collective-permute-start | bytes 1572872 | tf_op jit(solution)/shard_map/ppermute | solution.py:44
  147.1 13.8 %collective-permute-start.11 = (f32[2,128,512]{2,1,0:T(8,128)S(1)}, f32[2,128,512]{2,1,0:T(8,128)S(1)}, u32[]{:S(2)}, u32[]{:S(2)}) collective-permute-start(f32[2,128,512]{2,1,0:T(8,128)S(1)} %add_add_fusion.1), channel_id=1, source_target_pairs={{8,0},{9,1}} | collective-permute-start | bytes 1572872 | tf_op jit(solution)/shard_map/ppermute | solution.py:44
  149.9 35.8 %collective-permute-start.14 = (bf16[2,128,512]{2,1,0:T(8,128)(2,1)S(1)}, bf16[2,128,512]{2,1,0:T(8,128)(2,1)S(1)}, u32[]{:S(2)}, u32[]{:S(2)}) collective-permute-start(bf16[2,128,512]{2,1,0:T(8,128)(2,1)S(1)} %pad_maximum_fusion.6), channel_id=1, source_target_pairs={{0,2},{2,4},{4,6},{6,8},{8,10},{10,12},{12,14},{14,16},{16,18},{18... | collective-permute-start | bytes 786440 | tf_op jit(solution)/shard_map/ppermute | solution.py:57
  158.9 26.9 %collective-permute-start.15 = (bf16[2,128,512]{2,1,0:T(8,128)(2,1)S(1)}, bf16[2,128,512]{2,1,0:T(8,128)(2,1)S(1)}, u32[]{:S(2)}, u32[]{:S(2)}) collective-permute-start(bf16[2,128,512]{2,1,0:T(8,128)(2,1)S(1)} %pad_maximum_fusion.7), channel_id=1, source_target_pairs={{2,0},{4,2},{6,4},{8,6},{10,8},{12,10},{14,12},{16,14},{18,16},{20... | collective-permute-start | bytes 786440 | tf_op jit(solution)/shard_map/ppermute | solution.py:57
  185.8 34.4 %copy-start.9 = (f32[256,512]{1,0:T(8,128)S(1)}, f32[256,512]{1,0:T(8,128)}, u32[]{:S(2)}) copy-start(f32[256,512]{1,0:T(8,128)} %get-tuple-element.21) | copy-start | bytes 1572868
  185.8 34.4 %copy-start.10 = (bf16[2,128,512]{2,1,0:T(8,128)(2,1)}, bf16[2,128,512]{2,1,0:T(8,128)(2,1)S(1)}, u32[]{:S(2)}) copy-start(bf16[2,128,512]{2,1,0:T(8,128)(2,1)S(1)} %collective-permute-done.15) | copy-start | bytes 786436
  185.8 62.8 %all-to-all-start.1 = ((bf16[16,128,512]{2,1,0:T(8,128)(2,1)}), bf16[16,128,512]{2,1,0:T(8,128)(2,1)S(1)}, u32[]{:S(2)}, u32[]{:S(2)}) async-start(bf16[16,128,512]{2,1,0:T(8,128)(2,1)} %get-tuple-element.27), calls=%async_computation.1 | async-start | bytes 4194304 | tf_op jit(solution)/shard_map/all_to_all | solution.py:321
  (6 other events, 19.2 us)

commit v8 on v7

--- a/solution.py
+++ b/solution.py
@@ -247,31 +247,10 @@
     dq_rim = dq_rim.reshape(2, height, features)
     dk_rim = dk_rim.reshape(2, height, features)
     dv_rim = dv_rim.reshape(2, height, features)
-    glob_mode = (seq_blk >= WINDOW).astype(jnp.int32)
-    dq_glob, dk_glob, dv_glob = list_pairs(
-        table(0, 1, 2, 3), table(0, 1, 2, 3), table(1, 1, 1, 1), table(0, 0, 0, 0), glob_mode,
-        slot_count, queries, out_grad, norm3, delta3, global_kv[0], global_kv[1],
-    )
-    zero_blk = jnp.zeros((height, features), jnp.float32)
-    dq_local = (
-        dq_own + dq_glob
-        + jnp.concatenate([dq_rim[0:1], zero_blk[None], zero_blk[None], dq_rim[1:2]]).reshape(
-            row_count, features
-        )
-    )
-
     to_left = jnp.stack([dk_rim[0], dv_rim[0]]).astype(jnp.bfloat16)
     to_right = jnp.stack([dk_rim[1], dv_rim[1]]).astype(jnp.bfloat16)
     back_right = shift(to_left, "ctx", -1)
     back_left = shift(to_right, "ctx", 1)
-
-    part = jnp.stack(
-        [
-            jnp.sum(dk_glob.reshape(slot_count, height, features), axis=0),
-            jnp.sum(dv_glob.reshape(slot_count, height, features), axis=0),
-        ]
-    )
-    total = gather_to_root(part, "ctx")
 
     ref_valid = rand_blocks >= 0
     in_front = rand_blocks < block_total // 2
@@ -313,6 +292,30 @@
     ktab_r = jnp.maximum(slot_recv - 1, 0)
     mtab_r = (slot_recv > 0).astype(jnp.int32)
     dq_rand, dk_rand, dv_rand = rand_pairs(ktab_r, mtab_r, arrived, key_rows, values, heads)
+    global_kv, dq_rand, dk_rand, dv_rand = lax.optimization_barrier(
+        (global_kv, dq_rand, dk_rand, dv_rand)
+    )
+    glob_mode = (seq_blk >= WINDOW).astype(jnp.int32)
+    dq_glob, dk_glob, dv_glob = list_pairs(
+        table(0, 1, 2, 3), table(0, 1, 2, 3), table(1, 1, 1, 1), table(0, 0, 0, 0), glob_mode,
+        slot_count, queries, out_grad, norm3, delta3, global_kv[0], global_kv[1],
+    )
+    part = jnp.stack(
+        [
+            jnp.sum(dk_glob.reshape(slot_count, height, features), axis=0),
+            jnp.sum(dv_glob.reshape(slot_count, height, features), axis=0),
+        ]
+    )
+    total = gather_to_root(part, "ctx")
+
+    zero_blk = jnp.zeros((height, features), jnp.float32)
+    dq_local = (
+        dq_own + dq_glob
+        + jnp.concatenate([dq_rim[0:1], zero_blk[None], zero_blk[None], dq_rim[1:2]]).reshape(
+            row_count, features
+        )
+    )
+
     dq_rand, total, back_left, back_right = lax.optimization_barrier(
         (dq_rand, total, back_left, back_right)
     )

time: 253 us -> 260 us (1.028)
  waiting for transfers between devices: 87 us -> 105 us
  starting transfers between devices: 52 us -> 42.9 us
    all_to_all x1, waiting for transfers between devices: 0.01 us -> 10.3 us  [shards(): lax.all_to_all(routed, 'ctx', split_axis=0, concat_axis=0, tiled=True)]
    all_to_all x1, starting transfers between devices: 15.4 us -> 7.99 us  [shards(): lax.all_to_all(dq_rand, 'ctx', split_axis=0, concat_axis=0, tiled=True)]
    ppermute x4, waiting for transfers between devices: 0.01 us -> 5.7 us  [shift(): return lax.ppermute(array, axis, pairs)]
    ppermute x4, starting transfers between devices: 17.2 us -> 12.7 us  [shift(): return lax.ppermute(array, axis, pairs)]
    ppermute x6, starting transfers between devices: 8.04 us -> 10.9 us  [gather_to_root(): lax.ppermute(array, axis, [(i + j * step, i) for i in range(0, count, RAD...]
  transfers between devices with their start and end apart: 18 -> 18, of which waited for: 2 -> 5; matrix products, arithmetic and copies ran while one was open for 14% -> 13% of each run, Pallas kernels for 23% -> 22%
where the time goes in v8:
time: 260 us; the launch traced here: 257 us
  waiting for transfers between devices  105 us (40%)
  Pallas kernels  56 us (22%)
  starting transfers between devices  42.9 us (16%)
  other arithmetic  42.3 us (16%)
  local copies, waits for them, and re-layouts  10.5 us (4%)
    ppermute x6, waiting for transfers between devices, spread_2(): lax.ppermute(array, axis, [(i, i + j * step) for i in range(0, count, RAD...  72 us
    pallas_call x3, Pallas kernels, list_pairs(): pl.pallas_call(list_kernel, grid_spec=grid_spec, out_shape=[jax.ShapeDtyp...  35.7 us
    pallas_call x1, Pallas kernels, rand_pairs(): pl.pallas_call(functools.partial(rand_kernel, heads), grid_spec=grid_spec...  20.3 us
    all_to_all x1, waiting for transfers between devices, shards(): lax.all_to_all(dq_rand, 'ctx', split_axis=0, concat_axis=0, tiled=True)  16.6 us
    ppermute x4, starting transfers between devices, shift(): return lax.ppermute(array, axis, pairs)  12.7 us
    ppermute x6, starting transfers between devices, gather_to_root(): lax.ppermute(array, axis, [(i + j * step, i) for i in range(0, count, RAD...  10.9 us
    all_to_all x1, waiting for transfers between devices, shards(): lax.all_to_all(routed, 'ctx', split_axis=0, concat_axis=0, tiled=True)  10.3 us
    all_to_all x1, starting transfers between devices, shards(): lax.all_to_all(dq_rand, 'ctx', split_axis=0, concat_axis=0, tiled=True)  7.99 us
  transfers between devices with their start and end apart: 18, of which 5 were waited for; matrix products, arithmetic and copies ran while one was open for 13% of the time, Pallas kernels for 22%

profile of v8, /device:TPU:11, one launch (start us, length us, event | category | flops | bytes accessed | tf_op | source)
XLA Modules:
  0.0 257.5 jit_solution(9268829392962764888)
XLA Ops:
  2.5 1.3 convert_multiply_fusion
  5.9 5.3 %select_reduce_fusion = bf16[16,272,512]{2,1,0:T(8,128)(2,1)} fusion(pred[16,4]{1,0:T(8,128)(4,1)S(1)} %copy.21, bf16[4,272,512]{2,1,0:T(8,128)(2,1)S(1)} %concatenate.15), kind=kLoop, calls=%fused_computation | loop fusion | flops 15597568 | bytes 5570624 | tf_op jit(solution)/shard_map/reduce_sum | solution.py:283
  11.2 4.7 %broadcast_select_fusion = bf16[16,272,512]{2,1,0:T(8,128)(2,1)} fusion(bf16[16,272,512]{2,1,0:T(8,128)(2,1)} %select_reduce_fusion, pred[272]{0:T(512)(128)(4,1)S(1)} %iota_compare_fusion.2, bf16[16]{0:T(256)(128)(2,1)S(1)} %convert_element_type.104), kind=kLoop, calls=%fused_computation.4 | loop fusion | flops 2228224 | bytes 8913200 | tf_op jit(solution)/shard_map/jit(_where)/select_n | solution.py:287
  15.9 6.7 %all-to-all-start = ((bf16[16,272,512]{2,1,0:T(8,128)(2,1)}), bf16[16,272,512]{2,1,0:T(8,128)(2,1)}, u32[]{:S(2)}, u32[]{:S(2)}) async-start(bf16[16,272,512]{2,1,0:T(8,128)(2,1)} %broadcast_select_fusion), calls=%async_computation | async-start | bytes 8912896 | tf_op jit(solution)/shard_map/all_to_all | solution.py:290
  25.5 2.3 collective-permute-start.7
  28.5 4.2 %collective-permute-start.6 = (bf16[2,128,512]{2,1,0:T(8,128)(2,1)}, bf16[2,128,512]{2,1,0:T(8,128)(2,1)}, u32[]{:S(2)}, u32[]{:S(2)}) collective-permute-start(bf16[2,128,512]{2,1,0:T(8,128)(2,1)} %pad_maximum_fusion.4), channel_id=1, source_target_pairs={{0,2},{2,4},{4,6},{6,8},{8,10},{10,12},{12,14},{14,16},{16,18},{18... | collective-permute-start | bytes 786440 | tf_op jit(solution)/shard_map/ppermute | solution.py:57
  38.3 72.0 %collective-permute-done.5 = bf16[2,128,512]{2,1,0:T(8,128)(2,1)S(1)} collective-permute-done((bf16[2,128,512]{2,1,0:T(8,128)(2,1)S(1)}, bf16[2,128,512]{2,1,0:T(8,128)(2,1)S(1)}, u32[]{:S(2)}, u32[]{:S(2)}) %collective-permute-start.5) | collective-permute-done | bytes 262176 | tf_op jit(solution)/shard_map/ppermute | solution.py:29
  110.4 10.3 %all-to-all-done.q_ref.do_ref.st_ref = bf16[16,272,512]{2,1,0:T(8,128)(2,1)} async-done(((bf16[16,272,512]{2,1,0:T(8,128)(2,1)}), bf16[16,272,512]{2,1,0:T(8,128)(2,1)}, u32[]{:S(2)}, u32[]{:S(2)}) %all-to-all-start) | async-done | bytes 4456480 | tf_op jit(solution)/shard_map/all_to_all | solution.py:290
  122.9 20.3 %shard_map.95 = (bf16[16,128,512]{2,1,0:T(8,128)(2,1)}, f32[16,128,512]{2,1,0:T(8,128)}, f32[16,128,512]{2,1,0:T(8,128)}) custom-call(s32[16]{0:T(128)} %add_maximum_fusion.ktab, s32[16]{0:T(128)} %compare_convert_fusion.1.mtab, bf16[16,272,512]{2,1,0:T(8,128)(2,1)} %all-to-all-done.q_ref.do_ref.st_ref, ...), custom_call_target="tpu_custom_call" | custom-call | tf_op jit(solution)/shard_map/pallas_call | solution.py:185
  145.6 11.9 %shard_map.96 = (f32[512,512]{1,0:T(8,128)}, f32[512,512]{1,0:T(8,128)}, f32[512,512]{1,0:T(8,128)}) custom-call(s32[4]{0:T(128)} %iota.37.qin.qout, s32[4]{0:T(128)} %iota.37.qin.qout, s32[4]{0:T(128)} %broadcast_18_first.2.first, s32[4]{0:T(128)} %broadcast_17_ktab.2.ktab, s32[4]{0:T(128)} %compare_convert_fusion.2.mtab, bf16[512,512]{1,0:T(8,128)(2,1)} %q_ref.5, ...), custom_call_target="tpu_custom_call" | custom-call | tf_op jit(solution)/shard_map/pallas_call | solution.py:153
  157.4 1.3 reduce_sum.79
  158.8 1.3 reduce_sum.78
  161.0 7.4 %collective-permute-start.10 = (f32[2,128,512]{2,1,0:T(8,128)}, f32[2,128,512]{2,1,0:T(8,128)S(1)}, u32[]{:S(2)}, u32[]{:S(2)}) collective-permute-start(f32[2,128,512]{2,1,0:T(8,128)} %pad_maximum_fusion.3), channel_id=1, source_target_pairs={{6,0},{14,8},{22,16},{30,24},{7,1},{15,9},{23,17},{31,25}} | collective-permute-start | bytes 1572872 | tf_op jit(solution)/shard_map/ppermute | solution.py:44
  173.9 7.2 %shard_map.97 = (f32[256,512]{1,0:T(8,128)}, f32[256,512]{1,0:T(8,128)}, f32[256,512]{1,0:T(8,128)}) custom-call(s32[2]{0:T(128)} %iota_multiply_fusion.qin, s32[2]{0:T(128)} %iota.43.qout, s32[2]{0:T(128)} %broadcast_26_first.2.first, s32[2]{0:T(128)} %get-tuple-element.79.ktab, s32[2]{0:T(128)} %get-tuple-element.80.mtab, bf16[512,512]{1,0:T(8,128)(2,1)} %q_ref.5, ...), custom_call_target="tpu_custom_call" | custom-call | tf_op jit(solution)/shard_map/pallas_call | solution.py:153
  185.6 4.3 %collective-permute-start.14 = (bf16[2,128,512]{2,1,0:T(8,128)(2,1)S(1)}, bf16[2,128,512]{2,1,0:T(8,128)(2,1)}, u32[]{:S(2)}, u32[]{:S(2)}) collective-permute-start(bf16[2,128,512]{2,1,0:T(8,128)(2,1)S(1)} %pad_maximum_fusion.6), channel_id=1, source_target_pairs={{0,2},{2,4},{4,6},{6,8},{8,10},{10,12},{12,14},{14,16},{16,18},{18... | collective-permute-start | bytes 786440 | tf_op jit(solution)/shard_map/ppermute | solution.py:57
  190.0 1.9 collective-permute-start.15
  193.2 5.4 %collective-permute-done.15 = bf16[2,128,512]{2,1,0:T(8,128)(2,1)} collective-permute-done((bf16[2,128,512]{2,1,0:T(8,128)(2,1)S(1)}, bf16[2,128,512]{2,1,0:T(8,128)(2,1)}, u32[]{:S(2)}, u32[]{:S(2)}) %collective-permute-start.15) | collective-permute-done | bytes 262176 | tf_op jit(solution)/shard_map/ppermute | solution.py:57
  198.7 8.0 %all-to-all-start.1 = ((bf16[16,128,512]{2,1,0:T(8,128)(2,1)}), bf16[16,128,512]{2,1,0:T(8,128)(2,1)S(1)}, u32[]{:S(2)}, u32[]{:S(2)}) async-start(bf16[16,128,512]{2,1,0:T(8,128)(2,1)} %get-tuple-element.35), calls=%async_computation.1 | async-start | bytes 4194304 | tf_op jit(solution)/shard_map/all_to_all | solution.py:324
  206.8 16.6 %shard_map.94 = (f32[512,512]{1,0:T(8,128)}, f32[768,512]{1,0:T(8,128)}, f32[768,512]{1,0:T(8,128)}) custom-call(s32[6]{0:T(128)} %constant.35.clone.1.qin.qout, s32[6]{0:T(128)} %constant.35.clone.1.qin.qout, s32[6]{0:T(128)} %constant.36.clone.1.first, s32[6]{0:T(128)} %constant.37.clone.1.ktab, s32[6]{0:T(128)} %constant.38.clone.1.mtab, ...), custom_call_target="tpu_custom_call" | custom-call | tf_op jit(solution)/shard_map/pallas_call | solution.py:153
  223.5 2.1 add_bitcast_fusion
  226.0 5.1 %multiply_reduce_fusion = (f32[4,128,512]{2,1,0:T(8,128)S(1)}, f32[4,128,512]{2,1,0:T(8,128)S(1)}) fusion(f32[16,128,512]{2,1,0:T(8,128)} %get-tuple-element.42, f32[16,4]{1,0:T(8,128)S(1)} %compare_convert_fusion, f32[16,128,512]{2,1,0:T(8,128)S(1)} %copy-done.6), kind=kLoop, calls=%fused_computation.1 | loop fusion | flops 16252928 | bytes 10486016 | tf_op jit(solution)/shard_map/reduce_sum | solution.py:331
  233.2 2.3 bitcast_add_fusion.3
  237.5 16.6 %all-to-all-done.1 = bf16[16,128,512]{2,1,0:T(8,128)(2,1)S(1)} async-done(((bf16[16,128,512]{2,1,0:T(8,128)(2,1)}), bf16[16,128,512]{2,1,0:T(8,128)(2,1)S(1)}, u32[]{:S(2)}, u32[]{:S(2)}) %all-to-all-start.1) | async-done | bytes 2097184 | tf_op jit(solution)/shard_map/all_to_all | solution.py:324
  254.7 1.4 multiply_reduce_fusion.2
  (111 shorter events, 36.3 us)
Async XLA Ops:
  15.9 6.7 %copy-start.2 = (bf16[512,512]{1,0:T(8,128)(2,1)S(1)}, bf16[512,512]{1,0:T(8,128)(2,1)}, u32[]{:S(2)}) copy-start(bf16[512,512]{1,0:T(8,128)(2,1)} %k_ref.3) | copy-start | bytes 1572868
  15.9 6.7 %copy-start.4 = (bf16[512,512]{1,0:T(8,128)(2,1)S(1)}, bf16[512,512]{1,0:T(8,128)(2,1)}, u32[]{:S(2)}) copy-start(bf16[512,512]{1,0:T(8,128)(2,1)} %v_ref.3) | copy-start | bytes 1572868
  15.9 104.8 %all-to-all-start = ((bf16[16,272,512]{2,1,0:T(8,128)(2,1)}), bf16[16,272,512]{2,1,0:T(8,128)(2,1)}, u32[]{:S(2)}, u32[]{:S(2)}) async-start(bf16[16,272,512]{2,1,0:T(8,128)(2,1)} %broadcast_select_fusion), calls=%async_computation | async-start | bytes 8912896 | tf_op jit(solution)/shard_map/all_to_all | solution.py:290
  22.6 13.4 %copy-start.11 = (bf16[4,512]{1,0:T(4,128)(2,1)S(1)}, bf16[4,512]{1,0:T(4,128)(2,1)}, u32[]{:S(2)}) copy-start(bf16[4,512]{1,0:T(4,128)(2,1)} %param.12) | copy-start | bytes 12292
  22.7 10.0 %collective-permute-start.2 = (bf16[2,128,512]{2,1,0:T(8,128)(2,1)S(1)}, bf16[2,128,512]{2,1,0:T(8,128)(2,1)S(1)}, u32[]{:S(2)}, u32[]{:S(2)}) collective-permute-start(bf16[2,128,512]{2,1,0:T(8,128)(2,1)S(1)} %maximum_select_fusion), channel_id=1, source_target_pairs={{0,24},{1,25}} | collective-permute-start | bytes 786440 | tf_op jit(solution)/shard_map/ppermute | solution.py:29
  23.4 9.3 %collective-permute-start.1 = (bf16[2,128,512]{2,1,0:T(8,128)(2,1)S(1)}, bf16[2,128,512]{2,1,0:T(8,128)(2,1)S(1)}, u32[]{:S(2)}, u32[]{:S(2)}) collective-permute-start(bf16[2,128,512]{2,1,0:T(8,128)(2,1)S(1)} %maximum_select_fusion), channel_id=1, source_target_pairs={{0,16},{1,17}} | collective-permute-start | bytes 786440 | tf_op jit(solution)/shard_map/ppermute | solution.py:29
  24.1 8.6 %collective-permute-start = (bf16[2,128,512]{2,1,0:T(8,128)(2,1)S(1)}, bf16[2,128,512]{2,1,0:T(8,128)(2,1)S(1)}, u32[]{:S(2)}, u32[]{:S(2)}) collective-permute-start(bf16[2,128,512]{2,1,0:T(8,128)(2,1)S(1)} %maximum_select_fusion), channel_id=1, source_target_pairs={{0,8},{1,9}} | collective-permute-start | bytes 786440 | tf_op jit(solution)/shard_map/ppermute | solution.py:29
  25.5 144.3 %collective-permute-start.7 = (bf16[2,128,512]{2,1,0:T(8,128)(2,1)}, bf16[2,128,512]{2,1,0:T(8,128)(2,1)S(1)}, u32[]{:S(2)}, u32[]{:S(2)}) collective-permute-start(bf16[2,128,512]{2,1,0:T(8,128)(2,1)} %pad_maximum_fusion.5), channel_id=1, source_target_pairs={{2,0},{4,2},{6,4},{8,6},{10,8},{12,10},{14,12},{16,14},{18,16},{20... | collective-permute-start | bytes 786440 | tf_op jit(solution)/shard_map/ppermute | solution.py:57
  28.5 141.3 %collective-permute-start.6 = (bf16[2,128,512]{2,1,0:T(8,128)(2,1)}, bf16[2,128,512]{2,1,0:T(8,128)(2,1)}, u32[]{:S(2)}, u32[]{:S(2)}) collective-permute-start(bf16[2,128,512]{2,1,0:T(8,128)(2,1)} %pad_maximum_fusion.4), channel_id=1, source_target_pairs={{0,2},{2,4},{4,6},{6,8},{8,10},{10,12},{12,14},{14,16},{16,18},{18... | collective-permute-start | bytes 786440 | tf_op jit(solution)/shard_map/ppermute | solution.py:57
  32.8 77.5 %collective-permute-start.5 = (bf16[2,128,512]{2,1,0:T(8,128)(2,1)S(1)}, bf16[2,128,512]{2,1,0:T(8,128)(2,1)S(1)}, u32[]{:S(2)}, u32[]{:S(2)}) collective-permute-start(bf16[2,128,512]{2,1,0:T(8,128)(2,1)S(1)} %add_add_fusion.3), channel_id=1, source_target_pairs={{0,6},{8,14},{16,22},{24,30},{1,7},{9,15},{17,23},{25,31}} | collective-permute-start | bytes 786440 | tf_op jit(solution)/shard_map/ppermute | solution.py:29
  34.1 76.2 %collective-permute-start.4 = (bf16[2,128,512]{2,1,0:T(8,128)(2,1)S(1)}, bf16[2,128,512]{2,1,0:T(8,128)(2,1)S(1)}, u32[]{:S(2)}, u32[]{:S(2)}) collective-permute-start(bf16[2,128,512]{2,1,0:T(8,128)(2,1)S(1)} %add_add_fusion.3), channel_id=1, source_target_pairs={{0,4},{8,12},{16,20},{24,28},{1,5},{9,13},{17,21},{25,29}} | collective-permute-start | bytes 786440 | tf_op jit(solution)/shard_map/ppermute | solution.py:29
  34.8 75.6 %collective-permute-start.3 = (bf16[2,128,512]{2,1,0:T(8,128)(2,1)S(1)}, bf16[2,128,512]{2,1,0:T(8,128)(2,1)S(1)}, u32[]{:S(2)}, u32[]{:S(2)}) collective-permute-start(bf16[2,128,512]{2,1,0:T(8,128)(2,1)S(1)} %add_add_fusion.3), channel_id=1, source_target_pairs={{0,2},{8,10},{16,18},{24,26},{1,3},{9,11},{17,19},{25,27}} | collective-permute-start | bytes 786440 | tf_op jit(solution)/shard_map/ppermute | solution.py:29
  143.2 27.7 %copy-start.3 = (bf16[512,512]{1,0:T(8,128)(2,1)S(1)}, bf16[512,512]{1,0:T(8,128)(2,1)}, u32[]{:S(2)}) copy-start(bf16[512,512]{1,0:T(8,128)(2,1)} %k_ref.3) | copy-start | bytes 1572868
  143.2 28.6 %copy-start.5 = (bf16[512,512]{1,0:T(8,128)(2,1)S(1)}, bf16[512,512]{1,0:T(8,128)(2,1)}, u32[]{:S(2)}) copy-start(bf16[512,512]{1,0:T(8,128)(2,1)} %v_ref.3) | copy-start | bytes 1572868
  161.0 20.1 %collective-permute-start.10 = (f32[2,128,512]{2,1,0:T(8,128)}, f32[2,128,512]{2,1,0:T(8,128)S(1)}, u32[]{:S(2)}, u32[]{:S(2)}) collective-permute-start(f32[2,128,512]{2,1,0:T(8,128)} %pad_maximum_fusion.3), channel_id=1, source_target_pairs={{6,0},{14,8},{22,16},{30,24},{7,1},{15,9},{23,17},{31,25}} | collective-permute-start | bytes 1572872 | tf_op jit(solution)/shard_map/ppermute | solution.py:44
  168.4 12.7 %collective-permute-start.9 = (f32[2,128,512]{2,1,0:T(8,128)}, f32[2,128,512]{2,1,0:T(8,128)S(1)}, u32[]{:S(2)}, u32[]{:S(2)}) collective-permute-start(f32[2,128,512]{2,1,0:T(8,128)} %pad_maximum_fusion.3), channel_id=1, source_target_pairs={{4,0},{12,8},{20,16},{28,24},{5,1},{13,9},{21,17},{29,25}} | collective-permute-start | bytes 1572872 | tf_op jit(solution)/shard_map/ppermute | solution.py:44
  169.1 12.0 %collective-permute-start.8 = (f32[2,128,512]{2,1,0:T(8,128)}, f32[2,128,512]{2,1,0:T(8,128)S(1)}, u32[]{:S(2)}, u32[]{:S(2)}) collective-permute-start(f32[2,128,512]{2,1,0:T(8,128)} %pad_maximum_fusion.3), channel_id=1, source_target_pairs={{2,0},{10,8},{18,16},{26,24},{3,1},{11,9},{19,17},{27,25}} | collective-permute-start | bytes 1572872 | tf_op jit(solution)/shard_map/ppermute | solution.py:44
  181.4 10.6 %collective-permute-start.13 = (f32[2,128,512]{2,1,0:T(8,128)S(1)}, f32[2,128,512]{2,1,0:T(8,128)S(1)}, u32[]{:S(2)}, u32[]{:S(2)}) collective-permute-start(f32[2,128,512]{2,1,0:T(8,128)S(1)} %add_add_fusion.1), channel_id=1, source_target_pairs={{24,0},{25,1}} | collective-permute-start | bytes 1572872 | tf_op jit(solution)/shard_map/ppermute | solution.py:44
  182.1 9.9 %collective-permute-start.12 = (f32[2,128,512]{2,1,0:T(8,128)S(1)}, f32[2,128,512]{2,1,0:T(8,128)S(1)}, u32[]{:S(2)}, u32[]{:S(2)}) collective-permute-start(f32[2,128,512]{2,1,0:T(8,128)S(1)} %add_add_fusion.1), channel_id=1, source_target_pairs={{16,0},{17,1}} | collective-permute-start | bytes 1572872 | tf_op jit(solution)/shard_map/ppermute | solution.py:44
  182.8 9.2 %collective-permute-start.11 = (f32[2,128,512]{2,1,0:T(8,128)S(1)}, f32[2,128,512]{2,1,0:T(8,128)S(1)}, u32[]{:S(2)}, u32[]{:S(2)}) collective-permute-start(f32[2,128,512]{2,1,0:T(8,128)S(1)} %add_add_fusion.1), channel_id=1, source_target_pairs={{8,0},{9,1}} | collective-permute-start | bytes 1572872 | tf_op jit(solution)/shard_map/ppermute | solution.py:44
  185.6 7.6 %collective-permute-start.14 = (bf16[2,128,512]{2,1,0:T(8,128)(2,1)S(1)}, bf16[2,128,512]{2,1,0:T(8,128)(2,1)}, u32[]{:S(2)}, u32[]{:S(2)}) collective-permute-start(bf16[2,128,512]{2,1,0:T(8,128)(2,1)S(1)} %pad_maximum_fusion.6), channel_id=1, source_target_pairs={{0,2},{2,4},{4,6},{6,8},{8,10},{10,12},{12,14},{14,16},{16,18},{18... | collective-permute-start | bytes 786440 | tf_op jit(solution)/shard_map/ppermute | solution.py:57
  190.0 8.7 %collective-permute-start.15 = (bf16[2,128,512]{2,1,0:T(8,128)(2,1)S(1)}, bf16[2,128,512]{2,1,0:T(8,128)(2,1)}, u32[]{:S(2)}, u32[]{:S(2)}) collective-permute-start(bf16[2,128,512]{2,1,0:T(8,128)(2,1)S(1)} %pad_maximum_fusion.7), channel_id=1, source_target_pairs={{2,0},{4,2},{6,4},{8,6},{10,8},{12,10},{14,12},{16,14},{18,16},{20... | collective-permute-start | bytes 786440 | tf_op jit(solution)/shard_map/ppermute | solution.py:57
  193.0 32.6 %copy-start.10 = (f32[256,512]{1,0:T(8,128)S(1)}, f32[256,512]{1,0:T(8,128)}, u32[]{:S(2)}) copy-start(f32[256,512]{1,0:T(8,128)} %get-tuple-element.29) | copy-start | bytes 1572868
  198.7 55.4 %all-to-all-start.1 = ((bf16[16,128,512]{2,1,0:T(8,128)(2,1)}), bf16[16,128,512]{2,1,0:T(8,128)(2,1)S(1)}, u32[]{:S(2)}, u32[]{:S(2)}) async-start(bf16[16,128,512]{2,1,0:T(8,128)(2,1)} %get-tuple-element.35), calls=%async_computation.1 | async-start | bytes 4194304 | tf_op jit(solution)/shard_map/all_to_all | solution.py:324
  (6 other events, 19.3 us)

commit v9 on v7

--- a/solution.py
+++ b/solution.py
@@ -40,13 +40,14 @@
     count = lax.axis_size(axis)
     step = 1
     while step < count:
+        sent = array.astype(jnp.bfloat16)
         arrived = [
-            lax.ppermute(array, axis, [(i + j * step, i) for i in range(0, count, RADIX * step) if i + j * step < count])
+            lax.ppermute(sent, axis, [(i + j * step, i) for i in range(0, count, RADIX * step) if i + j * step < count])
             for j in range(1, RADIX)
             if j * step < count
         ]
         for part in arrived:
-            array = array + part
+            array = array + part.astype(jnp.float32)
         step *= RADIX
     return array
 

time: 253 us -> 250 us (0.988)
  waiting for transfers between devices: 87 us -> 102 us
  starting transfers between devices: 52 us -> 38.3 us
  other arithmetic: 44.1 us -> 41 us
    ppermute x4, waiting for transfers between devices: 0.01 us -> 86.3 us  [shift(): return lax.ppermute(array, axis, pairs)]
    ppermute x6, waiting for transfers between devices: 72 us -> 0.02 us  [spread_2(): lax.ppermute(array, axis, [(i, i + j * step) for i in range(0, count, RAD...]
    all_to_all x1, starting transfers between devices: 15.4 us -> 8.46 us  [shards(): lax.all_to_all(dq_rand, 'ctx', split_axis=0, concat_axis=0, tiled=True)]
    ppermute x4, starting transfers between devices: 17.2 us -> 13.8 us  [shift(): return lax.ppermute(array, axis, pairs)]
    ppermute x6, starting transfers between devices: 8.04 us -> 4.69 us  [gather_to_root(): lax.ppermute(sent, axis, [(i + j * step, i) for i in range(0, count, RADI...]
  transfers between devices with their start and end apart: 18 -> 18, of which waited for: 2 -> 2; matrix products, arithmetic and copies ran while one was open for 14% -> 13% of each run, Pallas kernels for 23% -> 23%
where the time goes in v9:
time: 250 us; the launch traced here: 249 us
  waiting for transfers between devices  102 us (41%)
  Pallas kernels  56.6 us (23%)
  other arithmetic  41 us (16%)
  starting transfers between devices  38.3 us (15%)
  local copies, waits for them, and re-layouts  9.95 us (4%)
    ppermute x4, waiting for transfers between devices, shift(): return lax.ppermute(array, axis, pairs)  86.3 us
    pallas_call x3, Pallas kernels, list_pairs(): pl.pallas_call(list_kernel, grid_spec=grid_spec, out_shape=[jax.ShapeDtyp...  35.8 us
    pallas_call x1, Pallas kernels, rand_pairs(): pl.pallas_call(functools.partial(rand_kernel, heads), grid_spec=grid_spec...  20.9 us
    all_to_all x1, waiting for transfers between devices, shards(): lax.all_to_all(dq_rand, 'ctx', split_axis=0, concat_axis=0, tiled=True)  15.9 us
    ppermute x4, starting transfers between devices, shift(): return lax.ppermute(array, axis, pairs)  13.8 us
    all_to_all x1, starting transfers between devices, shards(): lax.all_to_all(dq_rand, 'ctx', split_axis=0, concat_axis=0, tiled=True)  8.46 us
    all_to_all x1, starting transfers between devices, shards(): lax.all_to_all(routed, 'ctx', split_axis=0, concat_axis=0, tiled=True)  6.69 us
    reduce_sum x1, other arithmetic, shards(): jnp.sum(jnp.where(pick[:, :, None, None], packed[None], 0), axis=1)  5.3 us
  transfers between devices with their start and end apart: 18, of which 2 were waited for; matrix products, arithmetic and copies ran while one was open for 13% of the time, Pallas kernels for 23%

profile of v9, /device:TPU:11, one launch (start us, length us, event | category | flops | bytes accessed | tf_op | source)
XLA Modules:
  0.0 249.3 jit_solution(14015626844645379175)
XLA Ops:
  2.5 1.3 convert_multiply_fusion
  5.9 5.3 %select_reduce_fusion = bf16[16,272,512]{2,1,0:T(8,128)(2,1)} fusion(pred[16,4]{1,0:T(8,128)(4,1)S(1)} %copy.22, bf16[4,272,512]{2,1,0:T(8,128)(2,1)S(1)} %concatenate.19), kind=kLoop, calls=%fused_computation | loop fusion | flops 15597568 | bytes 5570624 | tf_op jit(solution)/shard_map/reduce_sum | solution.py:305
  11.2 4.7 %broadcast_select_fusion = bf16[16,272,512]{2,1,0:T(8,128)(2,1)} fusion(bf16[16,272,512]{2,1,0:T(8,128)(2,1)} %select_reduce_fusion, pred[272]{0:T(512)(128)(4,1)S(1)} %iota_compare_fusion.2, bf16[16]{0:T(256)(128)(2,1)S(1)} %convert_element_type.130), kind=kLoop, calls=%fused_computation.4 | loop fusion | flops 2228224 | bytes 8913200 | tf_op jit(solution)/shard_map/jit(_where)/select_n | solution.py:309
  15.9 6.7 %all-to-all-start = ((bf16[16,272,512]{2,1,0:T(8,128)(2,1)}), bf16[16,272,512]{2,1,0:T(8,128)(2,1)}, u32[]{:S(2)}, u32[]{:S(2)}) async-start(bf16[16,272,512]{2,1,0:T(8,128)(2,1)} %broadcast_select_fusion), calls=%async_computation | async-start | bytes 8912896 | tf_op jit(solution)/shard_map/all_to_all | solution.py:312
  24.8 2.3 collective-permute-start.7
  27.1 4.2 %collective-permute-start.6 = (bf16[2,128,512]{2,1,0:T(8,128)(2,1)S(1)}, bf16[2,128,512]{2,1,0:T(8,128)(2,1)S(1)}, u32[]{:S(2)}, u32[]{:S(2)}) collective-permute-start(bf16[2,128,512]{2,1,0:T(8,128)(2,1)S(1)} %pad_maximum_fusion.4), channel_id=1, source_target_pairs={{0,2},{2,4},{4,6},{6,8},{8,10},{10,12},{12,14},{14,16},{16,18},{18... | collective-permute-start | bytes 786440 | tf_op jit(solution)/shard_map/ppermute | solution.py:58
  37.1 86.3 %collective-permute-done.7 = bf16[2,128,512]{2,1,0:T(8,128)(2,1)S(1)} collective-permute-done((bf16[2,128,512]{2,1,0:T(8,128)(2,1)S(1)}, bf16[2,128,512]{2,1,0:T(8,128)(2,1)S(1)}, u32[]{:S(2)}, u32[]{:S(2)}) %collective-permute-start.7) | collective-permute-done | bytes 262176 | tf_op jit(solution)/shard_map/ppermute | solution.py:58
  126.7 11.9 %shard_map.95 = (f32[512,512]{1,0:T(8,128)}, f32[512,512]{1,0:T(8,128)}, f32[512,512]{1,0:T(8,128)}) custom-call(s32[4]{0:T(128)} %iota.37.qin.qout, s32[4]{0:T(128)} %iota.37.qin.qout, s32[4]{0:T(128)} %broadcast_25_first.2.first, s32[4]{0:T(128)} %broadcast_24_ktab.2.ktab, s32[4]{0:T(128)} %compare_convert_fusion.2.mtab, bf16[512,512]{1,0:T(8,128)(2,1)} %q_ref.5, ...), custom_call_target="tpu_custom_call" | custom-call | tf_op jit(solution)/shard_map/pallas_call | solution.py:154
  138.6 1.3 reduce_sum.79
  140.0 1.3 reduce_sum.78
  141.3 1.3 collective-permute-start.10
  146.1 7.2 %shard_map.96 = (f32[256,512]{1,0:T(8,128)}, f32[256,512]{1,0:T(8,128)}, f32[256,512]{1,0:T(8,128)}) custom-call(s32[2]{0:T(128)} %iota_multiply_fusion.qin, s32[2]{0:T(128)} %iota.42.qout, s32[2]{0:T(128)} %broadcast_26_first.2.first, s32[2]{0:T(128)} %get-tuple-element.71.ktab, s32[2]{0:T(128)} %get-tuple-element.72.mtab, bf16[512,512]{1,0:T(8,128)(2,1)} %q_ref.5, ...), custom_call_target="tpu_custom_call" | custom-call | tf_op jit(solution)/shard_map/pallas_call | solution.py:154
  157.7 5.4 %collective-permute-start.14 = (bf16[2,128,512]{2,1,0:T(8,128)(2,1)S(1)}, bf16[2,128,512]{2,1,0:T(8,128)(2,1)S(1)}, u32[]{:S(2)}, u32[]{:S(2)}) collective-permute-start(bf16[2,128,512]{2,1,0:T(8,128)(2,1)S(1)} %pad_maximum_fusion.6), channel_id=1, source_target_pairs={{0,2},{2,4},{4,6},{6,8},{8,10},{10,12},{12,14},{14,16},{16,18},{18... | collective-permute-start | bytes 786440 | tf_op jit(solution)/shard_map/ppermute | solution.py:58
  163.1 1.9 collective-permute-start.15
  168.4 20.9 %shard_map.97 = (bf16[16,128,512]{2,1,0:T(8,128)(2,1)}, f32[16,128,512]{2,1,0:T(8,128)}, f32[16,128,512]{2,1,0:T(8,128)}) custom-call(s32[16]{0:T(128)} %add_maximum_fusion.ktab, s32[16]{0:T(128)} %compare_convert_fusion.1.mtab, bf16[16,272,512]{2,1,0:T(8,128)(2,1)} %all-to-all-done.q_ref.do_ref.st_ref, ...), custom_call_target="tpu_custom_call" | custom-call | tf_op jit(solution)/shard_map/pallas_call | solution.py:186
  190.0 8.5 %all-to-all-start.1 = ((bf16[16,128,512]{2,1,0:T(8,128)(2,1)}), bf16[16,128,512]{2,1,0:T(8,128)(2,1)S(1)}, u32[]{:S(2)}, u32[]{:S(2)}) async-start(bf16[16,128,512]{2,1,0:T(8,128)(2,1)} %get-tuple-element.27), calls=%async_computation.1 | async-start | bytes 4194304 | tf_op jit(solution)/shard_map/all_to_all | solution.py:322
  198.6 16.6 %shard_map.94 = (f32[512,512]{1,0:T(8,128)}, f32[768,512]{1,0:T(8,128)}, f32[768,512]{1,0:T(8,128)}) custom-call(s32[6]{0:T(128)} %constant.35.clone.1.qin.qout, s32[6]{0:T(128)} %constant.35.clone.1.qin.qout, s32[6]{0:T(128)} %constant.36.clone.1.first, s32[6]{0:T(128)} %constant.37.clone.1.ktab, s32[6]{0:T(128)} %constant.38.clone.1.mtab, ...), custom_call_target="tpu_custom_call" | custom-call | tf_op jit(solution)/shard_map/pallas_call | solution.py:154
  215.3 2.2 add_bitcast_fusion
  217.9 2.7 %bitcast_add_fusion.3 = (f32[1,128,512]{2,1,0:T(8,128)}, f32[1,128,512]{2,1,0:T(8,128)}, f32[1,128,512]{2,1,0:T(8,128)}, f32[1,128,512]{2,1,0:T(8,128)S(1)}, f32[1,128,512]{2,1,0:T(8,128)}, /*index=5*/f32[1,128,512]{2,1,0:T(8,128)}) fusion(f32[2,128,512]{2,1,0:T(8,128)} %convert_add_fusion, f32[768,512]{1,0:T(8,128)S(1)} %copy-done.5, f32[]{:T(128)S(6)} %select_n.86, ...), kind=kLoop, calls=%fused_computation.32 | loop fusion | flops 917504 | bytes 5767176 | tf_op jit(solution)/shard_map/add | solution.py:337
  220.6 5.1 %multiply_reduce_fusion = (f32[4,128,512]{2,1,0:T(8,128)S(1)}, f32[4,128,512]{2,1,0:T(8,128)S(1)}) fusion(f32[16,128,512]{2,1,0:T(8,128)} %get-tuple-element.34, f32[16,4]{1,0:T(8,128)S(1)} %compare_convert_fusion, f32[16,128,512]{2,1,0:T(8,128)S(1)} %copy-done.4), kind=kLoop, calls=%fused_computation.1 | loop fusion | flops 16252928 | bytes 10486016 | tf_op jit(solution)/shard_map/reduce_sum | solution.py:329
  225.7 2.2 fusion
  227.9 2.1 fusion.1
  229.9 15.9 %all-to-all-done.1 = bf16[16,128,512]{2,1,0:T(8,128)(2,1)S(1)} async-done(((bf16[16,128,512]{2,1,0:T(8,128)(2,1)}), bf16[16,128,512]{2,1,0:T(8,128)(2,1)S(1)}, u32[]{:S(2)}, u32[]{:S(2)}) %all-to-all-start.1) | async-done | bytes 2097184 | tf_op jit(solution)/shard_map/all_to_all | solution.py:322
  246.5 1.4 multiply_reduce_fusion.2
  (113 shorter events, 29.4 us)
Async XLA Ops:
  0.6 4.7 %copy-start = (bf16[512,512]{1,0:T(8,128)(2,1)S(1)}, bf16[512,512]{1,0:T(8,128)(2,1)}, u32[]{:S(2)}) copy-start(bf16[512,512]{1,0:T(8,128)(2,1)} %do_ref.5) | copy-start | bytes 1572868
  0.6 4.7 %copy-start.1 = (bf16[512,512]{1,0:T(8,128)(2,1)S(1)}, bf16[512,512]{1,0:T(8,128)(2,1)}, u32[]{:S(2)}) copy-start(bf16[512,512]{1,0:T(8,128)(2,1)} %q_ref.5) | copy-start | bytes 1572868
  15.9 6.7 %copy-start.2 = (bf16[512,512]{1,0:T(8,128)(2,1)S(1)}, bf16[512,512]{1,0:T(8,128)(2,1)}, u32[]{:S(2)}) copy-start(bf16[512,512]{1,0:T(8,128)(2,1)} %k_ref.3) | copy-start | bytes 1572868
  15.9 6.7 %copy-start.3 = (bf16[512,512]{1,0:T(8,128)(2,1)S(1)}, bf16[512,512]{1,0:T(8,128)(2,1)}, u32[]{:S(2)}) copy-start(bf16[512,512]{1,0:T(8,128)(2,1)} %v_ref.3) | copy-start | bytes 1572868
  15.9 17.2 %copy-start.12 = (bf16[4,512]{1,0:T(4,128)(2,1)S(1)}, bf16[4,512]{1,0:T(4,128)(2,1)}, u32[]{:S(2)}) copy-start(bf16[4,512]{1,0:T(4,128)(2,1)} %param.12) | copy-start | bytes 12292
  15.9 150.2 %all-to-all-start = ((bf16[16,272,512]{2,1,0:T(8,128)(2,1)}), bf16[16,272,512]{2,1,0:T(8,128)(2,1)}, u32[]{:S(2)}, u32[]{:S(2)}) async-start(bf16[16,272,512]{2,1,0:T(8,128)(2,1)} %broadcast_select_fusion), calls=%async_computation | async-start | bytes 8912896 | tf_op jit(solution)/shard_map/all_to_all | solution.py:312
  22.7 11.6 %collective-permute-start.2 = (bf16[2,128,512]{2,1,0:T(8,128)(2,1)S(1)}, bf16[2,128,512]{2,1,0:T(8,128)(2,1)S(1)}, u32[]{:S(2)}, u32[]{:S(2)}) collective-permute-start(bf16[2,128,512]{2,1,0:T(8,128)(2,1)S(1)} %maximum_select_fusion), channel_id=1, source_target_pairs={{0,24},{1,25}} | collective-permute-start | bytes 786440 | tf_op jit(solution)/shard_map/ppermute | solution.py:29
  23.4 10.9 %collective-permute-start.1 = (bf16[2,128,512]{2,1,0:T(8,128)(2,1)S(1)}, bf16[2,128,512]{2,1,0:T(8,128)(2,1)S(1)}, u32[]{:S(2)}, u32[]{:S(2)}) collective-permute-start(bf16[2,128,512]{2,1,0:T(8,128)(2,1)S(1)} %maximum_select_fusion), channel_id=1, source_target_pairs={{0,16},{1,17}} | collective-permute-start | bytes 786440 | tf_op jit(solution)/shard_map/ppermute | solution.py:29
  24.1 10.2 %collective-permute-start = (bf16[2,128,512]{2,1,0:T(8,128)(2,1)S(1)}, bf16[2,128,512]{2,1,0:T(8,128)(2,1)S(1)}, u32[]{:S(2)}, u32[]{:S(2)}) collective-permute-start(bf16[2,128,512]{2,1,0:T(8,128)(2,1)S(1)} %maximum_select_fusion), channel_id=1, source_target_pairs={{0,8},{1,9}} | collective-permute-start | bytes 786440 | tf_op jit(solution)/shard_map/ppermute | solution.py:29
  24.8 98.6 %collective-permute-start.7 = (bf16[2,128,512]{2,1,0:T(8,128)(2,1)S(1)}, bf16[2,128,512]{2,1,0:T(8,128)(2,1)S(1)}, u32[]{:S(2)}, u32[]{:S(2)}) collective-permute-start(bf16[2,128,512]{2,1,0:T(8,128)(2,1)S(1)} %pad_maximum_fusion.5), channel_id=1, source_target_pairs={{2,0},{4,2},{6,4},{8,6},{10,8},{12,10},{14,12},{16,14},{18,16},{20... | collective-permute-start | bytes 786440 | tf_op jit(solution)/shard_map/ppermute | solution.py:58
  27.1 96.3 %collective-permute-start.6 = (bf16[2,128,512]{2,1,0:T(8,128)(2,1)S(1)}, bf16[2,128,512]{2,1,0:T(8,128)(2,1)S(1)}, u32[]{:S(2)}, u32[]{:S(2)}) collective-permute-start(bf16[2,128,512]{2,1,0:T(8,128)(2,1)S(1)} %pad_maximum_fusion.4), channel_id=1, source_target_pairs={{0,2},{2,4},{4,6},{6,8},{8,10},{10,12},{12,14},{14,16},{16,18},{18... | collective-permute-start | bytes 786440 | tf_op jit(solution)/shard_map/ppermute | solution.py:58
  34.4 90.0 %collective-permute-start.5 = (bf16[2,128,512]{2,1,0:T(8,128)(2,1)S(1)}, bf16[2,128,512]{2,1,0:T(8,128)(2,1)S(1)}, u32[]{:S(2)}, u32[]{:S(2)}) collective-permute-start(bf16[2,128,512]{2,1,0:T(8,128)(2,1)S(1)} %add_add_fusion.1), channel_id=1, source_target_pairs={{0,6},{8,14},{16,22},{24,30},{1,7},{9,15},{17,23},{25,31}} | collective-permute-start | bytes 786440 | tf_op jit(solution)/shard_map/ppermute | solution.py:29
  35.7 88.7 %collective-permute-start.4 = (bf16[2,128,512]{2,1,0:T(8,128)(2,1)S(1)}, bf16[2,128,512]{2,1,0:T(8,128)(2,1)S(1)}, u32[]{:S(2)}, u32[]{:S(2)}) collective-permute-start(bf16[2,128,512]{2,1,0:T(8,128)(2,1)S(1)} %add_add_fusion.1), channel_id=1, source_target_pairs={{0,4},{8,12},{16,20},{24,28},{1,5},{9,13},{17,21},{25,29}} | collective-permute-start | bytes 786440 | tf_op jit(solution)/shard_map/ppermute | solution.py:29
  36.4 88.0 %collective-permute-start.3 = (bf16[2,128,512]{2,1,0:T(8,128)(2,1)S(1)}, bf16[2,128,512]{2,1,0:T(8,128)(2,1)S(1)}, u32[]{:S(2)}, u32[]{:S(2)}) collective-permute-start(bf16[2,128,512]{2,1,0:T(8,128)(2,1)S(1)} %add_add_fusion.1), channel_id=1, source_target_pairs={{0,2},{8,10},{16,18},{24,26},{1,3},{9,11},{17,19},{25,27}} | collective-permute-start | bytes 786440 | tf_op jit(solution)/shard_map/ppermute | solution.py:29
  141.3 13.0 %collective-permute-start.10 = (bf16[2,128,512]{2,1,0:T(8,128)(2,1)S(1)}, bf16[2,128,512]{2,1,0:T(8,128)(2,1)S(1)}, u32[]{:S(2)}, u32[]{:S(2)}) collective-permute-start(bf16[2,128,512]{2,1,0:T(8,128)(2,1)S(1)} %fusion.3), channel_id=1, source_target_pairs={{6,0},{14,8},{22,16},{30,24},{7,1},{15,9},{23,17},{31,25}} | collective-permute-start | bytes 786440 | tf_op jit(solution)/shard_map/ppermute | solution.py:45
  142.7 11.7 %collective-permute-start.9 = (bf16[2,128,512]{2,1,0:T(8,128)(2,1)S(1)}, bf16[2,128,512]{2,1,0:T(8,128)(2,1)S(1)}, u32[]{:S(2)}, u32[]{:S(2)}) collective-permute-start(bf16[2,128,512]{2,1,0:T(8,128)(2,1)S(1)} %fusion.3), channel_id=1, source_target_pairs={{4,0},{12,8},{20,16},{28,24},{5,1},{13,9},{21,17},{29,25}} | collective-permute-start | bytes 786440 | tf_op jit(solution)/shard_map/ppermute | solution.py:45
  143.3 11.1 %collective-permute-start.8 = (bf16[2,128,512]{2,1,0:T(8,128)(2,1)S(1)}, bf16[2,128,512]{2,1,0:T(8,128)(2,1)S(1)}, u32[]{:S(2)}, u32[]{:S(2)}) collective-permute-start(bf16[2,128,512]{2,1,0:T(8,128)(2,1)S(1)} %fusion.3), channel_id=1, source_target_pairs={{2,0},{10,8},{18,16},{26,24},{3,1},{11,9},{19,17},{27,25}} | collective-permute-start | bytes 786440 | tf_op jit(solution)/shard_map/ppermute | solution.py:45
  154.6 10.5 %collective-permute-start.13 = (bf16[2,128,512]{2,1,0:T(8,128)(2,1)S(1)}, bf16[2,128,512]{2,1,0:T(8,128)(2,1)S(1)}, u32[]{:S(2)}, u32[]{:S(2)}) collective-permute-start(bf16[2,128,512]{2,1,0:T(8,128)(2,1)S(1)} %fusion.19), channel_id=1, source_target_pairs={{24,0},{25,1}} | collective-permute-start | bytes 786440 | tf_op jit(solution)/shard_map/ppermute | solution.py:45
  155.2 9.8 %collective-permute-start.12 = (bf16[2,128,512]{2,1,0:T(8,128)(2,1)S(1)}, bf16[2,128,512]{2,1,0:T(8,128)(2,1)S(1)}, u32[]{:S(2)}, u32[]{:S(2)}) collective-permute-start(bf16[2,128,512]{2,1,0:T(8,128)(2,1)S(1)} %fusion.19), channel_id=1, source_target_pairs={{16,0},{17,1}} | collective-permute-start | bytes 786440 | tf_op jit(solution)/shard_map/ppermute | solution.py:45
  155.9 9.2 %collective-permute-start.11 = (bf16[2,128,512]{2,1,0:T(8,128)(2,1)S(1)}, bf16[2,128,512]{2,1,0:T(8,128)(2,1)S(1)}, u32[]{:S(2)}, u32[]{:S(2)}) collective-permute-start(bf16[2,128,512]{2,1,0:T(8,128)(2,1)S(1)} %fusion.19), channel_id=1, source_target_pairs={{8,0},{9,1}} | collective-permute-start | bytes 786440 | tf_op jit(solution)/shard_map/ppermute | solution.py:45
  157.7 31.6 %collective-permute-start.14 = (bf16[2,128,512]{2,1,0:T(8,128)(2,1)S(1)}, bf16[2,128,512]{2,1,0:T(8,128)(2,1)S(1)}, u32[]{:S(2)}, u32[]{:S(2)}) collective-permute-start(bf16[2,128,512]{2,1,0:T(8,128)(2,1)S(1)} %pad_maximum_fusion.6), channel_id=1, source_target_pairs={{0,2},{2,4},{4,6},{6,8},{8,10},{10,12},{12,14},{14,16},{16,18},{18... | collective-permute-start | bytes 786440 | tf_op jit(solution)/shard_map/ppermute | solution.py:58
  163.1 26.2 %collective-permute-start.15 = (bf16[2,128,512]{2,1,0:T(8,128)(2,1)S(1)}, bf16[2,128,512]{2,1,0:T(8,128)(2,1)S(1)}, u32[]{:S(2)}, u32[]{:S(2)}) collective-permute-start(bf16[2,128,512]{2,1,0:T(8,128)(2,1)S(1)} %pad_maximum_fusion.7), channel_id=1, source_target_pairs={{2,0},{4,2},{6,4},{8,6},{10,8},{12,10},{14,12},{16,14},{18,16},{20... | collective-permute-start | bytes 786440 | tf_op jit(solution)/shard_map/ppermute | solution.py:58
  189.3 28.2 %copy-start.9 = (f32[256,512]{1,0:T(8,128)S(1)}, f32[256,512]{1,0:T(8,128)}, u32[]{:S(2)}) copy-start(f32[256,512]{1,0:T(8,128)} %get-tuple-element.21) | copy-start | bytes 1572868
  190.0 55.9 %all-to-all-start.1 = ((bf16[16,128,512]{2,1,0:T(8,128)(2,1)}), bf16[16,128,512]{2,1,0:T(8,128)(2,1)S(1)}, u32[]{:S(2)}, u32[]{:S(2)}) async-start(bf16[16,128,512]{2,1,0:T(8,128)(2,1)} %get-tuple-element.27), calls=%async_computation.1 | async-start | bytes 4194304 | tf_op jit(solution)/shard_map/all_to_all | solution.py:322
  (7 other events, 14.6 us)

commit v10 on v9

--- a/solution.py
+++ b/solution.py
@@ -21,19 +21,11 @@
     count = lax.axis_size(axis)
     mine = lax.axis_index(axis) == root
     array = jnp.where(mine, array, jnp.zeros_like(array))
-    step = 1
-    while step * RADIX < count:
-        step *= RADIX
-    while step >= 1:
-        arrived = [
-            lax.ppermute(array, axis, [(i, i + j * step) for i in range(0, count, RADIX * step) if i + j * step < count])
-            for j in range(1, RADIX)
-            if j * step < count
-        ]
-        for part in arrived:
-            array = array + part
-        step //= RADIX
-    return array
+    total = array
+    for target in range(count):
+        if target != root:
+            total = total + lax.ppermute(array, axis, [(root, target)])
+    return total
 
 
 def gather_to_root(array, axis):

time: 250 us -> 266 us (1.064)
  starting transfers between devices: 38.3 us -> 48.5 us
  other arithmetic: 41 us -> 45.3 us
    ppermute x6 -> x15, waiting for transfers between devices: 0.02 us -> 87.2 us  [spread_2(): total = total + lax.ppermute(array, axis, [(root, target)])]
    ppermute x4, waiting for transfers between devices: 86.3 us -> 0.01 us  [shift(): return lax.ppermute(array, axis, pairs)]
    ppermute x6 -> x15, starting transfers between devices: 4.68 us -> 12.8 us  [spread_2(): total = total + lax.ppermute(array, axis, [(root, target)])]
  transfers between devices with their start and end apart: 18 -> 27, of which waited for: 2 -> 2; matrix products, arithmetic and copies ran while one was open for 13% -> 14% of each run, Pallas kernels for 23% -> 21%
where the time goes in v10:
time: 266 us; the launch traced here: 265 us
  waiting for transfers between devices  102 us (38%)
  Pallas kernels  56 us (21%)
  starting transfers between devices  48.5 us (18%)
  other arithmetic  45.3 us (17%)
  local copies, waits for them, and re-layouts  11.2 us (4%)
    ppermute x15, waiting for transfers between devices, spread_2(): total = total + lax.ppermute(array, axis, [(root, target)])  87.2 us
    pallas_call x3, Pallas kernels, list_pairs(): pl.pallas_call(list_kernel, grid_spec=grid_spec, out_shape=[jax.ShapeDtyp...  35.7 us
    pallas_call x1, Pallas kernels, rand_pairs(): pl.pallas_call(functools.partial(rand_kernel, heads), grid_spec=grid_spec...  20.3 us
    ppermute x4, starting transfers between devices, shift(): return lax.ppermute(array, axis, pairs)  15.6 us
    all_to_all x1, waiting for transfers between devices, shards(): lax.all_to_all(dq_rand, 'ctx', split_axis=0, concat_axis=0, tiled=True)  15 us
    ppermute x15, starting transfers between devices, spread_2(): total = total + lax.ppermute(array, axis, [(root, target)])  12.8 us
    all_to_all x1, starting transfers between devices, shards(): lax.all_to_all(dq_rand, 'ctx', split_axis=0, concat_axis=0, tiled=True)  8.22 us
    all_to_all x1, starting transfers between devices, shards(): lax.all_to_all(routed, 'ctx', split_axis=0, concat_axis=0, tiled=True)  6.69 us
  transfers between devices with their start and end apart: 27, of which 2 were waited for; matrix products, arithmetic and copies ran while one was open for 14% of the time, Pallas kernels for 21%

profile of v10, /device:TPU:11, one launch (start us, length us, event | category | flops | bytes accessed | tf_op | source)
XLA Modules:
  0.0 264.6 jit_solution(13979610053550826273)
XLA Ops:
  5.9 5.3 %select_reduce_fusion = bf16[16,272,512]{2,1,0:T(8,128)(2,1)} fusion(pred[16,4]{1,0:T(8,128)(4,1)S(1)} %copy.22, bf16[4,272,512]{2,1,0:T(8,128)(2,1)S(1)} %concatenate.19), kind=kLoop, calls=%fused_computation | loop fusion | flops 15597568 | bytes 5570624 | tf_op jit(solution)/shard_map/reduce_sum | solution.py:297
  11.1 4.7 %broadcast_select_fusion = bf16[16,272,512]{2,1,0:T(8,128)(2,1)} fusion(bf16[16,272,512]{2,1,0:T(8,128)(2,1)} %select_reduce_fusion, pred[272]{0:T(512)(128)(4,1)S(1)} %iota_compare_fusion.2, bf16[16]{0:T(256)(128)(2,1)S(1)} %convert_element_type.130), kind=kLoop, calls=%fused_computation.4 | loop fusion | flops 2228224 | bytes 8913200 | tf_op jit(solution)/shard_map/jit(_where)/select_n | solution.py:301
  15.9 6.7 %all-to-all-start = ((bf16[16,272,512]{2,1,0:T(8,128)(2,1)}), bf16[16,272,512]{2,1,0:T(8,128)(2,1)}, u32[]{:S(2)}, u32[]{:S(2)}) async-start(bf16[16,272,512]{2,1,0:T(8,128)(2,1)} %broadcast_select_fusion), calls=%async_computation | async-start | bytes 8912896 | tf_op jit(solution)/shard_map/all_to_all | solution.py:304
  28.2 1.4 collective-permute-start.8
  32.2 1.4 collective-permute-start.5
  36.3 87.2 %collective-permute-done.6 = bf16[2,128,512]{2,1,0:T(8,128)(2,1)} collective-permute-done((bf16[2,128,512]{2,1,0:T(8,128)(2,1)}, bf16[2,128,512]{2,1,0:T(8,128)(2,1)}, u32[]{:S(2)}, u32[]{:S(2)}) %collective-permute-start.6) | collective-permute-done | bytes 262176 | tf_op jit(solution)/shard_map/ppermute | solution.py:27
  128.0 4.7 %collective-permute-start.16 = (bf16[2,128,512]{2,1,0:T(8,128)(2,1)}, bf16[2,128,512]{2,1,0:T(8,128)(2,1)}, u32[]{:S(2)}, u32[]{:S(2)}) collective-permute-start(bf16[2,128,512]{2,1,0:T(8,128)(2,1)} %pad_maximum_fusion.5), channel_id=1, source_target_pairs={{2,0},{4,2},{6,4},{8,6},{10,8},{12,10},{14,12},{16,14},{18,16},{20... | collective-permute-start | bytes 786440 | tf_op jit(solution)/shard_map/ppermute | solution.py:50
  132.7 1.9 collective-permute-start.15
  134.6 1.5 add_add_fusion
  138.5 11.9 %shard_map.95 = (f32[512,512]{1,0:T(8,128)}, f32[512,512]{1,0:T(8,128)}, f32[512,512]{1,0:T(8,128)}) custom-call(s32[4]{0:T(128)} %iota.37.qin.qout, s32[4]{0:T(128)} %iota.37.qin.qout, s32[4]{0:T(128)} %broadcast_25_first.2.first, s32[4]{0:T(128)} %broadcast_24_ktab.2.ktab, s32[4]{0:T(128)} %compare_convert_fusion.2.mtab, bf16[512,512]{1,0:T(8,128)(2,1)} %q_ref.5, ...), custom_call_target="tpu_custom_call" | custom-call | tf_op jit(solution)/shard_map/pallas_call | solution.py:146
  153.2 1.8 collective-permute-start.19
  161.2 7.2 %shard_map.96 = (f32[256,512]{1,0:T(8,128)}, f32[256,512]{1,0:T(8,128)}, f32[256,512]{1,0:T(8,128)}) custom-call(s32[2]{0:T(128)} %iota_multiply_fusion.qin, s32[2]{0:T(128)} %iota.42.qout, s32[2]{0:T(128)} %broadcast_26_first.2.first, s32[2]{0:T(128)} %get-tuple-element.71.ktab, s32[2]{0:T(128)} %get-tuple-element.72.mtab, bf16[512,512]{1,0:T(8,128)(2,1)} %q_ref.5, ...), custom_call_target="tpu_custom_call" | custom-call | tf_op jit(solution)/shard_map/pallas_call | solution.py:146
  172.9 6.9 %collective-permute-start.23 = (bf16[2,128,512]{2,1,0:T(8,128)(2,1)S(1)}, bf16[2,128,512]{2,1,0:T(8,128)(2,1)S(1)}, u32[]{:S(2)}, u32[]{:S(2)}) collective-permute-start(bf16[2,128,512]{2,1,0:T(8,128)(2,1)S(1)} %pad_maximum_fusion.6), channel_id=1, source_target_pairs={{0,2},{2,4},{4,6},{6,8},{8,10},{10,12},{12,14},{14,16},{16,18},{18... | collective-permute-start | bytes 786440 | tf_op jit(solution)/shard_map/ppermute | solution.py:50
  179.8 2.1 collective-permute-start.24
  185.2 20.3 %shard_map.97 = (bf16[16,128,512]{2,1,0:T(8,128)(2,1)}, f32[16,128,512]{2,1,0:T(8,128)}, f32[16,128,512]{2,1,0:T(8,128)}) custom-call(s32[16]{0:T(128)} %add_maximum_fusion.ktab, s32[16]{0:T(128)} %compare_convert_fusion.1.mtab, bf16[16,272,512]{2,1,0:T(8,128)(2,1)} %all-to-all-done.q_ref.do_ref.st_ref, ...), custom_call_target="tpu_custom_call" | custom-call | tf_op jit(solution)/shard_map/pallas_call | solution.py:178
  205.5 8.2 %all-to-all-start.1 = ((bf16[16,128,512]{2,1,0:T(8,128)(2,1)}), bf16[16,128,512]{2,1,0:T(8,128)(2,1)S(1)}, u32[]{:S(2)}, u32[]{:S(2)}) async-start(bf16[16,128,512]{2,1,0:T(8,128)(2,1)} %get-tuple-element.27), calls=%async_computation.1 | async-start | bytes 4194304 | tf_op jit(solution)/shard_map/all_to_all | solution.py:314
  213.9 16.6 %shard_map.94 = (f32[512,512]{1,0:T(8,128)}, f32[768,512]{1,0:T(8,128)}, f32[768,512]{1,0:T(8,128)}) custom-call(s32[6]{0:T(128)} %constant.35.clone.1.qin.qout, s32[6]{0:T(128)} %constant.35.clone.1.qin.qout, s32[6]{0:T(128)} %constant.36.clone.1.first, s32[6]{0:T(128)} %constant.37.clone.1.ktab, s32[6]{0:T(128)} %constant.38.clone.1.mtab, ...), custom_call_target="tpu_custom_call" | custom-call | tf_op jit(solution)/shard_map/pallas_call | solution.py:146
  230.5 2.2 add_bitcast_fusion
  234.3 2.5 bitcast_add_fusion.3
  236.8 5.1 %multiply_reduce_fusion = (f32[4,128,512]{2,1,0:T(8,128)S(1)}, f32[4,128,512]{2,1,0:T(8,128)S(1)}) fusion(f32[16,128,512]{2,1,0:T(8,128)} %get-tuple-element.34, f32[16,4]{1,0:T(8,128)S(1)} %compare_convert_fusion, f32[16,128,512]{2,1,0:T(8,128)S(1)} %copy-done.4), kind=kLoop, calls=%fused_computation.1 | loop fusion | flops 16252928 | bytes 10486016 | tf_op jit(solution)/shard_map/reduce_sum | solution.py:321
  241.9 2.2 fusion
  244.0 2.1 fusion.1
  246.1 15.0 %all-to-all-done.1 = bf16[16,128,512]{2,1,0:T(8,128)(2,1)S(1)} async-done(((bf16[16,128,512]{2,1,0:T(8,128)(2,1)}), bf16[16,128,512]{2,1,0:T(8,128)(2,1)S(1)}, u32[]{:S(2)}, u32[]{:S(2)}) %all-to-all-start.1) | async-done | bytes 2097184 | tf_op jit(solution)/shard_map/all_to_all | solution.py:314
  261.7 1.4 multiply_reduce_fusion.2
  (128 shorter events, 43.1 us)
Async XLA Ops:
  15.9 167.1 %all-to-all-start = ((bf16[16,272,512]{2,1,0:T(8,128)(2,1)}), bf16[16,272,512]{2,1,0:T(8,128)(2,1)}, u32[]{:S(2)}, u32[]{:S(2)}) async-start(bf16[16,272,512]{2,1,0:T(8,128)(2,1)} %broadcast_select_fusion), calls=%async_computation | async-start | bytes 8912896 | tf_op jit(solution)/shard_map/all_to_all | solution.py:304
  25.4 5.5 %collective-permute-start.11 = (bf16[2,128,512]{2,1,0:T(8,128)(2,1)}, bf16[2,128,512]{2,1,0:T(8,128)(2,1)S(1)}, u32[]{:S(2)}, u32[]{:S(2)}) collective-permute-start(bf16[2,128,512]{2,1,0:T(8,128)(2,1)} %maximum_select_fusion), channel_id=1, source_target_pairs={{0,24},{1,25}} | collective-permute-start | bytes 786440 | tf_op jit(solution)/shard_map/ppermute | solution.py:27
  26.1 6.1 %collective-permute-start.10 = (bf16[2,128,512]{2,1,0:T(8,128)(2,1)}, bf16[2,128,512]{2,1,0:T(8,128)(2,1)S(1)}, u32[]{:S(2)}, u32[]{:S(2)}) collective-permute-start(bf16[2,128,512]{2,1,0:T(8,128)(2,1)} %maximum_select_fusion), channel_id=1, source_target_pairs={{0,22},{1,23}} | collective-permute-start | bytes 786440 | tf_op jit(solution)/shard_map/ppermute | solution.py:27
  27.5 6.7 %collective-permute-start.9 = (bf16[2,128,512]{2,1,0:T(8,128)(2,1)}, bf16[2,128,512]{2,1,0:T(8,128)(2,1)S(1)}, u32[]{:S(2)}, u32[]{:S(2)}) collective-permute-start(bf16[2,128,512]{2,1,0:T(8,128)(2,1)} %maximum_select_fusion), channel_id=1, source_target_pairs={{0,20},{1,21}} | collective-permute-start | bytes 786440 | tf_op jit(solution)/shard_map/ppermute | solution.py:27
  28.2 6.7 %collective-permute-start.8 = (bf16[2,128,512]{2,1,0:T(8,128)(2,1)}, bf16[2,128,512]{2,1,0:T(8,128)(2,1)}, u32[]{:S(2)}, u32[]{:S(2)}) collective-permute-start(bf16[2,128,512]{2,1,0:T(8,128)(2,1)} %maximum_select_fusion), channel_id=1, source_target_pairs={{0,18},{1,19}} | collective-permute-start | bytes 786440 | tf_op jit(solution)/shard_map/ppermute | solution.py:27
  29.5 6.0 %collective-permute-start.7 = (bf16[2,128,512]{2,1,0:T(8,128)(2,1)}, bf16[2,128,512]{2,1,0:T(8,128)(2,1)}, u32[]{:S(2)}, u32[]{:S(2)}) collective-permute-start(bf16[2,128,512]{2,1,0:T(8,128)(2,1)} %maximum_select_fusion), channel_id=1, source_target_pairs={{0,16},{1,17}} | collective-permute-start | bytes 786440 | tf_op jit(solution)/shard_map/ppermute | solution.py:27
  30.9 92.5 %collective-permute-start.6 = (bf16[2,128,512]{2,1,0:T(8,128)(2,1)}, bf16[2,128,512]{2,1,0:T(8,128)(2,1)}, u32[]{:S(2)}, u32[]{:S(2)}) collective-permute-start(bf16[2,128,512]{2,1,0:T(8,128)(2,1)} %maximum_select_fusion), channel_id=1, source_target_pairs={{0,14},{1,15}} | collective-permute-start | bytes 786440 | tf_op jit(solution)/shard_map/ppermute | solution.py:27
  32.2 91.9 %collective-permute-start.5 = (bf16[2,128,512]{2,1,0:T(8,128)(2,1)}, bf16[2,128,512]{2,1,0:T(8,128)(2,1)}, u32[]{:S(2)}, u32[]{:S(2)}) collective-permute-start(bf16[2,128,512]{2,1,0:T(8,128)(2,1)} %maximum_select_fusion), channel_id=1, source_target_pairs={{0,12},{1,13}} | collective-permute-start | bytes 786440 | tf_op jit(solution)/shard_map/ppermute | solution.py:27
  34.2 93.8 %collective-permute-start.4 = (bf16[2,128,512]{2,1,0:T(8,128)(2,1)}, bf16[2,128,512]{2,1,0:T(8,128)(2,1)S(1)}, u32[]{:S(2)}, u32[]{:S(2)}) collective-permute-start(bf16[2,128,512]{2,1,0:T(8,128)(2,1)} %maximum_select_fusion), channel_id=1, source_target_pairs={{0,10},{1,11}} | collective-permute-start | bytes 786440 | tf_op jit(solution)/shard_map/ppermute | solution.py:27
  34.9 97.8 %collective-permute-start.3 = (bf16[2,128,512]{2,1,0:T(8,128)(2,1)}, bf16[2,128,512]{2,1,0:T(8,128)(2,1)S(1)}, u32[]{:S(2)}, u32[]{:S(2)}) collective-permute-start(bf16[2,128,512]{2,1,0:T(8,128)(2,1)} %maximum_select_fusion), channel_id=1, source_target_pairs={{0,8},{1,9}} | collective-permute-start | bytes 786440 | tf_op jit(solution)/shard_map/ppermute | solution.py:27
  35.6 99.0 %collective-permute-start.2 = (bf16[2,128,512]{2,1,0:T(8,128)(2,1)}, bf16[2,128,512]{2,1,0:T(8,128)(2,1)S(1)}, u32[]{:S(2)}, u32[]{:S(2)}) collective-permute-start(bf16[2,128,512]{2,1,0:T(8,128)(2,1)} %maximum_select_fusion), channel_id=1, source_target_pairs={{0,6},{1,7}} | collective-permute-start | bytes 786440 | tf_op jit(solution)/shard_map/ppermute | solution.py:27
  123.4 11.2 %collective-permute-start.1 = (bf16[2,128,512]{2,1,0:T(8,128)(2,1)}, bf16[2,128,512]{2,1,0:T(8,128)(2,1)S(1)}, u32[]{:S(2)}, u32[]{:S(2)}) collective-permute-start(bf16[2,128,512]{2,1,0:T(8,128)(2,1)} %maximum_select_fusion), channel_id=1, source_target_pairs={{0,4},{1,5}} | collective-permute-start | bytes 786440 | tf_op jit(solution)/shard_map/ppermute | solution.py:27
  124.1 10.5 %collective-permute-start = (bf16[2,128,512]{2,1,0:T(8,128)(2,1)}, bf16[2,128,512]{2,1,0:T(8,128)(2,1)S(1)}, u32[]{:S(2)}, u32[]{:S(2)}) collective-permute-start(bf16[2,128,512]{2,1,0:T(8,128)(2,1)} %maximum_select_fusion), channel_id=1, source_target_pairs={{0,2},{1,3}} | collective-permute-start | bytes 786440 | tf_op jit(solution)/shard_map/ppermute | solution.py:27
  128.0 28.4 %collective-permute-start.16 = (bf16[2,128,512]{2,1,0:T(8,128)(2,1)}, bf16[2,128,512]{2,1,0:T(8,128)(2,1)}, u32[]{:S(2)}, u32[]{:S(2)}) collective-permute-start(bf16[2,128,512]{2,1,0:T(8,128)(2,1)} %pad_maximum_fusion.5), channel_id=1, source_target_pairs={{2,0},{4,2},{6,4},{8,6},{10,8},{12,10},{14,12},{16,14},{18,16},{20... | collective-permute-start | bytes 786440 | tf_op jit(solution)/shard_map/ppermute | solution.py:50
  132.7 24.6 %collective-permute-start.15 = (bf16[2,128,512]{2,1,0:T(8,128)(2,1)}, bf16[2,128,512]{2,1,0:T(8,128)(2,1)}, u32[]{:S(2)}, u32[]{:S(2)}) collective-permute-start(bf16[2,128,512]{2,1,0:T(8,128)(2,1)} %pad_maximum_fusion.4), channel_id=1, source_target_pairs={{0,2},{2,4},{4,6},{6,8},{8,10},{10,12},{12,14},{14,16},{16,18},{18... | collective-permute-start | bytes 786440 | tf_op jit(solution)/shard_map/ppermute | solution.py:50
  153.2 16.4 %collective-permute-start.19 = (bf16[2,128,512]{2,1,0:T(8,128)(2,1)S(1)}, bf16[2,128,512]{2,1,0:T(8,128)(2,1)S(1)}, u32[]{:S(2)}, u32[]{:S(2)}) collective-permute-start(bf16[2,128,512]{2,1,0:T(8,128)(2,1)S(1)} %fusion.3), channel_id=1, source_target_pairs={{6,0},{14,8},{22,16},{30,24},{7,1},{15,9},{23,17},{31,25}} | collective-permute-start | bytes 786440 | tf_op jit(solution)/shard_map/ppermute | solution.py:37
  155.0 14.6 %collective-permute-start.18 = (bf16[2,128,512]{2,1,0:T(8,128)(2,1)S(1)}, bf16[2,128,512]{2,1,0:T(8,128)(2,1)S(1)}, u32[]{:S(2)}, u32[]{:S(2)}) collective-permute-start(bf16[2,128,512]{2,1,0:T(8,128)(2,1)S(1)} %fusion.3), channel_id=1, source_target_pairs={{4,0},{12,8},{20,16},{28,24},{5,1},{13,9},{21,17},{29,25}} | collective-permute-start | bytes 786440 | tf_op jit(solution)/shard_map/ppermute | solution.py:37
  155.6 13.9 %collective-permute-start.17 = (bf16[2,128,512]{2,1,0:T(8,128)(2,1)S(1)}, bf16[2,128,512]{2,1,0:T(8,128)(2,1)S(1)}, u32[]{:S(2)}, u32[]{:S(2)}) collective-permute-start(bf16[2,128,512]{2,1,0:T(8,128)(2,1)S(1)} %fusion.3), channel_id=1, source_target_pairs={{2,0},{10,8},{18,16},{26,24},{3,1},{11,9},{19,17},{27,25}} | collective-permute-start | bytes 786440 | tf_op jit(solution)/shard_map/ppermute | solution.py:37
  169.7 12.2 %collective-permute-start.22 = (bf16[2,128,512]{2,1,0:T(8,128)(2,1)S(1)}, bf16[2,128,512]{2,1,0:T(8,128)(2,1)S(1)}, u32[]{:S(2)}, u32[]{:S(2)}) collective-permute-start(bf16[2,128,512]{2,1,0:T(8,128)(2,1)S(1)} %fusion.19), channel_id=1, source_target_pairs={{24,0},{25,1}} | collective-permute-start | bytes 786440 | tf_op jit(solution)/shard_map/ppermute | solution.py:37
  170.4 11.5 %collective-permute-start.21 = (bf16[2,128,512]{2,1,0:T(8,128)(2,1)S(1)}, bf16[2,128,512]{2,1,0:T(8,128)(2,1)S(1)}, u32[]{:S(2)}, u32[]{:S(2)}) collective-permute-start(bf16[2,128,512]{2,1,0:T(8,128)(2,1)S(1)} %fusion.19), channel_id=1, source_target_pairs={{16,0},{17,1}} | collective-permute-start | bytes 786440 | tf_op jit(solution)/shard_map/ppermute | solution.py:37
  171.1 10.8 %collective-permute-start.20 = (bf16[2,128,512]{2,1,0:T(8,128)(2,1)S(1)}, bf16[2,128,512]{2,1,0:T(8,128)(2,1)S(1)}, u32[]{:S(2)}, u32[]{:S(2)}) collective-permute-start(bf16[2,128,512]{2,1,0:T(8,128)(2,1)S(1)} %fusion.19), channel_id=1, source_target_pairs={{8,0},{9,1}} | collective-permute-start | bytes 786440 | tf_op jit(solution)/shard_map/ppermute | solution.py:37
  172.9 32.6 %collective-permute-start.23 = (bf16[2,128,512]{2,1,0:T(8,128)(2,1)S(1)}, bf16[2,128,512]{2,1,0:T(8,128)(2,1)S(1)}, u32[]{:S(2)}, u32[]{:S(2)}) collective-permute-start(bf16[2,128,512]{2,1,0:T(8,128)(2,1)S(1)} %pad_maximum_fusion.6), channel_id=1, source_target_pairs={{0,2},{2,4},{4,6},{6,8},{8,10},{10,12},{12,14},{14,16},{16,18},{18... | collective-permute-start | bytes 786440 | tf_op jit(solution)/shard_map/ppermute | solution.py:50
  179.8 25.7 %collective-permute-start.24 = (bf16[2,128,512]{2,1,0:T(8,128)(2,1)S(1)}, bf16[2,128,512]{2,1,0:T(8,128)(2,1)S(1)}, u32[]{:S(2)}, u32[]{:S(2)}) collective-permute-start(bf16[2,128,512]{2,1,0:T(8,128)(2,1)S(1)} %pad_maximum_fusion.7), channel_id=1, source_target_pairs={{2,0},{4,2},{6,4},{8,6},{10,8},{12,10},{14,12},{16,14},{18,16},{20... | collective-permute-start | bytes 786440 | tf_op jit(solution)/shard_map/ppermute | solution.py:50
  205.5 55.6 %all-to-all-start.1 = ((bf16[16,128,512]{2,1,0:T(8,128)(2,1)}), bf16[16,128,512]{2,1,0:T(8,128)(2,1)S(1)}, u32[]{:S(2)}, u32[]{:S(2)}) async-start(bf16[16,128,512]{2,1,0:T(8,128)(2,1)} %get-tuple-element.27), calls=%async_computation.1 | async-start | bytes 4194304 | tf_op jit(solution)/shard_map/all_to_all | solution.py:314
  (15 other events, 214.2 us)

commit v11 on v9

--- a/solution.py
+++ b/solution.py
@@ -302,13 +302,12 @@
         axis=1,
     )
     pick = select > 0
-    routed = jnp.sum(jnp.where(pick[:, :, None, None], packed[None], 0), axis=1).astype(
-        jnp.bfloat16
-    )
     row_id = lax.broadcasted_iota(jnp.int32, (1, packed.shape[1], 1), 1)
     routed = jnp.where(
-        row_id == 2 * height + 2, slot_send.astype(jnp.bfloat16)[:, None, None], routed
-    )
+        row_id == 2 * height + 2, slot_send.astype(jnp.bfloat16)[:, None, None], jnp.bfloat16(0)
+    )
+    for slot in range(slot_count):
+        routed = routed + jnp.where(pick[:, slot, None, None], packed[slot][None], jnp.bfloat16(0))
     arrived = lax.all_to_all(routed, "ctx", split_axis=0, concat_axis=0, tiled=True)
     slot_recv = arrived[:, 2 * height + 2, 0].astype(jnp.float32).astype(jnp.int32)
     ktab_r = jnp.maximum(slot_recv - 1, 0)

time: 250 us -> 244 us (0.976)
  other arithmetic: 41 us -> 33.9 us
    reduce_sum x1 -> x0, other arithmetic: 5.3 us -> none  [shards(): jnp.sum(jnp.where(pick[:, :, None, None], packed[None], 0), axis=1)]
    select_n x1, other arithmetic: 4.75 us -> 0.08 us  [shards(): jnp.where(row_id == 2 * height + 2, slot_send.astype(jnp.bfloat16)[:, Non...]
    add x0 -> x1, other arithmetic: none -> 3.02 us  [shards(): routed + jnp.where(pick[:, slot, None, None], packed[slot][None], jnp.bfl...]
  transfers between devices with their start and end apart: 18 -> 18, of which waited for: 2 -> 2; matrix products, arithmetic and copies ran while one was open for 13% -> 13% of each run, Pallas kernels for 23% -> 24%
where the time goes in v11:
time: 244 us; the launch traced here: 242 us
  waiting for transfers between devices  102 us (42%)
  Pallas kernels  58.4 us (24%)
  starting transfers between devices  36 us (15%)
  other arithmetic  33.9 us (14%)
  local copies, waits for them, and re-layouts  10 us (4%)
    ppermute x4, waiting for transfers between devices, shift(): return lax.ppermute(array, axis, pairs)  86.5 us
    pallas_call x3, Pallas kernels, list_pairs(): pl.pallas_call(list_kernel, grid_spec=grid_spec, out_shape=[jax.ShapeDtyp...  35.7 us
    pallas_call x1, Pallas kernels, rand_pairs(): pl.pallas_call(functools.partial(rand_kernel, heads), grid_spec=grid_spec...  22.7 us
    all_to_all x1, waiting for transfers between devices, shards(): lax.all_to_all(dq_rand, 'ctx', split_axis=0, concat_axis=0, tiled=True)  15.9 us
    ppermute x4, starting transfers between devices, shift(): return lax.ppermute(array, axis, pairs)  13.8 us
    all_to_all x1, starting transfers between devices, shards(): lax.all_to_all(routed, 'ctx', split_axis=0, concat_axis=0, tiled=True)  6.69 us
    all_to_all x1, starting transfers between devices, shards(): lax.all_to_all(dq_rand, 'ctx', split_axis=0, concat_axis=0, tiled=True)  6.2 us
    reduce_sum x1, other arithmetic, shards(): rand_value = jnp.sum(choose[:, :, None, None] * dv_rand[:, None], axis=0)  5.09 us
  transfers between devices with their start and end apart: 18, of which 2 were waited for; matrix products, arithmetic and copies ran while one was open for 13% of the time, Pallas kernels for 24%

profile of v11, /device:TPU:11, one launch (start us, length us, event | category | flops | bytes accessed | tf_op | source)
XLA Modules:
  0.0 241.9 jit_solution(15742512197864364721)
XLA Ops:
  2.4 1.3 convert_multiply_fusion
  5.9 3.0 %select_add_fusion = bf16[16,272,512]{2,1,0:T(8,128)(2,1)} fusion(pred[16]{0:T(512)(128)(4,1)S(1)} %get-tuple-element.73, pred[16]{0:T(512)(128)(4,1)S(1)} %get-tuple-element.74, pred[16]{0:T(512)(128)(4,1)S(1)} %get-tuple-element.75, pred[16]{0:T(512)(128)(4,1)S(1)} %get-tuple-element.72, bf16[272,512]{1,0:T(8,128)(2,1)S(1)} %get-tuple-element.47, ...), kind=kLoop, calls=%fused_computation.3 | loop fusion | flops 17825792 | bytes 5579328 | tf_op jit(solution)/shard_map/add | solution.py:310
  9.0 6.7 %all-to-all-start = ((bf16[16,272,512]{2,1,0:T(8,128)(2,1)}), bf16[16,272,512]{2,1,0:T(8,128)(2,1)}, u32[]{:S(2)}, u32[]{:S(2)}) async-start(bf16[16,272,512]{2,1,0:T(8,128)(2,1)} %select_add_fusion), calls=%async_computation | async-start | bytes 8912896 | tf_op jit(solution)/shard_map/all_to_all | solution.py:311
  17.9 2.3 collective-permute-start.7
  20.2 4.2 %collective-permute-start.6 = (bf16[2,128,512]{2,1,0:T(8,128)(2,1)S(1)}, bf16[2,128,512]{2,1,0:T(8,128)(2,1)S(1)}, u32[]{:S(2)}, u32[]{:S(2)}) collective-permute-start(bf16[2,128,512]{2,1,0:T(8,128)(2,1)S(1)} %pad_maximum_fusion.4), channel_id=1, source_target_pairs={{0,2},{2,4},{4,6},{6,8},{8,10},{10,12},{12,14},{14,16},{16,18},{18... | collective-permute-start | bytes 786440 | tf_op jit(solution)/shard_map/ppermute | solution.py:58
  30.0 86.5 %collective-permute-done.7 = bf16[2,128,512]{2,1,0:T(8,128)(2,1)S(1)} collective-permute-done((bf16[2,128,512]{2,1,0:T(8,128)(2,1)S(1)}, bf16[2,128,512]{2,1,0:T(8,128)(2,1)S(1)}, u32[]{:S(2)}, u32[]{:S(2)}) %collective-permute-start.7) | collective-permute-done | bytes 262176 | tf_op jit(solution)/shard_map/ppermute | solution.py:58
  119.9 11.9 %shard_map.95 = (f32[512,512]{1,0:T(8,128)}, f32[512,512]{1,0:T(8,128)}, f32[512,512]{1,0:T(8,128)}) custom-call(s32[4]{0:T(128)} %iota.37.qin.qout, s32[4]{0:T(128)} %iota.37.qin.qout, s32[4]{0:T(128)} %broadcast_25_first.2.first, s32[4]{0:T(128)} %broadcast_24_ktab.2.ktab, s32[4]{0:T(128)} %compare_convert_fusion.2.mtab, bf16[512,512]{1,0:T(8,128)(2,1)} %q_ref.5, ...), custom_call_target="tpu_custom_call" | custom-call | tf_op jit(solution)/shard_map/pallas_call | solution.py:154
  131.8 1.3 reduce_sum.66
  133.1 1.3 reduce_sum.65
  134.5 1.3 collective-permute-start.10
  139.2 7.2 %shard_map.96 = (f32[256,512]{1,0:T(8,128)}, f32[256,512]{1,0:T(8,128)}, f32[256,512]{1,0:T(8,128)}) custom-call(s32[2]{0:T(128)} %iota_multiply_fusion.qin, s32[2]{0:T(128)} %iota.42.qout, s32[2]{0:T(128)} %broadcast_26_first.2.first, s32[2]{0:T(128)} %get-tuple-element.79.ktab, s32[2]{0:T(128)} %get-tuple-element.80.mtab, bf16[512,512]{1,0:T(8,128)(2,1)} %q_ref.5, ...), custom_call_target="tpu_custom_call" | custom-call | tf_op jit(solution)/shard_map/pallas_call | solution.py:154
  150.8 5.4 %collective-permute-start.14 = (bf16[2,128,512]{2,1,0:T(8,128)(2,1)S(1)}, bf16[2,128,512]{2,1,0:T(8,128)(2,1)S(1)}, u32[]{:S(2)}, u32[]{:S(2)}) collective-permute-start(bf16[2,128,512]{2,1,0:T(8,128)(2,1)S(1)} %pad_maximum_fusion.6), channel_id=1, source_target_pairs={{0,2},{2,4},{4,6},{6,8},{8,10},{10,12},{12,14},{14,16},{16,18},{18... | collective-permute-start | bytes 786440 | tf_op jit(solution)/shard_map/ppermute | solution.py:58
  156.2 1.9 collective-permute-start.15
  161.5 22.7 %shard_map.97 = (bf16[16,128,512]{2,1,0:T(8,128)(2,1)}, f32[16,128,512]{2,1,0:T(8,128)}, f32[16,128,512]{2,1,0:T(8,128)}) custom-call(s32[16]{0:T(128)} %add_maximum_fusion.ktab, s32[16]{0:T(128)} %compare_convert_fusion.1.mtab, bf16[16,272,512]{2,1,0:T(8,128)(2,1)} %all-to-all-done.q_ref.do_ref.st_ref, ...), custom_call_target="tpu_custom_call" | custom-call | tf_op jit(solution)/shard_map/pallas_call | solution.py:186
  184.9 6.2 %all-to-all-start.1 = ((bf16[16,128,512]{2,1,0:T(8,128)(2,1)}), bf16[16,128,512]{2,1,0:T(8,128)(2,1)S(1)}, u32[]{:S(2)}, u32[]{:S(2)}) async-start(bf16[16,128,512]{2,1,0:T(8,128)(2,1)} %get-tuple-element.27), calls=%async_computation.1 | async-start | bytes 4194304 | tf_op jit(solution)/shard_map/all_to_all | solution.py:321
  191.3 16.6 %shard_map.94 = (f32[512,512]{1,0:T(8,128)}, f32[768,512]{1,0:T(8,128)}, f32[768,512]{1,0:T(8,128)}) custom-call(s32[6]{0:T(128)} %constant.33.clone.1.qin.qout, s32[6]{0:T(128)} %constant.33.clone.1.qin.qout, s32[6]{0:T(128)} %constant.34.clone.1.first, s32[6]{0:T(128)} %constant.35.clone.1.ktab, s32[6]{0:T(128)} %constant.36.clone.1.mtab, ...), custom_call_target="tpu_custom_call" | custom-call | tf_op jit(solution)/shard_map/pallas_call | solution.py:154
  207.9 2.2 add_bitcast_fusion
  210.5 2.7 %bitcast_add_fusion.3 = (f32[1,128,512]{2,1,0:T(8,128)}, f32[1,128,512]{2,1,0:T(8,128)}, f32[1,128,512]{2,1,0:T(8,128)}, f32[1,128,512]{2,1,0:T(8,128)S(1)}, f32[1,128,512]{2,1,0:T(8,128)}, /*index=5*/f32[1,128,512]{2,1,0:T(8,128)}) fusion(f32[2,128,512]{2,1,0:T(8,128)} %convert_add_fusion, f32[768,512]{1,0:T(8,128)S(1)} %copy-done.5, f32[]{:T(128)S(6)} %select_n.103, ...), kind=kLoop, calls=%fused_computation.35 | loop fusion | flops 917504 | bytes 5767176 | tf_op jit(solution)/shard_map/add | solution.py:336
  213.2 5.1 %multiply_reduce_fusion = (f32[4,128,512]{2,1,0:T(8,128)S(1)}, f32[4,128,512]{2,1,0:T(8,128)S(1)}) fusion(f32[16,128,512]{2,1,0:T(8,128)} %get-tuple-element.34, f32[16,4]{1,0:T(8,128)S(1)} %compare_convert_fusion, f32[16,128,512]{2,1,0:T(8,128)S(1)} %copy-done.4), kind=kLoop, calls=%fused_computation | loop fusion | flops 16252928 | bytes 10486016 | tf_op jit(solution)/shard_map/reduce_sum | solution.py:328
  218.3 2.2 fusion
  220.5 2.1 fusion.1
  222.6 15.9 %all-to-all-done.1 = bf16[16,128,512]{2,1,0:T(8,128)(2,1)S(1)} async-done(((bf16[16,128,512]{2,1,0:T(8,128)(2,1)}), bf16[16,128,512]{2,1,0:T(8,128)(2,1)S(1)}, u32[]{:S(2)}, u32[]{:S(2)}) %all-to-all-start.1) | async-done | bytes 2097184 | tf_op jit(solution)/shard_map/all_to_all | solution.py:321
  239.1 1.4 multiply_reduce_fusion.2
  240.6 1.3 fusion.2
  (114 shorter events, 28.1 us)
Async XLA Ops:
  0.6 4.4 %copy-start = (bf16[512,512]{1,0:T(8,128)(2,1)S(1)}, bf16[512,512]{1,0:T(8,128)(2,1)}, u32[]{:S(2)}) copy-start(bf16[512,512]{1,0:T(8,128)(2,1)} %do_ref.5) | copy-start | bytes 1572868
  0.6 4.4 %copy-start.1 = (bf16[512,512]{1,0:T(8,128)(2,1)S(1)}, bf16[512,512]{1,0:T(8,128)(2,1)}, u32[]{:S(2)}) copy-start(bf16[512,512]{1,0:T(8,128)(2,1)} %q_ref.5) | copy-start | bytes 1572868
  9.0 6.7 %copy-start.2 = (bf16[512,512]{1,0:T(8,128)(2,1)S(1)}, bf16[512,512]{1,0:T(8,128)(2,1)}, u32[]{:S(2)}) copy-start(bf16[512,512]{1,0:T(8,128)(2,1)} %k_ref.3) | copy-start | bytes 1572868
  9.0 6.7 %copy-start.3 = (bf16[512,512]{1,0:T(8,128)(2,1)S(1)}, bf16[512,512]{1,0:T(8,128)(2,1)}, u32[]{:S(2)}) copy-start(bf16[512,512]{1,0:T(8,128)(2,1)} %v_ref.3) | copy-start | bytes 1572868
  9.0 17.0 %copy-start.12 = (bf16[4,512]{1,0:T(4,128)(2,1)S(1)}, bf16[4,512]{1,0:T(4,128)(2,1)}, u32[]{:S(2)}) copy-start(bf16[4,512]{1,0:T(4,128)(2,1)} %param.12) | copy-start | bytes 12292
  9.0 150.3 %all-to-all-start = ((bf16[16,272,512]{2,1,0:T(8,128)(2,1)}), bf16[16,272,512]{2,1,0:T(8,128)(2,1)}, u32[]{:S(2)}, u32[]{:S(2)}) async-start(bf16[16,272,512]{2,1,0:T(8,128)(2,1)} %select_add_fusion), calls=%async_computation | async-start | bytes 8912896 | tf_op jit(solution)/shard_map/all_to_all | solution.py:311
  15.8 11.4 %collective-permute-start.2 = (bf16[2,128,512]{2,1,0:T(8,128)(2,1)S(1)}, bf16[2,128,512]{2,1,0:T(8,128)(2,1)S(1)}, u32[]{:S(2)}, u32[]{:S(2)}) collective-permute-start(bf16[2,128,512]{2,1,0:T(8,128)(2,1)S(1)} %maximum_select_fusion), channel_id=1, source_target_pairs={{0,24},{1,25}} | collective-permute-start | bytes 786440 | tf_op jit(solution)/shard_map/ppermute | solution.py:29
  16.5 10.8 %collective-permute-start.1 = (bf16[2,128,512]{2,1,0:T(8,128)(2,1)S(1)}, bf16[2,128,512]{2,1,0:T(8,128)(2,1)S(1)}, u32[]{:S(2)}, u32[]{:S(2)}) collective-permute-start(bf16[2,128,512]{2,1,0:T(8,128)(2,1)S(1)} %maximum_select_fusion), channel_id=1, source_target_pairs={{0,16},{1,17}} | collective-permute-start | bytes 786440 | tf_op jit(solution)/shard_map/ppermute | solution.py:29
  17.1 10.1 %collective-permute-start = (bf16[2,128,512]{2,1,0:T(8,128)(2,1)S(1)}, bf16[2,128,512]{2,1,0:T(8,128)(2,1)S(1)}, u32[]{:S(2)}, u32[]{:S(2)}) collective-permute-start(bf16[2,128,512]{2,1,0:T(8,128)(2,1)S(1)} %maximum_select_fusion), channel_id=1, source_target_pairs={{0,8},{1,9}} | collective-permute-start | bytes 786440 | tf_op jit(solution)/shard_map/ppermute | solution.py:29
  17.9 98.6 %collective-permute-start.7 = (bf16[2,128,512]{2,1,0:T(8,128)(2,1)S(1)}, bf16[2,128,512]{2,1,0:T(8,128)(2,1)S(1)}, u32[]{:S(2)}, u32[]{:S(2)}) collective-permute-start(bf16[2,128,512]{2,1,0:T(8,128)(2,1)S(1)} %pad_maximum_fusion.5), channel_id=1, source_target_pairs={{2,0},{4,2},{6,4},{8,6},{10,8},{12,10},{14,12},{16,14},{18,16},{20... | collective-permute-start | bytes 786440 | tf_op jit(solution)/shard_map/ppermute | solution.py:58
  20.2 96.3 %collective-permute-start.6 = (bf16[2,128,512]{2,1,0:T(8,128)(2,1)S(1)}, bf16[2,128,512]{2,1,0:T(8,128)(2,1)S(1)}, u32[]{:S(2)}, u32[]{:S(2)}) collective-permute-start(bf16[2,128,512]{2,1,0:T(8,128)(2,1)S(1)} %pad_maximum_fusion.4), channel_id=1, source_target_pairs={{0,2},{2,4},{4,6},{6,8},{8,10},{10,12},{12,14},{14,16},{16,18},{18... | collective-permute-start | bytes 786440 | tf_op jit(solution)/shard_map/ppermute | solution.py:58
  27.3 90.1 %collective-permute-start.5 = (bf16[2,128,512]{2,1,0:T(8,128)(2,1)S(1)}, bf16[2,128,512]{2,1,0:T(8,128)(2,1)S(1)}, u32[]{:S(2)}, u32[]{:S(2)}) collective-permute-start(bf16[2,128,512]{2,1,0:T(8,128)(2,1)S(1)} %add_add_fusion.1), channel_id=1, source_target_pairs={{0,6},{8,14},{16,22},{24,30},{1,7},{9,15},{17,23},{25,31}} | collective-permute-start | bytes 786440 | tf_op jit(solution)/shard_map/ppermute | solution.py:29
  28.6 88.8 %collective-permute-start.4 = (bf16[2,128,512]{2,1,0:T(8,128)(2,1)S(1)}, bf16[2,128,512]{2,1,0:T(8,128)(2,1)S(1)}, u32[]{:S(2)}, u32[]{:S(2)}) collective-permute-start(bf16[2,128,512]{2,1,0:T(8,128)(2,1)S(1)} %add_add_fusion.1), channel_id=1, source_target_pairs={{0,4},{8,12},{16,20},{24,28},{1,5},{9,13},{17,21},{25,29}} | collective-permute-start | bytes 786440 | tf_op jit(solution)/shard_map/ppermute | solution.py:29
  29.3 88.2 %collective-permute-start.3 = (bf16[2,128,512]{2,1,0:T(8,128)(2,1)S(1)}, bf16[2,128,512]{2,1,0:T(8,128)(2,1)S(1)}, u32[]{:S(2)}, u32[]{:S(2)}) collective-permute-start(bf16[2,128,512]{2,1,0:T(8,128)(2,1)S(1)} %add_add_fusion.1), channel_id=1, source_target_pairs={{0,2},{8,10},{16,18},{24,26},{1,3},{9,11},{17,19},{25,27}} | collective-permute-start | bytes 786440 | tf_op jit(solution)/shard_map/ppermute | solution.py:29
  134.5 13.0 %collective-permute-start.10 = (bf16[2,128,512]{2,1,0:T(8,128)(2,1)S(1)}, bf16[2,128,512]{2,1,0:T(8,128)(2,1)S(1)}, u32[]{:S(2)}, u32[]{:S(2)}) collective-permute-start(bf16[2,128,512]{2,1,0:T(8,128)(2,1)S(1)} %fusion.3), channel_id=1, source_target_pairs={{6,0},{14,8},{22,16},{30,24},{7,1},{15,9},{23,17},{31,25}} | collective-permute-start | bytes 786440 | tf_op jit(solution)/shard_map/ppermute | solution.py:45
  135.8 11.7 %collective-permute-start.9 = (bf16[2,128,512]{2,1,0:T(8,128)(2,1)S(1)}, bf16[2,128,512]{2,1,0:T(8,128)(2,1)S(1)}, u32[]{:S(2)}, u32[]{:S(2)}) collective-permute-start(bf16[2,128,512]{2,1,0:T(8,128)(2,1)S(1)} %fusion.3), channel_id=1, source_target_pairs={{4,0},{12,8},{20,16},{28,24},{5,1},{13,9},{21,17},{29,25}} | collective-permute-start | bytes 786440 | tf_op jit(solution)/shard_map/ppermute | solution.py:45
  136.5 11.0 %collective-permute-start.8 = (bf16[2,128,512]{2,1,0:T(8,128)(2,1)S(1)}, bf16[2,128,512]{2,1,0:T(8,128)(2,1)S(1)}, u32[]{:S(2)}, u32[]{:S(2)}) collective-permute-start(bf16[2,128,512]{2,1,0:T(8,128)(2,1)S(1)} %fusion.3), channel_id=1, source_target_pairs={{2,0},{10,8},{18,16},{26,24},{3,1},{11,9},{19,17},{27,25}} | collective-permute-start | bytes 786440 | tf_op jit(solution)/shard_map/ppermute | solution.py:45
  147.6 10.5 %collective-permute-start.13 = (bf16[2,128,512]{2,1,0:T(8,128)(2,1)S(1)}, bf16[2,128,512]{2,1,0:T(8,128)(2,1)S(1)}, u32[]{:S(2)}, u32[]{:S(2)}) collective-permute-start(bf16[2,128,512]{2,1,0:T(8,128)(2,1)S(1)} %fusion.19), channel_id=1, source_target_pairs={{24,0},{25,1}} | collective-permute-start | bytes 786440 | tf_op jit(solution)/shard_map/ppermute | solution.py:45
  148.3 9.8 %collective-permute-start.12 = (bf16[2,128,512]{2,1,0:T(8,128)(2,1)S(1)}, bf16[2,128,512]{2,1,0:T(8,128)(2,1)S(1)}, u32[]{:S(2)}, u32[]{:S(2)}) collective-permute-start(bf16[2,128,512]{2,1,0:T(8,128)(2,1)S(1)} %fusion.19), channel_id=1, source_target_pairs={{16,0},{17,1}} | collective-permute-start | bytes 786440 | tf_op jit(solution)/shard_map/ppermute | solution.py:45
  149.0 9.2 %collective-permute-start.11 = (bf16[2,128,512]{2,1,0:T(8,128)(2,1)S(1)}, bf16[2,128,512]{2,1,0:T(8,128)(2,1)S(1)}, u32[]{:S(2)}, u32[]{:S(2)}) collective-permute-start(bf16[2,128,512]{2,1,0:T(8,128)(2,1)S(1)} %fusion.19), channel_id=1, source_target_pairs={{8,0},{9,1}} | collective-permute-start | bytes 786440 | tf_op jit(solution)/shard_map/ppermute | solution.py:45
  150.8 33.4 %collective-permute-start.14 = (bf16[2,128,512]{2,1,0:T(8,128)(2,1)S(1)}, bf16[2,128,512]{2,1,0:T(8,128)(2,1)S(1)}, u32[]{:S(2)}, u32[]{:S(2)}) collective-permute-start(bf16[2,128,512]{2,1,0:T(8,128)(2,1)S(1)} %pad_maximum_fusion.6), channel_id=1, source_target_pairs={{0,2},{2,4},{4,6},{6,8},{8,10},{10,12},{12,14},{14,16},{16,18},{18... | collective-permute-start | bytes 786440 | tf_op jit(solution)/shard_map/ppermute | solution.py:58
  156.2 28.0 %collective-permute-start.15 = (bf16[2,128,512]{2,1,0:T(8,128)(2,1)S(1)}, bf16[2,128,512]{2,1,0:T(8,128)(2,1)S(1)}, u32[]{:S(2)}, u32[]{:S(2)}) collective-permute-start(bf16[2,128,512]{2,1,0:T(8,128)(2,1)S(1)} %pad_maximum_fusion.7), channel_id=1, source_target_pairs={{2,0},{4,2},{6,4},{8,6},{10,8},{12,10},{14,12},{16,14},{18,16},{20... | collective-permute-start | bytes 786440 | tf_op jit(solution)/shard_map/ppermute | solution.py:58
  184.1 26.0 %copy-start.9 = (f32[256,512]{1,0:T(8,128)S(1)}, f32[256,512]{1,0:T(8,128)}, u32[]{:S(2)}) copy-start(f32[256,512]{1,0:T(8,128)} %get-tuple-element.21) | copy-start | bytes 1572868
  184.9 53.6 %all-to-all-start.1 = ((bf16[16,128,512]{2,1,0:T(8,128)(2,1)}), bf16[16,128,512]{2,1,0:T(8,128)(2,1)S(1)}, u32[]{:S(2)}, u32[]{:S(2)}) async-start(bf16[16,128,512]{2,1,0:T(8,128)(2,1)} %get-tuple-element.27), calls=%async_computation.1 | async-start | bytes 4194304 | tf_op jit(solution)/shard_map/all_to_all | solution.py:321
  (7 other events, 14.6 us)

commit v12 on v11

--- a/solution.py
+++ b/solution.py
@@ -77,7 +77,7 @@
     return dq, dk, dv
 
 
-def list_kernel(qin, qout, first, ktab, mtab, q_ref, do_ref, nrm_ref, dlt_ref, k_ref, v_ref, dq_ref, dk_ref, dv_ref):
+def list_kernel(fold, qin, qout, first, ktab, mtab, q_ref, do_ref, nrm_ref, dlt_ref, k_ref, v_ref, dq_ref, dk_ref, dv_ref):
     p = pl.program_id(0)
     mode = mtab[p]
     lead = first[p]
@@ -98,8 +98,19 @@
         def _():
             dq_ref[:, cols] += dq
 
-        dk_ref[:, cols] = dk
-        dv_ref[:, cols] = dv
+        if fold:
+            @pl.when(p == 0)
+            def _():
+                dk_ref[:, cols] = dk
+                dv_ref[:, cols] = dv
+
+            @pl.when(p > 0)
+            def _():
+                dk_ref[:, cols] += dk
+                dv_ref[:, cols] += dv
+        else:
+            dk_ref[:, cols] = dk
+            dv_ref[:, cols] = dv
 
 
 def rand_kernel(heads, ktab, mtab, q_ref, do_ref, st_ref, k_ref, v_ref, dq_ref, dk_ref, dv_ref):
@@ -127,7 +138,7 @@
             dv_ref[0, :, cols] = dv
 
 
-def list_pairs(qin, qout, first, ktab, mtab, outs, queries, out_grad, norm3, delta3, key_src, value_src):
+def list_pairs(qin, qout, first, ktab, mtab, outs, queries, out_grad, norm3, delta3, key_src, value_src, fold=False):
     rows, features = queries.shape
     heads = norm3.shape[0]
     height = rows // (2 * PAIR)
@@ -147,17 +158,17 @@
         ],
         out_specs=[
             pl.BlockSpec(blk, lambda p, qi, qo, f, kt, mt: (qo[p], 0)),
-            pl.BlockSpec(blk, lambda p, qi, qo, f, kt, mt: (p, 0)),
-            pl.BlockSpec(blk, lambda p, qi, qo, f, kt, mt: (p, 0)),
+            pl.BlockSpec(blk, lambda p, qi, qo, f, kt, mt: (0 if fold else p, 0)),
+            pl.BlockSpec(blk, lambda p, qi, qo, f, kt, mt: (0 if fold else p, 0)),
         ],
     )
     return pl.pallas_call(
-        list_kernel,
+        functools.partial(list_kernel, fold),
         grid_spec=grid_spec,
         out_shape=[
             jax.ShapeDtypeStruct((outs * height, features), jnp.float32),
-            jax.ShapeDtypeStruct((count * height, features), jnp.float32),
-            jax.ShapeDtypeStruct((count * height, features), jnp.float32),
+            jax.ShapeDtypeStruct(((1 if fold else count) * height, features), jnp.float32),
+            jax.ShapeDtypeStruct(((1 if fold else count) * height, features), jnp.float32),
         ],
     )(qin, qout, first, ktab, mtab, queries, out_grad, norm3, delta3, key_src, value_src)
 
@@ -251,7 +262,7 @@
     glob_mode = (seq_blk >= WINDOW).astype(jnp.int32)
     dq_glob, dk_glob, dv_glob = list_pairs(
         table(0, 1, 2, 3), table(0, 1, 2, 3), table(1, 1, 1, 1), table(0, 0, 0, 0), glob_mode,
-        slot_count, queries, out_grad, norm3, delta3, global_kv[0], global_kv[1],
+        slot_count, queries, out_grad, norm3, delta3, global_kv[0], global_kv[1], fold=True,
     )
     zero_blk = jnp.zeros((height, features), jnp.float32)
     dq_local = (
@@ -266,12 +277,7 @@
     back_right = shift(to_left, "ctx", -1)
     back_left = shift(to_right, "ctx", 1)
 
-    part = jnp.stack(
-        [
-            jnp.sum(dk_glob.reshape(slot_count, height, features), axis=0),
-            jnp.sum(dv_glob.reshape(slot_count, height, features), axis=0),
-        ]
-    )
+    part = jnp.stack([dk_glob, dv_glob])
     total = gather_to_root(part, "ctx")
 
     ref_valid = rand_blocks >= 0

time: 244 us -> 242 us (level)
    reduce_sum x2 -> x0, other arithmetic: 2.66 us -> none  [the longest x1 1.33 us: shards(): jnp.sum(dk_glob.reshape(slot_count, height, features), axis=0)]
  transfers between devices with their start and end apart: 18 -> 18, of which waited for: 2 -> 2; matrix products, arithmetic and copies ran while one was open for 13% -> 13% of each run, Pallas kernels for 24% -> 25%
where the time goes in v12:
time: 242 us; the launch traced here: 240 us
  waiting for transfers between devices  102 us (42%)
  Pallas kernels  59.5 us (25%)
  starting transfers between devices  33.8 us (14%)
  other arithmetic  33.5 us (14%)
  local copies, waits for them, and re-layouts  10.4 us (4%)
    ppermute x4, waiting for transfers between devices, shift(): return lax.ppermute(array, axis, pairs)  86.3 us
    pallas_call x3, Pallas kernels, list_pairs(): pl.pallas_call(functools.partial(list_kernel, fold), grid_spec=grid_spec,...  35.8 us
    pallas_call x1, Pallas kernels, rand_pairs(): pl.pallas_call(functools.partial(rand_kernel, heads), grid_spec=grid_spec...  23.8 us
    all_to_all x1, waiting for transfers between devices, shards(): lax.all_to_all(dq_rand, 'ctx', split_axis=0, concat_axis=0, tiled=True)  15.4 us
    ppermute x4, starting transfers between devices, shift(): return lax.ppermute(array, axis, pairs)  13.7 us
    all_to_all x1, starting transfers between devices, shards(): lax.all_to_all(routed, 'ctx', split_axis=0, concat_axis=0, tiled=True)  6.69 us
    reduce_sum x1, other arithmetic, shards(): rand_value = jnp.sum(choose[:, :, None, None] * dv_rand[:, None], axis=0)  5.12 us
  transfers between devices with their start and end apart: 18, of which 2 were waited for; matrix products, arithmetic and copies ran while one was open for 13% of the time, Pallas kernels for 25%

profile of v12, /device:TPU:11, one launch (start us, length us, event | category | flops | bytes accessed | tf_op | source)
XLA Modules:
  0.0 240.3 jit_solution(18362880302409094113)
XLA Ops:
  2.4 1.3 convert_multiply_fusion
  5.9 3.0 %select_add_fusion = bf16[16,272,512]{2,1,0:T(8,128)(2,1)} fusion(pred[16]{0:T(512)(128)(4,1)S(1)} %get-tuple-element.73, pred[16]{0:T(512)(128)(4,1)S(1)} %get-tuple-element.74, pred[16]{0:T(512)(128)(4,1)S(1)} %get-tuple-element.75, pred[16]{0:T(512)(128)(4,1)S(1)} %get-tuple-element.72, bf16[272,512]{1,0:T(8,128)(2,1)S(1)} %get-tuple-element.47, ...), kind=kLoop, calls=%fused_computation.3 | loop fusion | flops 17825792 | bytes 5579328 | tf_op jit(solution)/shard_map/add | solution.py:316
  9.0 6.7 %all-to-all-start = ((bf16[16,272,512]{2,1,0:T(8,128)(2,1)}), bf16[16,272,512]{2,1,0:T(8,128)(2,1)}, u32[]{:S(2)}, u32[]{:S(2)}) async-start(bf16[16,272,512]{2,1,0:T(8,128)(2,1)} %select_add_fusion), calls=%async_computation | async-start | bytes 8912896 | tf_op jit(solution)/shard_map/all_to_all | solution.py:317
  17.9 2.3 collective-permute-start.7
  20.2 4.2 %collective-permute-start.6 = (bf16[2,128,512]{2,1,0:T(8,128)(2,1)S(1)}, bf16[2,128,512]{2,1,0:T(8,128)(2,1)S(1)}, u32[]{:S(2)}, u32[]{:S(2)}) collective-permute-start(bf16[2,128,512]{2,1,0:T(8,128)(2,1)S(1)} %pad_maximum_fusion.4), channel_id=1, source_target_pairs={{0,2},{2,4},{4,6},{6,8},{8,10},{10,12},{12,14},{14,16},{16,18},{18... | collective-permute-start | bytes 786440 | tf_op jit(solution)/shard_map/ppermute | solution.py:58
  27.5 1.3 collective-permute-start.5
  30.1 86.3 %collective-permute-done.7 = bf16[2,128,512]{2,1,0:T(8,128)(2,1)S(1)} collective-permute-done((bf16[2,128,512]{2,1,0:T(8,128)(2,1)S(1)}, bf16[2,128,512]{2,1,0:T(8,128)(2,1)S(1)}, u32[]{:S(2)}, u32[]{:S(2)}) %collective-permute-start.7) | collective-permute-done | bytes 262176 | tf_op jit(solution)/shard_map/ppermute | solution.py:58
  119.9 11.9 %shard_map.95 = (f32[512,512]{1,0:T(8,128)}, f32[128,512]{1,0:T(8,128)}, f32[128,512]{1,0:T(8,128)}) custom-call(s32[4]{0:T(128)} %iota.37.qin.qout, s32[4]{0:T(128)} %iota.37.qin.qout, s32[4]{0:T(128)} %broadcast_25_first.2.first, s32[4]{0:T(128)} %broadcast_24_ktab.2.ktab, s32[4]{0:T(128)} %compare_convert_fusion.2.mtab, bf16[512,512]{1,0:T(8,128)(2,1)} %q_ref.5, ...), custom_call_target="tpu_custom_call" | custom-call | tf_op jit(solution)/shard_map/pallas_call | solution.py:165
  133.0 1.3 collective-permute-start.10
  137.8 7.2 %shard_map.96 = (f32[256,512]{1,0:T(8,128)}, f32[256,512]{1,0:T(8,128)}, f32[256,512]{1,0:T(8,128)}) custom-call(s32[2]{0:T(128)} %iota_multiply_fusion.qin, s32[2]{0:T(128)} %iota.42.qout, s32[2]{0:T(128)} %broadcast_26_first.2.first, s32[2]{0:T(128)} %get-tuple-element.79.ktab, s32[2]{0:T(128)} %get-tuple-element.80.mtab, bf16[512,512]{1,0:T(8,128)(2,1)} %q_ref.5, ...), custom_call_target="tpu_custom_call" | custom-call | tf_op jit(solution)/shard_map/pallas_call | solution.py:165
  150.1 5.4 %collective-permute-start.14 = (bf16[2,128,512]{2,1,0:T(8,128)(2,1)}, bf16[2,128,512]{2,1,0:T(8,128)(2,1)S(1)}, u32[]{:S(2)}, u32[]{:S(2)}) collective-permute-start(bf16[2,128,512]{2,1,0:T(8,128)(2,1)} %pad_maximum_fusion.6), channel_id=1, source_target_pairs={{0,2},{2,4},{4,6},{6,8},{8,10},{10,12},{12,14},{14,16},{16,18},{18... | collective-permute-start | bytes 786440 | tf_op jit(solution)/shard_map/ppermute | solution.py:58
  156.2 1.9 collective-permute-start.15
  160.7 23.8 %shard_map.97 = (bf16[16,128,512]{2,1,0:T(8,128)(2,1)}, f32[16,128,512]{2,1,0:T(8,128)}, f32[16,128,512]{2,1,0:T(8,128)}) custom-call(s32[16]{0:T(128)} %add_maximum_fusion.ktab, s32[16]{0:T(128)} %compare_convert_fusion.1.mtab, bf16[16,272,512]{2,1,0:T(8,128)(2,1)} %all-to-all-done.q_ref.do_ref.st_ref, ...), custom_call_target="tpu_custom_call" | custom-call | tf_op jit(solution)/shard_map/pallas_call | solution.py:197
  185.1 4.0 %all-to-all-start.1 = ((bf16[16,128,512]{2,1,0:T(8,128)(2,1)}), bf16[16,128,512]{2,1,0:T(8,128)(2,1)S(1)}, u32[]{:S(2)}, u32[]{:S(2)}) async-start(bf16[16,128,512]{2,1,0:T(8,128)(2,1)} %get-tuple-element.27), calls=%async_computation.1 | async-start | bytes 4194304 | tf_op jit(solution)/shard_map/all_to_all | solution.py:327
  189.3 16.6 %shard_map.94 = (f32[512,512]{1,0:T(8,128)}, f32[768,512]{1,0:T(8,128)}, f32[768,512]{1,0:T(8,128)}) custom-call(s32[6]{0:T(128)} %constant.33.clone.1.qin.qout, s32[6]{0:T(128)} %constant.33.clone.1.qin.qout, s32[6]{0:T(128)} %constant.34.clone.1.first, s32[6]{0:T(128)} %constant.35.clone.1.ktab, s32[6]{0:T(128)} %constant.36.clone.1.mtab, ...), custom_call_target="tpu_custom_call" | custom-call | tf_op jit(solution)/shard_map/pallas_call | solution.py:165
  205.9 2.2 add_bitcast_fusion
  208.2 1.2 pad_maximum_fusion
  209.6 2.5 %bitcast_add_fusion.3 = (f32[1,128,512]{2,1,0:T(8,128)}, f32[1,128,512]{2,1,0:T(8,128)}, f32[1,128,512]{2,1,0:T(8,128)}, f32[1,128,512]{2,1,0:T(8,128)S(1)}, f32...) fusion(f32[2,128,512]{2,1,0:T(8,128)S(1)} %convert_add_fusion, f32[768,512]{1,0:T(8,128)S(1)} %copy-done.8, ...), kind=kLoop, calls=%fused_computation.35 | loop fusion | flops 917504 | bytes 5767176 | tf_op jit(solution)/shard_map/add | solution.py:342
  212.1 5.1 %multiply_reduce_fusion = (f32[4,128,512]{2,1,0:T(8,128)S(1)}, f32[4,128,512]{2,1,0:T(8,128)S(1)}) fusion(f32[16,128,512]{2,1,0:T(8,128)} %get-tuple-element.34, f32[16,4]{1,0:T(8,128)S(1)} %compare_convert_fusion, f32[16,128,512]{2,1,0:T(8,128)S(1)} %copy-done.4), kind=kLoop, calls=%fused_computation | loop fusion | flops 16252928 | bytes 10486016 | tf_op jit(solution)/shard_map/reduce_sum | solution.py:334
  217.2 2.0 fusion
  219.2 1.9 fusion.1
  221.1 15.4 %all-to-all-done.1 = bf16[16,128,512]{2,1,0:T(8,128)(2,1)S(1)} async-done(((bf16[16,128,512]{2,1,0:T(8,128)(2,1)}), bf16[16,128,512]{2,1,0:T(8,128)(2,1)S(1)}, u32[]{:S(2)}, u32[]{:S(2)}) %all-to-all-start.1) | async-done | bytes 2097184 | tf_op jit(solution)/shard_map/all_to_all | solution.py:327
  237.1 1.4 multiply_reduce_fusion.2
  239.0 1.3 fusion.2
  (122 shorter events, 28.8 us)
Async XLA Ops:
  9.0 6.7 %copy-start.2 = (bf16[512,512]{1,0:T(8,128)(2,1)S(1)}, bf16[512,512]{1,0:T(8,128)(2,1)}, u32[]{:S(2)}) copy-start(bf16[512,512]{1,0:T(8,128)(2,1)} %k_ref.3) | copy-start | bytes 1572868
  9.0 6.7 %copy-start.3 = (bf16[512,512]{1,0:T(8,128)(2,1)S(1)}, bf16[512,512]{1,0:T(8,128)(2,1)}, u32[]{:S(2)}) copy-start(bf16[512,512]{1,0:T(8,128)(2,1)} %v_ref.3) | copy-start | bytes 1572868
  9.0 17.2 %copy-start.17 = (bf16[4,512]{1,0:T(4,128)(2,1)S(1)}, bf16[4,512]{1,0:T(4,128)(2,1)}, u32[]{:S(2)}) copy-start(bf16[4,512]{1,0:T(4,128)(2,1)} %param.12) | copy-start | bytes 12292
  9.0 149.5 %all-to-all-start = ((bf16[16,272,512]{2,1,0:T(8,128)(2,1)}), bf16[16,272,512]{2,1,0:T(8,128)(2,1)}, u32[]{:S(2)}, u32[]{:S(2)}) async-start(bf16[16,272,512]{2,1,0:T(8,128)(2,1)} %select_add_fusion), calls=%async_computation | async-start | bytes 8912896 | tf_op jit(solution)/shard_map/all_to_all | solution.py:317
  15.8 11.6 %collective-permute-start.2 = (bf16[2,128,512]{2,1,0:T(8,128)(2,1)S(1)}, bf16[2,128,512]{2,1,0:T(8,128)(2,1)S(1)}, u32[]{:S(2)}, u32[]{:S(2)}) collective-permute-start(bf16[2,128,512]{2,1,0:T(8,128)(2,1)S(1)} %maximum_select_fusion), channel_id=1, source_target_pairs={{0,24},{1,25}} | collective-permute-start | bytes 786440 | tf_op jit(solution)/shard_map/ppermute | solution.py:29
  16.5 10.9 %collective-permute-start.1 = (bf16[2,128,512]{2,1,0:T(8,128)(2,1)S(1)}, bf16[2,128,512]{2,1,0:T(8,128)(2,1)S(1)}, u32[]{:S(2)}, u32[]{:S(2)}) collective-permute-start(bf16[2,128,512]{2,1,0:T(8,128)(2,1)S(1)} %maximum_select_fusion), channel_id=1, source_target_pairs={{0,16},{1,17}} | collective-permute-start | bytes 786440 | tf_op jit(solution)/shard_map/ppermute | solution.py:29
  17.2 10.2 %collective-permute-start = (bf16[2,128,512]{2,1,0:T(8,128)(2,1)S(1)}, bf16[2,128,512]{2,1,0:T(8,128)(2,1)S(1)}, u32[]{:S(2)}, u32[]{:S(2)}) collective-permute-start(bf16[2,128,512]{2,1,0:T(8,128)(2,1)S(1)} %maximum_select_fusion), channel_id=1, source_target_pairs={{0,8},{1,9}} | collective-permute-start | bytes 786440 | tf_op jit(solution)/shard_map/ppermute | solution.py:29
  17.9 98.6 %collective-permute-start.7 = (bf16[2,128,512]{2,1,0:T(8,128)(2,1)S(1)}, bf16[2,128,512]{2,1,0:T(8,128)(2,1)S(1)}, u32[]{:S(2)}, u32[]{:S(2)}) collective-permute-start(bf16[2,128,512]{2,1,0:T(8,128)(2,1)S(1)} %pad_maximum_fusion.5), channel_id=1, source_target_pairs={{2,0},{4,2},{6,4},{8,6},{10,8},{12,10},{14,12},{16,14},{18,16},{20... | collective-permute-start | bytes 786440 | tf_op jit(solution)/shard_map/ppermute | solution.py:58
  20.2 96.3 %collective-permute-start.6 = (bf16[2,128,512]{2,1,0:T(8,128)(2,1)S(1)}, bf16[2,128,512]{2,1,0:T(8,128)(2,1)S(1)}, u32[]{:S(2)}, u32[]{:S(2)}) collective-permute-start(bf16[2,128,512]{2,1,0:T(8,128)(2,1)S(1)} %pad_maximum_fusion.4), channel_id=1, source_target_pairs={{0,2},{2,4},{4,6},{6,8},{8,10},{10,12},{12,14},{14,16},{16,18},{18... | collective-permute-start | bytes 786440 | tf_op jit(solution)/shard_map/ppermute | solution.py:58
  27.5 90.0 %collective-permute-start.5 = (bf16[2,128,512]{2,1,0:T(8,128)(2,1)S(1)}, bf16[2,128,512]{2,1,0:T(8,128)(2,1)S(1)}, u32[]{:S(2)}, u32[]{:S(2)}) collective-permute-start(bf16[2,128,512]{2,1,0:T(8,128)(2,1)S(1)} %add_add_fusion.1), channel_id=1, source_target_pairs={{0,6},{8,14},{16,22},{24,30},{1,7},{9,15},{17,23},{25,31}} | collective-permute-start | bytes 786440 | tf_op jit(solution)/shard_map/ppermute | solution.py:29
  28.8 88.7 %collective-permute-start.4 = (bf16[2,128,512]{2,1,0:T(8,128)(2,1)S(1)}, bf16[2,128,512]{2,1,0:T(8,128)(2,1)S(1)}, u32[]{:S(2)}, u32[]{:S(2)}) collective-permute-start(bf16[2,128,512]{2,1,0:T(8,128)(2,1)S(1)} %add_add_fusion.1), channel_id=1, source_target_pairs={{0,4},{8,12},{16,20},{24,28},{1,5},{9,13},{17,21},{25,29}} | collective-permute-start | bytes 786440 | tf_op jit(solution)/shard_map/ppermute | solution.py:29
  29.5 88.0 %collective-permute-start.3 = (bf16[2,128,512]{2,1,0:T(8,128)(2,1)S(1)}, bf16[2,128,512]{2,1,0:T(8,128)(2,1)S(1)}, u32[]{:S(2)}, u32[]{:S(2)}) collective-permute-start(bf16[2,128,512]{2,1,0:T(8,128)(2,1)S(1)} %add_add_fusion.1), channel_id=1, source_target_pairs={{0,2},{8,10},{16,18},{24,26},{1,3},{9,11},{17,19},{25,27}} | collective-permute-start | bytes 786440 | tf_op jit(solution)/shard_map/ppermute | solution.py:29
  131.8 14.3 %copy-start.6 = (f32[128,512]{1,0:T(8,128)S(1)}, f32[128,512]{1,0:T(8,128)}, u32[]{:S(2)}) copy-start(f32[128,512]{1,0:T(8,128)} %get-tuple-element.23) | copy-start | bytes 786436
  131.8 14.3 %copy-start.7 = (f32[128,512]{1,0:T(8,128)S(1)}, f32[128,512]{1,0:T(8,128)}, u32[]{:S(2)}) copy-start(f32[128,512]{1,0:T(8,128)} %get-tuple-element.24) | copy-start | bytes 786436
  133.0 13.1 %collective-permute-start.10 = (bf16[2,128,512]{2,1,0:T(8,128)(2,1)S(1)}, bf16[2,128,512]{2,1,0:T(8,128)(2,1)S(1)}, u32[]{:S(2)}, u32[]{:S(2)}) collective-permute-start(bf16[2,128,512]{2,1,0:T(8,128)(2,1)S(1)} %fusion.3), channel_id=1, source_target_pairs={{6,0},{14,8},{22,16},{30,24},{7,1},{15,9},{23,17},{31,25}} | collective-permute-start | bytes 786440 | tf_op jit(solution)/shard_map/ppermute | solution.py:45
  134.3 11.8 %collective-permute-start.9 = (bf16[2,128,512]{2,1,0:T(8,128)(2,1)S(1)}, bf16[2,128,512]{2,1,0:T(8,128)(2,1)S(1)}, u32[]{:S(2)}, u32[]{:S(2)}) collective-permute-start(bf16[2,128,512]{2,1,0:T(8,128)(2,1)S(1)} %fusion.3), channel_id=1, source_target_pairs={{4,0},{12,8},{20,16},{28,24},{5,1},{13,9},{21,17},{29,25}} | collective-permute-start | bytes 786440 | tf_op jit(solution)/shard_map/ppermute | solution.py:45
  135.0 11.1 %collective-permute-start.8 = (bf16[2,128,512]{2,1,0:T(8,128)(2,1)S(1)}, bf16[2,128,512]{2,1,0:T(8,128)(2,1)S(1)}, u32[]{:S(2)}, u32[]{:S(2)}) collective-permute-start(bf16[2,128,512]{2,1,0:T(8,128)(2,1)S(1)} %fusion.3), channel_id=1, source_target_pairs={{2,0},{10,8},{18,16},{26,24},{3,1},{11,9},{19,17},{27,25}} | collective-permute-start | bytes 786440 | tf_op jit(solution)/shard_map/ppermute | solution.py:45
  146.3 11.9 %collective-permute-start.13 = (bf16[2,128,512]{2,1,0:T(8,128)(2,1)S(1)}, bf16[2,128,512]{2,1,0:T(8,128)(2,1)S(1)}, u32[]{:S(2)}, u32[]{:S(2)}) collective-permute-start(bf16[2,128,512]{2,1,0:T(8,128)(2,1)S(1)} %fusion.19), channel_id=1, source_target_pairs={{24,0},{25,1}} | collective-permute-start | bytes 786440 | tf_op jit(solution)/shard_map/ppermute | solution.py:45
  147.0 11.2 %collective-permute-start.12 = (bf16[2,128,512]{2,1,0:T(8,128)(2,1)S(1)}, bf16[2,128,512]{2,1,0:T(8,128)(2,1)S(1)}, u32[]{:S(2)}, u32[]{:S(2)}) collective-permute-start(bf16[2,128,512]{2,1,0:T(8,128)(2,1)S(1)} %fusion.19), channel_id=1, source_target_pairs={{16,0},{17,1}} | collective-permute-start | bytes 786440 | tf_op jit(solution)/shard_map/ppermute | solution.py:45
  147.6 10.5 %collective-permute-start.11 = (bf16[2,128,512]{2,1,0:T(8,128)(2,1)S(1)}, bf16[2,128,512]{2,1,0:T(8,128)(2,1)S(1)}, u32[]{:S(2)}, u32[]{:S(2)}) collective-permute-start(bf16[2,128,512]{2,1,0:T(8,128)(2,1)S(1)} %fusion.19), channel_id=1, source_target_pairs={{8,0},{9,1}} | collective-permute-start | bytes 786440 | tf_op jit(solution)/shard_map/ppermute | solution.py:45
  150.1 34.3 %collective-permute-start.14 = (bf16[2,128,512]{2,1,0:T(8,128)(2,1)}, bf16[2,128,512]{2,1,0:T(8,128)(2,1)S(1)}, u32[]{:S(2)}, u32[]{:S(2)}) collective-permute-start(bf16[2,128,512]{2,1,0:T(8,128)(2,1)} %pad_maximum_fusion.6), channel_id=1, source_target_pairs={{0,2},{2,4},{4,6},{6,8},{8,10},{10,12},{12,14},{14,16},{16,18},{18... | collective-permute-start | bytes 786440 | tf_op jit(solution)/shard_map/ppermute | solution.py:58
  156.2 28.2 %collective-permute-start.15 = (bf16[2,128,512]{2,1,0:T(8,128)(2,1)}, bf16[2,128,512]{2,1,0:T(8,128)(2,1)S(1)}, u32[]{:S(2)}, u32[]{:S(2)}) collective-permute-start(bf16[2,128,512]{2,1,0:T(8,128)(2,1)} %pad_maximum_fusion.7), channel_id=1, source_target_pairs={{2,0},{4,2},{6,4},{8,6},{10,8},{12,10},{14,12},{16,14},{18,16},{20... | collective-permute-start | bytes 786440 | tf_op jit(solution)/shard_map/ppermute | solution.py:58
  184.4 23.7 %copy-start.14 = (f32[256,512]{1,0:T(8,128)S(1)}, f32[256,512]{1,0:T(8,128)}, u32[]{:S(2)}) copy-start(f32[256,512]{1,0:T(8,128)} %get-tuple-element.21) | copy-start | bytes 1572868
  185.1 51.4 %all-to-all-start.1 = ((bf16[16,128,512]{2,1,0:T(8,128)(2,1)}), bf16[16,128,512]{2,1,0:T(8,128)(2,1)S(1)}, u32[]{:S(2)}, u32[]{:S(2)}) async-start(bf16[16,128,512]{2,1,0:T(8,128)(2,1)} %get-tuple-element.27), calls=%async_computation.1 | async-start | bytes 4194304 | tf_op jit(solution)/shard_map/all_to_all | solution.py:327
  (12 other events, 39.3 us)

commit v13 on v11

--- a/solution.py
+++ b/solution.py
@@ -72,8 +72,8 @@
     dp_t = lax.dot_general(v, do, nt, preferred_element_type=jnp.float32)
     ds_t = (p_t * (dp_t - dlt)).astype(jnp.bfloat16)
     dk = jnp.dot(ds_t, q, preferred_element_type=jnp.float32) * scale
-    ds = jnp.transpose(ds_t.astype(jnp.float32)).astype(jnp.bfloat16)
-    dq = jnp.dot(ds, k, preferred_element_type=jnp.float32) * scale
+    tn = (((0,), (0,)), ((), ()))
+    dq = lax.dot_general(ds_t, k, tn, preferred_element_type=jnp.float32) * scale
     return dq, dk, dv
 
 

time: 244 us -> 241 us (0.988)
  Pallas kernels: 58.4 us -> 55.6 us
  transfers between devices with their start and end apart: 18 -> 18, of which waited for: 2 -> 2; matrix products, arithmetic and copies ran while one was open for 13% -> 13% of each run, Pallas kernels for 24% -> 23%
where the time goes in v13:
time: 241 us; the launch traced here: 240 us
  waiting for transfers between devices  103 us (43%)
  Pallas kernels  55.6 us (23%)
  starting transfers between devices  36.5 us (15%)
  other arithmetic  33.9 us (14%)
  local copies, waits for them, and re-layouts  10 us (4%)
    ppermute x4, waiting for transfers between devices, shift(): return lax.ppermute(array, axis, pairs)  86.5 us
    pallas_call x3, Pallas kernels, list_pairs(): pl.pallas_call(list_kernel, grid_spec=grid_spec, out_shape=[jax.ShapeDtyp...  34 us
    pallas_call x1, Pallas kernels, rand_pairs(): pl.pallas_call(functools.partial(rand_kernel, heads), grid_spec=grid_spec...  21.5 us
    all_to_all x1, waiting for transfers between devices, shards(): lax.all_to_all(dq_rand, 'ctx', split_axis=0, concat_axis=0, tiled=True)  16.8 us
    ppermute x4, starting transfers between devices, shift(): return lax.ppermute(array, axis, pairs)  13.8 us
    all_to_all x1, starting transfers between devices, shards(): lax.all_to_all(routed, 'ctx', split_axis=0, concat_axis=0, tiled=True)  6.69 us
    all_to_all x1, starting transfers between devices, shards(): lax.all_to_all(dq_rand, 'ctx', split_axis=0, concat_axis=0, tiled=True)  6.64 us
    reduce_sum x1, other arithmetic, shards(): rand_value = jnp.sum(choose[:, :, None, None] * dv_rand[:, None], axis=0)  5.09 us
  transfers between devices with their start and end apart: 18, of which 2 were waited for; matrix products, arithmetic and copies ran while one was open for 13% of the time, Pallas kernels for 23%

profile of v13, /device:TPU:11, one launch (start us, length us, event | category | flops | bytes accessed | tf_op | source)
XLA Modules:
  0.0 240.4 jit_solution(3766161207017561240)
XLA Ops:
  2.4 1.3 convert_multiply_fusion
  5.9 3.0 %select_add_fusion = bf16[16,272,512]{2,1,0:T(8,128)(2,1)} fusion(pred[16]{0:T(512)(128)(4,1)S(1)} %get-tuple-element.73, pred[16]{0:T(512)(128)(4,1)S(1)} %get-tuple-element.74, pred[16]{0:T(512)(128)(4,1)S(1)} %get-tuple-element.75, pred[16]{0:T(512)(128)(4,1)S(1)} %get-tuple-element.72, bf16[272,512]{1,0:T(8,128)(2,1)S(1)} %get-tuple-element.47, ...), kind=kLoop, calls=%fused_computation.3 | loop fusion | flops 17825792 | bytes 5579328 | tf_op jit(solution)/shard_map/add | solution.py:310
  9.0 6.7 %all-to-all-start = ((bf16[16,272,512]{2,1,0:T(8,128)(2,1)}), bf16[16,272,512]{2,1,0:T(8,128)(2,1)}, u32[]{:S(2)}, u32[]{:S(2)}) async-start(bf16[16,272,512]{2,1,0:T(8,128)(2,1)} %select_add_fusion), calls=%async_computation | async-start | bytes 8912896 | tf_op jit(solution)/shard_map/all_to_all | solution.py:311
  17.9 2.3 collective-permute-start.7
  20.2 4.2 %collective-permute-start.6 = (bf16[2,128,512]{2,1,0:T(8,128)(2,1)S(1)}, bf16[2,128,512]{2,1,0:T(8,128)(2,1)S(1)}, u32[]{:S(2)}, u32[]{:S(2)}) collective-permute-start(bf16[2,128,512]{2,1,0:T(8,128)(2,1)S(1)} %pad_maximum_fusion.4), channel_id=1, source_target_pairs={{0,2},{2,4},{4,6},{6,8},{8,10},{10,12},{12,14},{14,16},{16,18},{18... | collective-permute-start | bytes 786440 | tf_op jit(solution)/shard_map/ppermute | solution.py:58
  30.0 86.5 %collective-permute-done.7 = bf16[2,128,512]{2,1,0:T(8,128)(2,1)S(1)} collective-permute-done((bf16[2,128,512]{2,1,0:T(8,128)(2,1)S(1)}, bf16[2,128,512]{2,1,0:T(8,128)(2,1)S(1)}, u32[]{:S(2)}, u32[]{:S(2)}) %collective-permute-start.7) | collective-permute-done | bytes 262176 | tf_op jit(solution)/shard_map/ppermute | solution.py:58
  119.9 11.3 %shard_map.95 = (f32[512,512]{1,0:T(8,128)}, f32[512,512]{1,0:T(8,128)}, f32[512,512]{1,0:T(8,128)}) custom-call(s32[4]{0:T(128)} %iota.37.qin.qout, s32[4]{0:T(128)} %iota.37.qin.qout, s32[4]{0:T(128)} %broadcast_25_first.2.first, s32[4]{0:T(128)} %broadcast_24_ktab.2.ktab, s32[4]{0:T(128)} %compare_convert_fusion.2.mtab, bf16[512,512]{1,0:T(8,128)(2,1)} %q_ref.5, ...), custom_call_target="tpu_custom_call" | custom-call | tf_op jit(solution)/shard_map/pallas_call | solution.py:154
  131.2 1.3 reduce_sum.66
  132.6 1.3 reduce_sum.65
  133.9 1.3 collective-permute-start.10
  138.6 7.0 %shard_map.96 = (f32[256,512]{1,0:T(8,128)}, f32[256,512]{1,0:T(8,128)}, f32[256,512]{1,0:T(8,128)}) custom-call(s32[2]{0:T(128)} %iota_multiply_fusion.qin, s32[2]{0:T(128)} %iota.42.qout, s32[2]{0:T(128)} %broadcast_26_first.2.first, s32[2]{0:T(128)} %get-tuple-element.79.ktab, s32[2]{0:T(128)} %get-tuple-element.80.mtab, bf16[512,512]{1,0:T(8,128)(2,1)} %q_ref.5, ...), custom_call_target="tpu_custom_call" | custom-call | tf_op jit(solution)/shard_map/pallas_call | solution.py:154
  150.0 5.4 %collective-permute-start.14 = (bf16[2,128,512]{2,1,0:T(8,128)(2,1)S(1)}, bf16[2,128,512]{2,1,0:T(8,128)(2,1)S(1)}, u32[]{:S(2)}, u32[]{:S(2)}) collective-permute-start(bf16[2,128,512]{2,1,0:T(8,128)(2,1)S(1)} %pad_maximum_fusion.6), channel_id=1, source_target_pairs={{0,2},{2,4},{4,6},{6,8},{8,10},{10,12},{12,14},{14,16},{16,18},{18... | collective-permute-start | bytes 786440 | tf_op jit(solution)/shard_map/ppermute | solution.py:58
  155.4 1.9 collective-permute-start.15
  160.7 21.5 %shard_map.97 = (bf16[16,128,512]{2,1,0:T(8,128)(2,1)}, f32[16,128,512]{2,1,0:T(8,128)}, f32[16,128,512]{2,1,0:T(8,128)}) custom-call(s32[16]{0:T(128)} %add_maximum_fusion.ktab, s32[16]{0:T(128)} %compare_convert_fusion.1.mtab, bf16[16,272,512]{2,1,0:T(8,128)(2,1)} %all-to-all-done.q_ref.do_ref.st_ref, ...), custom_call_target="tpu_custom_call" | custom-call | tf_op jit(solution)/shard_map/pallas_call | solution.py:186
  182.9 6.6 %all-to-all-start.1 = ((bf16[16,128,512]{2,1,0:T(8,128)(2,1)}), bf16[16,128,512]{2,1,0:T(8,128)(2,1)S(1)}, u32[]{:S(2)}, u32[]{:S(2)}) async-start(bf16[16,128,512]{2,1,0:T(8,128)(2,1)} %get-tuple-element.27), calls=%async_computation.1 | async-start | bytes 4194304 | tf_op jit(solution)/shard_map/all_to_all | solution.py:321
  189.7 15.8 %shard_map.94 = (f32[512,512]{1,0:T(8,128)}, f32[768,512]{1,0:T(8,128)}, f32[768,512]{1,0:T(8,128)}) custom-call(s32[6]{0:T(128)} %constant.33.clone.1.qin.qout, s32[6]{0:T(128)} %constant.33.clone.1.qin.qout, s32[6]{0:T(128)} %constant.34.clone.1.first, s32[6]{0:T(128)} %constant.35.clone.1.ktab, s32[6]{0:T(128)} %constant.36.clone.1.mtab, ...), custom_call_target="tpu_custom_call" | custom-call | tf_op jit(solution)/shard_map/pallas_call | solution.py:154
  205.5 2.2 add_bitcast_fusion
  208.2 2.7 %bitcast_add_fusion.3 = (f32[1,128,512]{2,1,0:T(8,128)}, f32[1,128,512]{2,1,0:T(8,128)}, f32[1,128,512]{2,1,0:T(8,128)}, f32[1,128,512]{2,1,0:T(8,128)S(1)}, f32[1,128,512]{2,1,0:T(8,128)}, /*index=5*/f32[1,128,512]{2,1,0:T(8,128)}) fusion(f32[2,128,512]{2,1,0:T(8,128)} %convert_add_fusion, f32[768,512]{1,0:T(8,128)S(1)} %copy-done.5, f32[]{:T(128)S(6)} %select_n.103, ...), kind=kLoop, calls=%fused_computation.35 | loop fusion | flops 917504 | bytes 5767176 | tf_op jit(solution)/shard_map/add | solution.py:336
  210.9 5.1 %multiply_reduce_fusion = (f32[4,128,512]{2,1,0:T(8,128)S(1)}, f32[4,128,512]{2,1,0:T(8,128)S(1)}) fusion(f32[16,128,512]{2,1,0:T(8,128)} %get-tuple-element.34, f32[16,4]{1,0:T(8,128)S(1)} %compare_convert_fusion, f32[16,128,512]{2,1,0:T(8,128)S(1)} %copy-done.4), kind=kLoop, calls=%fused_computation | loop fusion | flops 16252928 | bytes 10486016 | tf_op jit(solution)/shard_map/reduce_sum | solution.py:328
  216.0 2.2 fusion
  218.1 2.1 fusion.1
  220.2 16.8 %all-to-all-done.1 = bf16[16,128,512]{2,1,0:T(8,128)(2,1)S(1)} async-done(((bf16[16,128,512]{2,1,0:T(8,128)(2,1)}), bf16[16,128,512]{2,1,0:T(8,128)(2,1)S(1)}, u32[]{:S(2)}, u32[]{:S(2)}) %all-to-all-start.1) | async-done | bytes 2097184 | tf_op jit(solution)/shard_map/all_to_all | solution.py:321
  237.6 1.4 multiply_reduce_fusion.2
  239.1 1.3 fusion.2
  (114 shorter events, 28.1 us)
Async XLA Ops:
  0.6 4.4 %copy-start = (bf16[512,512]{1,0:T(8,128)(2,1)S(1)}, bf16[512,512]{1,0:T(8,128)(2,1)}, u32[]{:S(2)}) copy-start(bf16[512,512]{1,0:T(8,128)(2,1)} %do_ref.5) | copy-start | bytes 1572868
  0.6 4.4 %copy-start.1 = (bf16[512,512]{1,0:T(8,128)(2,1)S(1)}, bf16[512,512]{1,0:T(8,128)(2,1)}, u32[]{:S(2)}) copy-start(bf16[512,512]{1,0:T(8,128)(2,1)} %q_ref.5) | copy-start | bytes 1572868
  9.0 6.7 %copy-start.2 = (bf16[512,512]{1,0:T(8,128)(2,1)S(1)}, bf16[512,512]{1,0:T(8,128)(2,1)}, u32[]{:S(2)}) copy-start(bf16[512,512]{1,0:T(8,128)(2,1)} %k_ref.3) | copy-start | bytes 1572868
  9.0 6.7 %copy-start.3 = (bf16[512,512]{1,0:T(8,128)(2,1)S(1)}, bf16[512,512]{1,0:T(8,128)(2,1)}, u32[]{:S(2)}) copy-start(bf16[512,512]{1,0:T(8,128)(2,1)} %v_ref.3) | copy-start | bytes 1572868
  9.0 17.0 %copy-start.12 = (bf16[4,512]{1,0:T(4,128)(2,1)S(1)}, bf16[4,512]{1,0:T(4,128)(2,1)}, u32[]{:S(2)}) copy-start(bf16[4,512]{1,0:T(4,128)(2,1)} %param.12) | copy-start | bytes 12292
  9.0 149.4 %all-to-all-start = ((bf16[16,272,512]{2,1,0:T(8,128)(2,1)}), bf16[16,272,512]{2,1,0:T(8,128)(2,1)}, u32[]{:S(2)}, u32[]{:S(2)}) async-start(bf16[16,272,512]{2,1,0:T(8,128)(2,1)} %select_add_fusion), calls=%async_computation | async-start | bytes 8912896 | tf_op jit(solution)/shard_map/all_to_all | solution.py:311
  15.8 11.4 %collective-permute-start.2 = (bf16[2,128,512]{2,1,0:T(8,128)(2,1)S(1)}, bf16[2,128,512]{2,1,0:T(8,128)(2,1)S(1)}, u32[]{:S(2)}, u32[]{:S(2)}) collective-permute-start(bf16[2,128,512]{2,1,0:T(8,128)(2,1)S(1)} %maximum_select_fusion), channel_id=1, source_target_pairs={{0,24},{1,25}} | collective-permute-start | bytes 786440 | tf_op jit(solution)/shard_map/ppermute | solution.py:29
  16.5 10.8 %collective-permute-start.1 = (bf16[2,128,512]{2,1,0:T(8,128)(2,1)S(1)}, bf16[2,128,512]{2,1,0:T(8,128)(2,1)S(1)}, u32[]{:S(2)}, u32[]{:S(2)}) collective-permute-start(bf16[2,128,512]{2,1,0:T(8,128)(2,1)S(1)} %maximum_select_fusion), channel_id=1, source_target_pairs={{0,16},{1,17}} | collective-permute-start | bytes 786440 | tf_op jit(solution)/shard_map/ppermute | solution.py:29
  17.1 10.1 %collective-permute-start = (bf16[2,128,512]{2,1,0:T(8,128)(2,1)S(1)}, bf16[2,128,512]{2,1,0:T(8,128)(2,1)S(1)}, u32[]{:S(2)}, u32[]{:S(2)}) collective-permute-start(bf16[2,128,512]{2,1,0:T(8,128)(2,1)S(1)} %maximum_select_fusion), channel_id=1, source_target_pairs={{0,8},{1,9}} | collective-permute-start | bytes 786440 | tf_op jit(solution)/shard_map/ppermute | solution.py:29
  17.9 98.6 %collective-permute-start.7 = (bf16[2,128,512]{2,1,0:T(8,128)(2,1)S(1)}, bf16[2,128,512]{2,1,0:T(8,128)(2,1)S(1)}, u32[]{:S(2)}, u32[]{:S(2)}) collective-permute-start(bf16[2,128,512]{2,1,0:T(8,128)(2,1)S(1)} %pad_maximum_fusion.5), channel_id=1, source_target_pairs={{2,0},{4,2},{6,4},{8,6},{10,8},{12,10},{14,12},{16,14},{18,16},{20... | collective-permute-start | bytes 786440 | tf_op jit(solution)/shard_map/ppermute | solution.py:58
  20.2 96.3 %collective-permute-start.6 = (bf16[2,128,512]{2,1,0:T(8,128)(2,1)S(1)}, bf16[2,128,512]{2,1,0:T(8,128)(2,1)S(1)}, u32[]{:S(2)}, u32[]{:S(2)}) collective-permute-start(bf16[2,128,512]{2,1,0:T(8,128)(2,1)S(1)} %pad_maximum_fusion.4), channel_id=1, source_target_pairs={{0,2},{2,4},{4,6},{6,8},{8,10},{10,12},{12,14},{14,16},{16,18},{18... | collective-permute-start | bytes 786440 | tf_op jit(solution)/shard_map/ppermute | solution.py:58
  27.3 90.1 %collective-permute-start.5 = (bf16[2,128,512]{2,1,0:T(8,128)(2,1)S(1)}, bf16[2,128,512]{2,1,0:T(8,128)(2,1)S(1)}, u32[]{:S(2)}, u32[]{:S(2)}) collective-permute-start(bf16[2,128,512]{2,1,0:T(8,128)(2,1)S(1)} %add_add_fusion.1), channel_id=1, source_target_pairs={{0,6},{8,14},{16,22},{24,30},{1,7},{9,15},{17,23},{25,31}} | collective-permute-start | bytes 786440 | tf_op jit(solution)/shard_map/ppermute | solution.py:29
  28.6 88.8 %collective-permute-start.4 = (bf16[2,128,512]{2,1,0:T(8,128)(2,1)S(1)}, bf16[2,128,512]{2,1,0:T(8,128)(2,1)S(1)}, u32[]{:S(2)}, u32[]{:S(2)}) collective-permute-start(bf16[2,128,512]{2,1,0:T(8,128)(2,1)S(1)} %add_add_fusion.1), channel_id=1, source_target_pairs={{0,4},{8,12},{16,20},{24,28},{1,5},{9,13},{17,21},{25,29}} | collective-permute-start | bytes 786440 | tf_op jit(solution)/shard_map/ppermute | solution.py:29
  29.3 88.2 %collective-permute-start.3 = (bf16[2,128,512]{2,1,0:T(8,128)(2,1)S(1)}, bf16[2,128,512]{2,1,0:T(8,128)(2,1)S(1)}, u32[]{:S(2)}, u32[]{:S(2)}) collective-permute-start(bf16[2,128,512]{2,1,0:T(8,128)(2,1)S(1)} %add_add_fusion.1), channel_id=1, source_target_pairs={{0,2},{8,10},{16,18},{24,26},{1,3},{9,11},{17,19},{25,27}} | collective-permute-start | bytes 786440 | tf_op jit(solution)/shard_map/ppermute | solution.py:29
  133.9 12.7 %collective-permute-start.10 = (bf16[2,128,512]{2,1,0:T(8,128)(2,1)S(1)}, bf16[2,128,512]{2,1,0:T(8,128)(2,1)S(1)}, u32[]{:S(2)}, u32[]{:S(2)}) collective-permute-start(bf16[2,128,512]{2,1,0:T(8,128)(2,1)S(1)} %fusion.3), channel_id=1, source_target_pairs={{6,0},{14,8},{22,16},{30,24},{7,1},{15,9},{23,17},{31,25}} | collective-permute-start | bytes 786440 | tf_op jit(solution)/shard_map/ppermute | solution.py:45
  135.2 11.4 %collective-permute-start.9 = (bf16[2,128,512]{2,1,0:T(8,128)(2,1)S(1)}, bf16[2,128,512]{2,1,0:T(8,128)(2,1)S(1)}, u32[]{:S(2)}, u32[]{:S(2)}) collective-permute-start(bf16[2,128,512]{2,1,0:T(8,128)(2,1)S(1)} %fusion.3), channel_id=1, source_target_pairs={{4,0},{12,8},{20,16},{28,24},{5,1},{13,9},{21,17},{29,25}} | collective-permute-start | bytes 786440 | tf_op jit(solution)/shard_map/ppermute | solution.py:45
  135.9 10.7 %collective-permute-start.8 = (bf16[2,128,512]{2,1,0:T(8,128)(2,1)S(1)}, bf16[2,128,512]{2,1,0:T(8,128)(2,1)S(1)}, u32[]{:S(2)}, u32[]{:S(2)}) collective-permute-start(bf16[2,128,512]{2,1,0:T(8,128)(2,1)S(1)} %fusion.3), channel_id=1, source_target_pairs={{2,0},{10,8},{18,16},{26,24},{3,1},{11,9},{19,17},{27,25}} | collective-permute-start | bytes 786440 | tf_op jit(solution)/shard_map/ppermute | solution.py:45
  146.8 10.5 %collective-permute-start.13 = (bf16[2,128,512]{2,1,0:T(8,128)(2,1)S(1)}, bf16[2,128,512]{2,1,0:T(8,128)(2,1)S(1)}, u32[]{:S(2)}, u32[]{:S(2)}) collective-permute-start(bf16[2,128,512]{2,1,0:T(8,128)(2,1)S(1)} %fusion.19), channel_id=1, source_target_pairs={{24,0},{25,1}} | collective-permute-start | bytes 786440 | tf_op jit(solution)/shard_map/ppermute | solution.py:45
  147.5 9.8 %collective-permute-start.12 = (bf16[2,128,512]{2,1,0:T(8,128)(2,1)S(1)}, bf16[2,128,512]{2,1,0:T(8,128)(2,1)S(1)}, u32[]{:S(2)}, u32[]{:S(2)}) collective-permute-start(bf16[2,128,512]{2,1,0:T(8,128)(2,1)S(1)} %fusion.19), channel_id=1, source_target_pairs={{16,0},{17,1}} | collective-permute-start | bytes 786440 | tf_op jit(solution)/shard_map/ppermute | solution.py:45
  148.2 9.2 %collective-permute-start.11 = (bf16[2,128,512]{2,1,0:T(8,128)(2,1)S(1)}, bf16[2,128,512]{2,1,0:T(8,128)(2,1)S(1)}, u32[]{:S(2)}, u32[]{:S(2)}) collective-permute-start(bf16[2,128,512]{2,1,0:T(8,128)(2,1)S(1)} %fusion.19), channel_id=1, source_target_pairs={{8,0},{9,1}} | collective-permute-start | bytes 786440 | tf_op jit(solution)/shard_map/ppermute | solution.py:45
  150.0 32.2 %collective-permute-start.14 = (bf16[2,128,512]{2,1,0:T(8,128)(2,1)S(1)}, bf16[2,128,512]{2,1,0:T(8,128)(2,1)S(1)}, u32[]{:S(2)}, u32[]{:S(2)}) collective-permute-start(bf16[2,128,512]{2,1,0:T(8,128)(2,1)S(1)} %pad_maximum_fusion.6), channel_id=1, source_target_pairs={{0,2},{2,4},{4,6},{6,8},{8,10},{10,12},{12,14},{14,16},{16,18},{18... | collective-permute-start | bytes 786440 | tf_op jit(solution)/shard_map/ppermute | solution.py:58
  155.4 26.8 %collective-permute-start.15 = (bf16[2,128,512]{2,1,0:T(8,128)(2,1)S(1)}, bf16[2,128,512]{2,1,0:T(8,128)(2,1)S(1)}, u32[]{:S(2)}, u32[]{:S(2)}) collective-permute-start(bf16[2,128,512]{2,1,0:T(8,128)(2,1)S(1)} %pad_maximum_fusion.7), channel_id=1, source_target_pairs={{2,0},{4,2},{6,4},{8,6},{10,8},{12,10},{14,12},{16,14},{18,16},{20... | collective-permute-start | bytes 786440 | tf_op jit(solution)/shard_map/ppermute | solution.py:58
  182.2 25.5 %copy-start.9 = (f32[256,512]{1,0:T(8,128)S(1)}, f32[256,512]{1,0:T(8,128)}, u32[]{:S(2)}) copy-start(f32[256,512]{1,0:T(8,128)} %get-tuple-element.21) | copy-start | bytes 1572868
  182.9 54.1 %all-to-all-start.1 = ((bf16[16,128,512]{2,1,0:T(8,128)(2,1)}), bf16[16,128,512]{2,1,0:T(8,128)(2,1)S(1)}, u32[]{:S(2)}, u32[]{:S(2)}) async-start(bf16[16,128,512]{2,1,0:T(8,128)(2,1)} %get-tuple-element.27), calls=%async_computation.1 | async-start | bytes 4194304 | tf_op jit(solution)/shard_map/all_to_all | solution.py:321
  (7 other events, 14.6 us)

commit v14 on v13

--- a/solution.py
+++ b/solution.py
@@ -123,8 +123,8 @@
                 stats[0:1, :], stats[1:2, :], mode,
             )
             dq_ref[0, :, cols] = dq.astype(jnp.bfloat16)
-            dk_ref[0, :, cols] = dk
-            dv_ref[0, :, cols] = dv
+            dk_ref[0, :, cols] = dk.astype(jnp.bfloat16)
+            dv_ref[0, :, cols] = dv.astype(jnp.bfloat16)
 
 
 def list_pairs(qin, qout, first, ktab, mtab, outs, queries, out_grad, norm3, delta3, key_src, value_src):
@@ -188,8 +188,8 @@
         grid_spec=grid_spec,
         out_shape=[
             jax.ShapeDtypeStruct((items, height, features), jnp.bfloat16),
-            jax.ShapeDtypeStruct((items, height, features), jnp.float32),
-            jax.ShapeDtypeStruct((items, height, features), jnp.float32),
+            jax.ShapeDtypeStruct((items, height, features), jnp.bfloat16),
+            jax.ShapeDtypeStruct((items, height, features), jnp.bfloat16),
         ],
     )(ktab, mtab, arrived, arrived, arrived, key_rows, value_rows)
 
@@ -324,8 +324,8 @@
         select_f[:, :, None, None] * returned.astype(jnp.float32)[:, None], axis=0
     )
     choose = (slot_recv[:, None] == jnp.arange(1, slot_count + 1)[None, :]).astype(jnp.float32)
-    rand_key = jnp.sum(choose[:, :, None, None] * dk_rand[:, None], axis=0)
-    rand_value = jnp.sum(choose[:, :, None, None] * dv_rand[:, None], axis=0)
+    rand_key = jnp.sum(choose[:, :, None, None] * dk_rand.astype(jnp.float32)[:, None], axis=0)
+    rand_value = jnp.sum(choose[:, :, None, None] * dv_rand.astype(jnp.float32)[:, None], axis=0)
 
     own_tail = jnp.where(last_dev, 1.0, 0.0).astype(jnp.float32)
 

time: 241 us -> 240 us (level)
  no operation moved by 1% of the time
where the time goes in v14:
time: 240 us; the launch traced here: 239 us
  waiting for transfers between devices  102 us (42%)
  Pallas kernels  55.1 us (23%)
  other arithmetic  35.4 us (15%)
  starting transfers between devices  34.5 us (14%)
  local copies, waits for them, and re-layouts  11.4 us (5%)
    ppermute x4, waiting for transfers between devices, shift(): return lax.ppermute(array, axis, pairs)  86.4 us
    pallas_call x3, Pallas kernels, list_pairs(): pl.pallas_call(list_kernel, grid_spec=grid_spec, out_shape=[jax.ShapeDtyp...  34.2 us
    pallas_call x1, Pallas kernels, rand_pairs(): pl.pallas_call(functools.partial(rand_kernel, heads), grid_spec=grid_spec...  20.9 us
    all_to_all x1, waiting for transfers between devices, shards(): lax.all_to_all(dq_rand, 'ctx', split_axis=0, concat_axis=0, tiled=True)  15.2 us
    ppermute x4, starting transfers between devices, shift(): return lax.ppermute(array, axis, pairs)  13.8 us
    all_to_all x1, starting transfers between devices, shards(): lax.all_to_all(routed, 'ctx', split_axis=0, concat_axis=0, tiled=True)  6.69 us
  transfers between devices with their start and end apart: 18, of which 2 were waited for; matrix products, arithmetic and copies ran while one was open for 13% of the time, Pallas kernels for 23%

profile of v14, /device:TPU:11, one launch (start us, length us, event | category | flops | bytes accessed | tf_op | source)
XLA Modules:
  0.0 239.2 jit_solution(14708901576756708793)
XLA Ops:
  2.6 1.3 convert_multiply_fusion
  5.9 3.1 %select_add_fusion = bf16[16,272,512]{2,1,0:T(8,128)(2,1)} fusion(pred[16]{0:T(512)(128)(4,1)S(1)} %get-tuple-element.73, pred[16]{0:T(512)(128)(4,1)S(1)} %get-tuple-element.74, pred[16]{0:T(512)(128)(4,1)S(1)} %get-tuple-element.75, pred[16]{0:T(512)(128)(4,1)S(1)} %get-tuple-element.72, bf16[272,512]{1,0:T(8,128)(2,1)S(1)} %get-tuple-element.47, ...), kind=kLoop, calls=%fused_computation.3 | loop fusion | flops 17825792 | bytes 5579328 | tf_op jit(solution)/shard_map/add | solution.py:310
  9.0 6.7 %all-to-all-start = ((bf16[16,272,512]{2,1,0:T(8,128)(2,1)}), bf16[16,272,512]{2,1,0:T(8,128)(2,1)}, u32[]{:S(2)}, u32[]{:S(2)}) async-start(bf16[16,272,512]{2,1,0:T(8,128)(2,1)} %select_add_fusion), calls=%async_computation | async-start | bytes 8912896 | tf_op jit(solution)/shard_map/all_to_all | solution.py:311
  17.9 2.3 collective-permute-start.7
  20.2 4.2 %collective-permute-start.6 = (bf16[2,128,512]{2,1,0:T(8,128)(2,1)S(1)}, bf16[2,128,512]{2,1,0:T(8,128)(2,1)S(1)}, u32[]{:S(2)}, u32[]{:S(2)}) collective-permute-start(bf16[2,128,512]{2,1,0:T(8,128)(2,1)S(1)} %pad_maximum_fusion.4), channel_id=1, source_target_pairs={{0,2},{2,4},{4,6},{6,8},{8,10},{10,12},{12,14},{14,16},{16,18},{18... | collective-permute-start | bytes 786440 | tf_op jit(solution)/shard_map/ppermute | solution.py:58
  30.1 86.3 %collective-permute-done.7 = bf16[2,128,512]{2,1,0:T(8,128)(2,1)S(1)} collective-permute-done((bf16[2,128,512]{2,1,0:T(8,128)(2,1)S(1)}, bf16[2,128,512]{2,1,0:T(8,128)(2,1)S(1)}, u32[]{:S(2)}, u32[]{:S(2)}) %collective-permute-start.7) | collective-permute-done | bytes 262176 | tf_op jit(solution)/shard_map/ppermute | solution.py:58
  119.9 11.4 %shard_map.95 = (f32[512,512]{1,0:T(8,128)}, f32[512,512]{1,0:T(8,128)}, f32[512,512]{1,0:T(8,128)}) custom-call(s32[4]{0:T(128)} %iota.37.qin.qout, s32[4]{0:T(128)} %iota.37.qin.qout, s32[4]{0:T(128)} %broadcast_25_first.2.first, s32[4]{0:T(128)} %broadcast_24_ktab.2.ktab, s32[4]{0:T(128)} %compare_convert_fusion.2.mtab, bf16[512,512]{1,0:T(8,128)(2,1)} %q_ref.5, ...), custom_call_target="tpu_custom_call" | custom-call | tf_op jit(solution)/shard_map/pallas_call | solution.py:154
  131.3 1.3 reduce_sum.65
  132.6 1.3 reduce_sum.66
  134.0 1.3 collective-permute-start.10
  138.7 7.0 %shard_map.96 = (f32[256,512]{1,0:T(8,128)}, f32[256,512]{1,0:T(8,128)}, f32[256,512]{1,0:T(8,128)}) custom-call(s32[2]{0:T(128)} %iota_multiply_fusion.qin, s32[2]{0:T(128)} %iota.42.qout, s32[2]{0:T(128)} %broadcast_26_first.2.first, s32[2]{0:T(128)} %get-tuple-element.79.ktab, s32[2]{0:T(128)} %get-tuple-element.80.mtab, bf16[512,512]{1,0:T(8,128)(2,1)} %q_ref.5, ...), custom_call_target="tpu_custom_call" | custom-call | tf_op jit(solution)/shard_map/pallas_call | solution.py:154
  150.1 5.4 %collective-permute-start.14 = (bf16[2,128,512]{2,1,0:T(8,128)(2,1)S(1)}, bf16[2,128,512]{2,1,0:T(8,128)(2,1)S(1)}, u32[]{:S(2)}, u32[]{:S(2)}) collective-permute-start(bf16[2,128,512]{2,1,0:T(8,128)(2,1)S(1)} %pad_maximum_fusion.6), channel_id=1, source_target_pairs={{0,2},{2,4},{4,6},{6,8},{8,10},{10,12},{12,14},{14,16},{16,18},{18... | collective-permute-start | bytes 786440 | tf_op jit(solution)/shard_map/ppermute | solution.py:58
  155.5 1.9 collective-permute-start.15
  160.9 20.9 %shard_map.97 = (bf16[16,128,512]{2,1,0:T(8,128)(2,1)}, bf16[16,128,512]{2,1,0:T(8,128)(2,1)}, bf16[16,128,512]{2,1,0:T(8,128)(2,1)}) custom-call(s32[16]{0:T(128)} %add_maximum_fusion.ktab, s32[16]{0:T(128)} %compare_convert_fusion.1.mtab, bf16[16,272,512]{2,1,0:T(8,128)(2,1)} %all-to-all-done.q_ref.do_ref.st_ref, ...), custom_call_target="tpu_custom_call" | custom-call | tf_op jit(solution)/shard_map/pallas_call | solution.py:186
  181.8 4.7 %all-to-all-start.1 = ((bf16[16,128,512]{2,1,0:T(8,128)(2,1)}), bf16[16,128,512]{2,1,0:T(8,128)(2,1)}, u32[]{:S(2)}, u32[]{:S(2)}) async-start(bf16[16,128,512]{2,1,0:T(8,128)(2,1)} %get-tuple-element.27), calls=%async_computation.1 | async-start | bytes 4194304 | tf_op jit(solution)/shard_map/all_to_all | solution.py:321
  186.6 15.9 %shard_map.94 = (f32[512,512]{1,0:T(8,128)}, f32[768,512]{1,0:T(8,128)}, f32[768,512]{1,0:T(8,128)}) custom-call(s32[6]{0:T(128)} %constant.33.clone.1.qin.qout, s32[6]{0:T(128)} %constant.33.clone.1.qin.qout, s32[6]{0:T(128)} %constant.34.clone.1.first, s32[6]{0:T(128)} %constant.35.clone.1.ktab, s32[6]{0:T(128)} %constant.36.clone.1.mtab, ...), custom_call_target="tpu_custom_call" | custom-call | tf_op jit(solution)/shard_map/pallas_call | solution.py:154
  202.5 2.1 add_bitcast_fusion
  209.0 1.3 bitcast_add_fusion.3
  210.3 3.9 %multiply_reduce_fusion = (f32[4,128,512]{2,1,0:T(8,128)S(1)}, f32[4,128,512]{2,1,0:T(8,128)}) fusion(f32[16,128,512]{2,1,0:T(8,128)S(1)} %convert_element_type.150, f32[16,4]{1,0:T(8,128)S(1)} %compare_convert_fusion, f32[16,128,512]{2,1,0:T(8,128)S(1)} %convert_element_type.147), kind=kLoop, calls=%fused_computation | loop fusion | flops 16252928 | bytes 10486016 | tf_op jit(solution)/shard_map/reduce_sum | solution.py:328
  214.2 2.4 %fusion = bf16[4,128,512]{2,1,0:T(8,128)(2,1)} fusion(f32[4,128,512]{2,1,0:T(8,128)} %get-tuple-element.36, f32[1,128,512]{2,1,0:T(8,128)} %get-tuple-element.82, f32[1,128,512]{2,1,0:T(8,128)} %get-tuple-element.41, f32[1,128,512]{2,1,0:T(8,128)} %get-tuple-element.42, f32[1,128,512]{2,1,0:T(8,128)} %get-tuple-element.40), kind=kLoop, calls=%fused_computation.6 | loop fusion | flops 1310720 | bytes 2621440 | tf_op jit(solution)/shard_map/convert_element_type | solution.py:342
  216.6 2.1 fusion.1
  218.7 15.2 %all-to-all-done.1 = bf16[16,128,512]{2,1,0:T(8,128)(2,1)} async-done(((bf16[16,128,512]{2,1,0:T(8,128)(2,1)}), bf16[16,128,512]{2,1,0:T(8,128)(2,1)}, u32[]{:S(2)}, u32[]{:S(2)}) %all-to-all-start.1) | async-done | bytes 2097184 | tf_op jit(solution)/shard_map/all_to_all | solution.py:321
  233.9 2.1 convert_element_type.142
  236.1 1.4 multiply_reduce_fusion.2
  (122 shorter events, 32.5 us)
Async XLA Ops:
  0.6 4.6 %copy-start = (bf16[512,512]{1,0:T(8,128)(2,1)S(1)}, bf16[512,512]{1,0:T(8,128)(2,1)}, u32[]{:S(2)}) copy-start(bf16[512,512]{1,0:T(8,128)(2,1)} %do_ref.5) | copy-start | bytes 1572868
  9.0 6.7 %copy-start.2 = (bf16[512,512]{1,0:T(8,128)(2,1)S(1)}, bf16[512,512]{1,0:T(8,128)(2,1)}, u32[]{:S(2)}) copy-start(bf16[512,512]{1,0:T(8,128)(2,1)} %k_ref.3) | copy-start | bytes 1572868
  9.0 6.7 %copy-start.3 = (bf16[512,512]{1,0:T(8,128)(2,1)S(1)}, bf16[512,512]{1,0:T(8,128)(2,1)}, u32[]{:S(2)}) copy-start(bf16[512,512]{1,0:T(8,128)(2,1)} %v_ref.3) | copy-start | bytes 1572868
  9.0 17.2 %copy-start.15 = (bf16[4,512]{1,0:T(4,128)(2,1)S(1)}, bf16[4,512]{1,0:T(4,128)(2,1)}, u32[]{:S(2)}) copy-start(bf16[4,512]{1,0:T(4,128)(2,1)} %param.12) | copy-start | bytes 12292
  9.0 149.5 %all-to-all-start = ((bf16[16,272,512]{2,1,0:T(8,128)(2,1)}), bf16[16,272,512]{2,1,0:T(8,128)(2,1)}, u32[]{:S(2)}, u32[]{:S(2)}) async-start(bf16[16,272,512]{2,1,0:T(8,128)(2,1)} %select_add_fusion), calls=%async_computation | async-start | bytes 8912896 | tf_op jit(solution)/shard_map/all_to_all | solution.py:311
  15.8 11.6 %collective-permute-start.1 = (bf16[2,128,512]{2,1,0:T(8,128)(2,1)S(1)}, bf16[2,128,512]{2,1,0:T(8,128)(2,1)S(1)}, u32[]{:S(2)}, u32[]{:S(2)}) collective-permute-start(bf16[2,128,512]{2,1,0:T(8,128)(2,1)S(1)} %maximum_select_fusion), channel_id=1, source_target_pairs={{0,16},{1,17}} | collective-permute-start | bytes 786440 | tf_op jit(solution)/shard_map/ppermute | solution.py:29
  16.5 10.9 %collective-permute-start.2 = (bf16[2,128,512]{2,1,0:T(8,128)(2,1)S(1)}, bf16[2,128,512]{2,1,0:T(8,128)(2,1)S(1)}, u32[]{:S(2)}, u32[]{:S(2)}) collective-permute-start(bf16[2,128,512]{2,1,0:T(8,128)(2,1)S(1)} %maximum_select_fusion), channel_id=1, source_target_pairs={{0,24},{1,25}} | collective-permute-start | bytes 786440 | tf_op jit(solution)/shard_map/ppermute | solution.py:29
  17.2 10.2 %collective-permute-start = (bf16[2,128,512]{2,1,0:T(8,128)(2,1)S(1)}, bf16[2,128,512]{2,1,0:T(8,128)(2,1)S(1)}, u32[]{:S(2)}, u32[]{:S(2)}) collective-permute-start(bf16[2,128,512]{2,1,0:T(8,128)(2,1)S(1)} %maximum_select_fusion), channel_id=1, source_target_pairs={{0,8},{1,9}} | collective-permute-start | bytes 786440 | tf_op jit(solution)/shard_map/ppermute | solution.py:29
  17.9 98.6 %collective-permute-start.7 = (bf16[2,128,512]{2,1,0:T(8,128)(2,1)S(1)}, bf16[2,128,512]{2,1,0:T(8,128)(2,1)S(1)}, u32[]{:S(2)}, u32[]{:S(2)}) collective-permute-start(bf16[2,128,512]{2,1,0:T(8,128)(2,1)S(1)} %pad_maximum_fusion.5), channel_id=1, source_target_pairs={{2,0},{4,2},{6,4},{8,6},{10,8},{12,10},{14,12},{16,14},{18,16},{20... | collective-permute-start | bytes 786440 | tf_op jit(solution)/shard_map/ppermute | solution.py:58
  20.2 96.3 %collective-permute-start.6 = (bf16[2,128,512]{2,1,0:T(8,128)(2,1)S(1)}, bf16[2,128,512]{2,1,0:T(8,128)(2,1)S(1)}, u32[]{:S(2)}, u32[]{:S(2)}) collective-permute-start(bf16[2,128,512]{2,1,0:T(8,128)(2,1)S(1)} %pad_maximum_fusion.4), channel_id=1, source_target_pairs={{0,2},{2,4},{4,6},{6,8},{8,10},{10,12},{12,14},{14,16},{16,18},{18... | collective-permute-start | bytes 786440 | tf_op jit(solution)/shard_map/ppermute | solution.py:58
  27.5 90.0 %collective-permute-start.5 = (bf16[2,128,512]{2,1,0:T(8,128)(2,1)S(1)}, bf16[2,128,512]{2,1,0:T(8,128)(2,1)S(1)}, u32[]{:S(2)}, u32[]{:S(2)}) collective-permute-start(bf16[2,128,512]{2,1,0:T(8,128)(2,1)S(1)} %add_add_fusion.1), channel_id=1, source_target_pairs={{0,6},{8,14},{16,22},{24,30},{1,7},{9,15},{17,23},{25,31}} | collective-permute-start | bytes 786440 | tf_op jit(solution)/shard_map/ppermute | solution.py:29
  28.8 88.7 %collective-permute-start.4 = (bf16[2,128,512]{2,1,0:T(8,128)(2,1)S(1)}, bf16[2,128,512]{2,1,0:T(8,128)(2,1)S(1)}, u32[]{:S(2)}, u32[]{:S(2)}) collective-permute-start(bf16[2,128,512]{2,1,0:T(8,128)(2,1)S(1)} %add_add_fusion.1), channel_id=1, source_target_pairs={{0,4},{8,12},{16,20},{24,28},{1,5},{9,13},{17,21},{25,29}} | collective-permute-start | bytes 786440 | tf_op jit(solution)/shard_map/ppermute | solution.py:29
  29.5 88.0 %collective-permute-start.3 = (bf16[2,128,512]{2,1,0:T(8,128)(2,1)S(1)}, bf16[2,128,512]{2,1,0:T(8,128)(2,1)S(1)}, u32[]{:S(2)}, u32[]{:S(2)}) collective-permute-start(bf16[2,128,512]{2,1,0:T(8,128)(2,1)S(1)} %add_add_fusion.1), channel_id=1, source_target_pairs={{0,2},{8,10},{16,18},{24,26},{1,3},{9,11},{17,19},{25,27}} | collective-permute-start | bytes 786440 | tf_op jit(solution)/shard_map/ppermute | solution.py:29
  134.0 12.8 %collective-permute-start.10 = (bf16[2,128,512]{2,1,0:T(8,128)(2,1)S(1)}, bf16[2,128,512]{2,1,0:T(8,128)(2,1)S(1)}, u32[]{:S(2)}, u32[]{:S(2)}) collective-permute-start(bf16[2,128,512]{2,1,0:T(8,128)(2,1)S(1)} %fusion.3), channel_id=1, source_target_pairs={{6,0},{14,8},{22,16},{30,24},{7,1},{15,9},{23,17},{31,25}} | collective-permute-start | bytes 786440 | tf_op jit(solution)/shard_map/ppermute | solution.py:45
  135.3 11.5 %collective-permute-start.9 = (bf16[2,128,512]{2,1,0:T(8,128)(2,1)S(1)}, bf16[2,128,512]{2,1,0:T(8,128)(2,1)S(1)}, u32[]{:S(2)}, u32[]{:S(2)}) collective-permute-start(bf16[2,128,512]{2,1,0:T(8,128)(2,1)S(1)} %fusion.3), channel_id=1, source_target_pairs={{4,0},{12,8},{20,16},{28,24},{5,1},{13,9},{21,17},{29,25}} | collective-permute-start | bytes 786440 | tf_op jit(solution)/shard_map/ppermute | solution.py:45
  136.0 10.8 %collective-permute-start.8 = (bf16[2,128,512]{2,1,0:T(8,128)(2,1)S(1)}, bf16[2,128,512]{2,1,0:T(8,128)(2,1)S(1)}, u32[]{:S(2)}, u32[]{:S(2)}) collective-permute-start(bf16[2,128,512]{2,1,0:T(8,128)(2,1)S(1)} %fusion.3), channel_id=1, source_target_pairs={{2,0},{10,8},{18,16},{26,24},{3,1},{11,9},{19,17},{27,25}} | collective-permute-start | bytes 786440 | tf_op jit(solution)/shard_map/ppermute | solution.py:45
  146.9 10.5 %collective-permute-start.13 = (bf16[2,128,512]{2,1,0:T(8,128)(2,1)S(1)}, bf16[2,128,512]{2,1,0:T(8,128)(2,1)S(1)}, u32[]{:S(2)}, u32[]{:S(2)}) collective-permute-start(bf16[2,128,512]{2,1,0:T(8,128)(2,1)S(1)} %fusion.19), channel_id=1, source_target_pairs={{24,0},{25,1}} | collective-permute-start | bytes 786440 | tf_op jit(solution)/shard_map/ppermute | solution.py:45
  147.6 9.8 %collective-permute-start.12 = (bf16[2,128,512]{2,1,0:T(8,128)(2,1)S(1)}, bf16[2,128,512]{2,1,0:T(8,128)(2,1)S(1)}, u32[]{:S(2)}, u32[]{:S(2)}) collective-permute-start(bf16[2,128,512]{2,1,0:T(8,128)(2,1)S(1)} %fusion.19), channel_id=1, source_target_pairs={{16,0},{17,1}} | collective-permute-start | bytes 786440 | tf_op jit(solution)/shard_map/ppermute | solution.py:45
  148.3 9.2 %collective-permute-start.11 = (bf16[2,128,512]{2,1,0:T(8,128)(2,1)S(1)}, bf16[2,128,512]{2,1,0:T(8,128)(2,1)S(1)}, u32[]{:S(2)}, u32[]{:S(2)}) collective-permute-start(bf16[2,128,512]{2,1,0:T(8,128)(2,1)S(1)} %fusion.19), channel_id=1, source_target_pairs={{8,0},{9,1}} | collective-permute-start | bytes 786440 | tf_op jit(solution)/shard_map/ppermute | solution.py:45
  150.1 31.7 %collective-permute-start.14 = (bf16[2,128,512]{2,1,0:T(8,128)(2,1)S(1)}, bf16[2,128,512]{2,1,0:T(8,128)(2,1)S(1)}, u32[]{:S(2)}, u32[]{:S(2)}) collective-permute-start(bf16[2,128,512]{2,1,0:T(8,128)(2,1)S(1)} %pad_maximum_fusion.6), channel_id=1, source_target_pairs={{0,2},{2,4},{4,6},{6,8},{8,10},{10,12},{12,14},{14,16},{16,18},{18... | collective-permute-start | bytes 786440 | tf_op jit(solution)/shard_map/ppermute | solution.py:58
  155.5 26.2 %collective-permute-start.15 = (bf16[2,128,512]{2,1,0:T(8,128)(2,1)S(1)}, bf16[2,128,512]{2,1,0:T(8,128)(2,1)S(1)}, u32[]{:S(2)}, u32[]{:S(2)}) collective-permute-start(bf16[2,128,512]{2,1,0:T(8,128)(2,1)S(1)} %pad_maximum_fusion.7), channel_id=1, source_target_pairs={{2,0},{4,2},{6,4},{8,6},{10,8},{12,10},{14,12},{16,14},{18,16},{20... | collective-permute-start | bytes 786440 | tf_op jit(solution)/shard_map/ppermute | solution.py:58
  181.8 22.9 %copy-start.14 = (f32[256,512]{1,0:T(8,128)S(1)}, f32[256,512]{1,0:T(8,128)}, u32[]{:S(2)}) copy-start(f32[256,512]{1,0:T(8,128)} %get-tuple-element.21) | copy-start | bytes 1572868
  181.8 52.1 %all-to-all-start.1 = ((bf16[16,128,512]{2,1,0:T(8,128)(2,1)}), bf16[16,128,512]{2,1,0:T(8,128)(2,1)}, u32[]{:S(2)}, u32[]{:S(2)}) async-start(bf16[16,128,512]{2,1,0:T(8,128)(2,1)} %get-tuple-element.27), calls=%async_computation.1 | async-start | bytes 4194304 | tf_op jit(solution)/shard_map/all_to_all | solution.py:321
  186.4 19.5 %copy-start.6 = (bf16[16,128,512]{2,1,0:T(8,128)(2,1)S(1)}, bf16[16,128,512]{2,1,0:T(8,128)(2,1)}, u32[]{:S(2)}) copy-start(bf16[16,128,512]{2,1,0:T(8,128)(2,1)} %get-tuple-element.32) | copy-start | bytes 6291460
  (10 other events, 21.1 us)

commit v15 on v8

--- a/solution.py
+++ b/solution.py
@@ -36,19 +36,22 @@
     return array
 
 
-def gather_to_root(array, axis):
+def gather_to_root(array, axis, tie):
     count = lax.axis_size(axis)
     step = 1
     while step < count:
+        if step == RADIX:
+            array, tie = lax.optimization_barrier((array, tie))
+        sent = array.astype(jnp.bfloat16)
         arrived = [
-            lax.ppermute(array, axis, [(i + j * step, i) for i in range(0, count, RADIX * step) if i + j * step < count])
+            lax.ppermute(sent, axis, [(i + j * step, i) for i in range(0, count, RADIX * step) if i + j * step < count])
             for j in range(1, RADIX)
             if j * step < count
         ]
         for part in arrived:
-            array = array + part
+            array = array + part.astype(jnp.float32)
         step *= RADIX
-    return array
+    return array, tie
 
 
 def shift(array, axis, offset):
@@ -71,8 +74,8 @@
     dp_t = lax.dot_general(v, do, nt, preferred_element_type=jnp.float32)
     ds_t = (p_t * (dp_t - dlt)).astype(jnp.bfloat16)
     dk = jnp.dot(ds_t, q, preferred_element_type=jnp.float32) * scale
-    ds = jnp.transpose(ds_t.astype(jnp.float32)).astype(jnp.bfloat16)
-    dq = jnp.dot(ds, k, preferred_element_type=jnp.float32) * scale
+    tn = (((0,), (0,)), ((), ()))
+    dq = lax.dot_general(ds_t, k, tn, preferred_element_type=jnp.float32) * scale
     return dq, dk, dv
 
 
@@ -280,21 +283,17 @@
         axis=1,
     )
     pick = select > 0
-    routed = jnp.sum(jnp.where(pick[:, :, None, None], packed[None], 0), axis=1).astype(
-        jnp.bfloat16
-    )
     row_id = lax.broadcasted_iota(jnp.int32, (1, packed.shape[1], 1), 1)
     routed = jnp.where(
-        row_id == 2 * height + 2, slot_send.astype(jnp.bfloat16)[:, None, None], routed
-    )
+        row_id == 2 * height + 2, slot_send.astype(jnp.bfloat16)[:, None, None], jnp.bfloat16(0)
+    )
+    for slot in range(slot_count):
+        routed = routed + jnp.where(pick[:, slot, None, None], packed[slot][None], jnp.bfloat16(0))
     arrived = lax.all_to_all(routed, "ctx", split_axis=0, concat_axis=0, tiled=True)
     slot_recv = arrived[:, 2 * height + 2, 0].astype(jnp.float32).astype(jnp.int32)
     ktab_r = jnp.maximum(slot_recv - 1, 0)
     mtab_r = (slot_recv > 0).astype(jnp.int32)
     dq_rand, dk_rand, dv_rand = rand_pairs(ktab_r, mtab_r, arrived, key_rows, values, heads)
-    global_kv, dq_rand, dk_rand, dv_rand = lax.optimization_barrier(
-        (global_kv, dq_rand, dk_rand, dv_rand)
-    )
     glob_mode = (seq_blk >= WINDOW).astype(jnp.int32)
     dq_glob, dk_glob, dv_glob = list_pairs(
         table(0, 1, 2, 3), table(0, 1, 2, 3), table(1, 1, 1, 1), table(0, 0, 0, 0), glob_mode,
@@ -306,7 +305,7 @@
             jnp.sum(dv_glob.reshape(slot_count, height, features), axis=0),
         ]
     )
-    total = gather_to_root(part, "ctx")
+    total, (dq_rand, dk_rand, dv_rand) = gather_to_root(part, "ctx", (dq_rand, dk_rand, dv_rand))
 
     zero_blk = jnp.zeros((height, features), jnp.float32)
     dq_local = (
@@ -316,9 +315,7 @@
         )
     )
 
-    dq_rand, total, back_left, back_right = lax.optimization_barrier(
-        (dq_rand, total, back_left, back_right)
-    )
+    dq_rand, back_left, back_right = lax.optimization_barrier((dq_rand, back_left, back_right))
     back_left = back_left.astype(jnp.float32)
     back_right = back_right.astype(jnp.float32)
     returned = lax.all_to_all(dq_rand, "ctx", split_axis=0, concat_axis=0, tiled=True)

time: 260 us -> 250 us (0.962)
  the two profiles are of different devices: /device:TPU:11 before, /device:TPU:0 now
where the time goes in v15:
time: 250 us; the launch traced here: 249 us
  waiting for transfers between devices  91.6 us (37%)
  starting transfers between devices  66.9 us (27%)
  Pallas kernels  46.5 us (19%)
  other arithmetic  33.2 us (13%)
  local copies, waits for them, and re-layouts  9.14 us (4%)
    ppermute x6, waiting for transfers between devices, spread_2(): lax.ppermute(array, axis, [(i, i + j * step) for i in range(0, count, RAD...  65.5 us
    pallas_call x3, Pallas kernels, list_pairs(): pl.pallas_call(list_kernel, grid_spec=grid_spec, out_shape=[jax.ShapeDtyp...  34 us
    all_to_all x1, starting transfers between devices, shards(): lax.all_to_all(dq_rand, 'ctx', split_axis=0, concat_axis=0, tiled=True)  30.7 us
    ppermute x6, waiting for transfers between devices, gather_to_root(): lax.ppermute(sent, axis, [(i + j * step, i) for i in range(0, count, RADI...  26.1 us
    pallas_call x1, Pallas kernels, rand_pairs(): pl.pallas_call(functools.partial(rand_kernel, heads), grid_spec=grid_spec...  12.4 us
    ppermute x6, starting transfers between devices, spread_2(): lax.ppermute(array, axis, [(i, i + j * step) for i in range(0, count, RAD...  12.1 us
    ppermute x4, starting transfers between devices, shift(): return lax.ppermute(array, axis, pairs)  8.69 us
    ppermute x6, starting transfers between devices, gather_to_root(): lax.ppermute(sent, axis, [(i + j * step, i) for i in range(0, count, RADI...  7.92 us
  transfers between devices with their start and end apart: 18, of which 7 were waited for; matrix products, arithmetic and copies ran while one was open for 12% of the time, Pallas kernels for 19%

profile of v15, /device:TPU:0, one launch (start us, length us, event | category | flops | bytes accessed | tf_op | source)
XLA Modules:
  0.0 248.6 jit_solution(9513338525172495728)
XLA Ops:
  1.6 1.3 convert_multiply_fusion
  5.3 3.0 %select_add_fusion = bf16[16,272,512]{2,1,0:T(8,128)(2,1)} fusion(pred[16]{0:T(512)(128)(4,1)S(1)} %get-tuple-element.79, pred[16]{0:T(512)(128)(4,1)S(1)} %get-tuple-element.80, pred[16]{0:T(512)(128)(4,1)S(1)} %get-tuple-element.81, pred[16]{0:T(512)(128)(4,1)S(1)} %get-tuple-element.78, bf16[272,512]{1,0:T(8,128)(2,1)S(1)} %get-tuple-element.53, ...), kind=kLoop, calls=%fused_computation.3 | loop fusion | flops 17825792 | bytes 5579328 | tf_op jit(solution)/shard_map/add | solution.py:291
  8.3 7.5 %all-to-all-start = ((bf16[16,272,512]{2,1,0:T(8,128)(2,1)}), bf16[16,272,512]{2,1,0:T(8,128)(2,1)}, u32[]{:S(2)}, u32[]{:S(2)}) async-start(bf16[16,272,512]{2,1,0:T(8,128)(2,1)} %select_add_fusion), calls=%async_computation | async-start | bytes 8912896 | tf_op jit(solution)/shard_map/all_to_all | solution.py:292
  16.0 5.6 %collective-permute-start.2 = (bf16[2,128,512]{2,1,0:T(8,128)(2,1)S(1)}, bf16[2,128,512]{2,1,0:T(8,128)(2,1)S(1)}, u32[]{:S(2)}, u32[]{:S(2)}) collective-permute-start(bf16[2,128,512]{2,1,0:T(8,128)(2,1)S(1)} %maximum_select_fusion), channel_id=1, source_target_pairs={{0,24},{1,25}} | collective-permute-start | bytes 786440 | tf_op jit(solution)/shard_map/ppermute | solution.py:29
  25.6 3.0 %collective-permute-start.6 = (bf16[2,128,512]{2,1,0:T(8,128)(2,1)S(1)}, bf16[2,128,512]{2,1,0:T(8,128)(2,1)S(1)}, u32[]{:S(2)}, u32[]{:S(2)}) collective-permute-start(bf16[2,128,512]{2,1,0:T(8,128)(2,1)S(1)} %pad_maximum_fusion.4), channel_id=1, source_target_pairs={{0,2},{2,4},{4,6},{6,8},{8,10},{10,12},{12,14},{14,16},{16,18},{18... | collective-permute-start | bytes 786440 | tf_op jit(solution)/shard_map/ppermute | solution.py:60
  31.6 59.9 %collective-permute-done.2 = bf16[2,128,512]{2,1,0:T(8,128)(2,1)S(1)} collective-permute-done((bf16[2,128,512]{2,1,0:T(8,128)(2,1)S(1)}, bf16[2,128,512]{2,1,0:T(8,128)(2,1)S(1)}, u32[]{:S(2)}, u32[]{:S(2)}) %collective-permute-start.2) | collective-permute-done | bytes 262176 | tf_op jit(solution)/shard_map/ppermute | solution.py:29
  91.5 2.8 %collective-permute-done.1 = bf16[2,128,512]{2,1,0:T(8,128)(2,1)S(1)} collective-permute-done((bf16[2,128,512]{2,1,0:T(8,128)(2,1)S(1)}, bf16[2,128,512]{2,1,0:T(8,128)(2,1)S(1)}, u32[]{:S(2)}, u32[]{:S(2)}) %collective-permute-start.1) | collective-permute-done | bytes 262176 | tf_op jit(solution)/shard_map/ppermute | solution.py:29
  94.3 2.8 %collective-permute-done = bf16[2,128,512]{2,1,0:T(8,128)(2,1)S(1)} collective-permute-done((bf16[2,128,512]{2,1,0:T(8,128)(2,1)S(1)}, bf16[2,128,512]{2,1,0:T(8,128)(2,1)S(1)}, u32[]{:S(2)}, u32[]{:S(2)}) %collective-permute-start) | collective-permute-done | bytes 262176 | tf_op jit(solution)/shard_map/ppermute | solution.py:29
  104.1 7.0 %shard_map.96 = (f32[256,512]{1,0:T(8,128)}, f32[256,512]{1,0:T(8,128)}, f32[256,512]{1,0:T(8,128)}) custom-call(s32[2]{0:T(128)} %iota_multiply_fusion.qin, s32[2]{0:T(128)} %iota.42.qout, s32[2]{0:T(128)} %broadcast_26_first.2.first, s32[2]{0:T(128)} %get-tuple-element.85.ktab, s32[2]{0:T(128)} %get-tuple-element.86.mtab, bf16[512,512]{1,0:T(8,128)(2,1)} %q_ref.5, ...), custom_call_target="tpu_custom_call" | custom-call | tf_op jit(solution)/shard_map/pallas_call | solution.py:156
  114.7 11.3 %shard_map.95 = (f32[512,512]{1,0:T(8,128)}, f32[512,512]{1,0:T(8,128)}, f32[512,512]{1,0:T(8,128)}) custom-call(s32[4]{0:T(128)} %iota.37.qin.qout, s32[4]{0:T(128)} %iota.37.qin.qout, s32[4]{0:T(128)} %broadcast_18_first.2.first, s32[4]{0:T(128)} %broadcast_17_ktab.2.ktab, s32[4]{0:T(128)} %compare_convert_fusion.2.mtab, bf16[512,512]{1,0:T(8,128)(2,1)} %q_ref.5, ...), custom_call_target="tpu_custom_call" | custom-call | tf_op jit(solution)/shard_map/pallas_call | solution.py:156
  126.0 1.3 reduce_sum.65
  127.4 1.3 reduce_sum.64
  132.7 3.1 %collective-permute-start.11 = (bf16[2,128,512]{2,1,0:T(8,128)(2,1)S(1)}, bf16[2,128,512]{2,1,0:T(8,128)(2,1)S(1)}, u32[]{:S(2)}, u32[]{:S(2)}) collective-permute-start(bf16[2,128,512]{2,1,0:T(8,128)(2,1)S(1)} %pad_maximum_fusion.6), channel_id=1, source_target_pairs={{0,2},{2,4},{4,6},{6,8},{8,10},{10,12},{12,14},{14,16},{16,18},{18... | collective-permute-start | bytes 786440 | tf_op jit(solution)/shard_map/ppermute | solution.py:60
  137.3 1.9 collective-permute-done.9
  141.6 12.4 %shard_map.97 = (bf16[16,128,512]{2,1,0:T(8,128)(2,1)}, f32[16,128,512]{2,1,0:T(8,128)}, f32[16,128,512]{2,1,0:T(8,128)}) custom-call(s32[16]{0:T(128)} %add_maximum_fusion.ktab, s32[16]{0:T(128)} %compare_convert_fusion.1.mtab, bf16[16,272,512]{2,1,0:T(8,128)(2,1)} %all-to-all-done.q_ref.do_ref.st_ref, ...), custom_call_target="tpu_custom_call" | custom-call | tf_op jit(solution)/shard_map/pallas_call | solution.py:188
  154.0 30.7 %all-to-all-start.1 = ((bf16[16,128,512]{2,1,0:T(8,128)(2,1)}), bf16[16,128,512]{2,1,0:T(8,128)(2,1)S(1)}, u32[]{:S(2)}, u32[]{:S(2)}) async-start(bf16[16,128,512]{2,1,0:T(8,128)(2,1)} %get-tuple-element.33), calls=%async_computation.1 | async-start | bytes 4194304 | tf_op jit(solution)/shard_map/all_to_all | solution.py:321
  184.9 15.8 %shard_map.94 = (f32[512,512]{1,0:T(8,128)}, f32[768,512]{1,0:T(8,128)}, f32[768,512]{1,0:T(8,128)}) custom-call(s32[6]{0:T(128)} %constant.33.clone.1.qin.qout, s32[6]{0:T(128)} %constant.33.clone.1.qin.qout, s32[6]{0:T(128)} %constant.34.clone.1.first, s32[6]{0:T(128)} %constant.35.clone.1.ktab, s32[6]{0:T(128)} %constant.36.clone.1.mtab, ...), custom_call_target="tpu_custom_call" | custom-call | tf_op jit(solution)/shard_map/pallas_call | solution.py:156
  200.7 1.4 add_bitcast_fusion
  207.8 1.5 collective-permute-start.13
  209.3 5.1 %multiply_reduce_fusion = (f32[4,128,512]{2,1,0:T(8,128)S(1)}, f32[4,128,512]{2,1,0:T(8,128)S(1)}) fusion(f32[16,128,512]{2,1,0:T(8,128)} %get-tuple-element.40, f32[16,4]{1,0:T(8,128)S(1)} %compare_convert_fusion, f32[16,128,512]{2,1,0:T(8,128)S(1)} %copy-done.4), kind=kLoop, calls=%fused_computation | loop fusion | flops 16252928 | bytes 10486016 | tf_op jit(solution)/shard_map/reduce_sum | solution.py:328
  215.5 11.0 %collective-permute-done.15 = bf16[2,128,512]{2,1,0:T(8,128)(2,1)} collective-permute-done((bf16[2,128,512]{2,1,0:T(8,128)(2,1)}, bf16[2,128,512]{2,1,0:T(8,128)(2,1)}, u32[]{:S(2)}, u32[]{:S(2)}) %collective-permute-start.15) | collective-permute-done | bytes 262176 | tf_op jit(solution)/shard_map/ppermute | solution.py:47
  226.5 13.0 %collective-permute-done.14 = bf16[2,128,512]{2,1,0:T(8,128)(2,1)} collective-permute-done((bf16[2,128,512]{2,1,0:T(8,128)(2,1)}, bf16[2,128,512]{2,1,0:T(8,128)(2,1)}, u32[]{:S(2)}, u32[]{:S(2)}) %collective-permute-start.14) | collective-permute-done | bytes 262176 | tf_op jit(solution)/shard_map/ppermute | solution.py:47
  240.8 2.2 fusion.5
  245.5 1.4 multiply_reduce_fusion.2
  (111 shorter events, 41.0 us)
Async XLA Ops:
  0.6 3.7 %copy-start = (bf16[512,512]{1,0:T(8,128)(2,1)S(1)}, bf16[512,512]{1,0:T(8,128)(2,1)}, u32[]{:S(2)}) copy-start(bf16[512,512]{1,0:T(8,128)(2,1)} %do_ref.5) | copy-start | bytes 1572868
  8.3 7.6 %copy-start.2 = (bf16[512,512]{1,0:T(8,128)(2,1)S(1)}, bf16[512,512]{1,0:T(8,128)(2,1)}, u32[]{:S(2)}) copy-start(bf16[512,512]{1,0:T(8,128)(2,1)} %k_ref.3) | copy-start | bytes 1572868
  8.3 7.6 %copy-start.3 = (bf16[512,512]{1,0:T(8,128)(2,1)S(1)}, bf16[512,512]{1,0:T(8,128)(2,1)}, u32[]{:S(2)}) copy-start(bf16[512,512]{1,0:T(8,128)(2,1)} %v_ref.3) | copy-start | bytes 1572868
  8.3 131.1 %all-to-all-start = ((bf16[16,272,512]{2,1,0:T(8,128)(2,1)}), bf16[16,272,512]{2,1,0:T(8,128)(2,1)}, u32[]{:S(2)}, u32[]{:S(2)}) async-start(bf16[16,272,512]{2,1,0:T(8,128)(2,1)} %select_add_fusion), calls=%async_computation | async-start | bytes 8912896 | tf_op jit(solution)/shard_map/all_to_all | solution.py:292
  16.0 75.5 %collective-permute-start.2 = (bf16[2,128,512]{2,1,0:T(8,128)(2,1)S(1)}, bf16[2,128,512]{2,1,0:T(8,128)(2,1)S(1)}, u32[]{:S(2)}, u32[]{:S(2)}) collective-permute-start(bf16[2,128,512]{2,1,0:T(8,128)(2,1)S(1)} %maximum_select_fusion), channel_id=1, source_target_pairs={{0,24},{1,25}} | collective-permute-start | bytes 786440 | tf_op jit(solution)/shard_map/ppermute | solution.py:29
  21.6 72.7 %collective-permute-start.1 = (bf16[2,128,512]{2,1,0:T(8,128)(2,1)S(1)}, bf16[2,128,512]{2,1,0:T(8,128)(2,1)S(1)}, u32[]{:S(2)}, u32[]{:S(2)}) collective-permute-start(bf16[2,128,512]{2,1,0:T(8,128)(2,1)S(1)} %maximum_select_fusion), channel_id=1, source_target_pairs={{0,16},{1,17}} | collective-permute-start | bytes 786440 | tf_op jit(solution)/shard_map/ppermute | solution.py:29
  22.9 74.2 %collective-permute-start = (bf16[2,128,512]{2,1,0:T(8,128)(2,1)S(1)}, bf16[2,128,512]{2,1,0:T(8,128)(2,1)S(1)}, u32[]{:S(2)}, u32[]{:S(2)}) collective-permute-start(bf16[2,128,512]{2,1,0:T(8,128)(2,1)S(1)} %maximum_select_fusion), channel_id=1, source_target_pairs={{0,8},{1,9}} | collective-permute-start | bytes 786440 | tf_op jit(solution)/shard_map/ppermute | solution.py:29
  24.2 76.8 %collective-permute-start.7 = (bf16[2,128,512]{2,1,0:T(8,128)(2,1)S(1)}, bf16[2,128,512]{2,1,0:T(8,128)(2,1)S(1)}, u32[]{:S(2)}, u32[]{:S(2)}) collective-permute-start(bf16[2,128,512]{2,1,0:T(8,128)(2,1)S(1)} %pad_maximum_fusion.5), channel_id=1, source_target_pairs={{2,0},{4,2},{6,4},{8,6},{10,8},{12,10},{14,12},{16,14},{18,16},{20... | collective-permute-start | bytes 786440 | tf_op jit(solution)/shard_map/ppermute | solution.py:60
  25.6 75.5 %collective-permute-start.6 = (bf16[2,128,512]{2,1,0:T(8,128)(2,1)S(1)}, bf16[2,128,512]{2,1,0:T(8,128)(2,1)S(1)}, u32[]{:S(2)}, u32[]{:S(2)}) collective-permute-start(bf16[2,128,512]{2,1,0:T(8,128)(2,1)S(1)} %pad_maximum_fusion.4), channel_id=1, source_target_pairs={{0,2},{2,4},{4,6},{6,8},{8,10},{10,12},{12,14},{14,16},{16,18},{18... | collective-permute-start | bytes 786440 | tf_op jit(solution)/shard_map/ppermute | solution.py:60
  97.1 15.1 %collective-permute-start.5 = (bf16[2,128,512]{2,1,0:T(8,128)(2,1)S(1)}, bf16[2,128,512]{2,1,0:T(8,128)(2,1)S(1)}, u32[]{:S(2)}, u32[]{:S(2)}) collective-permute-start(bf16[2,128,512]{2,1,0:T(8,128)(2,1)S(1)} %add_add_fusion.1), channel_id=1, source_target_pairs={{0,6},{8,14},{16,22},{24,30},{1,7},{9,15},{17,23},{25,31}} | collective-permute-start | bytes 786440 | tf_op jit(solution)/shard_map/ppermute | solution.py:29
  98.5 13.8 %collective-permute-start.4 = (bf16[2,128,512]{2,1,0:T(8,128)(2,1)S(1)}, bf16[2,128,512]{2,1,0:T(8,128)(2,1)S(1)}, u32[]{:S(2)}, u32[]{:S(2)}) collective-permute-start(bf16[2,128,512]{2,1,0:T(8,128)(2,1)S(1)} %add_add_fusion.1), channel_id=1, source_target_pairs={{0,4},{8,12},{16,20},{24,28},{1,5},{9,13},{17,21},{25,29}} | collective-permute-start | bytes 786440 | tf_op jit(solution)/shard_map/ppermute | solution.py:29
  99.8 12.5 %collective-permute-start.3 = (bf16[2,128,512]{2,1,0:T(8,128)(2,1)S(1)}, bf16[2,128,512]{2,1,0:T(8,128)(2,1)S(1)}, u32[]{:S(2)}, u32[]{:S(2)}) collective-permute-start(bf16[2,128,512]{2,1,0:T(8,128)(2,1)S(1)} %add_add_fusion.1), channel_id=1, source_target_pairs={{0,2},{8,10},{16,18},{24,26},{1,3},{9,11},{17,19},{25,27}} | collective-permute-start | bytes 786440 | tf_op jit(solution)/shard_map/ppermute | solution.py:29
  111.1 21.5 %copy-start.8 = (f32[256,512]{1,0:T(8,128)S(1)}, f32[256,512]{1,0:T(8,128)}, u32[]{:S(2)}) copy-start(f32[256,512]{1,0:T(8,128)} %get-tuple-element.31) | copy-start | bytes 1572868
  128.7 8.6 %collective-permute-start.10 = (bf16[2,128,512]{2,1,0:T(8,128)(2,1)S(1)}, bf16[2,128,512]{2,1,0:T(8,128)(2,1)S(1)}, u32[]{:S(2)}, u32[]{:S(2)}) collective-permute-start(bf16[2,128,512]{2,1,0:T(8,128)(2,1)S(1)} %fusion.3), channel_id=1, source_target_pairs={{6,0},{14,8},{22,16},{30,24},{7,1},{15,9},{23,17},{31,25}} | collective-permute-start | bytes 786440 | tf_op jit(solution)/shard_map/ppermute | solution.py:47
  130.0 9.2 %collective-permute-start.9 = (bf16[2,128,512]{2,1,0:T(8,128)(2,1)S(1)}, bf16[2,128,512]{2,1,0:T(8,128)(2,1)S(1)}, u32[]{:S(2)}, u32[]{:S(2)}) collective-permute-start(bf16[2,128,512]{2,1,0:T(8,128)(2,1)S(1)} %fusion.3), channel_id=1, source_target_pairs={{4,0},{12,8},{20,16},{28,24},{5,1},{13,9},{21,17},{29,25}} | collective-permute-start | bytes 786440 | tf_op jit(solution)/shard_map/ppermute | solution.py:47
  131.3 7.9 %collective-permute-start.8 = (bf16[2,128,512]{2,1,0:T(8,128)(2,1)S(1)}, bf16[2,128,512]{2,1,0:T(8,128)(2,1)S(1)}, u32[]{:S(2)}, u32[]{:S(2)}) collective-permute-start(bf16[2,128,512]{2,1,0:T(8,128)(2,1)S(1)} %fusion.3), channel_id=1, source_target_pairs={{2,0},{10,8},{18,16},{26,24},{3,1},{11,9},{19,17},{27,25}} | collective-permute-start | bytes 786440 | tf_op jit(solution)/shard_map/ppermute | solution.py:47
  132.7 21.3 %collective-permute-start.11 = (bf16[2,128,512]{2,1,0:T(8,128)(2,1)S(1)}, bf16[2,128,512]{2,1,0:T(8,128)(2,1)S(1)}, u32[]{:S(2)}, u32[]{:S(2)}) collective-permute-start(bf16[2,128,512]{2,1,0:T(8,128)(2,1)S(1)} %pad_maximum_fusion.6), channel_id=1, source_target_pairs={{0,2},{2,4},{4,6},{6,8},{8,10},{10,12},{12,14},{14,16},{16,18},{18... | collective-permute-start | bytes 786440 | tf_op jit(solution)/shard_map/ppermute | solution.py:60
  135.8 18.2 %collective-permute-start.12 = (bf16[2,128,512]{2,1,0:T(8,128)(2,1)S(1)}, bf16[2,128,512]{2,1,0:T(8,128)(2,1)S(1)}, u32[]{:S(2)}, u32[]{:S(2)}) collective-permute-start(bf16[2,128,512]{2,1,0:T(8,128)(2,1)S(1)} %pad_maximum_fusion.7), channel_id=1, source_target_pairs={{2,0},{4,2},{6,4},{8,6},{10,8},{12,10},{14,12},{16,14},{18,16},{20... | collective-permute-start | bytes 786440 | tf_op jit(solution)/shard_map/ppermute | solution.py:60
  154.0 46.6 %copy-start.9 = (bf16[2,128,512]{2,1,0:T(8,128)(2,1)}, bf16[2,128,512]{2,1,0:T(8,128)(2,1)S(1)}, u32[]{:S(2)}) copy-start(bf16[2,128,512]{2,1,0:T(8,128)(2,1)S(1)} %collective-permute-done.12) | copy-start | bytes 786436
  154.0 90.8 %all-to-all-start.1 = ((bf16[16,128,512]{2,1,0:T(8,128)(2,1)}), bf16[16,128,512]{2,1,0:T(8,128)(2,1)S(1)}, u32[]{:S(2)}, u32[]{:S(2)}) async-start(bf16[16,128,512]{2,1,0:T(8,128)(2,1)} %get-tuple-element.33), calls=%async_computation.1 | async-start | bytes 4194304 | tf_op jit(solution)/shard_map/all_to_all | solution.py:321
  200.7 8.7 %copy-start.4 = (f32[16,128,512]{2,1,0:T(8,128)S(1)}, f32[16,128,512]{2,1,0:T(8,128)}, u32[]{:S(2)}) copy-start(f32[16,128,512]{2,1,0:T(8,128)} %get-tuple-element.38) | copy-start | bytes 12582916
  205.2 21.3 %collective-permute-start.15 = (bf16[2,128,512]{2,1,0:T(8,128)(2,1)}, bf16[2,128,512]{2,1,0:T(8,128)(2,1)}, u32[]{:S(2)}, u32[]{:S(2)}) collective-permute-start(bf16[2,128,512]{2,1,0:T(8,128)(2,1)} %convert_element_type.134), channel_id=1, source_target_pairs={{24,0},{25,1}} | collective-permute-start | bytes 786440 | tf_op jit(solution)/shard_map/ppermute | solution.py:47
  206.5 33.0 %collective-permute-start.14 = (bf16[2,128,512]{2,1,0:T(8,128)(2,1)}, bf16[2,128,512]{2,1,0:T(8,128)(2,1)}, u32[]{:S(2)}, u32[]{:S(2)}) collective-permute-start(bf16[2,128,512]{2,1,0:T(8,128)(2,1)} %convert_element_type.134), channel_id=1, source_target_pairs={{16,0},{17,1}} | collective-permute-start | bytes 786440 | tf_op jit(solution)/shard_map/ppermute | solution.py:47
  207.8 31.7 %collective-permute-start.13 = (bf16[2,128,512]{2,1,0:T(8,128)(2,1)}, bf16[2,128,512]{2,1,0:T(8,128)(2,1)}, u32[]{:S(2)}, u32[]{:S(2)}) collective-permute-start(bf16[2,128,512]{2,1,0:T(8,128)(2,1)} %convert_element_type.134), channel_id=1, source_target_pairs={{8,0},{9,1}} | collective-permute-start | bytes 786440 | tf_op jit(solution)/shard_map/ppermute | solution.py:47
  (5 other events, 12.2 us)

commit v16 on v13

--- a/solution.py
+++ b/solution.py
@@ -14,7 +14,7 @@
 STAT_ROWS = 16
 
 
-RADIX = 4
+RADIX = 8
 
 
 def spread_2(array, axis, root):

time: 241 us -> 254 us (1.054)
  waiting for transfers between devices: 103 us -> 111 us
  starting transfers between devices: 36.5 us -> 40.9 us
    ppermute x4, waiting for transfers between devices: 86.5 us -> 93.1 us  [shift(): return lax.ppermute(array, axis, pairs)]
    ppermute x4, starting transfers between devices: 13.8 us -> 17 us  [shift(): return lax.ppermute(array, axis, pairs)]
    ppermute x6 -> x8, starting transfers between devices: 4.68 us -> 6.01 us  [spread_2(): lax.ppermute(array, axis, [(i, i + j * step) for i in range(0, count, RAD...]
    ppermute x6 -> x8, starting transfers between devices: 4.69 us -> 6.02 us  [gather_to_root(): lax.ppermute(sent, axis, [(i + j * step, i) for i in range(0, count, RADI...]
  transfers between devices with their start and end apart: 18 -> 22, of which waited for: 2 -> 3; matrix products, arithmetic and copies ran while one was open for 13% -> 13% of each run, Pallas kernels for 23% -> 22%
where the time goes in v16:
time: 254 us; the launch traced here: 253 us
  waiting for transfers between devices  111 us (44%)
  Pallas kernels  55.2 us (22%)
  starting transfers between devices  40.9 us (16%)
  other arithmetic  35 us (14%)
  local copies, waits for them, and re-layouts  9.34 us (4%)
    ppermute x4, waiting for transfers between devices, shift(): return lax.ppermute(array, axis, pairs)  93.1 us
    pallas_call x3, Pallas kernels, list_pairs(): pl.pallas_call(list_kernel, grid_spec=grid_spec, out_shape=[jax.ShapeDtyp...  34 us
    pallas_call x1, Pallas kernels, rand_pairs(): pl.pallas_call(functools.partial(rand_kernel, heads), grid_spec=grid_spec...  21.1 us
    ppermute x4, starting transfers between devices, shift(): return lax.ppermute(array, axis, pairs)  17 us
    all_to_all x1, waiting for transfers between devices, shards(): lax.all_to_all(dq_rand, 'ctx', split_axis=0, concat_axis=0, tiled=True)  15.9 us
    all_to_all x1, starting transfers between devices, shards(): lax.all_to_all(routed, 'ctx', split_axis=0, concat_axis=0, tiled=True)  6.69 us
    ppermute x8, starting transfers between devices, gather_to_root(): lax.ppermute(sent, axis, [(i + j * step, i) for i in range(0, count, RADI...  6.02 us
    ppermute x8, starting transfers between devices, spread_2(): lax.ppermute(array, axis, [(i, i + j * step) for i in range(0, count, RAD...  6.01 us
  transfers between devices with their start and end apart: 22, of which 3 were waited for; matrix products, arithmetic and copies ran while one was open for 13% of the time, Pallas kernels for 22%

profile of v16, /device:TPU:11, one launch (start us, length us, event | category | flops | bytes accessed | tf_op | source)
XLA Modules:
  0.0 252.8 jit_solution(4072829925535974960)
XLA Ops:
  2.4 1.3 convert_multiply_fusion
  5.9 3.0 %select_add_fusion = bf16[16,272,512]{2,1,0:T(8,128)(2,1)} fusion(pred[16]{0:T(512)(128)(4,1)S(1)} %get-tuple-element.75, pred[16]{0:T(512)(128)(4,1)S(1)} %get-tuple-element.76, pred[16]{0:T(512)(128)(4,1)S(1)} %get-tuple-element.77, pred[16]{0:T(512)(128)(4,1)S(1)} %get-tuple-element.74, bf16[272,512]{1,0:T(8,128)(2,1)S(1)} %get-tuple-element.49, ...), kind=kLoop, calls=%fused_computation.3 | loop fusion | flops 17825792 | bytes 5579328 | tf_op jit(solution)/shard_map/add | solution.py:310
  9.0 6.7 %all-to-all-start = ((bf16[16,272,512]{2,1,0:T(8,128)(2,1)}), bf16[16,272,512]{2,1,0:T(8,128)(2,1)}, u32[]{:S(2)}, u32[]{:S(2)}) async-start(bf16[16,272,512]{2,1,0:T(8,128)(2,1)} %select_add_fusion), calls=%async_computation | async-start | bytes 8912896 | tf_op jit(solution)/shard_map/all_to_all | solution.py:311
  16.5 2.3 collective-permute-start.9
  23.5 93.1 %collective-permute-done.9 = bf16[2,128,512]{2,1,0:T(8,128)(2,1)S(1)} collective-permute-done((bf16[2,128,512]{2,1,0:T(8,128)(2,1)S(1)}, bf16[2,128,512]{2,1,0:T(8,128)(2,1)S(1)}, u32[]{:S(2)}, u32[]{:S(2)}) %collective-permute-start.9) | collective-permute-done | bytes 262176 | tf_op jit(solution)/shard_map/ppermute | solution.py:58
  120.4 3.6 %collective-permute-start.8 = (bf16[2,128,512]{2,1,0:T(8,128)(2,1)S(1)}, bf16[2,128,512]{2,1,0:T(8,128)(2,1)S(1)}, u32[]{:S(2)}, u32[]{:S(2)}) collective-permute-start(bf16[2,128,512]{2,1,0:T(8,128)(2,1)S(1)} %pad_maximum_fusion.4), channel_id=1, source_target_pairs={{0,2},{2,4},{4,6},{6,8},{8,10},{10,12},{12,14},{14,16},{16,18},{18... | collective-permute-start | bytes 786440 | tf_op jit(solution)/shard_map/ppermute | solution.py:58
  126.5 11.3 %shard_map.95 = (f32[512,512]{1,0:T(8,128)}, f32[512,512]{1,0:T(8,128)}, f32[512,512]{1,0:T(8,128)}) custom-call(s32[4]{0:T(128)} %iota.37.qin.qout, s32[4]{0:T(128)} %iota.37.qin.qout, s32[4]{0:T(128)} %broadcast_25_first.2.first, s32[4]{0:T(128)} %broadcast_24_ktab.2.ktab, s32[4]{0:T(128)} %compare_convert_fusion.2.mtab, bf16[512,512]{1,0:T(8,128)(2,1)} %q_ref.5, ...), custom_call_target="tpu_custom_call" | custom-call | tf_op jit(solution)/shard_map/pallas_call | solution.py:154
  137.8 1.3 reduce_sum.66
  139.2 1.3 reduce_sum.65
  140.5 1.3 collective-permute-start.16
  145.6 2.1 collective-permute-done.16
  151.1 7.0 %shard_map.96 = (f32[256,512]{1,0:T(8,128)}, f32[256,512]{1,0:T(8,128)}, f32[256,512]{1,0:T(8,128)}) custom-call(s32[2]{0:T(128)} %iota_multiply_fusion.qin, s32[2]{0:T(128)} %iota.42.qout, s32[2]{0:T(128)} %broadcast_26_first.2.first, s32[2]{0:T(128)} %get-tuple-element.81.ktab, s32[2]{0:T(128)} %get-tuple-element.82.mtab, bf16[512,512]{1,0:T(8,128)(2,1)} %q_ref.5, ...), custom_call_target="tpu_custom_call" | custom-call | tf_op jit(solution)/shard_map/pallas_call | solution.py:154
  161.2 9.2 %collective-permute-start.18 = (bf16[2,128,512]{2,1,0:T(8,128)(2,1)S(1)}, bf16[2,128,512]{2,1,0:T(8,128)(2,1)S(1)}, u32[]{:S(2)}, u32[]{:S(2)}) collective-permute-start(bf16[2,128,512]{2,1,0:T(8,128)(2,1)S(1)} %pad_maximum_fusion.6), channel_id=1, source_target_pairs={{0,2},{2,4},{4,6},{6,8},{8,10},{10,12},{12,14},{14,16},{16,18},{18... | collective-permute-start | bytes 786440 | tf_op jit(solution)/shard_map/ppermute | solution.py:58
  170.5 1.9 collective-permute-start.19
  175.6 21.1 %shard_map.97 = (bf16[16,128,512]{2,1,0:T(8,128)(2,1)}, f32[16,128,512]{2,1,0:T(8,128)}, f32[16,128,512]{2,1,0:T(8,128)}) custom-call(s32[16]{0:T(128)} %add_maximum_fusion.ktab, s32[16]{0:T(128)} %compare_convert_fusion.1.mtab, bf16[16,272,512]{2,1,0:T(8,128)(2,1)} %all-to-all-done.q_ref.do_ref.st_ref, ...), custom_call_target="tpu_custom_call" | custom-call | tf_op jit(solution)/shard_map/pallas_call | solution.py:186
  196.7 5.2 %all-to-all-start.1 = ((bf16[16,128,512]{2,1,0:T(8,128)(2,1)}), bf16[16,128,512]{2,1,0:T(8,128)(2,1)S(1)}, u32[]{:S(2)}, u32[]{:S(2)}) async-start(bf16[16,128,512]{2,1,0:T(8,128)(2,1)} %get-tuple-element.27), calls=%async_computation.1 | async-start | bytes 4194304 | tf_op jit(solution)/shard_map/all_to_all | solution.py:321
  202.1 15.8 %shard_map.94 = (f32[512,512]{1,0:T(8,128)}, f32[768,512]{1,0:T(8,128)}, f32[768,512]{1,0:T(8,128)}) custom-call(s32[6]{0:T(128)} %constant.33.clone.1.qin.qout, s32[6]{0:T(128)} %constant.33.clone.1.qin.qout, s32[6]{0:T(128)} %constant.34.clone.1.first, s32[6]{0:T(128)} %constant.35.clone.1.ktab, s32[6]{0:T(128)} %constant.36.clone.1.mtab, ...), custom_call_target="tpu_custom_call" | custom-call | tf_op jit(solution)/shard_map/pallas_call | solution.py:154
  217.9 2.2 add_bitcast_fusion
  221.7 2.5 bitcast_add_fusion.3
  224.2 5.1 %multiply_reduce_fusion = (f32[4,128,512]{2,1,0:T(8,128)S(1)}, f32[4,128,512]{2,1,0:T(8,128)S(1)}) fusion(f32[16,128,512]{2,1,0:T(8,128)} %get-tuple-element.34, f32[16,4]{1,0:T(8,128)S(1)} %compare_convert_fusion, f32[16,128,512]{2,1,0:T(8,128)S(1)} %copy-done.4), kind=kLoop, calls=%fused_computation | loop fusion | flops 16252928 | bytes 10486016 | tf_op jit(solution)/shard_map/reduce_sum | solution.py:328
  229.3 2.2 fusion
  231.4 2.1 fusion.1
  233.5 15.9 %all-to-all-done.1 = bf16[16,128,512]{2,1,0:T(8,128)(2,1)S(1)} async-done(((bf16[16,128,512]{2,1,0:T(8,128)(2,1)}), bf16[16,128,512]{2,1,0:T(8,128)(2,1)S(1)}, u32[]{:S(2)}, u32[]{:S(2)}) %all-to-all-start.1) | async-done | bytes 2097184 | tf_op jit(solution)/shard_map/all_to_all | solution.py:321
  250.0 1.4 multiply_reduce_fusion.2
  (120 shorter events, 32.7 us)
Async XLA Ops:
  9.0 110.2 %copy-start.11 = (bf16[4,512]{1,0:T(4,128)(2,1)S(1)}, bf16[4,512]{1,0:T(4,128)(2,1)}, u32[]{:S(2)}) copy-start(bf16[4,512]{1,0:T(4,128)(2,1)} %param.12) | copy-start | bytes 12292
  9.0 164.3 %all-to-all-start = ((bf16[16,272,512]{2,1,0:T(8,128)(2,1)}), bf16[16,272,512]{2,1,0:T(8,128)(2,1)}, u32[]{:S(2)}, u32[]{:S(2)}) async-start(bf16[16,272,512]{2,1,0:T(8,128)(2,1)} %select_add_fusion), calls=%async_computation | async-start | bytes 8912896 | tf_op jit(solution)/shard_map/all_to_all | solution.py:311
  15.8 3.7 %collective-permute-start = (bf16[2,128,512]{2,1,0:T(8,128)(2,1)S(1)}, bf16[2,128,512]{2,1,0:T(8,128)(2,1)S(1)}, u32[]{:S(2)}, u32[]{:S(2)}) collective-permute-start(bf16[2,128,512]{2,1,0:T(8,128)(2,1)S(1)} %maximum_select_fusion), channel_id=1, source_target_pairs={{0,16},{1,17}} | collective-permute-start | bytes 786440 | tf_op jit(solution)/shard_map/ppermute | solution.py:29
  16.5 100.0 %collective-permute-start.9 = (bf16[2,128,512]{2,1,0:T(8,128)(2,1)S(1)}, bf16[2,128,512]{2,1,0:T(8,128)(2,1)S(1)}, u32[]{:S(2)}, u32[]{:S(2)}) collective-permute-start(bf16[2,128,512]{2,1,0:T(8,128)(2,1)S(1)} %pad_maximum_fusion.5), channel_id=1, source_target_pairs={{2,0},{4,2},{6,4},{8,6},{10,8},{12,10},{14,12},{16,14},{18,16},{20... | collective-permute-start | bytes 786440 | tf_op jit(solution)/shard_map/ppermute | solution.py:58
  19.6 97.7 %collective-permute-start.7 = (bf16[2,128,512]{2,1,0:T(8,128)(2,1)S(1)}, bf16[2,128,512]{2,1,0:T(8,128)(2,1)S(1)}, u32[]{:S(2)}, u32[]{:S(2)}) collective-permute-start(bf16[2,128,512]{2,1,0:T(8,128)(2,1)S(1)} %fusion.20), channel_id=1, source_target_pairs={{0,14},{16,30},{1,15},{17,31}} | collective-permute-start | bytes 786440 | tf_op jit(solution)/shard_map/ppermute | solution.py:29
  20.9 97.1 %collective-permute-start.6 = (bf16[2,128,512]{2,1,0:T(8,128)(2,1)S(1)}, bf16[2,128,512]{2,1,0:T(8,128)(2,1)S(1)}, u32[]{:S(2)}, u32[]{:S(2)}) collective-permute-start(bf16[2,128,512]{2,1,0:T(8,128)(2,1)S(1)} %fusion.20), channel_id=1, source_target_pairs={{0,12},{16,28},{1,13},{17,29}} | collective-permute-start | bytes 786440 | tf_op jit(solution)/shard_map/ppermute | solution.py:29
  22.1 98.3 %collective-permute-start.5 = (bf16[2,128,512]{2,1,0:T(8,128)(2,1)S(1)}, bf16[2,128,512]{2,1,0:T(8,128)(2,1)S(1)}, u32[]{:S(2)}, u32[]{:S(2)}) collective-permute-start(bf16[2,128,512]{2,1,0:T(8,128)(2,1)S(1)} %fusion.20), channel_id=1, source_target_pairs={{0,10},{16,26},{1,11},{17,27}} | collective-permute-start | bytes 786440 | tf_op jit(solution)/shard_map/ppermute | solution.py:29
  22.8 101.2 %collective-permute-start.4 = (bf16[2,128,512]{2,1,0:T(8,128)(2,1)S(1)}, bf16[2,128,512]{2,1,0:T(8,128)(2,1)S(1)}, u32[]{:S(2)}, u32[]{:S(2)}) collective-permute-start(bf16[2,128,512]{2,1,0:T(8,128)(2,1)S(1)} %fusion.20), channel_id=1, source_target_pairs={{0,8},{16,24},{1,9},{17,25}} | collective-permute-start | bytes 786440 | tf_op jit(solution)/shard_map/ppermute | solution.py:29
  116.5 7.4 %collective-permute-start.3 = (bf16[2,128,512]{2,1,0:T(8,128)(2,1)S(1)}, bf16[2,128,512]{2,1,0:T(8,128)(2,1)S(1)}, u32[]{:S(2)}, u32[]{:S(2)}) collective-permute-start(bf16[2,128,512]{2,1,0:T(8,128)(2,1)S(1)} %fusion.20), channel_id=1, source_target_pairs={{0,6},{16,22},{1,7},{17,23}} | collective-permute-start | bytes 786440 | tf_op jit(solution)/shard_map/ppermute | solution.py:29
  117.2 6.8 %collective-permute-start.2 = (bf16[2,128,512]{2,1,0:T(8,128)(2,1)S(1)}, bf16[2,128,512]{2,1,0:T(8,128)(2,1)S(1)}, u32[]{:S(2)}, u32[]{:S(2)}) collective-permute-start(bf16[2,128,512]{2,1,0:T(8,128)(2,1)S(1)} %fusion.20), channel_id=1, source_target_pairs={{0,4},{16,20},{1,5},{17,21}} | collective-permute-start | bytes 786440 | tf_op jit(solution)/shard_map/ppermute | solution.py:29
  117.9 6.1 %collective-permute-start.1 = (bf16[2,128,512]{2,1,0:T(8,128)(2,1)S(1)}, bf16[2,128,512]{2,1,0:T(8,128)(2,1)S(1)}, u32[]{:S(2)}, u32[]{:S(2)}) collective-permute-start(bf16[2,128,512]{2,1,0:T(8,128)(2,1)S(1)} %fusion.20), channel_id=1, source_target_pairs={{0,2},{16,18},{1,3},{17,19}} | collective-permute-start | bytes 786440 | tf_op jit(solution)/shard_map/ppermute | solution.py:29
  120.4 22.1 %collective-permute-start.8 = (bf16[2,128,512]{2,1,0:T(8,128)(2,1)S(1)}, bf16[2,128,512]{2,1,0:T(8,128)(2,1)S(1)}, u32[]{:S(2)}, u32[]{:S(2)}) collective-permute-start(bf16[2,128,512]{2,1,0:T(8,128)(2,1)S(1)} %pad_maximum_fusion.4), channel_id=1, source_target_pairs={{0,2},{2,4},{4,6},{6,8},{8,10},{10,12},{12,14},{14,16},{16,18},{18... | collective-permute-start | bytes 786440 | tf_op jit(solution)/shard_map/ppermute | solution.py:58
  140.5 7.1 %collective-permute-start.16 = (bf16[2,128,512]{2,1,0:T(8,128)(2,1)S(1)}, bf16[2,128,512]{2,1,0:T(8,128)(2,1)S(1)}, u32[]{:S(2)}, u32[]{:S(2)}) collective-permute-start(bf16[2,128,512]{2,1,0:T(8,128)(2,1)S(1)} %fusion.3), channel_id=1, source_target_pairs={{14,0},{30,16},{15,1},{31,17}} | collective-permute-start | bytes 786440 | tf_op jit(solution)/shard_map/ppermute | solution.py:45
  141.8 6.5 %collective-permute-start.15 = (bf16[2,128,512]{2,1,0:T(8,128)(2,1)S(1)}, bf16[2,128,512]{2,1,0:T(8,128)(2,1)S(1)}, u32[]{:S(2)}, u32[]{:S(2)}) collective-permute-start(bf16[2,128,512]{2,1,0:T(8,128)(2,1)S(1)} %fusion.3), channel_id=1, source_target_pairs={{12,0},{28,16},{13,1},{29,17}} | collective-permute-start | bytes 786440 | tf_op jit(solution)/shard_map/ppermute | solution.py:45
  143.5 15.6 %collective-permute-start.14 = (bf16[2,128,512]{2,1,0:T(8,128)(2,1)S(1)}, bf16[2,128,512]{2,1,0:T(8,128)(2,1)S(1)}, u32[]{:S(2)}, u32[]{:S(2)}) collective-permute-start(bf16[2,128,512]{2,1,0:T(8,128)(2,1)S(1)} %fusion.3), channel_id=1, source_target_pairs={{10,0},{26,16},{11,1},{27,17}} | collective-permute-start | bytes 786440 | tf_op jit(solution)/shard_map/ppermute | solution.py:45
  144.2 14.9 %collective-permute-start.13 = (bf16[2,128,512]{2,1,0:T(8,128)(2,1)S(1)}, bf16[2,128,512]{2,1,0:T(8,128)(2,1)S(1)}, u32[]{:S(2)}, u32[]{:S(2)}) collective-permute-start(bf16[2,128,512]{2,1,0:T(8,128)(2,1)S(1)} %fusion.3), channel_id=1, source_target_pairs={{8,0},{24,16},{9,1},{25,17}} | collective-permute-start | bytes 786440 | tf_op jit(solution)/shard_map/ppermute | solution.py:45
  144.9 14.2 %collective-permute-start.12 = (bf16[2,128,512]{2,1,0:T(8,128)(2,1)S(1)}, bf16[2,128,512]{2,1,0:T(8,128)(2,1)S(1)}, u32[]{:S(2)}, u32[]{:S(2)}) collective-permute-start(bf16[2,128,512]{2,1,0:T(8,128)(2,1)S(1)} %fusion.3), channel_id=1, source_target_pairs={{6,0},{22,16},{7,1},{23,17}} | collective-permute-start | bytes 786440 | tf_op jit(solution)/shard_map/ppermute | solution.py:45
  147.6 11.5 %collective-permute-start.11 = (bf16[2,128,512]{2,1,0:T(8,128)(2,1)S(1)}, bf16[2,128,512]{2,1,0:T(8,128)(2,1)S(1)}, u32[]{:S(2)}, u32[]{:S(2)}) collective-permute-start(bf16[2,128,512]{2,1,0:T(8,128)(2,1)S(1)} %fusion.3), channel_id=1, source_target_pairs={{4,0},{20,16},{5,1},{21,17}} | collective-permute-start | bytes 786440 | tf_op jit(solution)/shard_map/ppermute | solution.py:45
  148.3 10.8 %collective-permute-start.10 = (bf16[2,128,512]{2,1,0:T(8,128)(2,1)S(1)}, bf16[2,128,512]{2,1,0:T(8,128)(2,1)S(1)}, u32[]{:S(2)}, u32[]{:S(2)}) collective-permute-start(bf16[2,128,512]{2,1,0:T(8,128)(2,1)S(1)} %fusion.3), channel_id=1, source_target_pairs={{2,0},{18,16},{3,1},{19,17}} | collective-permute-start | bytes 786440 | tf_op jit(solution)/shard_map/ppermute | solution.py:45
  159.4 13.0 %collective-permute-start.17 = (bf16[2,128,512]{2,1,0:T(8,128)(2,1)S(1)}, bf16[2,128,512]{2,1,0:T(8,128)(2,1)S(1)}, u32[]{:S(2)}, u32[]{:S(2)}) collective-permute-start(bf16[2,128,512]{2,1,0:T(8,128)(2,1)S(1)} %get-tuple-element.37), channel_id=1, source_target_pairs={{16,0},{17,1}} | collective-permute-start | bytes 786440 | tf_op jit(solution)/shard_map/ppermute | solution.py:45
  161.2 35.5 %collective-permute-start.18 = (bf16[2,128,512]{2,1,0:T(8,128)(2,1)S(1)}, bf16[2,128,512]{2,1,0:T(8,128)(2,1)S(1)}, u32[]{:S(2)}, u32[]{:S(2)}) collective-permute-start(bf16[2,128,512]{2,1,0:T(8,128)(2,1)S(1)} %pad_maximum_fusion.6), channel_id=1, source_target_pairs={{0,2},{2,4},{4,6},{6,8},{8,10},{10,12},{12,14},{14,16},{16,18},{18... | collective-permute-start | bytes 786440 | tf_op jit(solution)/shard_map/ppermute | solution.py:58
  170.5 26.2 %collective-permute-start.19 = (bf16[2,128,512]{2,1,0:T(8,128)(2,1)S(1)}, bf16[2,128,512]{2,1,0:T(8,128)(2,1)S(1)}, u32[]{:S(2)}, u32[]{:S(2)}) collective-permute-start(bf16[2,128,512]{2,1,0:T(8,128)(2,1)S(1)} %pad_maximum_fusion.7), channel_id=1, source_target_pairs={{2,0},{4,2},{6,4},{8,6},{10,8},{12,10},{14,12},{16,14},{18,16},{20... | collective-permute-start | bytes 786440 | tf_op jit(solution)/shard_map/ppermute | solution.py:58
  196.7 23.4 %copy-start.10 = (bf16[2,128,512]{2,1,0:T(8,128)(2,1)}, bf16[2,128,512]{2,1,0:T(8,128)(2,1)S(1)}, u32[]{:S(2)}) copy-start(bf16[2,128,512]{2,1,0:T(8,128)(2,1)S(1)} %collective-permute-done.19) | copy-start | bytes 786436
  196.7 52.7 %all-to-all-start.1 = ((bf16[16,128,512]{2,1,0:T(8,128)(2,1)}), bf16[16,128,512]{2,1,0:T(8,128)(2,1)S(1)}, u32[]{:S(2)}, u32[]{:S(2)}) async-start(bf16[16,128,512]{2,1,0:T(8,128)(2,1)} %get-tuple-element.27), calls=%async_computation.1 | async-start | bytes 4194304 | tf_op jit(solution)/shard_map/all_to_all | solution.py:321
  (10 other events, 60.1 us)

commit v17 on v13

--- a/solution.py
+++ b/solution.py
@@ -102,7 +102,7 @@
         dv_ref[:, cols] = dv
 
 
-def rand_kernel(heads, ktab, mtab, q_ref, do_ref, st_ref, k_ref, v_ref, dq_ref, dk_ref, dv_ref):
+def rand_kernel(heads, ftab, ktab, mtab, q_ref, do_ref, st_ref, k_ref, v_ref, dq_ref, dk_ref, dv_ref):
     p = pl.program_id(0)
     mode = mtab[p]
     width = q_ref.shape[2] // heads
@@ -162,25 +162,25 @@
     )(qin, qout, first, ktab, mtab, queries, out_grad, norm3, delta3, key_src, value_src)
 
 
-def rand_pairs(ktab, mtab, arrived, key_rows, value_rows, heads):
+def rand_pairs(ftab, ktab, mtab, arrived, key_rows, value_rows, heads):
     items, packed_rows, features = arrived.shape
     height = (packed_rows - STAT_ROWS) // 2
     grid_spec = pltpu.PrefetchScalarGridSpec(
-        num_scalar_prefetch=2,
+        num_scalar_prefetch=3,
         grid=(items,),
         in_specs=[
-            pl.BlockSpec((1, height, features), lambda p, kt, mt: (p, 0, 0)),
-            pl.BlockSpec((1, height, features), lambda p, kt, mt: (p, 1, 0)),
+            pl.BlockSpec((1, height, features), lambda p, ft, kt, mt: (ft[p], 0, 0)),
+            pl.BlockSpec((1, height, features), lambda p, ft, kt, mt: (ft[p], 1, 0)),
             pl.BlockSpec(
-                (1, STAT_ROWS, features), lambda p, kt, mt: (p, 2 * height // STAT_ROWS, 0)
+                (1, STAT_ROWS, features), lambda p, ft, kt, mt: (ft[p], 2 * height // STAT_ROWS, 0)
             ),
-            pl.BlockSpec((height, features), lambda p, kt, mt: (kt[p], 0)),
-            pl.BlockSpec((height, features), lambda p, kt, mt: (kt[p], 0)),
+            pl.BlockSpec((height, features), lambda p, ft, kt, mt: (kt[p], 0)),
+            pl.BlockSpec((height, features), lambda p, ft, kt, mt: (kt[p], 0)),
         ],
         out_specs=[
-            pl.BlockSpec((1, height, features), lambda p, kt, mt: (p, 0, 0)),
-            pl.BlockSpec((1, height, features), lambda p, kt, mt: (p, 0, 0)),
-            pl.BlockSpec((1, height, features), lambda p, kt, mt: (p, 0, 0)),
+            pl.BlockSpec((1, height, features), lambda p, ft, kt, mt: (p, 0, 0)),
+            pl.BlockSpec((1, height, features), lambda p, ft, kt, mt: (p, 0, 0)),
+            pl.BlockSpec((1, height, features), lambda p, ft, kt, mt: (p, 0, 0)),
         ],
     )
     return pl.pallas_call(
@@ -191,7 +191,7 @@
             jax.ShapeDtypeStruct((items, height, features), jnp.float32),
             jax.ShapeDtypeStruct((items, height, features), jnp.float32),
         ],
-    )(ktab, mtab, arrived, arrived, arrived, key_rows, value_rows)
+    )(ftab, ktab, mtab, arrived, arrived, arrived, key_rows, value_rows)
 
 
 def shards(queries, key_rows, values, outputs, out_grad, log_norm, rand_blocks):
@@ -312,7 +312,9 @@
     slot_recv = arrived[:, 2 * height + 2, 0].astype(jnp.float32).astype(jnp.int32)
     ktab_r = jnp.maximum(slot_recv - 1, 0)
     mtab_r = (slot_recv > 0).astype(jnp.int32)
-    dq_rand, dk_rand, dv_rand = rand_pairs(ktab_r, mtab_r, arrived, key_rows, values, heads)
+    item_ids = jnp.arange(ctx_size, dtype=jnp.int32)
+    ftab_r = lax.cummax(jnp.where(mtab_r > 0, item_ids, 0), axis=0)
+    dq_rand, dk_rand, dv_rand = rand_pairs(ftab_r, ktab_r, mtab_r, arrived, key_rows, values, heads)
     dq_rand, total, back_left, back_right = lax.optimization_barrier(
         (dq_rand, total, back_left, back_right)
     )

time: 241 us -> 244 us (1.012)
  transfers between devices with their start and end apart: 18 -> 18, of which waited for: 2 -> 2; matrix products, arithmetic and copies ran while one was open for 13% -> 14% of each run, Pallas kernels for 23% -> 23%
where the time goes in v17:
time: 244 us; the launch traced here: 243 us
  waiting for transfers between devices  103 us (42%)
  Pallas kernels  55.3 us (23%)
  starting transfers between devices  37.2 us (15%)
  other arithmetic  35.7 us (15%)
  local copies, waits for them, and re-layouts  10.1 us (4%)
    ppermute x4, waiting for transfers between devices, shift(): return lax.ppermute(array, axis, pairs)  86.5 us
    pallas_call x3, Pallas kernels, list_pairs(): pl.pallas_call(list_kernel, grid_spec=grid_spec, out_shape=[jax.ShapeDtyp...  34.1 us
    pallas_call x1, Pallas kernels, rand_pairs(): pl.pallas_call(functools.partial(rand_kernel, heads), grid_spec=grid_spec...  21.2 us
    all_to_all x1, waiting for transfers between devices, shards(): lax.all_to_all(dq_rand, 'ctx', split_axis=0, concat_axis=0, tiled=True)  16.8 us
    ppermute x4, starting transfers between devices, shift(): return lax.ppermute(array, axis, pairs)  13.8 us
    all_to_all x1, starting transfers between devices, shards(): lax.all_to_all(dq_rand, 'ctx', split_axis=0, concat_axis=0, tiled=True)  7.42 us
    all_to_all x1, starting transfers between devices, shards(): lax.all_to_all(routed, 'ctx', split_axis=0, concat_axis=0, tiled=True)  6.69 us
    reduce_sum x1, other arithmetic, shards(): rand_value = jnp.sum(choose[:, :, None, None] * dv_rand[:, None], axis=0)  5.09 us
  transfers between devices with their start and end apart: 18, of which 2 were waited for; matrix products, arithmetic and copies ran while one was open for 14% of the time, Pallas kernels for 23%

profile of v17, /device:TPU:11, one launch (start us, length us, event | category | flops | bytes accessed | tf_op | source)
XLA Modules:
  0.0 242.8 jit_solution(2419088827706275586)
XLA Ops:
  2.4 1.3 convert_multiply_fusion
  5.9 3.0 %select_add_fusion = bf16[16,272,512]{2,1,0:T(8,128)(2,1)} fusion(pred[16]{0:T(512)(128)(4,1)S(1)} %get-tuple-element.73, pred[16]{0:T(512)(128)(4,1)S(1)} %get-tuple-element.74, pred[16]{0:T(512)(128)(4,1)S(1)} %get-tuple-element.75, pred[16]{0:T(512)(128)(4,1)S(1)} %get-tuple-element.72, bf16[272,512]{1,0:T(8,128)(2,1)S(1)} %get-tuple-element.47, ...), kind=kLoop, calls=%fused_computation.3 | loop fusion | flops 17825792 | bytes 5579328 | tf_op jit(solution)/shard_map/add | solution.py:310
  9.0 6.7 %all-to-all-start = ((bf16[16,272,512]{2,1,0:T(8,128)(2,1)}), bf16[16,272,512]{2,1,0:T(8,128)(2,1)}, u32[]{:S(2)}, u32[]{:S(2)}) async-start(bf16[16,272,512]{2,1,0:T(8,128)(2,1)} %select_add_fusion), calls=%async_computation | async-start | bytes 8912896 | tf_op jit(solution)/shard_map/all_to_all | solution.py:311
  17.9 2.3 collective-permute-start.7
  20.2 4.2 %collective-permute-start.6 = (bf16[2,128,512]{2,1,0:T(8,128)(2,1)S(1)}, bf16[2,128,512]{2,1,0:T(8,128)(2,1)S(1)}, u32[]{:S(2)}, u32[]{:S(2)}) collective-permute-start(bf16[2,128,512]{2,1,0:T(8,128)(2,1)S(1)} %pad_maximum_fusion.4), channel_id=1, source_target_pairs={{0,2},{2,4},{4,6},{6,8},{8,10},{10,12},{12,14},{14,16},{16,18},{18... | collective-permute-start | bytes 786440 | tf_op jit(solution)/shard_map/ppermute | solution.py:58
  30.0 86.4 %collective-permute-done.7 = bf16[2,128,512]{2,1,0:T(8,128)(2,1)S(1)} collective-permute-done((bf16[2,128,512]{2,1,0:T(8,128)(2,1)S(1)}, bf16[2,128,512]{2,1,0:T(8,128)(2,1)S(1)}, u32[]{:S(2)}, u32[]{:S(2)}) %collective-permute-start.7) | collective-permute-done | bytes 262176 | tf_op jit(solution)/shard_map/ppermute | solution.py:58
  119.9 11.3 %shard_map.95 = (f32[512,512]{1,0:T(8,128)}, f32[512,512]{1,0:T(8,128)}, f32[512,512]{1,0:T(8,128)}) custom-call(s32[4]{0:T(128)} %iota.41.qin.qout, s32[4]{0:T(128)} %iota.41.qin.qout, s32[4]{0:T(128)} %broadcast_25_first.2.first, s32[4]{0:T(128)} %broadcast_24_ktab.2.ktab, s32[4]{0:T(128)} %compare_convert_fusion.3.mtab, bf16[512,512]{1,0:T(8,128)(2,1)} %q_ref.5, ...), custom_call_target="tpu_custom_call" | custom-call | tf_op jit(solution)/shard_map/pallas_call | solution.py:154
  131.2 1.3 reduce_sum.66
  132.6 1.3 reduce_sum.65
  133.9 1.3 collective-permute-start.10
  138.7 7.0 %shard_map.96 = (f32[256,512]{1,0:T(8,128)}, f32[256,512]{1,0:T(8,128)}, f32[256,512]{1,0:T(8,128)}) custom-call(s32[2]{0:T(128)} %iota_multiply_fusion.qin, s32[2]{0:T(128)} %iota.46.qout, s32[2]{0:T(128)} %broadcast_26_first.2.first, s32[2]{0:T(128)} %get-tuple-element.79.ktab, s32[2]{0:T(128)} %get-tuple-element.80.mtab, bf16[512,512]{1,0:T(8,128)(2,1)} %q_ref.5, ...), custom_call_target="tpu_custom_call" | custom-call | tf_op jit(solution)/shard_map/pallas_call | solution.py:154
  150.0 5.4 %collective-permute-start.14 = (bf16[2,128,512]{2,1,0:T(8,128)(2,1)S(1)}, bf16[2,128,512]{2,1,0:T(8,128)(2,1)S(1)}, u32[]{:S(2)}, u32[]{:S(2)}) collective-permute-start(bf16[2,128,512]{2,1,0:T(8,128)(2,1)S(1)} %pad_maximum_fusion.6), channel_id=1, source_target_pairs={{0,2},{2,4},{4,6},{6,8},{8,10},{10,12},{12,14},{14,16},{16,18},{18... | collective-permute-start | bytes 786440 | tf_op jit(solution)/shard_map/ppermute | solution.py:58
  155.5 1.9 collective-permute-start.15
  162.6 21.2 %shard_map.97 = (bf16[16,128,512]{2,1,0:T(8,128)(2,1)}, f32[16,128,512]{2,1,0:T(8,128)}, f32[16,128,512]{2,1,0:T(8,128)}) custom-call(s32[16]{0:T(128)} %reduce.1.ftab, s32[16]{0:T(128)} %add_maximum_fusion.ktab, s32[16]{0:T(128)} %compare_convert_fusion.2.mtab, bf16[16,272,512]{2,1,0:T(8,128)(2,1)} %all-to-all-done.q_ref.do_ref.st_ref, ...), custom_call_target="tpu_custom_call" | custom-call | tf_op jit(solution)/shard_map/pallas_call | solution.py:186
  184.6 7.4 %all-to-all-start.1 = ((bf16[16,128,512]{2,1,0:T(8,128)(2,1)}), bf16[16,128,512]{2,1,0:T(8,128)(2,1)S(1)}, u32[]{:S(2)}, u32[]{:S(2)}) async-start(bf16[16,128,512]{2,1,0:T(8,128)(2,1)} %get-tuple-element.27), calls=%async_computation.1 | async-start | bytes 4194304 | tf_op jit(solution)/shard_map/all_to_all | solution.py:323
  192.2 15.8 %shard_map.94 = (f32[512,512]{1,0:T(8,128)}, f32[768,512]{1,0:T(8,128)}, f32[768,512]{1,0:T(8,128)}) custom-call(s32[6]{0:T(128)} %constant.34.clone.1.qin.qout, s32[6]{0:T(128)} %constant.34.clone.1.qin.qout, s32[6]{0:T(128)} %constant.35.clone.1.first, s32[6]{0:T(128)} %constant.36.clone.1.ktab, s32[6]{0:T(128)} %constant.37.clone.1.mtab, ...), custom_call_target="tpu_custom_call" | custom-call | tf_op jit(solution)/shard_map/pallas_call | solution.py:154
  207.9 2.2 add_bitcast_fusion
  210.6 2.7 %bitcast_add_fusion.3 = (f32[1,128,512]{2,1,0:T(8,128)}, f32[1,128,512]{2,1,0:T(8,128)}, f32[1,128,512]{2,1,0:T(8,128)}, f32[1,128,512]{2,1,0:T(8,128)S(1)}, f32[1,128,512]{2,1,0:T(8,128)}, /*index=5*/f32[1,128,512]{2,1,0:T(8,128)}) fusion(f32[2,128,512]{2,1,0:T(8,128)} %convert_add_fusion, f32[768,512]{1,0:T(8,128)S(1)} %copy-done.5, f32[]{:T(128)S(6)} %select_n.115, ...), kind=kLoop, calls=%fused_computation.35 | loop fusion | flops 917504 | bytes 5767176 | tf_op jit(solution)/shard_map/add | solution.py:338
  213.3 5.1 %multiply_reduce_fusion = (f32[4,128,512]{2,1,0:T(8,128)S(1)}, f32[4,128,512]{2,1,0:T(8,128)S(1)}) fusion(f32[16,128,512]{2,1,0:T(8,128)} %get-tuple-element.34, f32[16,4]{1,0:T(8,128)S(1)} %compare_convert_fusion.1, f32[16,128,512]{2,1,0:T(8,128)S(1)} %copy-done.4), kind=kLoop, calls=%fused_computation | loop fusion | flops 16252928 | bytes 10486016 | tf_op jit(solution)/shard_map/reduce_sum | solution.py:330
  218.4 2.2 fusion
  220.5 2.1 fusion.1
  222.6 16.8 %all-to-all-done.1 = bf16[16,128,512]{2,1,0:T(8,128)(2,1)S(1)} async-done(((bf16[16,128,512]{2,1,0:T(8,128)(2,1)}), bf16[16,128,512]{2,1,0:T(8,128)(2,1)S(1)}, u32[]{:S(2)}, u32[]{:S(2)}) %all-to-all-start.1) | async-done | bytes 2097184 | tf_op jit(solution)/shard_map/all_to_all | solution.py:323
  240.0 1.4 multiply_reduce_fusion.2
  241.5 1.3 fusion.2
  (119 shorter events, 30.0 us)
Async XLA Ops:
  0.6 4.4 %copy-start = (bf16[512,512]{1,0:T(8,128)(2,1)S(1)}, bf16[512,512]{1,0:T(8,128)(2,1)}, u32[]{:S(2)}) copy-start(bf16[512,512]{1,0:T(8,128)(2,1)} %do_ref.5) | copy-start | bytes 1572868
  0.6 4.4 %copy-start.1 = (bf16[512,512]{1,0:T(8,128)(2,1)S(1)}, bf16[512,512]{1,0:T(8,128)(2,1)}, u32[]{:S(2)}) copy-start(bf16[512,512]{1,0:T(8,128)(2,1)} %q_ref.5) | copy-start | bytes 1572868
  9.0 6.7 %copy-start.2 = (bf16[512,512]{1,0:T(8,128)(2,1)S(1)}, bf16[512,512]{1,0:T(8,128)(2,1)}, u32[]{:S(2)}) copy-start(bf16[512,512]{1,0:T(8,128)(2,1)} %k_ref.3) | copy-start | bytes 1572868
  9.0 6.7 %copy-start.3 = (bf16[512,512]{1,0:T(8,128)(2,1)S(1)}, bf16[512,512]{1,0:T(8,128)(2,1)}, u32[]{:S(2)}) copy-start(bf16[512,512]{1,0:T(8,128)(2,1)} %v_ref.3) | copy-start | bytes 1572868
  9.0 17.1 %copy-start.12 = (bf16[4,512]{1,0:T(4,128)(2,1)S(1)}, bf16[4,512]{1,0:T(4,128)(2,1)}, u32[]{:S(2)}) copy-start(bf16[4,512]{1,0:T(4,128)(2,1)} %param.12) | copy-start | bytes 12292
  9.0 149.5 %all-to-all-start = ((bf16[16,272,512]{2,1,0:T(8,128)(2,1)}), bf16[16,272,512]{2,1,0:T(8,128)(2,1)}, u32[]{:S(2)}, u32[]{:S(2)}) async-start(bf16[16,272,512]{2,1,0:T(8,128)(2,1)} %select_add_fusion), calls=%async_computation | async-start | bytes 8912896 | tf_op jit(solution)/shard_map/all_to_all | solution.py:311
  15.8 11.5 %collective-permute-start.2 = (bf16[2,128,512]{2,1,0:T(8,128)(2,1)S(1)}, bf16[2,128,512]{2,1,0:T(8,128)(2,1)S(1)}, u32[]{:S(2)}, u32[]{:S(2)}) collective-permute-start(bf16[2,128,512]{2,1,0:T(8,128)(2,1)S(1)} %maximum_select_fusion), channel_id=1, source_target_pairs={{0,24},{1,25}} | collective-permute-start | bytes 786440 | tf_op jit(solution)/shard_map/ppermute | solution.py:29
  16.5 10.8 %collective-permute-start.1 = (bf16[2,128,512]{2,1,0:T(8,128)(2,1)S(1)}, bf16[2,128,512]{2,1,0:T(8,128)(2,1)S(1)}, u32[]{:S(2)}, u32[]{:S(2)}) collective-permute-start(bf16[2,128,512]{2,1,0:T(8,128)(2,1)S(1)} %maximum_select_fusion), channel_id=1, source_target_pairs={{0,16},{1,17}} | collective-permute-start | bytes 786440 | tf_op jit(solution)/shard_map/ppermute | solution.py:29
  17.2 10.1 %collective-permute-start = (bf16[2,128,512]{2,1,0:T(8,128)(2,1)S(1)}, bf16[2,128,512]{2,1,0:T(8,128)(2,1)S(1)}, u32[]{:S(2)}, u32[]{:S(2)}) collective-permute-start(bf16[2,128,512]{2,1,0:T(8,128)(2,1)S(1)} %maximum_select_fusion), channel_id=1, source_target_pairs={{0,8},{1,9}} | collective-permute-start | bytes 786440 | tf_op jit(solution)/shard_map/ppermute | solution.py:29
  17.9 98.6 %collective-permute-start.7 = (bf16[2,128,512]{2,1,0:T(8,128)(2,1)S(1)}, bf16[2,128,512]{2,1,0:T(8,128)(2,1)S(1)}, u32[]{:S(2)}, u32[]{:S(2)}) collective-permute-start(bf16[2,128,512]{2,1,0:T(8,128)(2,1)S(1)} %pad_maximum_fusion.5), channel_id=1, source_target_pairs={{2,0},{4,2},{6,4},{8,6},{10,8},{12,10},{14,12},{16,14},{18,16},{20... | collective-permute-start | bytes 786440 | tf_op jit(solution)/shard_map/ppermute | solution.py:58
  20.2 96.3 %collective-permute-start.6 = (bf16[2,128,512]{2,1,0:T(8,128)(2,1)S(1)}, bf16[2,128,512]{2,1,0:T(8,128)(2,1)S(1)}, u32[]{:S(2)}, u32[]{:S(2)}) collective-permute-start(bf16[2,128,512]{2,1,0:T(8,128)(2,1)S(1)} %pad_maximum_fusion.4), channel_id=1, source_target_pairs={{0,2},{2,4},{4,6},{6,8},{8,10},{10,12},{12,14},{14,16},{16,18},{18... | collective-permute-start | bytes 786440 | tf_op jit(solution)/shard_map/ppermute | solution.py:58
  27.3 90.1 %collective-permute-start.5 = (bf16[2,128,512]{2,1,0:T(8,128)(2,1)S(1)}, bf16[2,128,512]{2,1,0:T(8,128)(2,1)S(1)}, u32[]{:S(2)}, u32[]{:S(2)}) collective-permute-start(bf16[2,128,512]{2,1,0:T(8,128)(2,1)S(1)} %add_add_fusion.1), channel_id=1, source_target_pairs={{0,6},{8,14},{16,22},{24,30},{1,7},{9,15},{17,23},{25,31}} | collective-permute-start | bytes 786440 | tf_op jit(solution)/shard_map/ppermute | solution.py:29
  28.6 88.8 %collective-permute-start.4 = (bf16[2,128,512]{2,1,0:T(8,128)(2,1)S(1)}, bf16[2,128,512]{2,1,0:T(8,128)(2,1)S(1)}, u32[]{:S(2)}, u32[]{:S(2)}) collective-permute-start(bf16[2,128,512]{2,1,0:T(8,128)(2,1)S(1)} %add_add_fusion.1), channel_id=1, source_target_pairs={{0,4},{8,12},{16,20},{24,28},{1,5},{9,13},{17,21},{25,29}} | collective-permute-start | bytes 786440 | tf_op jit(solution)/shard_map/ppermute | solution.py:29
  29.3 88.1 %collective-permute-start.3 = (bf16[2,128,512]{2,1,0:T(8,128)(2,1)S(1)}, bf16[2,128,512]{2,1,0:T(8,128)(2,1)S(1)}, u32[]{:S(2)}, u32[]{:S(2)}) collective-permute-start(bf16[2,128,512]{2,1,0:T(8,128)(2,1)S(1)} %add_add_fusion.1), channel_id=1, source_target_pairs={{0,2},{8,10},{16,18},{24,26},{1,3},{9,11},{17,19},{25,27}} | collective-permute-start | bytes 786440 | tf_op jit(solution)/shard_map/ppermute | solution.py:29
  133.9 12.8 %collective-permute-start.10 = (bf16[2,128,512]{2,1,0:T(8,128)(2,1)S(1)}, bf16[2,128,512]{2,1,0:T(8,128)(2,1)S(1)}, u32[]{:S(2)}, u32[]{:S(2)}) collective-permute-start(bf16[2,128,512]{2,1,0:T(8,128)(2,1)S(1)} %fusion.3), channel_id=1, source_target_pairs={{6,0},{14,8},{22,16},{30,24},{7,1},{15,9},{23,17},{31,25}} | collective-permute-start | bytes 786440 | tf_op jit(solution)/shard_map/ppermute | solution.py:45
  135.2 11.5 %collective-permute-start.9 = (bf16[2,128,512]{2,1,0:T(8,128)(2,1)S(1)}, bf16[2,128,512]{2,1,0:T(8,128)(2,1)S(1)}, u32[]{:S(2)}, u32[]{:S(2)}) collective-permute-start(bf16[2,128,512]{2,1,0:T(8,128)(2,1)S(1)} %fusion.3), channel_id=1, source_target_pairs={{4,0},{12,8},{20,16},{28,24},{5,1},{13,9},{21,17},{29,25}} | collective-permute-start | bytes 786440 | tf_op jit(solution)/shard_map/ppermute | solution.py:45
  135.9 10.8 %collective-permute-start.8 = (bf16[2,128,512]{2,1,0:T(8,128)(2,1)S(1)}, bf16[2,128,512]{2,1,0:T(8,128)(2,1)S(1)}, u32[]{:S(2)}, u32[]{:S(2)}) collective-permute-start(bf16[2,128,512]{2,1,0:T(8,128)(2,1)S(1)} %fusion.3), channel_id=1, source_target_pairs={{2,0},{10,8},{18,16},{26,24},{3,1},{11,9},{19,17},{27,25}} | collective-permute-start | bytes 786440 | tf_op jit(solution)/shard_map/ppermute | solution.py:45
  146.9 10.5 %collective-permute-start.13 = (bf16[2,128,512]{2,1,0:T(8,128)(2,1)S(1)}, bf16[2,128,512]{2,1,0:T(8,128)(2,1)S(1)}, u32[]{:S(2)}, u32[]{:S(2)}) collective-permute-start(bf16[2,128,512]{2,1,0:T(8,128)(2,1)S(1)} %fusion.19), channel_id=1, source_target_pairs={{24,0},{25,1}} | collective-permute-start | bytes 786440 | tf_op jit(solution)/shard_map/ppermute | solution.py:45
  147.6 9.8 %collective-permute-start.12 = (bf16[2,128,512]{2,1,0:T(8,128)(2,1)S(1)}, bf16[2,128,512]{2,1,0:T(8,128)(2,1)S(1)}, u32[]{:S(2)}, u32[]{:S(2)}) collective-permute-start(bf16[2,128,512]{2,1,0:T(8,128)(2,1)S(1)} %fusion.19), channel_id=1, source_target_pairs={{16,0},{17,1}} | collective-permute-start | bytes 786440 | tf_op jit(solution)/shard_map/ppermute | solution.py:45
  148.3 9.2 %collective-permute-start.11 = (bf16[2,128,512]{2,1,0:T(8,128)(2,1)S(1)}, bf16[2,128,512]{2,1,0:T(8,128)(2,1)S(1)}, u32[]{:S(2)}, u32[]{:S(2)}) collective-permute-start(bf16[2,128,512]{2,1,0:T(8,128)(2,1)S(1)} %fusion.19), channel_id=1, source_target_pairs={{8,0},{9,1}} | collective-permute-start | bytes 786440 | tf_op jit(solution)/shard_map/ppermute | solution.py:45
  150.0 33.8 %collective-permute-start.14 = (bf16[2,128,512]{2,1,0:T(8,128)(2,1)S(1)}, bf16[2,128,512]{2,1,0:T(8,128)(2,1)S(1)}, u32[]{:S(2)}, u32[]{:S(2)}) collective-permute-start(bf16[2,128,512]{2,1,0:T(8,128)(2,1)S(1)} %pad_maximum_fusion.6), channel_id=1, source_target_pairs={{0,2},{2,4},{4,6},{6,8},{8,10},{10,12},{12,14},{14,16},{16,18},{18... | collective-permute-start | bytes 786440 | tf_op jit(solution)/shard_map/ppermute | solution.py:58
  155.5 28.4 %collective-permute-start.15 = (bf16[2,128,512]{2,1,0:T(8,128)(2,1)S(1)}, bf16[2,128,512]{2,1,0:T(8,128)(2,1)S(1)}, u32[]{:S(2)}, u32[]{:S(2)}) collective-permute-start(bf16[2,128,512]{2,1,0:T(8,128)(2,1)S(1)} %pad_maximum_fusion.7), channel_id=1, source_target_pairs={{2,0},{4,2},{6,4},{8,6},{10,8},{12,10},{14,12},{16,14},{18,16},{20... | collective-permute-start | bytes 786440 | tf_op jit(solution)/shard_map/ppermute | solution.py:58
  183.9 26.3 %copy-start.9 = (f32[256,512]{1,0:T(8,128)S(1)}, f32[256,512]{1,0:T(8,128)}, u32[]{:S(2)}) copy-start(f32[256,512]{1,0:T(8,128)} %get-tuple-element.21) | copy-start | bytes 1572868
  184.6 54.8 %all-to-all-start.1 = ((bf16[16,128,512]{2,1,0:T(8,128)(2,1)}), bf16[16,128,512]{2,1,0:T(8,128)(2,1)S(1)}, u32[]{:S(2)}, u32[]{:S(2)}) async-start(bf16[16,128,512]{2,1,0:T(8,128)(2,1)} %get-tuple-element.27), calls=%async_computation.1 | async-start | bytes 4194304 | tf_op jit(solution)/shard_map/all_to_all | solution.py:323
  (7 other events, 14.6 us)

commit v18 on v13

--- a/solution.py
+++ b/solution.py
@@ -11,7 +11,7 @@
 WINDOW = 2
 GLOBAL = 1
 RANDOM = 3
-STAT_ROWS = 16
+STAT_ROWS = 8
 
 
 RADIX = 4

time: 241 us -> 238 us (0.988)
  waiting for transfers between devices: 103 us -> 100 us
    ppermute x4, waiting for transfers between devices: 86.5 us -> 83.6 us  [shift(): return lax.ppermute(array, axis, pairs)]
  transfers between devices with their start and end apart: 18 -> 18, of which waited for: 2 -> 2; matrix products, arithmetic and copies ran while one was open for 13% -> 13% of each run, Pallas kernels for 23% -> 24%
where the time goes in v18:
time: 238 us; the launch traced here: 236 us
  waiting for transfers between devices  100 us (42%)
  Pallas kernels  55.5 us (23%)
  starting transfers between devices  35.1 us (15%)
  other arithmetic  34 us (14%)
  local copies, waits for them, and re-layouts  9.79 us (4%)
    ppermute x4, waiting for transfers between devices, shift(): return lax.ppermute(array, axis, pairs)  83.6 us
    pallas_call x3, Pallas kernels, list_pairs(): pl.pallas_call(list_kernel, grid_spec=grid_spec, out_shape=[jax.ShapeDtyp...  34.1 us
    pallas_call x1, Pallas kernels, rand_pairs(): pl.pallas_call(functools.partial(rand_kernel, heads), grid_spec=grid_spec...  21.4 us
    all_to_all x1, waiting for transfers between devices, shards(): lax.all_to_all(dq_rand, 'ctx', split_axis=0, concat_axis=0, tiled=True)  16.8 us
    ppermute x4, starting transfers between devices, shift(): return lax.ppermute(array, axis, pairs)  13.8 us
    all_to_all x1, starting transfers between devices, shards(): lax.all_to_all(routed, 'ctx', split_axis=0, concat_axis=0, tiled=True)  6.69 us
    all_to_all x1, starting transfers between devices, shards(): lax.all_to_all(dq_rand, 'ctx', split_axis=0, concat_axis=0, tiled=True)  5.27 us
    reduce_sum x1, other arithmetic, shards(): rand_value = jnp.sum(choose[:, :, None, None] * dv_rand[:, None], axis=0)  5.09 us
  transfers between devices with their start and end apart: 18, of which 2 were waited for; matrix products, arithmetic and copies ran while one was open for 13% of the time, Pallas kernels for 24%

profile of v18, /device:TPU:11, one launch (start us, length us, event | category | flops | bytes accessed | tf_op | source)
XLA Modules:
  0.0 236.0 jit_solution(12258786121728832797)
XLA Ops:
  2.4 1.3 convert_multiply_fusion
  5.8 3.0 %select_add_fusion = bf16[16,264,512]{2,1,0:T(8,128)(2,1)} fusion(pred[16]{0:T(512)(128)(4,1)S(1)} %get-tuple-element.73, pred[16]{0:T(512)(128)(4,1)S(1)} %get-tuple-element.74, pred[16]{0:T(512)(128)(4,1)S(1)} %get-tuple-element.75, pred[16]{0:T(512)(128)(4,1)S(1)} %get-tuple-element.72, bf16[264,512]{1,0:T(8,128)(2,1)S(1)} %get-tuple-element.47, ...), kind=kLoop, calls=%fused_computation.3 | loop fusion | flops 17301504 | bytes 5415232 | tf_op jit(solution)/shard_map/add | solution.py:310
  8.8 6.7 %all-to-all-start = ((bf16[16,264,512]{2,1,0:T(8,128)(2,1)}), bf16[16,264,512]{2,1,0:T(8,128)(2,1)}, u32[]{:S(2)}, u32[]{:S(2)}) async-start(bf16[16,264,512]{2,1,0:T(8,128)(2,1)} %select_add_fusion), calls=%async_computation | async-start | bytes 8650752 | tf_op jit(solution)/shard_map/all_to_all | solution.py:311
  17.7 2.3 collective-permute-start.7
  20.0 4.2 %collective-permute-start.6 = (bf16[2,128,512]{2,1,0:T(8,128)(2,1)S(1)}, bf16[2,128,512]{2,1,0:T(8,128)(2,1)S(1)}, u32[]{:S(2)}, u32[]{:S(2)}) collective-permute-start(bf16[2,128,512]{2,1,0:T(8,128)(2,1)S(1)} %pad_maximum_fusion.4), channel_id=1, source_target_pairs={{0,2},{2,4},{4,6},{6,8},{8,10},{10,12},{12,14},{14,16},{16,18},{18... | collective-permute-start | bytes 786440 | tf_op jit(solution)/shard_map/ppermute | solution.py:58
  29.9 83.5 %collective-permute-done.7 = bf16[2,128,512]{2,1,0:T(8,128)(2,1)S(1)} collective-permute-done((bf16[2,128,512]{2,1,0:T(8,128)(2,1)S(1)}, bf16[2,128,512]{2,1,0:T(8,128)(2,1)S(1)}, u32[]{:S(2)}, u32[]{:S(2)}) %collective-permute-start.7) | collective-permute-done | bytes 262176 | tf_op jit(solution)/shard_map/ppermute | solution.py:58
  116.9 11.4 %shard_map.95 = (f32[512,512]{1,0:T(8,128)}, f32[512,512]{1,0:T(8,128)}, f32[512,512]{1,0:T(8,128)}) custom-call(s32[4]{0:T(128)} %iota.37.qin.qout, s32[4]{0:T(128)} %iota.37.qin.qout, s32[4]{0:T(128)} %broadcast_25_first.2.first, s32[4]{0:T(128)} %broadcast_24_ktab.2.ktab, s32[4]{0:T(128)} %compare_convert_fusion.2.mtab, bf16[512,512]{1,0:T(8,128)(2,1)} %q_ref.5, ...), custom_call_target="tpu_custom_call" | custom-call | tf_op jit(solution)/shard_map/pallas_call | solution.py:154
  128.2 1.3 reduce_sum.66
  129.5 1.3 reduce_sum.65
  130.9 1.3 collective-permute-start.10
  135.7 7.0 %shard_map.96 = (f32[256,512]{1,0:T(8,128)}, f32[256,512]{1,0:T(8,128)}, f32[256,512]{1,0:T(8,128)}) custom-call(s32[2]{0:T(128)} %iota_multiply_fusion.qin, s32[2]{0:T(128)} %iota.42.qout, s32[2]{0:T(128)} %broadcast_26_first.2.first, s32[2]{0:T(128)} %get-tuple-element.79.ktab, s32[2]{0:T(128)} %get-tuple-element.80.mtab, bf16[512,512]{1,0:T(8,128)(2,1)} %q_ref.5, ...), custom_call_target="tpu_custom_call" | custom-call | tf_op jit(solution)/shard_map/pallas_call | solution.py:154
  147.1 5.4 %collective-permute-start.14 = (bf16[2,128,512]{2,1,0:T(8,128)(2,1)S(1)}, bf16[2,128,512]{2,1,0:T(8,128)(2,1)S(1)}, u32[]{:S(2)}, u32[]{:S(2)}) collective-permute-start(bf16[2,128,512]{2,1,0:T(8,128)(2,1)S(1)} %pad_maximum_fusion.6), channel_id=1, source_target_pairs={{0,2},{2,4},{4,6},{6,8},{8,10},{10,12},{12,14},{14,16},{16,18},{18... | collective-permute-start | bytes 786440 | tf_op jit(solution)/shard_map/ppermute | solution.py:58
  152.5 1.9 collective-permute-start.15
  157.7 21.4 %shard_map.97 = (bf16[16,128,512]{2,1,0:T(8,128)(2,1)}, f32[16,128,512]{2,1,0:T(8,128)}, f32[16,128,512]{2,1,0:T(8,128)}) custom-call(s32[16]{0:T(128)} %add_maximum_fusion.ktab, s32[16]{0:T(128)} %compare_convert_fusion.1.mtab, bf16[16,264,512]{2,1,0:T(8,128)(2,1)} %all-to-all-done.q_ref.do_ref.st_ref, ...), custom_call_target="tpu_custom_call" | custom-call | tf_op jit(solution)/shard_map/pallas_call | solution.py:186
  179.9 5.3 %all-to-all-start.1 = ((bf16[16,128,512]{2,1,0:T(8,128)(2,1)}), bf16[16,128,512]{2,1,0:T(8,128)(2,1)S(1)}, u32[]{:S(2)}, u32[]{:S(2)}) async-start(bf16[16,128,512]{2,1,0:T(8,128)(2,1)} %get-tuple-element.27), calls=%async_computation.1 | async-start | bytes 4194304 | tf_op jit(solution)/shard_map/all_to_all | solution.py:321
  185.3 15.7 %shard_map.94 = (f32[512,512]{1,0:T(8,128)}, f32[768,512]{1,0:T(8,128)}, f32[768,512]{1,0:T(8,128)}) custom-call(s32[6]{0:T(128)} %constant.33.clone.1.qin.qout, s32[6]{0:T(128)} %constant.33.clone.1.qin.qout, s32[6]{0:T(128)} %constant.34.clone.1.first, s32[6]{0:T(128)} %constant.35.clone.1.ktab, s32[6]{0:T(128)} %constant.36.clone.1.mtab, ...), custom_call_target="tpu_custom_call" | custom-call | tf_op jit(solution)/shard_map/pallas_call | solution.py:154
  201.1 2.2 add_bitcast_fusion
  203.7 2.7 %bitcast_add_fusion.3 = (f32[1,128,512]{2,1,0:T(8,128)}, f32[1,128,512]{2,1,0:T(8,128)}, f32[1,128,512]{2,1,0:T(8,128)}, f32[1,128,512]{2,1,0:T(8,128)S(1)}, f32[1,128,512]{2,1,0:T(8,128)}, /*index=5*/f32[1,128,512]{2,1,0:T(8,128)}) fusion(f32[2,128,512]{2,1,0:T(8,128)} %convert_add_fusion, f32[768,512]{1,0:T(8,128)S(1)} %copy-done.5, f32[]{:T(128)S(6)} %select_n.103, ...), kind=kLoop, calls=%fused_computation.35 | loop fusion | flops 917504 | bytes 5767176 | tf_op jit(solution)/shard_map/add | solution.py:336
  206.4 5.1 %multiply_reduce_fusion = (f32[4,128,512]{2,1,0:T(8,128)S(1)}, f32[4,128,512]{2,1,0:T(8,128)S(1)}) fusion(f32[16,128,512]{2,1,0:T(8,128)} %get-tuple-element.34, f32[16,4]{1,0:T(8,128)S(1)} %compare_convert_fusion, f32[16,128,512]{2,1,0:T(8,128)S(1)} %copy-done.4), kind=kLoop, calls=%fused_computation | loop fusion | flops 16252928 | bytes 10486016 | tf_op jit(solution)/shard_map/reduce_sum | solution.py:328
  211.5 2.2 fusion
  213.7 2.1 fusion.1
  215.8 16.8 %all-to-all-done.1 = bf16[16,128,512]{2,1,0:T(8,128)(2,1)S(1)} async-done(((bf16[16,128,512]{2,1,0:T(8,128)(2,1)}), bf16[16,128,512]{2,1,0:T(8,128)(2,1)S(1)}, u32[]{:S(2)}, u32[]{:S(2)}) %all-to-all-start.1) | async-done | bytes 2097184 | tf_op jit(solution)/shard_map/all_to_all | solution.py:321
  233.1 1.4 multiply_reduce_fusion.2
  234.7 1.3 fusion.2
  (114 shorter events, 28.0 us)
Async XLA Ops:
  0.6 4.4 %copy-start = (bf16[512,512]{1,0:T(8,128)(2,1)S(1)}, bf16[512,512]{1,0:T(8,128)(2,1)}, u32[]{:S(2)}) copy-start(bf16[512,512]{1,0:T(8,128)(2,1)} %do_ref.5) | copy-start | bytes 1572868
  0.6 4.4 %copy-start.1 = (bf16[512,512]{1,0:T(8,128)(2,1)S(1)}, bf16[512,512]{1,0:T(8,128)(2,1)}, u32[]{:S(2)}) copy-start(bf16[512,512]{1,0:T(8,128)(2,1)} %q_ref.5) | copy-start | bytes 1572868
  8.8 6.7 %copy-start.2 = (bf16[512,512]{1,0:T(8,128)(2,1)S(1)}, bf16[512,512]{1,0:T(8,128)(2,1)}, u32[]{:S(2)}) copy-start(bf16[512,512]{1,0:T(8,128)(2,1)} %k_ref.3) | copy-start | bytes 1572868
  8.8 6.7 %copy-start.3 = (bf16[512,512]{1,0:T(8,128)(2,1)S(1)}, bf16[512,512]{1,0:T(8,128)(2,1)}, u32[]{:S(2)}) copy-start(bf16[512,512]{1,0:T(8,128)(2,1)} %v_ref.3) | copy-start | bytes 1572868
  8.8 17.2 %copy-start.12 = (bf16[4,512]{1,0:T(4,128)(2,1)S(1)}, bf16[4,512]{1,0:T(4,128)(2,1)}, u32[]{:S(2)}) copy-start(bf16[4,512]{1,0:T(4,128)(2,1)} %param.12) | copy-start | bytes 12292
  8.8 146.7 %all-to-all-start = ((bf16[16,264,512]{2,1,0:T(8,128)(2,1)}), bf16[16,264,512]{2,1,0:T(8,128)(2,1)}, u32[]{:S(2)}, u32[]{:S(2)}) async-start(bf16[16,264,512]{2,1,0:T(8,128)(2,1)} %select_add_fusion), calls=%async_computation | async-start | bytes 8650752 | tf_op jit(solution)/shard_map/all_to_all | solution.py:311
  15.6 11.6 %collective-permute-start.2 = (bf16[2,128,512]{2,1,0:T(8,128)(2,1)S(1)}, bf16[2,128,512]{2,1,0:T(8,128)(2,1)S(1)}, u32[]{:S(2)}, u32[]{:S(2)}) collective-permute-start(bf16[2,128,512]{2,1,0:T(8,128)(2,1)S(1)} %maximum_select_fusion), channel_id=1, source_target_pairs={{0,24},{1,25}} | collective-permute-start | bytes 786440 | tf_op jit(solution)/shard_map/ppermute | solution.py:29
  16.3 10.9 %collective-permute-start.1 = (bf16[2,128,512]{2,1,0:T(8,128)(2,1)S(1)}, bf16[2,128,512]{2,1,0:T(8,128)(2,1)S(1)}, u32[]{:S(2)}, u32[]{:S(2)}) collective-permute-start(bf16[2,128,512]{2,1,0:T(8,128)(2,1)S(1)} %maximum_select_fusion), channel_id=1, source_target_pairs={{0,16},{1,17}} | collective-permute-start | bytes 786440 | tf_op jit(solution)/shard_map/ppermute | solution.py:29
  17.0 10.2 %collective-permute-start = (bf16[2,128,512]{2,1,0:T(8,128)(2,1)S(1)}, bf16[2,128,512]{2,1,0:T(8,128)(2,1)S(1)}, u32[]{:S(2)}, u32[]{:S(2)}) collective-permute-start(bf16[2,128,512]{2,1,0:T(8,128)(2,1)S(1)} %maximum_select_fusion), channel_id=1, source_target_pairs={{0,8},{1,9}} | collective-permute-start | bytes 786440 | tf_op jit(solution)/shard_map/ppermute | solution.py:29
  17.7 95.8 %collective-permute-start.7 = (bf16[2,128,512]{2,1,0:T(8,128)(2,1)S(1)}, bf16[2,128,512]{2,1,0:T(8,128)(2,1)S(1)}, u32[]{:S(2)}, u32[]{:S(2)}) collective-permute-start(bf16[2,128,512]{2,1,0:T(8,128)(2,1)S(1)} %pad_maximum_fusion.5), channel_id=1, source_target_pairs={{2,0},{4,2},{6,4},{8,6},{10,8},{12,10},{14,12},{16,14},{18,16},{20... | collective-permute-start | bytes 786440 | tf_op jit(solution)/shard_map/ppermute | solution.py:58
  20.0 93.5 %collective-permute-start.6 = (bf16[2,128,512]{2,1,0:T(8,128)(2,1)S(1)}, bf16[2,128,512]{2,1,0:T(8,128)(2,1)S(1)}, u32[]{:S(2)}, u32[]{:S(2)}) collective-permute-start(bf16[2,128,512]{2,1,0:T(8,128)(2,1)S(1)} %pad_maximum_fusion.4), channel_id=1, source_target_pairs={{0,2},{2,4},{4,6},{6,8},{8,10},{10,12},{12,14},{14,16},{16,18},{18... | collective-permute-start | bytes 786440 | tf_op jit(solution)/shard_map/ppermute | solution.py:58
  27.3 87.2 %collective-permute-start.5 = (bf16[2,128,512]{2,1,0:T(8,128)(2,1)S(1)}, bf16[2,128,512]{2,1,0:T(8,128)(2,1)S(1)}, u32[]{:S(2)}, u32[]{:S(2)}) collective-permute-start(bf16[2,128,512]{2,1,0:T(8,128)(2,1)S(1)} %add_add_fusion.1), channel_id=1, source_target_pairs={{0,6},{8,14},{16,22},{24,30},{1,7},{9,15},{17,23},{25,31}} | collective-permute-start | bytes 786440 | tf_op jit(solution)/shard_map/ppermute | solution.py:29
  28.6 85.9 %collective-permute-start.4 = (bf16[2,128,512]{2,1,0:T(8,128)(2,1)S(1)}, bf16[2,128,512]{2,1,0:T(8,128)(2,1)S(1)}, u32[]{:S(2)}, u32[]{:S(2)}) collective-permute-start(bf16[2,128,512]{2,1,0:T(8,128)(2,1)S(1)} %add_add_fusion.1), channel_id=1, source_target_pairs={{0,4},{8,12},{16,20},{24,28},{1,5},{9,13},{17,21},{25,29}} | collective-permute-start | bytes 786440 | tf_op jit(solution)/shard_map/ppermute | solution.py:29
  29.3 85.2 %collective-permute-start.3 = (bf16[2,128,512]{2,1,0:T(8,128)(2,1)S(1)}, bf16[2,128,512]{2,1,0:T(8,128)(2,1)S(1)}, u32[]{:S(2)}, u32[]{:S(2)}) collective-permute-start(bf16[2,128,512]{2,1,0:T(8,128)(2,1)S(1)} %add_add_fusion.1), channel_id=1, source_target_pairs={{0,2},{8,10},{16,18},{24,26},{1,3},{9,11},{17,19},{25,27}} | collective-permute-start | bytes 786440 | tf_op jit(solution)/shard_map/ppermute | solution.py:29
  130.9 12.8 %collective-permute-start.10 = (bf16[2,128,512]{2,1,0:T(8,128)(2,1)S(1)}, bf16[2,128,512]{2,1,0:T(8,128)(2,1)S(1)}, u32[]{:S(2)}, u32[]{:S(2)}) collective-permute-start(bf16[2,128,512]{2,1,0:T(8,128)(2,1)S(1)} %fusion.3), channel_id=1, source_target_pairs={{6,0},{14,8},{22,16},{30,24},{7,1},{15,9},{23,17},{31,25}} | collective-permute-start | bytes 786440 | tf_op jit(solution)/shard_map/ppermute | solution.py:45
  132.2 11.5 %collective-permute-start.9 = (bf16[2,128,512]{2,1,0:T(8,128)(2,1)S(1)}, bf16[2,128,512]{2,1,0:T(8,128)(2,1)S(1)}, u32[]{:S(2)}, u32[]{:S(2)}) collective-permute-start(bf16[2,128,512]{2,1,0:T(8,128)(2,1)S(1)} %fusion.3), channel_id=1, source_target_pairs={{4,0},{12,8},{20,16},{28,24},{5,1},{13,9},{21,17},{29,25}} | collective-permute-start | bytes 786440 | tf_op jit(solution)/shard_map/ppermute | solution.py:45
  132.9 10.8 %collective-permute-start.8 = (bf16[2,128,512]{2,1,0:T(8,128)(2,1)S(1)}, bf16[2,128,512]{2,1,0:T(8,128)(2,1)S(1)}, u32[]{:S(2)}, u32[]{:S(2)}) collective-permute-start(bf16[2,128,512]{2,1,0:T(8,128)(2,1)S(1)} %fusion.3), channel_id=1, source_target_pairs={{2,0},{10,8},{18,16},{26,24},{3,1},{11,9},{19,17},{27,25}} | collective-permute-start | bytes 786440 | tf_op jit(solution)/shard_map/ppermute | solution.py:45
  143.9 10.5 %collective-permute-start.13 = (bf16[2,128,512]{2,1,0:T(8,128)(2,1)S(1)}, bf16[2,128,512]{2,1,0:T(8,128)(2,1)S(1)}, u32[]{:S(2)}, u32[]{:S(2)}) collective-permute-start(bf16[2,128,512]{2,1,0:T(8,128)(2,1)S(1)} %fusion.19), channel_id=1, source_target_pairs={{24,0},{25,1}} | collective-permute-start | bytes 786440 | tf_op jit(solution)/shard_map/ppermute | solution.py:45
  144.6 9.8 %collective-permute-start.12 = (bf16[2,128,512]{2,1,0:T(8,128)(2,1)S(1)}, bf16[2,128,512]{2,1,0:T(8,128)(2,1)S(1)}, u32[]{:S(2)}, u32[]{:S(2)}) collective-permute-start(bf16[2,128,512]{2,1,0:T(8,128)(2,1)S(1)} %fusion.19), channel_id=1, source_target_pairs={{16,0},{17,1}} | collective-permute-start | bytes 786440 | tf_op jit(solution)/shard_map/ppermute | solution.py:45
  145.3 9.2 %collective-permute-start.11 = (bf16[2,128,512]{2,1,0:T(8,128)(2,1)S(1)}, bf16[2,128,512]{2,1,0:T(8,128)(2,1)S(1)}, u32[]{:S(2)}, u32[]{:S(2)}) collective-permute-start(bf16[2,128,512]{2,1,0:T(8,128)(2,1)S(1)} %fusion.19), channel_id=1, source_target_pairs={{8,0},{9,1}} | collective-permute-start | bytes 786440 | tf_op jit(solution)/shard_map/ppermute | solution.py:45
  147.1 32.1 %collective-permute-start.14 = (bf16[2,128,512]{2,1,0:T(8,128)(2,1)S(1)}, bf16[2,128,512]{2,1,0:T(8,128)(2,1)S(1)}, u32[]{:S(2)}, u32[]{:S(2)}) collective-permute-start(bf16[2,128,512]{2,1,0:T(8,128)(2,1)S(1)} %pad_maximum_fusion.6), channel_id=1, source_target_pairs={{0,2},{2,4},{4,6},{6,8},{8,10},{10,12},{12,14},{14,16},{16,18},{18... | collective-permute-start | bytes 786440 | tf_op jit(solution)/shard_map/ppermute | solution.py:58
  152.5 26.7 %collective-permute-start.15 = (bf16[2,128,512]{2,1,0:T(8,128)(2,1)S(1)}, bf16[2,128,512]{2,1,0:T(8,128)(2,1)S(1)}, u32[]{:S(2)}, u32[]{:S(2)}) collective-permute-start(bf16[2,128,512]{2,1,0:T(8,128)(2,1)S(1)} %pad_maximum_fusion.7), channel_id=1, source_target_pairs={{2,0},{4,2},{6,4},{8,6},{10,8},{12,10},{14,12},{16,14},{18,16},{20... | collective-permute-start | bytes 786440 | tf_op jit(solution)/shard_map/ppermute | solution.py:58
  179.2 24.1 %copy-start.9 = (f32[256,512]{1,0:T(8,128)S(1)}, f32[256,512]{1,0:T(8,128)}, u32[]{:S(2)}) copy-start(f32[256,512]{1,0:T(8,128)} %get-tuple-element.21) | copy-start | bytes 1572868
  179.9 52.7 %all-to-all-start.1 = ((bf16[16,128,512]{2,1,0:T(8,128)(2,1)}), bf16[16,128,512]{2,1,0:T(8,128)(2,1)S(1)}, u32[]{:S(2)}, u32[]{:S(2)}) async-start(bf16[16,128,512]{2,1,0:T(8,128)(2,1)} %get-tuple-element.27), calls=%async_computation.1 | async-start | bytes 4194304 | tf_op jit(solution)/shard_map/all_to_all | solution.py:321
  (7 other events, 14.6 us)
